TPU v7x, 32 devices: a whole 2x2x4 slice. The times are simulated.
32 devices in a mesh: grid: 8 (over y, x, core), band: 4 (over z).
Axes of the slice: x: 2, y: 2, z: 4, core: 2. Of those that a mesh axis runs over, the one named last changes fastest.
Arguments:
- occupied: bfloat16 [1024, 32, 24, 128], P('band', 'grid'), may hold values from -6 to 6
- potential: float32 [32, 24, 128], P('grid'), may hold values from 0.2 to 4
- shifts: float32 [64], P('band'), may hold values from 0.5 to 4
- source_term: float32 [64, 32, 24, 128], P('band', 'grid'), may hold values from -125 to 125
Outputs:
- solution: float32 [64, 32, 24, 128], P('band', 'grid')
- residual: float32 [64, 32, 24, 128], P('band', 'grid')
All inputs are finite; a program needn't handle non-finite values.
Results may differ from a plain program's by a relative error of at most 0.022.
Values may be sent and summed in bfloat16 or wider, within the bound.
No kernel may reach another device: no remote copies, remote signals or barrier semaphores. Data moves between devices by JAX's collectives and lax.ppermute only.
A program may use at most 128 MiB of HBM per device.

v0:
```python
import math

import jax
import jax.numpy as jnp
from jax import lax
from jax.sharding import PartitionSpec as P

ITERS = 2


COEFFICIENTS = (-205.0 / 72.0, 8.0 / 5.0, -1.0 / 5.0, 8.0 / 315.0, -1.0 / 560.0)


def with_halo(shard, sides, width):
    for axis, dim in sides:
        peers, length = (lax.axis_size(axis), shard.shape[dim])
        up = [(i, (i + 1) % peers) for i in range(peers - 1)]
        down = [(j, i) for i, j in up]
        last = lax.slice_in_dim(shard, length - width, length, axis=dim)
        leading = lax.slice_in_dim(shard, 0, width, axis=dim)
        before = lax.ppermute(last, axis, up)
        after = lax.ppermute(leading, axis, down)
        shard = jnp.concatenate([before, shard, after], axis=dim)
    return shard


def second_sum(padded, extent_x, extent_y, extent_z):
    middle = padded[:, 4 : 4 + extent_x, 4 : 4 + extent_y, 4 : 4 + extent_z]
    summed = 3.0 * COEFFICIENTS[0] * middle
    for offset in range(1, 5):
        along_x = (
            padded[:, 4 + offset : 4 + offset + extent_x, 4 : 4 + extent_y, 4 : 4 + extent_z]
            + padded[:, 4 - offset : 4 - offset + extent_x, 4 : 4 + extent_y, 4 : 4 + extent_z]
        )
        along_y = (
            padded[:, 4 : 4 + extent_x, 4 + offset : 4 + offset + extent_y, 4 : 4 + extent_z]
            + padded[:, 4 : 4 + extent_x, 4 - offset : 4 - offset + extent_y, 4 : 4 + extent_z]
        )
        along_z = (
            padded[:, 4 : 4 + extent_x, 4 : 4 + extent_y, 4 + offset : 4 + offset + extent_z]
            + padded[:, 4 : 4 + extent_x, 4 : 4 + extent_y, 4 - offset : 4 - offset + extent_z]
        )
        summed = (
            summed
            + COEFFICIENTS[offset] * along_x
            + COEFFICIENTS[offset] * along_y
            + COEFFICIENTS[offset] * along_z
        )
    return summed


def inner_product(first_field, second_field):
    return jnp.sum(first_field * second_field, axis=(1, 2, 3))


def expand(vector):
    return vector[:, None, None, None]


def body(occupied, potential, shifts, source_term):
    local_bands, width_x, width_y, width_z = source_term.shape
    local_occupied = occupied.shape[0]
    band_count = lax.axis_size("band")
    local_cells = width_x * width_y * width_z
    weight_scale = 2.0 / math.sqrt(
        local_occupied * band_count * local_cells * lax.axis_size("grid")
    )
    occupied_rows = occupied.reshape(local_occupied, local_cells)
    potential_shift = potential[None] + shifts[:, None, None, None]
    solution = jnp.zeros_like(source_term)
    residual = source_term
    direction = source_term
    norm_now = lax.psum(inner_product(source_term, source_term), "grid")
    for iteration in range(ITERS):
        padded = with_halo(direction.astype(jnp.bfloat16), (("grid", 1),), 4).astype(
            direction.dtype
        )
        padded = jnp.pad(padded, ((0, 0), (0, 0), (4, 4), (4, 4)))
        kinetic = -0.5 * second_sum(padded, width_x, width_y, width_z)
        rounded = direction.astype(jnp.bfloat16).reshape(local_bands, local_cells)
        partial_margin = lax.dot_general(
            occupied_rows,
            lax.all_gather(rounded, "band", axis=0, tiled=True),
            (((1,), (1,)), ((), ())),
            preferred_element_type=jnp.float32,
        )
        margins = lax.psum(partial_margin, "grid")
        scaled = (margins * weight_scale).astype(jnp.bfloat16)
        projected = lax.psum_scatter(
            lax.dot_general(
                scaled, occupied_rows, (((0,), (0,)), ((), ())), preferred_element_type=jnp.float32
            ).astype(jnp.bfloat16),
            "band",
            scatter_dimension=0,
            tiled=True,
        ).astype(jnp.float32)
        applied = kinetic + potential_shift * direction + projected.reshape(direction.shape)
        curvature = lax.psum(inner_product(direction, applied), "grid")
        step_size = norm_now / curvature
        solution = solution + expand(step_size) * direction
        residual = residual - expand(step_size) * applied
        if iteration + 1 < ITERS:
            norm_next = lax.psum(inner_product(residual, residual), "grid")
            direction = residual + expand(norm_next / norm_now) * direction
            norm_now = norm_next
    return (solution, residual)


def solution(mesh):
    in_specs = (
        P("band", "grid", None, None),
        P("grid", None, None),
        P("band"),
        P("band", "grid", None, None),
    )
    out_specs = (P("band", "grid", None, None), P("band", "grid", None, None))
    return jax.shard_map(body, mesh=mesh, in_specs=in_specs, out_specs=out_specs, check_vma=False)
```

profile of v0, /device:TPU:8, one launch (start us, length us, event | category | flops | bytes accessed | tf_op | source)
XLA Modules:
  0.0 342.5 jit_solution(5779249794180429042)
XLA Ops:
  7.2 0.0 all-gather.3.cloned.1.call-start
  7.2 1.2 convert_element_type.31
  8.4 0.9 copy.32
  9.3 0.0 all-gather.3.cloned.1.call-update
  9.3 0.0 all-reduce.6.cloned.1.call-start
  9.4 38.0 %all-gather.3.cloned.1.call-done = bf16[64,12288]{1,0:T(8,128)(2,1)} async-done(((bf16[16,12288]{1,0:T(8,128)(2,1)}), bf16[64,12288]{1,0:T(8,128)(2,1)}) %all-gather.3.cloned.1.call-update) | async-done | bytes 1572880 | tf_op jit(solution)/shard_map/all_gather | solution.py:83
  47.4 5.8 %fusion.4 = f32[256,64]{1,0:T(8,128)} fusion(bf16[64,12288]{1,0:T(8,128)(2,1)} %all-gather.3.cloned.1.call-done, bf16[32,8,96,128]{3,2,1,0:T(8,128)(2,1)} %bitcast.35), kind=kOutput, calls=%fused_computation.38 | convolution fusion | flops 402653184 | bytes 7929856 | tf_op jit(solution)/shard_map/dot_general | solution.py:81
  53.2 0.0 all-reduce.6.cloned.1.call-update
  53.3 0.0 reduce-scatter.3.cloned.1.call-start
  53.3 52.9 %all-reduce.6.cloned.1.call-done = f32[256,64]{1,0:T(8,128)} async-done(((f32[256,64]{1,0:T(8,128)}), f32[256,64]{1,0:T(8,128)}) %all-reduce.6.cloned.1.call-update) | async-done | bytes 65552 | tf_op jit(solution)/shard_map/psum | solution.py:87
  106.2 6.2 %convolution_convert_fusion.1 = bf16[64,12288]{1,0:T(8,128)(2,1)} fusion(bf16[32,8,96,128]{3,2,1,0:T(8,128)(2,1)} %bitcast.36, f32[256,64]{1,0:T(8,128)} %all-reduce.6.cloned.1.call-done), kind=kOutput, calls=%fused_computation.33 | convolution fusion | flops 403472384 | bytes 7929856 | tf_op jit(solution)/shard_map/dot_general | solution.py:90
  112.4 0.0 reduce-scatter.3.cloned.1.call-update
  112.4 0.0 copy-start
  112.4 0.0 copy-start.2
  112.4 0.0 all-gather.5.cloned.1.call-start
  112.5 1.4 collective-permute-start.1
  113.9 3.1 collective-permute-start
  117.0 0.0 collective-permute-done.1
  117.0 1.3 collective-permute-done
  118.3 0.2 maximum_convert_fusion
  118.5 27.7 %reduce-scatter.3.cloned.1.call-done = bf16[16,12288]{1,0:T(8,128)(2,1)} async-done(((bf16[64,12288]{1,0:T(8,128)(2,1)}), bf16[16,12288]{1,0:T(8,128)(2,1)}) %reduce-scatter.3.cloned.1.call-update) | async-done | bytes 393232 | tf_op jit(solution)/shard_map/reduce_scatter | solution.py:89
  146.1 1.0 convert_bitcast_fusion.1
  147.2 0.2 copy.8
  147.3 3.8 %multiply_reduce_fusion.2 = (f32[16]{0:T(128)S(1)}, f32[16]{0:T(128)S(1)}, f32[16,4,24,128]{3,2,1,0:T(8,128)}) fusion(f32[16,4,24,128]{3,2,1,0:T(8,128)S(1)} %copy-done, f32[16,4,24,128]{3,2,1,0:T(8,128)S(1)} %bitcast.41, f32[16]{0:T(128)S(1)} %copy-done.2, f32[4,24,128]{2,1,0:T(8,128)} %param.5, f32[16,12,24,128]{3,2,1,0:T(8,128)S(1)} %maximum_convert_fusion), kind=kLoop, calls=%fused_computation.135 | loop fusion | flops 9043936 | bytes 11846272 | tf_op jit(solution)/shard_map/reduce_sum | solution.py:53
  151.2 12.8 %all-reduce.2 = (f32[16]{0:T(128)S(1)}, f32[16]{0:T(128)S(1)}) all-reduce(f32[16]{0:T(128)S(1)} %get-tuple-element.3, f32[16]{0:T(128)S(1)} %get-tuple-element.2), channel_id=1, replica_groups=mesh['grid'=8,'band'=4] {'grid'}, use_global_device_ids=true, to_apply=%region_1.0 | all-reduce | flops 32 | bytes 256 | tf_op jit(solution)/shard_map/psum | solution.py:73
  164.0 1.4 multiply_reduce_fusion.1
  165.5 11.8 %psum.45 = f32[16]{0:T(128)S(1)} all-reduce(f32[16]{0:T(128)S(1)} %multiply_reduce_fusion.1), channel_id=1, replica_groups=mesh['grid'=8,'band'=4] {'grid'}, use_global_device_ids=true, to_apply=%region_7.8 | all-reduce | flops 16 | bytes 128 | tf_op jit(solution)/shard_map/psum | solution.py:103
  177.2 2.3 fusion.86
  179.5 0.9 copy.31
  180.4 0.0 all-gather.5.cloned.1.call-update
  180.4 0.0 all-reduce.8.cloned.1.call-start
  180.5 35.3 %all-gather.5.cloned.1.call-done = bf16[64,12288]{1,0:T(8,128)(2,1)} async-done(((bf16[16,12288]{1,0:T(8,128)(2,1)}), bf16[64,12288]{1,0:T(8,128)(2,1)}) %all-gather.5.cloned.1.call-update) | async-done | bytes 1572880 | tf_op jit(solution)/shard_map/all_gather | solution.py:83
  215.8 5.9 %fusion.10 = f32[256,64]{1,0:T(8,128)} fusion(bf16[64,12288]{1,0:T(8,128)(2,1)} %all-gather.5.cloned.1.call-done, bf16[32,8,96,128]{3,2,1,0:T(8,128)(2,1)} %bitcast.37), kind=kOutput, calls=%fused_computation.46 | convolution fusion | flops 402653184 | bytes 7929856 | tf_op jit(solution)/shard_map/dot_general | solution.py:81
  221.7 0.0 all-reduce.8.cloned.1.call-update
  221.7 0.0 reduce-scatter.5.cloned.1.call-start
  221.7 52.9 %all-reduce.8.cloned.1.call-done = f32[256,64]{1,0:T(8,128)} async-done(((f32[256,64]{1,0:T(8,128)}), f32[256,64]{1,0:T(8,128)}) %all-reduce.8.cloned.1.call-update) | async-done | bytes 65552 | tf_op jit(solution)/shard_map/psum | solution.py:87
  274.7 6.1 %convolution_convert_fusion = bf16[64,12288]{1,0:T(8,128)(2,1)} fusion(bf16[32,8,96,128]{3,2,1,0:T(8,128)(2,1)} %bitcast.38, f32[256,64]{1,0:T(8,128)} %all-reduce.8.cloned.1.call-done), kind=kOutput, calls=%fused_computation.32 | convolution fusion | flops 403472384 | bytes 7929856 | tf_op jit(solution)/shard_map/dot_general | solution.py:90
  280.8 0.0 reduce-scatter.5.cloned.1.call-update
  280.8 1.3 collective-permute-start.3
  282.1 3.1 collective-permute-start.2
  285.2 1.3 collective-permute-done.2
  286.5 0.2 maximum_convert_fusion.1
  286.7 27.9 %reduce-scatter.5.cloned.1.call-done = bf16[16,12288]{1,0:T(8,128)(2,1)} async-done(((bf16[64,12288]{1,0:T(8,128)(2,1)}), bf16[16,12288]{1,0:T(8,128)(2,1)}) %reduce-scatter.5.cloned.1.call-update) | async-done | bytes 393232 | tf_op jit(solution)/shard_map/reduce_scatter | solution.py:89
  314.5 1.1 convert_bitcast_fusion
  315.7 0.2 copy.10
  315.8 3.9 %multiply_reduce_fusion = (f32[16]{0:T(128)S(1)}, f32[16,4,24,128]{3,2,1,0:T(8,128)}) fusion(f32[16,4,24,128]{3,2,1,0:T(8,128)S(1)} %copy-done.1, f32[16,4,24,128]{3,2,1,0:T(8,128)S(1)} %bitcast.42, f32[16]{0:T(128)S(1)} %copy-done.2, f32[4,24,128]{2,1,0:T(8,128)} %param.5, f32[16,12,24,128]{3,2,1,0:T(8,128)S(1)} %maximum_convert_fusion.1), kind=kLoop, calls=%fused_computation.131 | loop fusion | flops 8650736 | bytes 11846208 | tf_op jit(solution)/shard_map/reduce_sum | solution.py:53
  319.7 12.8 %psum.47 = f32[16]{0:T(128)S(1)} all-reduce(f32[16]{0:T(128)S(1)} %get-tuple-element.6), channel_id=1, replica_groups=mesh['grid'=8,'band'=4] {'grid'}, use_global_device_ids=true, to_apply=%region_11.12 | all-reduce | flops 16 | bytes 128 | tf_op jit(solution)/shard_map/psum | solution.py:98
  332.5 3.2 multiply_subtract_fusion
  (8 shorter events, 0.0 us)
Async XLA Ops:
  7.2 40.2 %all-gather.3.cloned.1.call-start = ((), (), s32[]{:S(2)}) async-start(), calls=%async_computation.2 | async-start | bytes 1966080 | tf_op jit(solution)/shard_map/all_gather | solution.py:83
  9.3 96.9 %all-reduce.6.cloned.1.call-start = ((), (), s32[]{:S(2)}) async-start(), calls=%async_computation.3 | async-start | bytes 262144 | tf_op jit(solution)/shard_map/psum | solution.py:87
  53.3 92.8 %reduce-scatter.3.cloned.1.call-start = ((), (), s32[]{:S(2)}) async-start(), calls=%async_computation.4 | async-start | bytes 1966080 | tf_op jit(solution)/shard_map/reduce_scatter | solution.py:89
  112.4 34.9 %copy-start = (f32[16,4,24,128]{3,2,1,0:T(8,128)S(1)}, f32[16,4,24,128]{3,2,1,0:T(8,128)}, u32[]{:S(2)}) copy-start(f32[16,4,24,128]{3,2,1,0:T(8,128)} %param.7) | copy-start | bytes 2359300
  112.4 34.9 %copy-start.2 = (f32[16]{0:T(128)S(1)}, f32[16]{0:T(128)}, u32[]{:S(2)}) copy-start(f32[16]{0:T(128)} %param.6) | copy-start | bytes 196
  112.4 103.3 %all-gather.5.cloned.1.call-start = ((), (), s32[]{:S(2)}) async-start(), calls=%async_computation.5 | async-start | bytes 1966080 | tf_op jit(solution)/shard_map/all_gather | solution.py:83
  112.5 4.5 %collective-permute-start.1 = (bf16[16,4,24,128]{3,2,1,0:T(8,128)(2,1)S(1)}, bf16[16,4,24,128]{3,2,1,0:T(8,128)(2,1)S(1)}, u32[]{:S(2)}, u32[]{:S(2)}) collective-permute-start(bf16[16,4,24,128]{3,2,1,0:T(8,128)(2,1)S(1)} %convert_element_type.31), channel_id=1, source_target_pairs={{4,0},{8,4},{12,8},{16,12},{20,16},{24,20},{28,24},{5,1},{9,5},{13... | collective-permute-start | bytes 1179656 | tf_op jit(solution)/shard_map/ppermute | solution.py:22
  113.9 4.4 %collective-permute-start = (bf16[16,4,24,128]{3,2,1,0:T(8,128)(2,1)S(1)}, bf16[16,4,24,128]{3,2,1,0:T(8,128)(2,1)S(1)}, u32[]{:S(2)}, u32[]{:S(2)}) collective-permute-start(bf16[16,4,24,128]{3,2,1,0:T(8,128)(2,1)S(1)} %convert_element_type.31), channel_id=1, source_target_pairs={{0,4},{4,8},{8,12},{12,16},{16,20},{20,24},{24,28},{1,5},{5,9},{9,... | collective-permute-start | bytes 1179656 | tf_op jit(solution)/shard_map/ppermute | solution.py:21
  180.4 94.2 %all-reduce.8.cloned.1.call-start = ((), (), s32[]{:S(2)}) async-start(), calls=%async_computation.6 | async-start | bytes 262144 | tf_op jit(solution)/shard_map/psum | solution.py:87
  221.7 92.8 %reduce-scatter.5.cloned.1.call-start = ((), (), s32[]{:S(2)}) async-start(), calls=%async_computation.7 | async-start | bytes 1966080 | tf_op jit(solution)/shard_map/reduce_scatter | solution.py:89
  280.8 4.4 %collective-permute-start.3 = (bf16[16,4,24,128]{3,2,1,0:T(8,128)(2,1)S(1)}, bf16[16,4,24,128]{3,2,1,0:T(8,128)(2,1)S(1)}, u32[]{:S(2)}, u32[]{:S(2)}) collective-permute-start(bf16[16,4,24,128]{3,2,1,0:T(8,128)(2,1)S(1)} %get-tuple-element.8), channel_id=1, source_target_pairs={{4,0},{8,4},{12,8},{16,12},{20,16},{24,20},{28,24},{5,1},{9,5},{13... | collective-permute-start | bytes 1179656 | tf_op jit(solution)/shard_map/ppermute | solution.py:22
  282.1 4.4 %collective-permute-start.2 = (bf16[16,4,24,128]{3,2,1,0:T(8,128)(2,1)S(1)}, bf16[16,4,24,128]{3,2,1,0:T(8,128)(2,1)S(1)}, u32[]{:S(2)}, u32[]{:S(2)}) collective-permute-start(bf16[16,4,24,128]{3,2,1,0:T(8,128)(2,1)S(1)} %get-tuple-element.8), channel_id=1, source_target_pairs={{0,4},{4,8},{8,12},{12,16},{16,20},{20,24},{24,28},{1,5},{5,9},{9,... | collective-permute-start | bytes 1179656 | tf_op jit(solution)/shard_map/ppermute | solution.py:21
  314.5 1.3 copy-start.1
Sparse Core Ops, SparseCore 0:
  10.1 37.2 all-gather.2
  53.4 52.7 all-reduce.5
  112.5 33.5 reduce-scatter.2
  180.6 35.1 all-gather.4
  221.8 52.8 all-reduce.7
  280.9 33.5 reduce-scatter.4
where the time goes:
time: 346 us; the launch traced here: 343 us
  waiting for transfers between devices  237 us (68%)
  blocking collectives  37.4 us (11%)
  matrix products  24 us (7%)
  other arithmetic  18.3 us (5%)
  between operations  14.2 us (4%)
  starting transfers between devices  9.07 us (3%)
    psum x2, waiting for transfers between devices, body(): margins = lax.psum(partial_margin, 'grid')  106 us
    all_gather x2, waiting for transfers between devices, body(): lax.all_gather(rounded, 'band', axis=0, tiled=True)  73.3 us
    reduce_scatter x2, waiting for transfers between devices, body(): lax.psum_scatter(lax.dot_general(scaled, occupied_rows, (((0,), (0,)), ((...  55.5 us
    psum x1, blocking collectives, body(): curvature = lax.psum(inner_product(direction, applied), 'grid')  12.8 us
    psum x1, blocking collectives, body(): norm_now = lax.psum(inner_product(source_term, source_term), 'grid')  12.8 us
    dot_general x2, matrix products, body(): lax.dot_general(scaled, occupied_rows, (((0,), (0,)), ((), ())), preferre...  12.3 us
    psum x1, blocking collectives, body(): norm_next = lax.psum(inner_product(residual, residual), 'grid')  11.8 us
    dot_general x2, matrix products, body(): lax.dot_general(occupied_rows, lax.all_gather(rounded, 'band', axis=0, ti...  11.7 us
  transfers between devices with their start and end apart: 10, of which 8 were waited for; matrix products, arithmetic and copies ran while one was open for 0% of the time, Pallas kernels for 0%

commit v1 on v0

--- a/solution.py
+++ b/solution.py
@@ -22,6 +22,17 @@
         after = lax.ppermute(leading, axis, down)
         shard = jnp.concatenate([before, shard, after], axis=dim)
     return shard
+
+
+def grid_sum(value, axis):
+    peers = lax.axis_size(axis)
+    assert peers & (peers - 1) == 0
+    stride = 1
+    while stride < peers:
+        pairs = [(i, i ^ stride) for i in range(peers)]
+        value = value + lax.ppermute(value, axis, pairs)
+        stride *= 2
+    return value
 
 
 def second_sum(padded, extent_x, extent_y, extent_z):
@@ -70,7 +81,7 @@
     solution = jnp.zeros_like(source_term)
     residual = source_term
     direction = source_term
-    norm_now = lax.psum(inner_product(source_term, source_term), "grid")
+    norm_now = grid_sum(inner_product(source_term, source_term), "grid")
     for iteration in range(ITERS):
         padded = with_halo(direction.astype(jnp.bfloat16), (("grid", 1),), 4).astype(
             direction.dtype
@@ -84,7 +95,7 @@
             (((1,), (1,)), ((), ())),
             preferred_element_type=jnp.float32,
         )
-        margins = lax.psum(partial_margin, "grid")
+        margins = grid_sum(partial_margin, "grid")
         scaled = (margins * weight_scale).astype(jnp.bfloat16)
         projected = lax.psum_scatter(
             lax.dot_general(
@@ -95,12 +106,12 @@
             tiled=True,
         ).astype(jnp.float32)
         applied = kinetic + potential_shift * direction + projected.reshape(direction.shape)
-        curvature = lax.psum(inner_product(direction, applied), "grid")
+        curvature = grid_sum(inner_product(direction, applied), "grid")
         step_size = norm_now / curvature
         solution = solution + expand(step_size) * direction
         residual = residual - expand(step_size) * applied
         if iteration + 1 < ITERS:
-            norm_next = lax.psum(inner_product(residual, residual), "grid")
+            norm_next = grid_sum(inner_product(residual, residual), "grid")
             direction = residual + expand(norm_next / norm_now) * direction
             norm_now = norm_next
     return (solution, residual)

time: 346 us -> 241 us (0.70)
  waiting for transfers between devices: 237 us -> 161 us
  blocking collectives: 37.4 us -> 0 us
  starting transfers between devices: 9.07 us -> 27 us
  other arithmetic: 18.3 us -> 13.4 us
  matrix products: 24 us -> 20.5 us
    psum x2 -> x0, waiting for transfers between devices: 106 us -> none  [body(): margins = lax.psum(partial_margin, 'grid')]
    psum x3 -> x0, blocking collectives: 37.4 us -> none  [the longest x1 12.8 us: body(): curvature = lax.psum(inner_product(direction, applied), 'grid')]
    ppermute x0 -> x18, waiting for transfers between devices: none -> 28.3 us  [grid_sum(): value = value + lax.ppermute(value, axis, pairs)]
    ppermute x0 -> x18, starting transfers between devices: none -> 17.8 us  [grid_sum(): value = value + lax.ppermute(value, axis, pairs)]
  transfers between devices with their start and end apart: 10 -> 26, of which waited for: 8 -> 22; matrix products, arithmetic and copies ran while one was open for 0% -> 0% of each run, Pallas kernels for 0% -> 0%
where the time goes in v1:
time: 241 us; the launch traced here: 238 us
  waiting for transfers between devices  161 us (67%)
  starting transfers between devices  27 us (11%)
  matrix products  20.5 us (9%)
  between operations  14 us (6%)
  other arithmetic  13.4 us (6%)
    all_gather x2, waiting for transfers between devices, body(): lax.all_gather(rounded, 'band', axis=0, tiled=True)  73 us
    reduce_scatter x2, waiting for transfers between devices, body(): lax.psum_scatter(lax.dot_general(scaled, occupied_rows, (((0,), (0,)), ((...  56.5 us
    ppermute x18, waiting for transfers between devices, grid_sum(): value = value + lax.ppermute(value, axis, pairs)  28.3 us
    ppermute x18, starting transfers between devices, grid_sum(): value = value + lax.ppermute(value, axis, pairs)  17.8 us
    dot_general x2, matrix products, body(): lax.dot_general(occupied_rows, lax.all_gather(rounded, 'band', axis=0, ti...  11 us
    dot_general x2, matrix products, body(): lax.dot_general(scaled, occupied_rows, (((0,), (0,)), ((), ())), preferre...  9.5 us
    reduce_sum x3, other arithmetic, inner_product(): return jnp.sum(first_field * second_field, axis=(1, 2, 3))  6.73 us
    ppermute x2, starting transfers between devices, with_halo(): before = lax.ppermute(last, axis, up)  6.11 us
  transfers between devices with their start and end apart: 26, of which 22 were waited for; matrix products, arithmetic and copies ran while one was open for 0% of the time, Pallas kernels for 0%

profile of v1, /device:TPU:8, one launch (start us, length us, event | category | flops | bytes accessed | tf_op | source)
XLA Modules:
  0.0 237.6 jit_solution(15001182419213856844)
XLA Ops:
  7.2 1.3 convert_element_type.31
  8.6 0.9 copy.32
  9.5 37.9 %all-gather.3.cloned.1.call-done = bf16[64,12288]{1,0:T(8,128)(2,1)} async-done(((bf16[16,12288]{1,0:T(8,128)(2,1)}), bf16[64,12288]{1,0:T(8,128)(2,1)}) %all-gather.3.cloned.1.call-update) | async-done | bytes 1572880 | tf_op jit(solution)/shard_map/all_gather | solution.py:94
  47.4 5.5 %fusion.4 = f32[256,64]{0,1:T(8,128)S(1)} fusion(bf16[64,12288]{1,0:T(8,128)(2,1)} %all-gather.3.cloned.1.call-done, bf16[32,8,96,128]{3,2,1,0:T(8,128)(2,1)} %bitcast.35), kind=kOutput, calls=%fused_computation.38 | convolution fusion | flops 402653184 | bytes 7929856 | tf_op jit(solution)/shard_map/dot_general | solution.py:92
  53.0 1.2 collective-permute-done.5
  54.3 1.5 collective-permute-start.6
  55.8 2.8 %collective-permute-done.6 = f32[256,64]{0,1:T(8,128)S(1)} collective-permute-done((f32[256,64]{0,1:T(8,128)S(1)}, f32[256,64]{0,1:T(8,128)S(1)}, u32[]{:S(2)}, u32[]{:S(2)}) %collective-permute-start.6) | collective-permute-done | bytes 65568 | tf_op jit(solution)/shard_map/ppermute | solution.py:33
  58.6 1.5 collective-permute-start.7
  60.2 2.8 %collective-permute-done.7 = f32[256,64]{0,1:T(8,128)S(1)} collective-permute-done((f32[256,64]{0,1:T(8,128)S(1)}, f32[256,64]{0,1:T(8,128)S(1)}, u32[]{:S(2)}, u32[]{:S(2)}) %collective-permute-start.7) | collective-permute-done | bytes 65568 | tf_op jit(solution)/shard_map/ppermute | solution.py:33
  63.0 3.4 %convolution_convert_fusion.1 = bf16[64,12288]{1,0:T(8,128)(2,1)} fusion(bf16[32,8,96,128]{3,2,1,0:T(8,128)(2,1)S(1)} %bitcast.40, f32[256,64]{0,1:T(8,128)S(1)} %add.269, f32[256,64]{0,1:T(8,128)S(1)} %collective-permute-done.7), kind=kOutput, calls=%fused_computation.33 | convolution fusion | flops 403488768 | bytes 7995392 | tf_op jit(solution)/shard_map/dot_general | solution.py:101
  66.4 1.4 collective-permute-start.4
  67.9 3.1 %collective-permute-start.3 = (bf16[16,4,24,128]{3,2,1,0:T(8,128)(2,1)S(1)}, bf16[16,4,24,128]{3,2,1,0:T(8,128)(2,1)S(1)}, u32[]{:S(2)}, u32[]{:S(2)}) collective-permute-start(bf16[16,4,24,128]{3,2,1,0:T(8,128)(2,1)S(1)} %convert_element_type.31), channel_id=1, source_target_pairs={{0,4},{4,8},{8,12},{12,16},{16,20},{20,24},{24,28},{1,5},{5,9},{9,... | collective-permute-start | bytes 1179656 | tf_op jit(solution)/shard_map/ppermute | solution.py:21
  70.9 1.3 collective-permute-done.3
  72.4 28.2 %reduce-scatter.3.cloned.1.call-done = bf16[16,12288]{1,0:T(8,128)(2,1)} async-done(((bf16[64,12288]{1,0:T(8,128)(2,1)}), bf16[16,12288]{1,0:T(8,128)(2,1)}) %reduce-scatter.3.cloned.1.call-update) | async-done | bytes 393232 | tf_op jit(solution)/shard_map/reduce_scatter | solution.py:100
  100.6 1.0 convert_bitcast_fusion.1
  101.8 3.2 %multiply_reduce_fusion.2 = (f32[16]{0:T(128)S(1)}, f32[16]{0:T(128)S(1)}, f32[16,4,24,128]{3,2,1,0:T(8,128)S(1)}) fusion(f32[16,4,24,128]{3,2,1,0:T(8,128)S(1)} %copy-done, f32[16,4,24,128]{3,2,1,0:T(8,128)S(1)} %bitcast.43, f32[16]{0:T(128)S(1)} %copy-done.4, f32[4,24,128]{2,1,0:T(8,128)} %param.5, f32[16,12,24,128]{3,2,1,0:T(8,128)S(1)} %maximum_convert_fusion), kind=kLoop, calls=%fused_computation.135 | loop fusion | flops 9043936 | bytes 11846272 | tf_op jit(solution)/shard_map/reduce_sum | solution.py:64
  106.2 1.5 collective-permute-start.9
  108.2 1.5 collective-permute-done.9
  109.7 1.5 collective-permute-start.10
  111.2 1.5 collective-permute-start.2
  113.3 1.5 collective-permute-done.2
  115.1 1.1 collective-permute-done.11
  116.3 1.5 collective-permute-start.12
  117.7 2.1 collective-permute-done.12
  119.8 1.5 collective-permute-start.13
  121.3 2.1 collective-permute-done.13
  123.4 1.2 fusion.86
  124.5 0.9 copy.31
  125.7 35.2 %all-gather.5.cloned.1.call-done = bf16[64,12288]{1,0:T(8,128)(2,1)} async-done(((bf16[16,12288]{1,0:T(8,128)(2,1)}), bf16[64,12288]{1,0:T(8,128)(2,1)}) %all-gather.5.cloned.1.call-update) | async-done | bytes 1572880 | tf_op jit(solution)/shard_map/all_gather | solution.py:94
  160.9 5.4 %fusion.10 = f32[256,64]{0,1:T(8,128)S(1)} fusion(bf16[64,12288]{1,0:T(8,128)(2,1)} %all-gather.5.cloned.1.call-done, bf16[32,8,96,128]{3,2,1,0:T(8,128)(2,1)} %bitcast.36), kind=kOutput, calls=%fused_computation.48 | convolution fusion | flops 402653184 | bytes 7929856 | tf_op jit(solution)/shard_map/dot_general | solution.py:92
  166.4 1.2 collective-permute-done.16
  167.6 1.5 collective-permute-start.17
  169.2 2.8 %collective-permute-done.17 = f32[256,64]{0,1:T(8,128)S(1)} collective-permute-done((f32[256,64]{0,1:T(8,128)S(1)}, f32[256,64]{0,1:T(8,128)S(1)}, u32[]{:S(2)}, u32[]{:S(2)}) %collective-permute-start.17) | collective-permute-done | bytes 65568 | tf_op jit(solution)/shard_map/ppermute | solution.py:33
  172.0 1.5 collective-permute-start.18
  173.5 2.8 %collective-permute-done.18 = f32[256,64]{0,1:T(8,128)S(1)} collective-permute-done((f32[256,64]{0,1:T(8,128)S(1)}, f32[256,64]{0,1:T(8,128)S(1)}, u32[]{:S(2)}, u32[]{:S(2)}) %collective-permute-start.18) | collective-permute-done | bytes 65568 | tf_op jit(solution)/shard_map/ppermute | solution.py:33
  176.3 6.1 %convolution_convert_fusion = bf16[64,12288]{1,0:T(8,128)(2,1)} fusion(bf16[32,8,96,128]{3,2,1,0:T(8,128)(2,1)} %bitcast.37, f32[256,64]{0,1:T(8,128)S(1)} %add.305, f32[256,64]{0,1:T(8,128)S(1)} %collective-permute-done.18), kind=kOutput, calls=%fused_computation.32 | convolution fusion | flops 403488768 | bytes 7995392 | tf_op jit(solution)/shard_map/dot_general | solution.py:101
  182.5 1.3 collective-permute-start.15
  183.8 3.1 %collective-permute-start.14 = (bf16[16,4,24,128]{3,2,1,0:T(8,128)(2,1)S(1)}, bf16[16,4,24,128]{3,2,1,0:T(8,128)(2,1)S(1)}, u32[]{:S(2)}, u32[]{:S(2)}) collective-permute-start(bf16[16,4,24,128]{3,2,1,0:T(8,128)(2,1)S(1)} %get-tuple-element.6), channel_id=1, source_target_pairs={{0,4},{4,8},{8,12},{12,16},{16,20},{20,24},{24,28},{1,5},{5,9},{9,... | collective-permute-start | bytes 1179656 | tf_op jit(solution)/shard_map/ppermute | solution.py:21
  186.8 1.3 collective-permute-done.14
  188.3 28.4 %reduce-scatter.5.cloned.1.call-done = bf16[16,12288]{1,0:T(8,128)(2,1)} async-done(((bf16[64,12288]{1,0:T(8,128)(2,1)}), bf16[16,12288]{1,0:T(8,128)(2,1)}) %reduce-scatter.5.cloned.1.call-update) | async-done | bytes 393232 | tf_op jit(solution)/shard_map/reduce_scatter | solution.py:100
  216.7 1.1 convert_bitcast_fusion
  218.0 3.2 %multiply_reduce_fusion = (f32[16]{0:T(128)S(1)}, f32[16,4,24,128]{3,2,1,0:T(8,128)S(1)}) fusion(f32[16,4,24,128]{3,2,1,0:T(8,128)S(1)} %copy-done.3, f32[16,4,24,128]{3,2,1,0:T(8,128)S(1)} %bitcast.44, f32[16]{0:T(128)S(1)} %copy-done.4, f32[4,24,128]{2,1,0:T(8,128)} %param.5, f32[16,12,24,128]{3,2,1,0:T(8,128)S(1)} %maximum_convert_fusion.1), kind=kLoop, calls=%fused_computation.131 | loop fusion | flops 8650736 | bytes 11846208 | tf_op jit(solution)/shard_map/reduce_sum | solution.py:64
  221.3 1.1 collective-permute-done.19
  222.4 1.5 collective-permute-start.20
  223.9 2.1 collective-permute-done.20
  226.0 1.5 collective-permute-start.21
  227.4 2.1 collective-permute-done.21
  229.5 1.6 multiply_subtract_fusion
  (56 shorter events, 4.1 us)
Async XLA Ops:
  7.2 40.2 %all-gather.3.cloned.1.call-start = ((), (), s32[]{:S(2)}) async-start(), calls=%async_computation.2 | async-start | bytes 1966080 | tf_op jit(solution)/shard_map/all_gather | solution.py:94
  7.2 55.8 %slice-start = ((s8[6291456]{0:T(1024)(128)(4,1)}), s8[2097152]{0:T(1024)(128)(4,1)S(1)}, s32[]{:S(2)}) async-start(s8[6291456]{0:T(1024)(128)(4,1)} %bitcast.38), calls=%async_computation.6 | async-start | bytes 4194304
  9.5 91.1 %reduce-scatter.3.cloned.1.call-start = ((), (), s32[]{:S(2)}) async-start(), calls=%async_computation.3 | async-start | bytes 1966080 | tf_op jit(solution)/shard_map/reduce_scatter | solution.py:100
  47.4 15.6 %slice-start.1 = ((s8[6291456]{0:T(1024)(128)(4,1)}), s8[4194304]{0:T(1024)(128)(4,1)S(1)}, s32[]{:S(2)}) async-start(s8[6291456]{0:T(1024)(128)(4,1)} %bitcast.38), calls=%async_computation.7 | async-start | bytes 8388608
  53.0 1.3 collective-permute-start.5
  54.3 4.3 %collective-permute-start.6 = (f32[256,64]{0,1:T(8,128)S(1)}, f32[256,64]{0,1:T(8,128)S(1)}, u32[]{:S(2)}, u32[]{:S(2)}) collective-permute-start(f32[256,64]{0,1:T(8,128)S(1)} %add.268), channel_id=1, source_target_pairs={{0,8},{4,12},{8,0},{12,4},{16,24},{20,28},{24,16},{28,20},{1,9},{5... | collective-permute-start | bytes 196616 | tf_op jit(solution)/shard_map/ppermute | solution.py:33
  58.6 4.3 %collective-permute-start.7 = (f32[256,64]{0,1:T(8,128)S(1)}, f32[256,64]{0,1:T(8,128)S(1)}, u32[]{:S(2)}, u32[]{:S(2)}) collective-permute-start(f32[256,64]{0,1:T(8,128)S(1)} %add.269), channel_id=1, source_target_pairs={{0,16},{4,20},{8,24},{12,28},{16,0},{20,4},{24,8},{28,12},{1,17},{... | collective-permute-start | bytes 196616 | tf_op jit(solution)/shard_map/ppermute | solution.py:33
  66.4 35.4 %copy-start = (f32[16,4,24,128]{3,2,1,0:T(8,128)S(1)}, f32[16,4,24,128]{3,2,1,0:T(8,128)}, u32[]{:S(2)}) copy-start(f32[16,4,24,128]{3,2,1,0:T(8,128)} %param.7) | copy-start | bytes 2359300
  66.4 35.4 %copy-start.4 = (f32[16]{0:T(128)S(1)}, f32[16]{0:T(128)}, u32[]{:S(2)}) copy-start(f32[16]{0:T(128)} %param.6) | copy-start | bytes 196
  66.4 94.5 %all-gather.5.cloned.1.call-start = ((), (), s32[]{:S(2)}) async-start(), calls=%async_computation.4 | async-start | bytes 1966080 | tf_op jit(solution)/shard_map/all_gather | solution.py:94
  66.4 4.5 %collective-permute-start.4 = (bf16[16,4,24,128]{3,2,1,0:T(8,128)(2,1)S(1)}, bf16[16,4,24,128]{3,2,1,0:T(8,128)(2,1)S(1)}, u32[]{:S(2)}, u32[]{:S(2)}) collective-permute-start(bf16[16,4,24,128]{3,2,1,0:T(8,128)(2,1)S(1)} %convert_element_type.31), channel_id=1, source_target_pairs={{4,0},{8,4},{12,8},{16,12},{20,16},{24,20},{28,24},{5,1},{9,5},{13... | collective-permute-start | bytes 1179656 | tf_op jit(solution)/shard_map/ppermute | solution.py:22
  67.9 4.4 %collective-permute-start.3 = (bf16[16,4,24,128]{3,2,1,0:T(8,128)(2,1)S(1)}, bf16[16,4,24,128]{3,2,1,0:T(8,128)(2,1)S(1)}, u32[]{:S(2)}, u32[]{:S(2)}) collective-permute-start(bf16[16,4,24,128]{3,2,1,0:T(8,128)(2,1)S(1)} %convert_element_type.31), channel_id=1, source_target_pairs={{0,4},{4,8},{8,12},{12,16},{16,20},{20,24},{24,28},{1,5},{5,9},{9,... | collective-permute-start | bytes 1179656 | tf_op jit(solution)/shard_map/ppermute | solution.py:21
  105.0 20.5 %copy-start.1 = (f32[16,4,24,128]{3,2,1,0:T(8,128)}, f32[16,4,24,128]{3,2,1,0:T(8,128)S(1)}, u32[]{:S(2)}) copy-start(f32[16,4,24,128]{3,2,1,0:T(8,128)S(1)} %get-tuple-element.12) | copy-start | bytes 2359300
  105.0 1.2 collective-permute-start.8
  105.1 2.6 %collective-permute-start = (f32[16]{0:T(128)S(1)}, f32[16]{0:T(128)S(1)}, u32[]{:S(2)}, u32[]{:S(2)}) collective-permute-start(f32[16]{0:T(128)S(1)} %get-tuple-element.3), channel_id=1, source_target_pairs={{0,4},{4,0},{8,12},{12,8},{16,20},{20,16},{24,28},{28,24},{1,5},{5... | collective-permute-start | bytes 200 | tf_op jit(solution)/shard_map/ppermute | solution.py:33
  106.2 3.5 %collective-permute-start.9 = (f32[16]{0:T(128)S(1)}, f32[16]{0:T(128)S(1)}, u32[]{:S(2)}, u32[]{:S(2)}) collective-permute-start(f32[16]{0:T(128)S(1)} %add.272), channel_id=1, source_target_pairs={{0,8},{4,12},{8,0},{12,4},{16,24},{20,28},{24,16},{28,20},{1,9},{5... | collective-permute-start | bytes 200 | tf_op jit(solution)/shard_map/ppermute | solution.py:33
  107.7 3.5 %collective-permute-start.1 = (f32[16]{0:T(128)S(1)}, f32[16]{0:T(128)S(1)}, u32[]{:S(2)}, u32[]{:S(2)}) collective-permute-start(f32[16]{0:T(128)S(1)} %add.237), channel_id=1, source_target_pairs={{0,8},{4,12},{8,0},{12,4},{16,24},{20,28},{24,16},{28,20},{1,9},{5... | collective-permute-start | bytes 200 | tf_op jit(solution)/shard_map/ppermute | solution.py:33
  109.7 3.5 %collective-permute-start.10 = (f32[16]{0:T(128)S(1)}, f32[16]{0:T(128)S(1)}, u32[]{:S(2)}, u32[]{:S(2)}) collective-permute-start(f32[16]{0:T(128)S(1)} %add.273), channel_id=1, source_target_pairs={{0,16},{4,20},{8,24},{12,28},{16,0},{20,4},{24,8},{28,12},{1,17},{... | collective-permute-start | bytes 200 | tf_op jit(solution)/shard_map/ppermute | solution.py:33
  111.2 3.5 %collective-permute-start.2 = (f32[16]{0:T(128)S(1)}, f32[16]{0:T(128)S(1)}, u32[]{:S(2)}, u32[]{:S(2)}) collective-permute-start(f32[16]{0:T(128)S(1)} %add.238), channel_id=1, source_target_pairs={{0,16},{4,20},{8,24},{12,28},{16,0},{20,4},{24,8},{28,12},{1,17},{... | collective-permute-start | bytes 200 | tf_op jit(solution)/shard_map/ppermute | solution.py:33
  115.1 1.2 collective-permute-start.11
  116.3 3.5 %collective-permute-start.12 = (f32[16]{0:T(128)S(1)}, f32[16]{0:T(128)S(1)}, u32[]{:S(2)}, u32[]{:S(2)}) collective-permute-start(f32[16]{0:T(128)S(1)} %add.275), channel_id=1, source_target_pairs={{0,8},{4,12},{8,0},{12,4},{16,24},{20,28},{24,16},{28,20},{1,9},{5... | collective-permute-start | bytes 200 | tf_op jit(solution)/shard_map/ppermute | solution.py:33
  119.8 3.5 %collective-permute-start.13 = (f32[16]{0:T(128)S(1)}, f32[16]{0:T(128)S(1)}, u32[]{:S(2)}, u32[]{:S(2)}) collective-permute-start(f32[16]{0:T(128)S(1)} %add.276), channel_id=1, source_target_pairs={{0,16},{4,20},{8,24},{12,28},{16,0},{20,4},{24,8},{28,12},{1,17},{... | collective-permute-start | bytes 200 | tf_op jit(solution)/shard_map/ppermute | solution.py:33
  125.5 91.2 %reduce-scatter.5.cloned.1.call-start = ((), (), s32[]{:S(2)}) async-start(), calls=%async_computation.5 | async-start | bytes 1966080 | tf_op jit(solution)/shard_map/reduce_scatter | solution.py:100
  166.3 1.3 collective-permute-start.16
  167.6 4.3 %collective-permute-start.17 = (f32[256,64]{0,1:T(8,128)S(1)}, f32[256,64]{0,1:T(8,128)S(1)}, u32[]{:S(2)}, u32[]{:S(2)}) collective-permute-start(f32[256,64]{0,1:T(8,128)S(1)} %add.304), channel_id=1, source_target_pairs={{0,8},{4,12},{8,0},{12,4},{16,24},{20,28},{24,16},{28,20},{1,9},{5... | collective-permute-start | bytes 196616 | tf_op jit(solution)/shard_map/ppermute | solution.py:33
  172.0 4.3 %collective-permute-start.18 = (f32[256,64]{0,1:T(8,128)S(1)}, f32[256,64]{0,1:T(8,128)S(1)}, u32[]{:S(2)}, u32[]{:S(2)}) collective-permute-start(f32[256,64]{0,1:T(8,128)S(1)} %add.305), channel_id=1, source_target_pairs={{0,16},{4,20},{8,24},{12,28},{16,0},{20,4},{24,8},{28,12},{1,17},{... | collective-permute-start | bytes 196616 | tf_op jit(solution)/shard_map/ppermute | solution.py:33
  182.5 4.4 %collective-permute-start.15 = (bf16[16,4,24,128]{3,2,1,0:T(8,128)(2,1)S(1)}, bf16[16,4,24,128]{3,2,1,0:T(8,128)(2,1)S(1)}, u32[]{:S(2)}, u32[]{:S(2)}) collective-permute-start(bf16[16,4,24,128]{3,2,1,0:T(8,128)(2,1)S(1)} %get-tuple-element.6), channel_id=1, source_target_pairs={{4,0},{8,4},{12,8},{16,12},{20,16},{24,20},{28,24},{5,1},{9,5},{13... | collective-permute-start | bytes 1179656 | tf_op jit(solution)/shard_map/ppermute | solution.py:22
  183.8 4.4 %collective-permute-start.14 = (bf16[16,4,24,128]{3,2,1,0:T(8,128)(2,1)S(1)}, bf16[16,4,24,128]{3,2,1,0:T(8,128)(2,1)S(1)}, u32[]{:S(2)}, u32[]{:S(2)}) collective-permute-start(bf16[16,4,24,128]{3,2,1,0:T(8,128)(2,1)S(1)} %get-tuple-element.6), channel_id=1, source_target_pairs={{0,4},{4,8},{8,12},{12,16},{16,20},{20,24},{24,28},{1,5},{5,9},{9,... | collective-permute-start | bytes 1179656 | tf_op jit(solution)/shard_map/ppermute | solution.py:21
  216.7 1.3 copy-start.3
  218.0 11.5 %copy-start.2 = (f32[16,4,24,128]{3,2,1,0:T(8,128)S(1)}, f32[16,4,24,128]{3,2,1,0:T(8,128)}, u32[]{:S(2)}) copy-start(f32[16,4,24,128]{3,2,1,0:T(8,128)} %copy-done.1) | copy-start | bytes 2359300
  221.2 1.2 collective-permute-start.19
  222.4 3.5 %collective-permute-start.20 = (f32[16]{0:T(128)S(1)}, f32[16]{0:T(128)S(1)}, u32[]{:S(2)}, u32[]{:S(2)}) collective-permute-start(f32[16]{0:T(128)S(1)} %add.308), channel_id=1, source_target_pairs={{0,8},{4,12},{8,0},{12,4},{16,24},{20,28},{24,16},{28,20},{1,9},{5... | collective-permute-start | bytes 200 | tf_op jit(solution)/shard_map/ppermute | solution.py:33
  226.0 3.5 %collective-permute-start.21 = (f32[16]{0:T(128)S(1)}, f32[16]{0:T(128)S(1)}, u32[]{:S(2)}, u32[]{:S(2)}) collective-permute-start(f32[16]{0:T(128)S(1)} %add.309), channel_id=1, source_target_pairs={{0,16},{4,20},{8,24},{12,28},{16,0},{20,4},{24,8},{28,12},{1,17},{... | collective-permute-start | bytes 200 | tf_op jit(solution)/shard_map/ppermute | solution.py:33
Sparse Core Ops, SparseCore 0:
  10.1 37.2 all-gather.2
  66.5 34.0 reduce-scatter.2
  125.6 35.2 all-gather.4
  182.6 34.0 reduce-scatter.4

commit v2 on v1

--- a/solution.py
+++ b/solution.py
@@ -89,22 +89,24 @@
         padded = jnp.pad(padded, ((0, 0), (0, 0), (4, 4), (4, 4)))
         kinetic = -0.5 * second_sum(padded, width_x, width_y, width_z)
         rounded = direction.astype(jnp.bfloat16).reshape(local_bands, local_cells)
+        blocks = [rounded] + [
+            lax.ppermute(rounded, "band", [(i, (i + d) % band_count) for i in range(band_count)])
+            for d in range(1, band_count)
+        ]
+        gathered = jnp.concatenate(blocks, axis=0)
         partial_margin = lax.dot_general(
-            occupied_rows,
-            lax.all_gather(rounded, "band", axis=0, tiled=True),
-            (((1,), (1,)), ((), ())),
-            preferred_element_type=jnp.float32,
+            occupied_rows, gathered, (((1,), (1,)), ((), ())), preferred_element_type=jnp.float32
         )
         margins = grid_sum(partial_margin, "grid")
         scaled = (margins * weight_scale).astype(jnp.bfloat16)
-        projected = lax.psum_scatter(
-            lax.dot_general(
-                scaled, occupied_rows, (((0,), (0,)), ((), ())), preferred_element_type=jnp.float32
-            ).astype(jnp.bfloat16),
-            "band",
-            scatter_dimension=0,
-            tiled=True,
-        ).astype(jnp.float32)
+        terms = lax.dot_general(
+            scaled, occupied_rows, (((0,), (0,)), ((), ())), preferred_element_type=jnp.float32
+        ).astype(jnp.bfloat16)
+        projected = terms[:local_bands].astype(jnp.float32)
+        for d in range(1, band_count):
+            part = terms[d * local_bands : (d + 1) * local_bands]
+            back = lax.ppermute(part, "band", [((i + d) % band_count, i) for i in range(band_count)])
+            projected = projected + back.astype(jnp.float32)
         applied = kinetic + potential_shift * direction + projected.reshape(direction.shape)
         curvature = grid_sum(inner_product(direction, applied), "grid")
         step_size = norm_now / curvature

time: 241 us -> 221 us (0.917); the launches traced: 238 us -> 221 us
  starting transfers between devices: 27 us -> 40.2 us
  between operations: 14 us -> 0.96 us
  matrix products: 20.5 us -> 14.1 us
  waiting for transfers between devices: 161 us -> 156 us
  other arithmetic: 13.4 us -> 8.92 us
    ppermute x0 -> x12, waiting for transfers between devices: none -> 128 us  [the longest x6 68.5 us: body(): lax.ppermute(part, 'band', [((i + d) % band_count, i) for i in range(band...]
    all_gather x2 -> x0, waiting for transfers between devices: 73 us -> none  [body(): lax.all_gather(rounded, 'band', axis=0, tiled=True)]
    reduce_scatter x2 -> x0, waiting for transfers between devices: 56.5 us -> none  [body(): lax.psum_scatter(lax.dot_general(scaled, occupied_rows, (((0,), (0,)), ((...]
    ppermute x0 -> x12, starting transfers between devices: none -> 19.1 us  [the longest x6 10.7 us: body(): lax.ppermute(rounded, 'band', [(i, (i + d) % band_count) for i in range(b...]
    ppermute x18, starting transfers between devices: 17.8 us -> 12.3 us  [grid_sum(): value = value + lax.ppermute(value, axis, pairs)]
    dot_general x2, matrix products: 9.5 us -> 4.33 us  [body(): lax.dot_general(scaled, occupied_rows, (((0,), (0,)), ((), ())), preferre...]
    ppermute x2, waiting for transfers between devices: 2.59 us -> 0.01 us  [with_halo(): before = lax.ppermute(last, axis, up)]
  transfers between devices with their start and end apart: 26 -> 34, of which waited for: 22 -> 26; matrix products, arithmetic and copies ran while one was open for 0% -> 2% of each run, Pallas kernels for 0% -> 0%
where the time goes in v2:
time: 221 us
  waiting for transfers between devices  156 us (71%)
  starting transfers between devices  40.2 us (18%)
  matrix products  14.1 us (6%)
  other arithmetic  8.92 us (4%)
    ppermute x6, waiting for transfers between devices, body(): lax.ppermute(part, 'band', [((i + d) % band_count, i) for i in range(band...  68.5 us
    ppermute x6, waiting for transfers between devices, body(): lax.ppermute(rounded, 'band', [(i, (i + d) % band_count) for i in range(b...  59.9 us
    ppermute x18, waiting for transfers between devices, grid_sum(): value = value + lax.ppermute(value, axis, pairs)  27.2 us
    ppermute x18, starting transfers between devices, grid_sum(): value = value + lax.ppermute(value, axis, pairs)  12.3 us
    ppermute x6, starting transfers between devices, body(): lax.ppermute(rounded, 'band', [(i, (i + d) % band_count) for i in range(b...  10.7 us
    dot_general x2, matrix products, body(): lax.dot_general(occupied_rows, gathered, (((1,), (1,)), ((), ())), prefer...  9.73 us
    ppermute x6, starting transfers between devices, body(): lax.ppermute(part, 'band', [((i + d) % band_count, i) for i in range(band...  8.4 us
    ppermute x2, starting transfers between devices, with_halo(): before = lax.ppermute(last, axis, up)  6.29 us
  transfers between devices with their start and end apart: 34, of which 26 were waited for; matrix products, arithmetic and copies ran while one was open for 2% of the time, Pallas kernels for 0%

profile of v2, /device:TPU:8, one launch (start us, length us, event | category | flops | bytes accessed | tf_op | source)
XLA Modules:
  0.0 220.6 jit_solution(4138006855315081291)
XLA Ops:
  0.6 1.2 convert_element_type.53
  2.1 3.0 %collective-permute-start.6 = (bf16[16,12288]{1,0:T(8,128)(2,1)S(1)}, bf16[16,12288]{1,0:T(8,128)(2,1)S(1)}, u32[]{:S(2)}, u32[]{:S(2)}) collective-permute-start(bf16[16,12288]{1,0:T(8,128)(2,1)S(1)} %bitcast.48), channel_id=1, source_target_pairs={{0,2},{1,3},{2,0},{3,1},{4,6},{5,7},{6,4},{7,5},{8,10},{9,11},{10,... | collective-permute-start | bytes 1179656 | tf_op jit(solution)/shard_map/ppermute | solution.py:93
  5.1 2.5 %collective-permute-start.5 = (bf16[16,12288]{1,0:T(8,128)(2,1)S(1)}, bf16[16,12288]{1,0:T(8,128)(2,1)S(1)}, u32[]{:S(2)}, u32[]{:S(2)}) collective-permute-start(bf16[16,12288]{1,0:T(8,128)(2,1)S(1)} %bitcast.49), channel_id=1, source_target_pairs={{0,1},{1,2},{2,3},{3,0},{4,5},{5,6},{6,7},{7,4},{8,9},{9,10},{10,1... | collective-permute-start | bytes 1179656 | tf_op jit(solution)/shard_map/ppermute | solution.py:93
  7.6 23.3 %collective-permute-done.7 = bf16[16,12288]{1,0:T(8,128)(2,1)S(1)} collective-permute-done((bf16[16,12288]{1,0:T(8,128)(2,1)S(1)}, bf16[16,12288]{1,0:T(8,128)(2,1)S(1)}, u32[]{:S(2)}, u32[]{:S(2)}) %collective-permute-start.7) | collective-permute-done | bytes 393248 | tf_op jit(solution)/shard_map/ppermute | solution.py:93
  31.0 7.5 %collective-permute-done.5 = bf16[16,12288]{1,0:T(8,128)(2,1)S(1)} collective-permute-done((bf16[16,12288]{1,0:T(8,128)(2,1)S(1)}, bf16[16,12288]{1,0:T(8,128)(2,1)S(1)}, u32[]{:S(2)}, u32[]{:S(2)}) %collective-permute-start.5) | collective-permute-done | bytes 393248 | tf_op jit(solution)/shard_map/ppermute | solution.py:93
  38.5 7.5 %fusion.24 = f32[256,64]{0,1:T(8,128)S(1)} fusion(bf16[32,8,96,128]{3,2,1,0:T(8,128)(2,1)} %bitcast.37, bf16[16,12288]{1,0:T(8,128)(2,1)S(1)} %collective-permute-done.7, bf16[16,12288]{1,0:T(8,128)(2,1)S(1)} %collective-permute-done.6, bf16[16,12288]{1,0:T(8,128)(2,1)S(1)} %collective-permute-done.5, bf16[16,12288]{1,0:T(8,128)(2,1)S(1)} %bitcast.50), kind=kOutput, calls=%fused_computation.62 | convolution fusion | flops 408944640 | bytes 7929856 | tf_op jit(solution)/shard_map/dot_general | solution.py:97
  46.1 1.2 collective-permute-done.8
  47.3 1.6 collective-permute-start.9
  48.9 2.8 %collective-permute-done.9 = f32[256,64]{0,1:T(8,128)S(1)} collective-permute-done((f32[256,64]{0,1:T(8,128)S(1)}, f32[256,64]{0,1:T(8,128)S(1)}, u32[]{:S(2)}, u32[]{:S(2)}) %collective-permute-start.9) | collective-permute-done | bytes 65568 | tf_op jit(solution)/shard_map/ppermute | solution.py:33
  51.7 1.6 collective-permute-start.10
  53.3 1.3 collective-permute-start.4
  54.6 3.1 %collective-permute-start.3 = (bf16[16,4,24,128]{3,2,1,0:T(8,128)(2,1)S(1)}, bf16[16,4,24,128]{3,2,1,0:T(8,128)(2,1)S(1)}, u32[]{:S(2)}, u32[]{:S(2)}) collective-permute-start(bf16[16,4,24,128]{3,2,1,0:T(8,128)(2,1)S(1)} %convert_element_type.53), channel_id=1, source_target_pairs={{0,4},{4,8},{8,12},{12,16},{16,20},{20,24},{24,28},{1,5},{5,9},{9,... | collective-permute-start | bytes 1179656 | tf_op jit(solution)/shard_map/ppermute | solution.py:21
  57.7 2.2 convolution_convert_fusion.1
  59.9 2.5 %collective-permute-start.13 = (bf16[16,12288]{1,0:T(8,128)(2,1)S(1)}, bf16[16,12288]{1,0:T(8,128)(2,1)S(1)}, u32[]{:S(2)}, u32[]{:S(2)}) collective-permute-start(bf16[16,12288]{1,0:T(8,128)(2,1)S(1)} %get-tuple-element.17), channel_id=1, source_target_pairs={{3,0},{0,1},{1,2},{2,3},{7,4},{4,5},{5,6},{6,7},{11,8},{8,9},{9,10... | collective-permute-start | bytes 1179656 | tf_op jit(solution)/shard_map/ppermute | solution.py:108
  62.4 1.0 collective-permute-start.12
  64.2 24.3 %collective-permute-done.13 = bf16[16,12288]{1,0:T(8,128)(2,1)S(1)} collective-permute-done((bf16[16,12288]{1,0:T(8,128)(2,1)S(1)}, bf16[16,12288]{1,0:T(8,128)(2,1)S(1)}, u32[]{:S(2)}, u32[]{:S(2)}) %collective-permute-start.13) | collective-permute-done | bytes 393248 | tf_op jit(solution)/shard_map/ppermute | solution.py:108
  88.5 8.6 %collective-permute-done.12 = bf16[16,12288]{1,0:T(8,128)(2,1)S(1)} collective-permute-done((bf16[16,12288]{1,0:T(8,128)(2,1)S(1)}, bf16[16,12288]{1,0:T(8,128)(2,1)S(1)}, u32[]{:S(2)}, u32[]{:S(2)}) %collective-permute-start.12) | collective-permute-done | bytes 393248 | tf_op jit(solution)/shard_map/ppermute | solution.py:108
  97.1 1.5 collective-permute-done.11
  99.0 2.4 %multiply_reduce_fusion.2 = (f32[16]{0:T(128)S(1)}, f32[16]{0:T(128)S(1)}, f32[16,4,24,128]{3,2,1,0:T(8,128)S(1)}) fusion(f32[16,4,24,128]{3,2,1,0:T(8,128)S(1)} %copy-done, f32[16,4,24,128]{3,2,1,0:T(8,128)S(1)} %bitcast.45, f32[16]{0:T(128)S(1)} %copy-done.2, f32[4,24,128]{2,1,0:T(8,128)S(1)} %copy-done.1, f32[16,12,24,128]{3,2,1,0:T(8,128)S(1)} %maximum_convert_fusion), kind=kLoop, calls=%fused_computation.149 | loop fusion | flops 9043936 | bytes 11846272 | tf_op jit(solution)/shard_map/reduce_sum | solution.py:64
  102.6 1.2 collective-permute-start.15
  103.8 0.8 collective-permute-start.1
  104.6 1.5 collective-permute-done.15
  108.1 1.5 collective-permute-done.16
  109.6 1.3 collective-permute-done.2
  111.3 1.1 collective-permute-done.17
  113.2 2.8 %collective-permute-done.18 = f32[16]{0:T(128)S(1)} collective-permute-done((f32[16]{0:T(128)S(1)}, f32[16]{0:T(128)S(1)}, u32[]{:S(2)}, u32[]{:S(2)}) %collective-permute-start.18) | collective-permute-done | bytes 96 | tf_op jit(solution)/shard_map/ppermute | solution.py:33
  116.7 2.8 %collective-permute-done.19 = f32[16]{0:T(128)S(1)} collective-permute-done((f32[16]{0:T(128)S(1)}, f32[16]{0:T(128)S(1)}, u32[]{:S(2)}, u32[]{:S(2)}) %collective-permute-start.19) | collective-permute-done | bytes 96 | tf_op jit(solution)/shard_map/ppermute | solution.py:33
  120.0 2.2 %collective-permute-start.23 = (bf16[16,12288]{1,0:T(8,128)(2,1)S(1)}, bf16[16,12288]{1,0:T(8,128)(2,1)S(1)}, u32[]{:S(2)}, u32[]{:S(2)}) collective-permute-start(bf16[16,12288]{1,0:T(8,128)(2,1)S(1)} %bitcast.52), channel_id=1, source_target_pairs={{0,2},{1,3},{2,0},{3,1},{4,6},{5,7},{6,4},{7,5},{8,10},{9,11},{10,... | collective-permute-start | bytes 1179656 | tf_op jit(solution)/shard_map/ppermute | solution.py:93
  122.2 2.8 %collective-permute-start.22 = (bf16[16,12288]{1,0:T(8,128)(2,1)S(1)}, bf16[16,12288]{1,0:T(8,128)(2,1)S(1)}, u32[]{:S(2)}, u32[]{:S(2)}) collective-permute-start(bf16[16,12288]{1,0:T(8,128)(2,1)S(1)} %bitcast.53), channel_id=1, source_target_pairs={{0,1},{1,2},{2,3},{3,0},{4,5},{5,6},{6,7},{7,4},{8,9},{9,10},{10,1... | collective-permute-start | bytes 1179656 | tf_op jit(solution)/shard_map/ppermute | solution.py:93
  125.1 23.8 %collective-permute-done.24 = bf16[16,12288]{1,0:T(8,128)(2,1)S(1)} collective-permute-done((bf16[16,12288]{1,0:T(8,128)(2,1)S(1)}, bf16[16,12288]{1,0:T(8,128)(2,1)S(1)}, u32[]{:S(2)}, u32[]{:S(2)}) %collective-permute-start.24) | collective-permute-done | bytes 393248 | tf_op jit(solution)/shard_map/ppermute | solution.py:93
  148.9 5.1 %collective-permute-done.22 = bf16[16,12288]{1,0:T(8,128)(2,1)S(1)} collective-permute-done((bf16[16,12288]{1,0:T(8,128)(2,1)S(1)}, bf16[16,12288]{1,0:T(8,128)(2,1)S(1)}, u32[]{:S(2)}, u32[]{:S(2)}) %collective-permute-start.22) | collective-permute-done | bytes 393248 | tf_op jit(solution)/shard_map/ppermute | solution.py:93
  154.0 2.2 %fusion.29 = f32[256,64]{0,1:T(8,128)S(1)} fusion(bf16[32,8,96,128]{3,2,1,0:T(8,128)(2,1)S(1)} %bitcast.41, bf16[16,12288]{1,0:T(8,128)(2,1)S(1)} %collective-permute-done.24, bf16[16,12288]{1,0:T(8,128)(2,1)S(1)} %collective-permute-done.23, bf16[16,12288]{1,0:T(8,128)(2,1)S(1)} %collective-permute-done.22, bf16[16,12288]{1,0:T(8,128)(2,1)S(1)} %bitcast.54), kind=kOutput, calls=%fused_computation.63 | convolution fusion | flops 408944640 | bytes 7929856 | tf_op jit(solution)/shard_map/dot_general | solution.py:97
  156.3 1.2 collective-permute-done.25
  158.2 3.7 %collective-permute-done.26 = f32[256,64]{0,1:T(8,128)S(1)} collective-permute-done((f32[256,64]{0,1:T(8,128)S(1)}, f32[256,64]{0,1:T(8,128)S(1)}, u32[]{:S(2)}, u32[]{:S(2)}) %collective-permute-start.26) | collective-permute-done | bytes 65568 | tf_op jit(solution)/shard_map/ppermute | solution.py:33
  162.5 1.3 collective-permute-start.21
  163.8 3.2 %collective-permute-start.20 = (bf16[16,4,24,128]{3,2,1,0:T(8,128)(2,1)S(1)}, bf16[16,4,24,128]{3,2,1,0:T(8,128)(2,1)S(1)}, u32[]{:S(2)}, u32[]{:S(2)}) collective-permute-start(bf16[16,4,24,128]{3,2,1,0:T(8,128)(2,1)S(1)} %get-tuple-element.6), channel_id=1, source_target_pairs={{0,4},{4,8},{8,12},{12,16},{16,20},{20,24},{24,28},{1,5},{5,9},{9,... | collective-permute-start | bytes 1179656 | tf_op jit(solution)/shard_map/ppermute | solution.py:21
  167.1 2.2 convolution_convert_fusion
  169.3 2.5 %collective-permute-start.30 = (bf16[16,12288]{1,0:T(8,128)(2,1)S(1)}, bf16[16,12288]{1,0:T(8,128)(2,1)S(1)}, u32[]{:S(2)}, u32[]{:S(2)}) collective-permute-start(bf16[16,12288]{1,0:T(8,128)(2,1)S(1)} %get-tuple-element.14), channel_id=1, source_target_pairs={{3,0},{0,1},{1,2},{2,3},{7,4},{4,5},{5,6},{6,7},{11,8},{8,9},{9,10... | collective-permute-start | bytes 1179656 | tf_op jit(solution)/shard_map/ppermute | solution.py:108
  171.9 1.8 collective-permute-start.29
  173.8 24.3 %collective-permute-done.30 = bf16[16,12288]{1,0:T(8,128)(2,1)S(1)} collective-permute-done((bf16[16,12288]{1,0:T(8,128)(2,1)S(1)}, bf16[16,12288]{1,0:T(8,128)(2,1)S(1)}, u32[]{:S(2)}, u32[]{:S(2)}) %collective-permute-start.30) | collective-permute-done | bytes 393248 | tf_op jit(solution)/shard_map/ppermute | solution.py:108
  198.1 8.4 %collective-permute-done.29 = bf16[16,12288]{1,0:T(8,128)(2,1)S(1)} collective-permute-done((bf16[16,12288]{1,0:T(8,128)(2,1)S(1)}, bf16[16,12288]{1,0:T(8,128)(2,1)S(1)}, u32[]{:S(2)}, u32[]{:S(2)}) %collective-permute-start.29) | collective-permute-done | bytes 393248 | tf_op jit(solution)/shard_map/ppermute | solution.py:108
  206.5 1.4 collective-permute-done.28
  208.3 2.4 %multiply_reduce_fusion = (f32[16]{0:T(128)S(1)}, f32[16,4,24,128]{3,2,1,0:T(8,128)S(1)}) fusion(f32[16,4,24,128]{3,2,1,0:T(8,128)S(1)} %get-tuple-element.7, f32[16,4,24,128]{3,2,1,0:T(8,128)S(1)} %bitcast.46, f32[16]{0:T(128)S(1)} %copy-done.2, f32[4,24,128]{2,1,0:T(8,128)S(1)} %copy-done.1, f32[16,12,24,128]{3,2,1,0:T(8,128)S(1)} %maximum_convert_fusion.1), kind=kLoop, calls=%fused_computation.144 | loop fusion | flops 8650736 | bytes 11846208 | tf_op jit(solution)/shard_map/reduce_sum | solution.py:64
  210.8 1.1 collective-permute-done.31
  211.9 1.5 collective-permute-start.32
  213.4 2.1 collective-permute-done.32
  216.2 2.8 %collective-permute-done.33 = f32[16]{0:T(128)S(1)} collective-permute-done((f32[16]{0:T(128)S(1)}, f32[16]{0:T(128)S(1)}, u32[]{:S(2)}, u32[]{:S(2)}) %collective-permute-start.33) | collective-permute-done | bytes 96 | tf_op jit(solution)/shard_map/ppermute | solution.py:33
  219.0 1.6 multiply_subtract_fusion
  (66 shorter events, 9.9 us)
Async XLA Ops:
  1.8 55.8 %slice-start = ((s8[6291456]{0:T(1024)(128)(4,1)}), s8[4194304]{0:T(1024)(128)(4,1)S(1)}, s32[]{:S(2)}) async-start(s8[6291456]{0:T(1024)(128)(4,1)} %bitcast.38), calls=%async_computation | async-start | bytes 8388608
  2.0 28.9 %collective-permute-start.7 = (bf16[16,12288]{1,0:T(8,128)(2,1)S(1)}, bf16[16,12288]{1,0:T(8,128)(2,1)S(1)}, u32[]{:S(2)}, u32[]{:S(2)}) collective-permute-start(bf16[16,12288]{1,0:T(8,128)(2,1)S(1)} %bitcast.47), channel_id=1, source_target_pairs={{0,3},{1,0},{2,1},{3,2},{4,7},{5,4},{6,5},{7,6},{8,11},{9,8},{10,9... | collective-permute-start | bytes 1179656 | tf_op jit(solution)/shard_map/ppermute | solution.py:93
  2.1 28.9 %collective-permute-start.6 = (bf16[16,12288]{1,0:T(8,128)(2,1)S(1)}, bf16[16,12288]{1,0:T(8,128)(2,1)S(1)}, u32[]{:S(2)}, u32[]{:S(2)}) collective-permute-start(bf16[16,12288]{1,0:T(8,128)(2,1)S(1)} %bitcast.48), channel_id=1, source_target_pairs={{0,2},{1,3},{2,0},{3,1},{4,6},{5,7},{6,4},{7,5},{8,10},{9,11},{10,... | collective-permute-start | bytes 1179656 | tf_op jit(solution)/shard_map/ppermute | solution.py:93
  5.1 33.4 %collective-permute-start.5 = (bf16[16,12288]{1,0:T(8,128)(2,1)S(1)}, bf16[16,12288]{1,0:T(8,128)(2,1)S(1)}, u32[]{:S(2)}, u32[]{:S(2)}) collective-permute-start(bf16[16,12288]{1,0:T(8,128)(2,1)S(1)} %bitcast.49), channel_id=1, source_target_pairs={{0,1},{1,2},{2,3},{3,0},{4,5},{5,6},{6,7},{7,4},{8,9},{9,10},{10,1... | collective-permute-start | bytes 1179656 | tf_op jit(solution)/shard_map/ppermute | solution.py:93
  38.5 19.1 %slice-start.1 = ((s8[6291456]{0:T(1024)(128)(4,1)}), s8[2097152]{0:T(1024)(128)(4,1)S(1)}, s32[]{:S(2)}) async-start(s8[6291456]{0:T(1024)(128)(4,1)} %bitcast.38), calls=%async_computation.1 | async-start | bytes 4194304
  46.0 1.3 collective-permute-start.8
  47.3 4.3 %collective-permute-start.9 = (f32[256,64]{0,1:T(8,128)S(1)}, f32[256,64]{0,1:T(8,128)S(1)}, u32[]{:S(2)}, u32[]{:S(2)}) collective-permute-start(f32[256,64]{0,1:T(8,128)S(1)} %add.282), channel_id=1, source_target_pairs={{0,8},{4,12},{8,0},{12,4},{16,24},{20,28},{24,16},{28,20},{1,9},{5... | collective-permute-start | bytes 196616 | tf_op jit(solution)/shard_map/ppermute | solution.py:33
  51.7 5.9 %collective-permute-start.10 = (f32[256,64]{0,1:T(8,128)S(1)}, f32[256,64]{0,1:T(8,128)S(1)}, u32[]{:S(2)}, u32[]{:S(2)}) collective-permute-start(f32[256,64]{0,1:T(8,128)S(1)} %add.283), channel_id=1, source_target_pairs={{0,16},{4,20},{8,24},{12,28},{16,0},{20,4},{24,8},{28,12},{1,17},{... | collective-permute-start | bytes 196616 | tf_op jit(solution)/shard_map/ppermute | solution.py:33
  53.3 10.7 %collective-permute-start.4 = (bf16[16,4,24,128]{3,2,1,0:T(8,128)(2,1)S(1)}, bf16[16,4,24,128]{3,2,1,0:T(8,128)(2,1)S(1)}, u32[]{:S(2)}, u32[]{:S(2)}) collective-permute-start(bf16[16,4,24,128]{3,2,1,0:T(8,128)(2,1)S(1)} %convert_element_type.53), channel_id=1, source_target_pairs={{4,0},{8,4},{12,8},{16,12},{20,16},{24,20},{28,24},{5,1},{9,5},{13... | collective-permute-start | bytes 1179656 | tf_op jit(solution)/shard_map/ppermute | solution.py:22
  54.6 9.4 %collective-permute-start.3 = (bf16[16,4,24,128]{3,2,1,0:T(8,128)(2,1)S(1)}, bf16[16,4,24,128]{3,2,1,0:T(8,128)(2,1)S(1)}, u32[]{:S(2)}, u32[]{:S(2)}) collective-permute-start(bf16[16,4,24,128]{3,2,1,0:T(8,128)(2,1)S(1)} %convert_element_type.53), channel_id=1, source_target_pairs={{0,4},{4,8},{8,12},{12,16},{16,20},{20,24},{24,28},{1,5},{5,9},{9,... | collective-permute-start | bytes 1179656 | tf_op jit(solution)/shard_map/ppermute | solution.py:21
  59.9 28.6 %collective-permute-start.13 = (bf16[16,12288]{1,0:T(8,128)(2,1)S(1)}, bf16[16,12288]{1,0:T(8,128)(2,1)S(1)}, u32[]{:S(2)}, u32[]{:S(2)}) collective-permute-start(bf16[16,12288]{1,0:T(8,128)(2,1)S(1)} %get-tuple-element.17), channel_id=1, source_target_pairs={{3,0},{0,1},{1,2},{2,3},{7,4},{4,5},{5,6},{6,7},{11,8},{8,9},{9,10... | collective-permute-start | bytes 1179656 | tf_op jit(solution)/shard_map/ppermute | solution.py:108
  62.4 34.7 %collective-permute-start.12 = (bf16[16,12288]{1,0:T(8,128)(2,1)S(1)}, bf16[16,12288]{1,0:T(8,128)(2,1)S(1)}, u32[]{:S(2)}, u32[]{:S(2)}) collective-permute-start(bf16[16,12288]{1,0:T(8,128)(2,1)S(1)} %get-tuple-element.18), channel_id=1, source_target_pairs={{2,0},{3,1},{0,2},{1,3},{6,4},{7,5},{4,6},{5,7},{10,8},{11,9},{8,1... | collective-permute-start | bytes 1179656 | tf_op jit(solution)/shard_map/ppermute | solution.py:108
  63.5 35.1 %collective-permute-start.11 = (bf16[16,12288]{1,0:T(8,128)(2,1)S(1)}, bf16[16,12288]{1,0:T(8,128)(2,1)S(1)}, u32[]{:S(2)}, u32[]{:S(2)}) collective-permute-start(bf16[16,12288]{1,0:T(8,128)(2,1)S(1)} %get-tuple-element.16), channel_id=1, source_target_pairs={{1,0},{2,1},{3,2},{0,3},{5,4},{6,5},{7,6},{4,7},{9,8},{10,9},{11,1... | collective-permute-start | bytes 1179656 | tf_op jit(solution)/shard_map/ppermute | solution.py:108
  64.2 34.8 %copy-start = (f32[16,4,24,128]{3,2,1,0:T(8,128)S(1)}, f32[16,4,24,128]{3,2,1,0:T(8,128)}, u32[]{:S(2)}) copy-start(f32[16,4,24,128]{3,2,1,0:T(8,128)} %param.7) | copy-start | bytes 2359300
  64.2 34.8 %copy-start.1 = (f32[4,24,128]{2,1,0:T(8,128)S(1)}, f32[4,24,128]{2,1,0:T(8,128)}, u32[]{:S(2)}) copy-start(f32[4,24,128]{2,1,0:T(8,128)} %param.5) | copy-start | bytes 147460
  64.2 34.8 %copy-start.2 = (f32[16]{0:T(128)S(1)}, f32[16]{0:T(128)}, u32[]{:S(2)}) copy-start(f32[16]{0:T(128)} %param.6) | copy-start | bytes 196
  101.4 1.2 collective-permute-start.14
  101.4 2.4 %collective-permute-start = (f32[16]{0:T(128)S(1)}, f32[16]{0:T(128)S(1)}, u32[]{:S(2)}, u32[]{:S(2)}) collective-permute-start(f32[16]{0:T(128)S(1)} %get-tuple-element.3), channel_id=1, source_target_pairs={{0,4},{4,0},{8,12},{12,8},{16,20},{20,16},{24,28},{28,24},{1,5},{5... | collective-permute-start | bytes 200 | tf_op jit(solution)/shard_map/ppermute | solution.py:33
  102.6 3.5 %collective-permute-start.15 = (f32[16]{0:T(128)S(1)}, f32[16]{0:T(128)S(1)}, u32[]{:S(2)}, u32[]{:S(2)}) collective-permute-start(f32[16]{0:T(128)S(1)} %add.289), channel_id=1, source_target_pairs={{0,8},{4,12},{8,0},{12,4},{16,24},{20,28},{24,16},{28,20},{1,9},{5... | collective-permute-start | bytes 200 | tf_op jit(solution)/shard_map/ppermute | solution.py:33
  103.8 3.5 %collective-permute-start.1 = (f32[16]{0:T(128)S(1)}, f32[16]{0:T(128)S(1)}, u32[]{:S(2)}, u32[]{:S(2)}) collective-permute-start(f32[16]{0:T(128)S(1)} %add.251), channel_id=1, source_target_pairs={{0,8},{4,12},{8,0},{12,4},{16,24},{20,28},{24,16},{28,20},{1,9},{5... | collective-permute-start | bytes 200 | tf_op jit(solution)/shard_map/ppermute | solution.py:33
  106.1 3.5 %collective-permute-start.16 = (f32[16]{0:T(128)S(1)}, f32[16]{0:T(128)S(1)}, u32[]{:S(2)}, u32[]{:S(2)}) collective-permute-start(f32[16]{0:T(128)S(1)} %add.290), channel_id=1, source_target_pairs={{0,16},{4,20},{8,24},{12,28},{16,0},{20,4},{24,8},{28,12},{1,17},{... | collective-permute-start | bytes 200 | tf_op jit(solution)/shard_map/ppermute | solution.py:33
  107.4 3.5 %collective-permute-start.2 = (f32[16]{0:T(128)S(1)}, f32[16]{0:T(128)S(1)}, u32[]{:S(2)}, u32[]{:S(2)}) collective-permute-start(f32[16]{0:T(128)S(1)} %add.252), channel_id=1, source_target_pairs={{0,16},{4,20},{8,24},{12,28},{16,0},{20,4},{24,8},{28,12},{1,17},{... | collective-permute-start | bytes 200 | tf_op jit(solution)/shard_map/ppermute | solution.py:33
  111.2 1.2 collective-permute-start.17
  112.4 3.5 %collective-permute-start.18 = (f32[16]{0:T(128)S(1)}, f32[16]{0:T(128)S(1)}, u32[]{:S(2)}, u32[]{:S(2)}) collective-permute-start(f32[16]{0:T(128)S(1)} %add.292), channel_id=1, source_target_pairs={{0,8},{4,12},{8,0},{12,4},{16,24},{20,28},{24,16},{28,20},{1,9},{5... | collective-permute-start | bytes 200 | tf_op jit(solution)/shard_map/ppermute | solution.py:33
  115.9 3.5 %collective-permute-start.19 = (f32[16]{0:T(128)S(1)}, f32[16]{0:T(128)S(1)}, u32[]{:S(2)}, u32[]{:S(2)}) collective-permute-start(f32[16]{0:T(128)S(1)} %add.293), channel_id=1, source_target_pairs={{0,16},{4,20},{8,24},{12,28},{16,0},{20,4},{24,8},{28,12},{1,17},{... | collective-permute-start | bytes 200 | tf_op jit(solution)/shard_map/ppermute | solution.py:33
  119.9 29.0 %collective-permute-start.24 = (bf16[16,12288]{1,0:T(8,128)(2,1)S(1)}, bf16[16,12288]{1,0:T(8,128)(2,1)S(1)}, u32[]{:S(2)}, u32[]{:S(2)}) collective-permute-start(bf16[16,12288]{1,0:T(8,128)(2,1)S(1)} %bitcast.51), channel_id=1, source_target_pairs={{0,3},{1,0},{2,1},{3,2},{4,7},{5,4},{6,5},{7,6},{8,11},{9,8},{10,9... | collective-permute-start | bytes 1179656 | tf_op jit(solution)/shard_map/ppermute | solution.py:93
  120.0 28.9 %collective-permute-start.23 = (bf16[16,12288]{1,0:T(8,128)(2,1)S(1)}, bf16[16,12288]{1,0:T(8,128)(2,1)S(1)}, u32[]{:S(2)}, u32[]{:S(2)}) collective-permute-start(bf16[16,12288]{1,0:T(8,128)(2,1)S(1)} %bitcast.52), channel_id=1, source_target_pairs={{0,2},{1,3},{2,0},{3,1},{4,6},{5,7},{6,4},{7,5},{8,10},{9,11},{10,... | collective-permute-start | bytes 1179656 | tf_op jit(solution)/shard_map/ppermute | solution.py:93
  122.2 31.8 %collective-permute-start.22 = (bf16[16,12288]{1,0:T(8,128)(2,1)S(1)}, bf16[16,12288]{1,0:T(8,128)(2,1)S(1)}, u32[]{:S(2)}, u32[]{:S(2)}) collective-permute-start(bf16[16,12288]{1,0:T(8,128)(2,1)S(1)} %bitcast.53), channel_id=1, source_target_pairs={{0,1},{1,2},{2,3},{3,0},{4,5},{5,6},{6,7},{7,4},{8,9},{9,10},{10,1... | collective-permute-start | bytes 1179656 | tf_op jit(solution)/shard_map/ppermute | solution.py:93
  156.2 1.3 collective-permute-start.25
  157.6 4.3 %collective-permute-start.26 = (f32[256,64]{0,1:T(8,128)S(1)}, f32[256,64]{0,1:T(8,128)S(1)}, u32[]{:S(2)}, u32[]{:S(2)}) collective-permute-start(f32[256,64]{0,1:T(8,128)S(1)} %add.321), channel_id=1, source_target_pairs={{0,8},{4,12},{8,0},{12,4},{16,24},{20,28},{24,16},{28,20},{1,9},{5... | collective-permute-start | bytes 196616 | tf_op jit(solution)/shard_map/ppermute | solution.py:33
  161.9 5.1 %collective-permute-start.27 = (f32[256,64]{0,1:T(8,128)S(1)}, f32[256,64]{0,1:T(8,128)S(1)}, u32[]{:S(2)}, u32[]{:S(2)}) collective-permute-start(f32[256,64]{0,1:T(8,128)S(1)} %add.322), channel_id=1, source_target_pairs={{0,16},{4,20},{8,24},{12,28},{16,0},{20,4},{24,8},{28,12},{1,17},{... | collective-permute-start | bytes 196616 | tf_op jit(solution)/shard_map/ppermute | solution.py:33
  162.5 11.1 %collective-permute-start.21 = (bf16[16,4,24,128]{3,2,1,0:T(8,128)(2,1)S(1)}, bf16[16,4,24,128]{3,2,1,0:T(8,128)(2,1)S(1)}, u32[]{:S(2)}, u32[]{:S(2)}) collective-permute-start(bf16[16,4,24,128]{3,2,1,0:T(8,128)(2,1)S(1)} %get-tuple-element.6), channel_id=1, source_target_pairs={{4,0},{8,4},{12,8},{16,12},{20,16},{24,20},{28,24},{5,1},{9,5},{13... | collective-permute-start | bytes 1179656 | tf_op jit(solution)/shard_map/ppermute | solution.py:22
  163.8 9.8 %collective-permute-start.20 = (bf16[16,4,24,128]{3,2,1,0:T(8,128)(2,1)S(1)}, bf16[16,4,24,128]{3,2,1,0:T(8,128)(2,1)S(1)}, u32[]{:S(2)}, u32[]{:S(2)}) collective-permute-start(bf16[16,4,24,128]{3,2,1,0:T(8,128)(2,1)S(1)} %get-tuple-element.6), channel_id=1, source_target_pairs={{0,4},{4,8},{8,12},{12,16},{16,20},{20,24},{24,28},{1,5},{5,9},{9,... | collective-permute-start | bytes 1179656 | tf_op jit(solution)/shard_map/ppermute | solution.py:21
  169.3 28.8 %collective-permute-start.30 = (bf16[16,12288]{1,0:T(8,128)(2,1)S(1)}, bf16[16,12288]{1,0:T(8,128)(2,1)S(1)}, u32[]{:S(2)}, u32[]{:S(2)}) collective-permute-start(bf16[16,12288]{1,0:T(8,128)(2,1)S(1)} %get-tuple-element.14), channel_id=1, source_target_pairs={{3,0},{0,1},{1,2},{2,3},{7,4},{4,5},{5,6},{6,7},{11,8},{8,9},{9,10... | collective-permute-start | bytes 1179656 | tf_op jit(solution)/shard_map/ppermute | solution.py:108
  171.9 34.7 %collective-permute-start.29 = (bf16[16,12288]{1,0:T(8,128)(2,1)S(1)}, bf16[16,12288]{1,0:T(8,128)(2,1)S(1)}, u32[]{:S(2)}, u32[]{:S(2)}) collective-permute-start(bf16[16,12288]{1,0:T(8,128)(2,1)S(1)} %get-tuple-element.15), channel_id=1, source_target_pairs={{2,0},{3,1},{0,2},{1,3},{6,4},{7,5},{4,6},{5,7},{10,8},{11,9},{8,1... | collective-permute-start | bytes 1179656 | tf_op jit(solution)/shard_map/ppermute | solution.py:108
  173.6 34.3 %collective-permute-start.28 = (bf16[16,12288]{1,0:T(8,128)(2,1)S(1)}, bf16[16,12288]{1,0:T(8,128)(2,1)S(1)}, u32[]{:S(2)}, u32[]{:S(2)}) collective-permute-start(bf16[16,12288]{1,0:T(8,128)(2,1)S(1)} %get-tuple-element.13), channel_id=1, source_target_pairs={{1,0},{2,1},{3,2},{0,3},{5,4},{6,5},{7,6},{4,7},{9,8},{10,9},{11,1... | collective-permute-start | bytes 1179656 | tf_op jit(solution)/shard_map/ppermute | solution.py:108
  210.7 1.2 collective-permute-start.31
  211.9 3.5 %collective-permute-start.32 = (f32[16]{0:T(128)S(1)}, f32[16]{0:T(128)S(1)}, u32[]{:S(2)}, u32[]{:S(2)}) collective-permute-start(f32[16]{0:T(128)S(1)} %add.328), channel_id=1, source_target_pairs={{0,8},{4,12},{8,0},{12,4},{16,24},{20,28},{24,16},{28,20},{1,9},{5... | collective-permute-start | bytes 200 | tf_op jit(solution)/shard_map/ppermute | solution.py:33
  215.5 3.5 %collective-permute-start.33 = (f32[16]{0:T(128)S(1)}, f32[16]{0:T(128)S(1)}, u32[]{:S(2)}, u32[]{:S(2)}) collective-permute-start(f32[16]{0:T(128)S(1)} %add.329), channel_id=1, source_target_pairs={{0,16},{4,20},{8,24},{12,28},{16,0},{20,4},{24,8},{28,12},{1,17},{... | collective-permute-start | bytes 200 | tf_op jit(solution)/shard_map/ppermute | solution.py:33

commit v3 on v2

--- a/solution.py
+++ b/solution.py
@@ -68,7 +68,7 @@
     return vector[:, None, None, None]
 
 
-def body(occupied, potential, shifts, source_term):
+def chain(occupied, potential, shifts, source_term):
     local_bands, width_x, width_y, width_z = source_term.shape
     local_occupied = occupied.shape[0]
     band_count = lax.axis_size("band")
@@ -119,6 +119,16 @@
     return (solution, residual)
 
 
+def body(occupied, potential, shifts, source_term):
+    pieces = 2 if source_term.shape[0] % 2 == 0 else 1
+    width = source_term.shape[0] // pieces
+    results = [
+        chain(occupied, potential, shifts[k * width : (k + 1) * width], source_term[k * width : (k + 1) * width])
+        for k in range(pieces)
+    ]
+    return tuple(jnp.concatenate([r[i] for r in results], axis=0) for i in range(2))
+
+
 def solution(mesh):
     in_specs = (
         P("band", "grid", None, None),

time: 221 us -> 214 us (0.968)
  waiting for transfers between devices: 156 us -> 96.9 us
  starting transfers between devices: 40.2 us -> 86.9 us
  matrix products: 14.1 us -> 19.1 us
    ppermute x12 -> x24, waiting for transfers between devices: 128 us -> 61.7 us  [the longest x12 42.4 us: chain(): lax.ppermute(part, 'band', [((i + d) % band_count, i) for i in range(band...]
    ppermute x12 -> x24, starting transfers between devices: 19.1 us -> 42.4 us  [the longest x12 25.9 us: chain(): lax.ppermute(rounded, 'band', [(i, (i + d) % band_count) for i in range(b...]
    ppermute x18 -> x36, starting transfers between devices: 12.3 us -> 28.9 us  [grid_sum(): value = value + lax.ppermute(value, axis, pairs)]
    ppermute x18 -> x36, waiting for transfers between devices: 27.2 us -> 35.2 us  [grid_sum(): value = value + lax.ppermute(value, axis, pairs)]
    dot_general x4 -> x8, matrix products: 14.1 us -> 19.1 us  [the longest x4 11.1 us: chain(): lax.dot_general(occupied_rows, gathered, (((1,), (1,)), ((), ())), prefer...]
    ppermute x2 -> x4, starting transfers between devices: 6.29 us -> 10.5 us  [with_halo(): before = lax.ppermute(last, axis, up)]
    ppermute x2 -> x4, starting transfers between devices: 2.56 us -> 5.13 us  [with_halo(): after = lax.ppermute(leading, axis, down)]
    reduce_sum x3 -> x4, other arithmetic: 5.1 us -> 5.09 us  [inner_product(): return jnp.sum(first_field * second_field, axis=(1, 2, 3))]
  transfers between devices with their start and end apart: 34 -> 68, of which waited for: 26 -> 30; matrix products, arithmetic and copies ran while one was open for 2% -> 10% of each run, Pallas kernels for 0% -> 0%
where the time goes in v3:
time: 214 us
  waiting for transfers between devices  96.9 us (45%)
  starting transfers between devices  86.9 us (41%)
  matrix products  19.1 us (9%)
  other arithmetic  7.82 us (4%)
    ppermute x12, waiting for transfers between devices, chain(): lax.ppermute(part, 'band', [((i + d) % band_count, i) for i in range(band...  42.4 us
    ppermute x36, waiting for transfers between devices, grid_sum(): value = value + lax.ppermute(value, axis, pairs)  35.2 us
    ppermute x36, starting transfers between devices, grid_sum(): value = value + lax.ppermute(value, axis, pairs)  28.9 us
    ppermute x12, starting transfers between devices, chain(): lax.ppermute(rounded, 'band', [(i, (i + d) % band_count) for i in range(b...  25.9 us
    ppermute x12, waiting for transfers between devices, chain(): lax.ppermute(rounded, 'band', [(i, (i + d) % band_count) for i in range(b...  19.2 us
    ppermute x12, starting transfers between devices, chain(): lax.ppermute(part, 'band', [((i + d) % band_count, i) for i in range(band...  16.5 us
    dot_general x4, matrix products, chain(): lax.dot_general(occupied_rows, gathered, (((1,), (1,)), ((), ())), prefer...  11.1 us
    ppermute x4, starting transfers between devices, with_halo(): before = lax.ppermute(last, axis, up)  10.5 us
  transfers between devices with their start and end apart: 68, of which 30 were waited for; matrix products, arithmetic and copies ran while one was open for 10% of the time, Pallas kernels for 0%

profile of v3, /device:TPU:8, one launch (start us, length us, event | category | flops | bytes accessed | tf_op | source)
XLA Modules:
  0.0 213.6 jit_solution(13953616740788290693)
XLA Ops:
  2.0 3.0 %collective-permute-start.6 = (bf16[8,12288]{1,0:T(8,128)(2,1)S(1)}, bf16[8,12288]{1,0:T(8,128)(2,1)S(1)}, u32[]{:S(2)}, u32[]{:S(2)}) collective-permute-start(bf16[8,12288]{1,0:T(8,128)(2,1)S(1)} %bitcast.88), channel_id=1, source_target_pairs={{0,2},{1,3},{2,0},{3,1},{4,6},{5,7},{6,4},{7,5},{8,10},{9,11},{10,... | collective-permute-start | bytes 589832 | tf_op jit(solution)/shard_map/ppermute | solution.py:93
  5.0 2.5 %collective-permute-start.5 = (bf16[8,12288]{1,0:T(8,128)(2,1)S(1)}, bf16[8,12288]{1,0:T(8,128)(2,1)S(1)}, u32[]{:S(2)}, u32[]{:S(2)}) collective-permute-start(bf16[8,12288]{1,0:T(8,128)(2,1)S(1)} %bitcast.89), channel_id=1, source_target_pairs={{0,1},{1,2},{2,3},{3,0},{4,5},{5,6},{6,7},{7,4},{8,9},{9,10},{10,1... | collective-permute-start | bytes 589832 | tf_op jit(solution)/shard_map/ppermute | solution.py:93
  8.8 3.0 %collective-permute-start.3 = (bf16[8,4,24,128]{3,2,1,0:T(8,128)(2,1)S(1)}, bf16[8,4,24,128]{3,2,1,0:T(8,128)(2,1)S(1)}, u32[]{:S(2)}, u32[]{:S(2)}) collective-permute-start(bf16[8,4,24,128]{3,2,1,0:T(8,128)(2,1)S(1)} %get-tuple-element.42), channel_id=1, source_target_pairs={{0,4},{4,8},{8,12},{12,16},{16,20},{20,24},{24,28},{1,5},{5,9},{9,... | collective-permute-start | bytes 589832 | tf_op jit(solution)/shard_map/ppermute | solution.py:21
  12.0 6.9 %collective-permute-done.6 = bf16[8,12288]{1,0:T(8,128)(2,1)S(1)} collective-permute-done((bf16[8,12288]{1,0:T(8,128)(2,1)S(1)}, bf16[8,12288]{1,0:T(8,128)(2,1)S(1)}, u32[]{:S(2)}, u32[]{:S(2)}) %collective-permute-start.6) | collective-permute-done | bytes 196640 | tf_op jit(solution)/shard_map/ppermute | solution.py:93
  18.9 9.0 %collective-permute-start.40 = (bf16[8,12288]{1,0:T(8,128)(2,1)S(1)}, bf16[8,12288]{1,0:T(8,128)(2,1)S(1)}, u32[]{:S(2)}, u32[]{:S(2)}) collective-permute-start(bf16[8,12288]{1,0:T(8,128)(2,1)S(1)} %bitcast.80), channel_id=1, source_target_pairs={{0,2},{1,3},{2,0},{3,1},{4,6},{5,7},{6,4},{7,5},{8,10},{9,11},{10,... | collective-permute-start | bytes 589832 | tf_op jit(solution)/shard_map/ppermute | solution.py:93
  27.9 2.9 %collective-permute-done.5 = bf16[8,12288]{1,0:T(8,128)(2,1)S(1)} collective-permute-done((bf16[8,12288]{1,0:T(8,128)(2,1)S(1)}, bf16[8,12288]{1,0:T(8,128)(2,1)S(1)}, u32[]{:S(2)}, u32[]{:S(2)}) %collective-permute-start.5) | collective-permute-done | bytes 196640 | tf_op jit(solution)/shard_map/ppermute | solution.py:93
  30.9 2.5 %collective-permute-start.39 = (bf16[8,12288]{1,0:T(8,128)(2,1)S(1)}, bf16[8,12288]{1,0:T(8,128)(2,1)S(1)}, u32[]{:S(2)}, u32[]{:S(2)}) collective-permute-start(bf16[8,12288]{1,0:T(8,128)(2,1)S(1)} %bitcast.81), channel_id=1, source_target_pairs={{0,1},{1,2},{2,3},{3,0},{4,5},{5,6},{6,7},{7,4},{8,9},{9,10},{10,1... | collective-permute-start | bytes 589832 | tf_op jit(solution)/shard_map/ppermute | solution.py:93
  33.3 5.0 %fusion.12 = f32[256,32]{0,1:T(8,128)S(1)} fusion(bf16[32,8,96,128]{3,2,1,0:T(8,128)(2,1)} %bitcast.59, bf16[8,12288]{1,0:T(8,128)(2,1)S(1)} %collective-permute-done.7, bf16[8,12288]{1,0:T(8,128)(2,1)S(1)} %collective-permute-done.6, bf16[8,12288]{1,0:T(8,128)(2,1)S(1)} %collective-permute-done.5, bf16[8,12288]{1,0:T(8,128)(2,1)S(1)} %bitcast.90), kind=kOutput, calls=%fused_computation.80 | convolution fusion | flops 204472320 | bytes 7110656 | tf_op jit(solution)/shard_map/dot_general | solution.py:97
  39.7 3.0 %collective-permute-start.37 = (bf16[8,4,24,128]{3,2,1,0:T(8,128)(2,1)S(1)}, bf16[8,4,24,128]{3,2,1,0:T(8,128)(2,1)S(1)}, u32[]{:S(2)}, u32[]{:S(2)}) collective-permute-start(bf16[8,4,24,128]{3,2,1,0:T(8,128)(2,1)S(1)} %get-tuple-element.41), channel_id=1, source_target_pairs={{0,4},{4,8},{8,12},{12,16},{16,20},{20,24},{24,28},{1,5},{5,9},{9,... | collective-permute-start | bytes 589832 | tf_op jit(solution)/shard_map/ppermute | solution.py:21
  43.9 2.0 fusion.18
  46.1 1.6 collective-permute-start.9
  50.1 1.6 collective-permute-start.10
  54.1 2.0 convolution_convert_fusion.3
  56.2 1.9 collective-permute-start.12
  58.3 2.0 convolution_convert_fusion.1
  60.4 2.0 collective-permute-start.47
  62.3 2.9 %collective-permute-start.46 = (bf16[8,12288]{1,0:T(8,128)(2,1)S(1)}, bf16[8,12288]{1,0:T(8,128)(2,1)S(1)}, u32[]{:S(2)}, u32[]{:S(2)}) collective-permute-start(bf16[8,12288]{1,0:T(8,128)(2,1)S(1)} %get-tuple-element.40), channel_id=1, source_target_pairs={{2,0},{3,1},{0,2},{1,3},{6,4},{7,5},{4,6},{5,7},{10,8},{11,9},{8,1... | collective-permute-start | bytes 589832 | tf_op jit(solution)/shard_map/ppermute | solution.py:108
  65.2 2.9 %collective-permute-done.13 = bf16[8,12288]{1,0:T(8,128)(2,1)S(1)} collective-permute-done((bf16[8,12288]{1,0:T(8,128)(2,1)S(1)}, bf16[8,12288]{1,0:T(8,128)(2,1)S(1)}, u32[]{:S(2)}, u32[]{:S(2)}) %collective-permute-start.13) | collective-permute-done | bytes 196640 | tf_op jit(solution)/shard_map/ppermute | solution.py:108
  68.1 14.6 %collective-permute-done.12 = bf16[8,12288]{1,0:T(8,128)(2,1)S(1)} collective-permute-done((bf16[8,12288]{1,0:T(8,128)(2,1)S(1)}, bf16[8,12288]{1,0:T(8,128)(2,1)S(1)}, u32[]{:S(2)}, u32[]{:S(2)}) %collective-permute-start.12) | collective-permute-done | bytes 196640 | tf_op jit(solution)/shard_map/ppermute | solution.py:108
  82.8 3.5 %collective-permute-done.47 = bf16[8,12288]{1,0:T(8,128)(2,1)S(1)} collective-permute-done((bf16[8,12288]{1,0:T(8,128)(2,1)S(1)}, bf16[8,12288]{1,0:T(8,128)(2,1)S(1)}, u32[]{:S(2)}, u32[]{:S(2)}) %collective-permute-start.47) | collective-permute-done | bytes 196640 | tf_op jit(solution)/shard_map/ppermute | solution.py:108
  86.3 2.1 collective-permute-done.46
  88.4 2.2 %collective-permute-done.45 = bf16[8,12288]{1,0:T(8,128)(2,1)S(1)} collective-permute-done((bf16[8,12288]{1,0:T(8,128)(2,1)S(1)}, bf16[8,12288]{1,0:T(8,128)(2,1)S(1)}, u32[]{:S(2)}, u32[]{:S(2)}) %collective-permute-start.45) | collective-permute-done | bytes 196640 | tf_op jit(solution)/shard_map/ppermute | solution.py:108
  90.6 2.5 %multiply_reduce_fusion.6 = (f32[8]{0:T(128)S(1)}, f32[8]{0:T(128)S(1)}, f32[8]{0:T(128)S(1)}, f32[8]{0:T(128)S(1)}, f32[8,4,24,128]{3,2,1,0:T(8,128)S(1)}, /*index=5*/f32[8,4,24,128]{3,2,1,0:T(8,128)S(1)}) fusion(f32[16,4,24,128]{3,2,1,0:T(8,128)S(1)} %copy-done.1, f32[8,4,24,128]{3,0,2,1:T(8,128)S(1)} %bitcast.71, f32[8]{0:T(128)S(1)} %get-tuple-element.49, ...), kind=kLoop, calls=%fused_computation.303 | loop fusion | flops 9043936 | bytes 11846784 | tf_op jit(solution)/shard_map/reduce_sum | solution.py:64
  106.1 3.1 %collective-permute-done.18 = f32[8]{0:T(128)S(1)} collective-permute-done((f32[8]{0:T(128)S(1)}, f32[8]{0:T(128)S(1)}, u32[]{:S(2)}, u32[]{:S(2)}) %collective-permute-start.18) | collective-permute-done | bytes 64 | tf_op jit(solution)/shard_map/ppermute | solution.py:33
  109.7 3.0 %collective-permute-done.19 = f32[8]{0:T(128)S(1)} collective-permute-done((f32[8]{0:T(128)S(1)}, f32[8]{0:T(128)S(1)}, u32[]{:S(2)}, u32[]{:S(2)}) %collective-permute-start.19) | collective-permute-done | bytes 64 | tf_op jit(solution)/shard_map/ppermute | solution.py:33
  114.4 2.8 %collective-permute-start.22 = (bf16[8,12288]{1,0:T(8,128)(2,1)S(1)}, bf16[8,12288]{1,0:T(8,128)(2,1)S(1)}, u32[]{:S(2)}, u32[]{:S(2)}) collective-permute-start(bf16[8,12288]{1,0:T(8,128)(2,1)S(1)} %bitcast.77), channel_id=1, source_target_pairs={{0,1},{1,2},{2,3},{3,0},{4,5},{5,6},{6,7},{7,4},{8,9},{9,10},{10,1... | collective-permute-start | bytes 589832 | tf_op jit(solution)/shard_map/ppermute | solution.py:93
  121.0 3.1 %collective-permute-done.52 = f32[8]{0:T(128)S(1)} collective-permute-done((f32[8]{0:T(128)S(1)}, f32[8]{0:T(128)S(1)}, u32[]{:S(2)}, u32[]{:S(2)}) %collective-permute-start.52) | collective-permute-done | bytes 64 | tf_op jit(solution)/shard_map/ppermute | solution.py:33
  124.8 2.9 %collective-permute-done.53 = f32[8]{0:T(128)S(1)} collective-permute-done((f32[8]{0:T(128)S(1)}, f32[8]{0:T(128)S(1)}, u32[]{:S(2)}, u32[]{:S(2)}) %collective-permute-start.53) | collective-permute-done | bytes 64 | tf_op jit(solution)/shard_map/ppermute | solution.py:33
  129.3 1.8 collective-permute-start.57
  131.0 2.8 %collective-permute-start.56 = (bf16[8,12288]{1,0:T(8,128)(2,1)S(1)}, bf16[8,12288]{1,0:T(8,128)(2,1)S(1)}, u32[]{:S(2)}, u32[]{:S(2)}) collective-permute-start(bf16[8,12288]{1,0:T(8,128)(2,1)S(1)} %bitcast.85), channel_id=1, source_target_pairs={{0,1},{1,2},{2,3},{3,0},{4,5},{5,6},{6,7},{7,4},{8,9},{9,10},{10,1... | collective-permute-start | bytes 589832 | tf_op jit(solution)/shard_map/ppermute | solution.py:93
  133.9 2.0 fusion.15
  135.9 9.3 %collective-permute-done.58 = bf16[8,12288]{1,0:T(8,128)(2,1)S(1)} collective-permute-done((bf16[8,12288]{1,0:T(8,128)(2,1)S(1)}, bf16[8,12288]{1,0:T(8,128)(2,1)S(1)}, u32[]{:S(2)}, u32[]{:S(2)}) %collective-permute-start.58) | collective-permute-done | bytes 196640 | tf_op jit(solution)/shard_map/ppermute | solution.py:93
  146.5 3.1 %collective-permute-start.54 = (bf16[8,4,24,128]{3,2,1,0:T(8,128)(2,1)S(1)}, bf16[8,4,24,128]{3,2,1,0:T(8,128)(2,1)S(1)}, u32[]{:S(2)}, u32[]{:S(2)}) collective-permute-start(bf16[8,4,24,128]{3,2,1,0:T(8,128)(2,1)S(1)} %get-tuple-element.18), channel_id=1, source_target_pairs={{0,4},{4,8},{8,12},{12,16},{16,20},{20,24},{24,28},{1,5},{5,9},{9,... | collective-permute-start | bytes 589832 | tf_op jit(solution)/shard_map/ppermute | solution.py:21
  149.6 1.8 collective-permute-start.25
  151.4 2.0 fusion.21
  153.6 2.3 %collective-permute-start.26 = (f32[256,32]{0,1:T(8,128)S(1)}, f32[256,32]{0,1:T(8,128)S(1)}, u32[]{:S(2)}, u32[]{:S(2)}) collective-permute-start(f32[256,32]{0,1:T(8,128)S(1)} %add.570), channel_id=1, source_target_pairs={{0,8},{4,12},{8,0},{12,4},{16,24},{20,28},{24,16},{28,20},{1,9},{5... | collective-permute-start | bytes 98312 | tf_op jit(solution)/shard_map/ppermute | solution.py:33
  160.1 1.9 collective-permute-done.27
  162.0 2.0 convolution_convert_fusion.2
  164.2 4.2 %collective-permute-start.29 = (bf16[8,12288]{1,0:T(8,128)(2,1)S(1)}, bf16[8,12288]{1,0:T(8,128)(2,1)S(1)}, u32[]{:S(2)}, u32[]{:S(2)}) collective-permute-start(bf16[8,12288]{1,0:T(8,128)(2,1)S(1)} %get-tuple-element.32), channel_id=1, source_target_pairs={{2,0},{3,1},{0,2},{1,3},{6,4},{7,5},{4,6},{5,7},{10,8},{11,9},{8,1... | collective-permute-start | bytes 589832 | tf_op jit(solution)/shard_map/ppermute | solution.py:108
  168.4 2.0 convolution_convert_fusion
  170.5 2.1 collective-permute-start.64
  172.5 1.8 collective-permute-start.63
  175.8 6.4 %collective-permute-done.29 = bf16[8,12288]{1,0:T(8,128)(2,1)S(1)} collective-permute-done((bf16[8,12288]{1,0:T(8,128)(2,1)S(1)}, bf16[8,12288]{1,0:T(8,128)(2,1)S(1)}, u32[]{:S(2)}, u32[]{:S(2)}) %collective-permute-start.29) | collective-permute-done | bytes 196640 | tf_op jit(solution)/shard_map/ppermute | solution.py:108
  182.2 10.8 %collective-permute-done.28 = bf16[8,12288]{1,0:T(8,128)(2,1)S(1)} collective-permute-done((bf16[8,12288]{1,0:T(8,128)(2,1)S(1)}, bf16[8,12288]{1,0:T(8,128)(2,1)S(1)}, u32[]{:S(2)}, u32[]{:S(2)}) %collective-permute-start.28) | collective-permute-done | bytes 196640 | tf_op jit(solution)/shard_map/ppermute | solution.py:108
  196.8 2.2 %collective-permute-done.32 = f32[8]{0:T(128)S(1)} collective-permute-done((f32[8]{0:T(128)S(1)}, f32[8]{0:T(128)S(1)}, u32[]{:S(2)}, u32[]{:S(2)}) %collective-permute-start.32) | collective-permute-done | bytes 64 | tf_op jit(solution)/shard_map/ppermute | solution.py:33
  199.3 3.2 %collective-permute-done.33 = f32[8]{0:T(128)S(1)} collective-permute-done((f32[8]{0:T(128)S(1)}, f32[8]{0:T(128)S(1)}, u32[]{:S(2)}, u32[]{:S(2)}) %collective-permute-start.33) | collective-permute-done | bytes 64 | tf_op jit(solution)/shard_map/ppermute | solution.py:33
  206.4 2.2 %collective-permute-done.66 = f32[8]{0:T(128)S(1)} collective-permute-done((f32[8]{0:T(128)S(1)}, f32[8]{0:T(128)S(1)}, u32[]{:S(2)}, u32[]{:S(2)}) %collective-permute-start.66) | collective-permute-done | bytes 64 | tf_op jit(solution)/shard_map/ppermute | solution.py:33
  208.9 3.2 %collective-permute-done.67 = f32[8]{0:T(128)S(1)} collective-permute-done((f32[8]{0:T(128)S(1)}, f32[8]{0:T(128)S(1)}, u32[]{:S(2)}, u32[]{:S(2)}) %collective-permute-start.67) | collective-permute-done | bytes 64 | tf_op jit(solution)/shard_map/ppermute | solution.py:33
  (160 shorter events, 48.9 us)
Async XLA Ops:
  1.9 10.1 %collective-permute-start.7 = (bf16[8,12288]{1,0:T(8,128)(2,1)S(1)}, bf16[8,12288]{1,0:T(8,128)(2,1)S(1)}, u32[]{:S(2)}, u32[]{:S(2)}) collective-permute-start(bf16[8,12288]{1,0:T(8,128)(2,1)S(1)} %bitcast.87), channel_id=1, source_target_pairs={{0,3},{1,0},{2,1},{3,2},{4,7},{5,4},{6,5},{7,6},{8,11},{9,8},{10,9... | collective-permute-start | bytes 589832 | tf_op jit(solution)/shard_map/ppermute | solution.py:93
  2.0 17.0 %collective-permute-start.6 = (bf16[8,12288]{1,0:T(8,128)(2,1)S(1)}, bf16[8,12288]{1,0:T(8,128)(2,1)S(1)}, u32[]{:S(2)}, u32[]{:S(2)}) collective-permute-start(bf16[8,12288]{1,0:T(8,128)(2,1)S(1)} %bitcast.88), channel_id=1, source_target_pairs={{0,2},{1,3},{2,0},{3,1},{4,6},{5,7},{6,4},{7,5},{8,10},{9,11},{10,... | collective-permute-start | bytes 589832 | tf_op jit(solution)/shard_map/ppermute | solution.py:93
  5.0 25.9 %collective-permute-start.5 = (bf16[8,12288]{1,0:T(8,128)(2,1)S(1)}, bf16[8,12288]{1,0:T(8,128)(2,1)S(1)}, u32[]{:S(2)}, u32[]{:S(2)}) collective-permute-start(bf16[8,12288]{1,0:T(8,128)(2,1)S(1)} %bitcast.89), channel_id=1, source_target_pairs={{0,1},{1,2},{2,3},{3,0},{4,5},{5,6},{6,7},{7,4},{8,9},{9,10},{10,1... | collective-permute-start | bytes 589832 | tf_op jit(solution)/shard_map/ppermute | solution.py:93
  7.5 38.6 %collective-permute-start.4 = (bf16[8,4,24,128]{3,2,1,0:T(8,128)(2,1)S(1)}, bf16[8,4,24,128]{3,2,1,0:T(8,128)(2,1)S(1)}, u32[]{:S(2)}, u32[]{:S(2)}) collective-permute-start(bf16[8,4,24,128]{3,2,1,0:T(8,128)(2,1)S(1)} %get-tuple-element.42), channel_id=1, source_target_pairs={{4,0},{8,4},{12,8},{16,12},{20,16},{24,20},{28,24},{5,1},{9,5},{13... | collective-permute-start | bytes 589832 | tf_op jit(solution)/shard_map/ppermute | solution.py:22
  8.8 38.9 %collective-permute-start.3 = (bf16[8,4,24,128]{3,2,1,0:T(8,128)(2,1)S(1)}, bf16[8,4,24,128]{3,2,1,0:T(8,128)(2,1)S(1)}, u32[]{:S(2)}, u32[]{:S(2)}) collective-permute-start(bf16[8,4,24,128]{3,2,1,0:T(8,128)(2,1)S(1)} %get-tuple-element.42), channel_id=1, source_target_pairs={{0,4},{4,8},{8,12},{12,16},{16,20},{20,24},{24,28},{1,5},{5,9},{9,... | collective-permute-start | bytes 589832 | tf_op jit(solution)/shard_map/ppermute | solution.py:21
  12.0 26.4 %collective-permute-start.41 = (bf16[8,12288]{1,0:T(8,128)(2,1)S(1)}, bf16[8,12288]{1,0:T(8,128)(2,1)S(1)}, u32[]{:S(2)}, u32[]{:S(2)}) collective-permute-start(bf16[8,12288]{1,0:T(8,128)(2,1)S(1)} %bitcast.79), channel_id=1, source_target_pairs={{0,3},{1,0},{2,1},{3,2},{4,7},{5,4},{6,5},{7,6},{8,11},{9,8},{10,9... | collective-permute-start | bytes 589832 | tf_op jit(solution)/shard_map/ppermute | solution.py:93
  18.9 20.7 %collective-permute-start.40 = (bf16[8,12288]{1,0:T(8,128)(2,1)S(1)}, bf16[8,12288]{1,0:T(8,128)(2,1)S(1)}, u32[]{:S(2)}, u32[]{:S(2)}) collective-permute-start(bf16[8,12288]{1,0:T(8,128)(2,1)S(1)} %bitcast.80), channel_id=1, source_target_pairs={{0,2},{1,3},{2,0},{3,1},{4,6},{5,7},{6,4},{7,5},{8,10},{9,11},{10,... | collective-permute-start | bytes 589832 | tf_op jit(solution)/shard_map/ppermute | solution.py:93
  30.9 11.9 %collective-permute-start.39 = (bf16[8,12288]{1,0:T(8,128)(2,1)S(1)}, bf16[8,12288]{1,0:T(8,128)(2,1)S(1)}, u32[]{:S(2)}, u32[]{:S(2)}) collective-permute-start(bf16[8,12288]{1,0:T(8,128)(2,1)S(1)} %bitcast.81), channel_id=1, source_target_pairs={{0,1},{1,2},{2,3},{3,0},{4,5},{5,6},{6,7},{7,4},{8,9},{9,10},{10,1... | collective-permute-start | bytes 589832 | tf_op jit(solution)/shard_map/ppermute | solution.py:93
  38.4 13.3 %collective-permute-start.38 = (bf16[8,4,24,128]{3,2,1,0:T(8,128)(2,1)S(1)}, bf16[8,4,24,128]{3,2,1,0:T(8,128)(2,1)S(1)}, u32[]{:S(2)}, u32[]{:S(2)}) collective-permute-start(bf16[8,4,24,128]{3,2,1,0:T(8,128)(2,1)S(1)} %get-tuple-element.41), channel_id=1, source_target_pairs={{4,0},{8,4},{12,8},{16,12},{20,16},{24,20},{28,24},{5,1},{9,5},{13... | collective-permute-start | bytes 589832 | tf_op jit(solution)/shard_map/ppermute | solution.py:22
  39.7 11.9 %collective-permute-start.37 = (bf16[8,4,24,128]{3,2,1,0:T(8,128)(2,1)S(1)}, bf16[8,4,24,128]{3,2,1,0:T(8,128)(2,1)S(1)}, u32[]{:S(2)}, u32[]{:S(2)}) collective-permute-start(bf16[8,4,24,128]{3,2,1,0:T(8,128)(2,1)S(1)} %get-tuple-element.41), channel_id=1, source_target_pairs={{0,4},{4,8},{8,12},{12,16},{16,20},{20,24},{24,28},{1,5},{5,9},{9,... | collective-permute-start | bytes 589832 | tf_op jit(solution)/shard_map/ppermute | solution.py:21
  46.1 4.0 %collective-permute-start.9 = (f32[256,32]{0,1:T(8,128)S(1)}, f32[256,32]{0,1:T(8,128)S(1)}, u32[]{:S(2)}, u32[]{:S(2)}) collective-permute-start(f32[256,32]{0,1:T(8,128)S(1)} %add.531), channel_id=1, source_target_pairs={{0,8},{4,12},{8,0},{12,4},{16,24},{20,28},{24,16},{28,20},{1,9},{5... | collective-permute-start | bytes 98312 | tf_op jit(solution)/shard_map/ppermute | solution.py:33
  47.7 4.0 %collective-permute-start.43 = (f32[256,32]{0,1:T(8,128)S(1)}, f32[256,32]{0,1:T(8,128)S(1)}, u32[]{:S(2)}, u32[]{:S(2)}) collective-permute-start(f32[256,32]{0,1:T(8,128)S(1)} %add.611), channel_id=1, source_target_pairs={{0,8},{4,12},{8,0},{12,4},{16,24},{20,28},{24,16},{28,20},{1,9},{5... | collective-permute-start | bytes 98312 | tf_op jit(solution)/shard_map/ppermute | solution.py:33
  50.1 4.1 %collective-permute-start.10 = (f32[256,32]{0,1:T(8,128)S(1)}, f32[256,32]{0,1:T(8,128)S(1)}, u32[]{:S(2)}, u32[]{:S(2)}) collective-permute-start(f32[256,32]{0,1:T(8,128)S(1)} %add.532), channel_id=1, source_target_pairs={{0,16},{4,20},{8,24},{12,28},{16,0},{20,4},{24,8},{28,12},{1,17},{... | collective-permute-start | bytes 98312 | tf_op jit(solution)/shard_map/ppermute | solution.py:33
  51.7 6.5 %collective-permute-start.44 = (f32[256,32]{0,1:T(8,128)S(1)}, f32[256,32]{0,1:T(8,128)S(1)}, u32[]{:S(2)}, u32[]{:S(2)}) collective-permute-start(f32[256,32]{0,1:T(8,128)S(1)} %add.612), channel_id=1, source_target_pairs={{0,16},{4,20},{8,24},{12,28},{16,0},{20,4},{24,8},{28,12},{1,17},{... | collective-permute-start | bytes 98312 | tf_op jit(solution)/shard_map/ppermute | solution.py:33
  56.2 11.9 %collective-permute-start.13 = (bf16[8,12288]{1,0:T(8,128)(2,1)S(1)}, bf16[8,12288]{1,0:T(8,128)(2,1)S(1)}, u32[]{:S(2)}, u32[]{:S(2)}) collective-permute-start(bf16[8,12288]{1,0:T(8,128)(2,1)S(1)} %get-tuple-element.44), channel_id=1, source_target_pairs={{3,0},{0,1},{1,2},{2,3},{7,4},{4,5},{5,6},{6,7},{11,8},{8,9},{9,10... | collective-permute-start | bytes 589832 | tf_op jit(solution)/shard_map/ppermute | solution.py:108
  56.2 26.4 %collective-permute-start.12 = (bf16[8,12288]{1,0:T(8,128)(2,1)S(1)}, bf16[8,12288]{1,0:T(8,128)(2,1)S(1)}, u32[]{:S(2)}, u32[]{:S(2)}) collective-permute-start(bf16[8,12288]{1,0:T(8,128)(2,1)S(1)} %get-tuple-element.45), channel_id=1, source_target_pairs={{2,0},{3,1},{0,2},{1,3},{6,4},{7,5},{4,6},{5,7},{10,8},{11,9},{8,1... | collective-permute-start | bytes 589832 | tf_op jit(solution)/shard_map/ppermute | solution.py:108
  58.1 24.5 %collective-permute-start.11 = (bf16[8,12288]{1,0:T(8,128)(2,1)S(1)}, bf16[8,12288]{1,0:T(8,128)(2,1)S(1)}, u32[]{:S(2)}, u32[]{:S(2)}) collective-permute-start(bf16[8,12288]{1,0:T(8,128)(2,1)S(1)} %get-tuple-element.43), channel_id=1, source_target_pairs={{1,0},{2,1},{3,2},{0,3},{5,4},{6,5},{7,6},{4,7},{9,8},{10,9},{11,1... | collective-permute-start | bytes 589832 | tf_op jit(solution)/shard_map/ppermute | solution.py:108
  60.4 25.9 %collective-permute-start.47 = (bf16[8,12288]{1,0:T(8,128)(2,1)S(1)}, bf16[8,12288]{1,0:T(8,128)(2,1)S(1)}, u32[]{:S(2)}, u32[]{:S(2)}) collective-permute-start(bf16[8,12288]{1,0:T(8,128)(2,1)S(1)} %get-tuple-element.39), channel_id=1, source_target_pairs={{3,0},{0,1},{1,2},{2,3},{7,4},{4,5},{5,6},{6,7},{11,8},{8,9},{9,10... | collective-permute-start | bytes 589832 | tf_op jit(solution)/shard_map/ppermute | solution.py:108
  62.3 26.1 %collective-permute-start.46 = (bf16[8,12288]{1,0:T(8,128)(2,1)S(1)}, bf16[8,12288]{1,0:T(8,128)(2,1)S(1)}, u32[]{:S(2)}, u32[]{:S(2)}) collective-permute-start(bf16[8,12288]{1,0:T(8,128)(2,1)S(1)} %get-tuple-element.40), channel_id=1, source_target_pairs={{2,0},{3,1},{0,2},{1,3},{6,4},{7,5},{4,6},{5,7},{10,8},{11,9},{8,1... | collective-permute-start | bytes 589832 | tf_op jit(solution)/shard_map/ppermute | solution.py:108
  68.1 22.5 %collective-permute-start.45 = (bf16[8,12288]{1,0:T(8,128)(2,1)S(1)}, bf16[8,12288]{1,0:T(8,128)(2,1)S(1)}, u32[]{:S(2)}, u32[]{:S(2)}) collective-permute-start(bf16[8,12288]{1,0:T(8,128)(2,1)S(1)} %get-tuple-element.38), channel_id=1, source_target_pairs={{1,0},{2,1},{3,2},{0,3},{5,4},{6,5},{7,6},{4,7},{9,8},{10,9},{11,1... | collective-permute-start | bytes 589832 | tf_op jit(solution)/shard_map/ppermute | solution.py:108
  93.8 4.1 %collective-permute-start.34 = (f32[8]{0:T(128)S(1)}, f32[8]{0:T(128)S(1)}, u32[]{:S(2)}, u32[]{:S(2)}) collective-permute-start(f32[8]{0:T(128)S(1)} %get-tuple-element.4), channel_id=1, source_target_pairs={{0,4},{4,0},{8,12},{12,8},{16,20},{20,16},{24,28},{28,24},{1,5},{5... | collective-permute-start | bytes 104 | tf_op jit(solution)/shard_map/ppermute | solution.py:33
  94.3 4.1 %collective-permute-start.15 = (f32[8]{0:T(128)S(1)}, f32[8]{0:T(128)S(1)}, u32[]{:S(2)}, u32[]{:S(2)}) collective-permute-start(f32[8]{0:T(128)S(1)} %add.538), channel_id=1, source_target_pairs={{0,8},{4,12},{8,0},{12,4},{16,24},{20,28},{24,16},{28,20},{1,9},{5... | collective-permute-start | bytes 104 | tf_op jit(solution)/shard_map/ppermute | solution.py:33
  95.8 4.1 %collective-permute-start.1 = (f32[8]{0:T(128)S(1)}, f32[8]{0:T(128)S(1)}, u32[]{:S(2)}, u32[]{:S(2)}) collective-permute-start(f32[8]{0:T(128)S(1)} %add.500), channel_id=1, source_target_pairs={{0,8},{4,12},{8,0},{12,4},{16,24},{20,28},{24,16},{28,20},{1,9},{5... | collective-permute-start | bytes 104 | tf_op jit(solution)/shard_map/ppermute | solution.py:33
  96.4 4.1 %collective-permute-start.49 = (f32[8]{0:T(128)S(1)}, f32[8]{0:T(128)S(1)}, u32[]{:S(2)}, u32[]{:S(2)}) collective-permute-start(f32[8]{0:T(128)S(1)} %add.618), channel_id=1, source_target_pairs={{0,8},{4,12},{8,0},{12,4},{16,24},{20,28},{24,16},{28,20},{1,9},{5... | collective-permute-start | bytes 104 | tf_op jit(solution)/shard_map/ppermute | solution.py:33
  97.9 4.1 %collective-permute-start.35 = (f32[8]{0:T(128)S(1)}, f32[8]{0:T(128)S(1)}, u32[]{:S(2)}, u32[]{:S(2)}) collective-permute-start(f32[8]{0:T(128)S(1)} %add.581), channel_id=1, source_target_pairs={{0,8},{4,12},{8,0},{12,4},{16,24},{20,28},{24,16},{28,20},{1,9},{5... | collective-permute-start | bytes 104 | tf_op jit(solution)/shard_map/ppermute | solution.py:33
  98.4 4.1 %collective-permute-start.16 = (f32[8]{0:T(128)S(1)}, f32[8]{0:T(128)S(1)}, u32[]{:S(2)}, u32[]{:S(2)}) collective-permute-start(f32[8]{0:T(128)S(1)} %add.539), channel_id=1, source_target_pairs={{0,16},{4,20},{8,24},{12,28},{16,0},{20,4},{24,8},{28,12},{1,17},{... | collective-permute-start | bytes 104 | tf_op jit(solution)/shard_map/ppermute | solution.py:33
  105.5 3.6 %collective-permute-start.18 = (f32[8]{0:T(128)S(1)}, f32[8]{0:T(128)S(1)}, u32[]{:S(2)}, u32[]{:S(2)}) collective-permute-start(f32[8]{0:T(128)S(1)} %add.541), channel_id=1, source_target_pairs={{0,8},{4,12},{8,0},{12,4},{16,24},{20,28},{24,16},{28,20},{1,9},{5... | collective-permute-start | bytes 104 | tf_op jit(solution)/shard_map/ppermute | solution.py:33
  113.0 16.2 %collective-permute-start.24 = (bf16[8,12288]{1,0:T(8,128)(2,1)S(1)}, bf16[8,12288]{1,0:T(8,128)(2,1)S(1)}, u32[]{:S(2)}, u32[]{:S(2)}) collective-permute-start(bf16[8,12288]{1,0:T(8,128)(2,1)S(1)} %bitcast.75), channel_id=1, source_target_pairs={{0,3},{1,0},{2,1},{3,2},{4,7},{5,4},{6,5},{7,6},{8,11},{9,8},{10,9... | collective-permute-start | bytes 589832 | tf_op jit(solution)/shard_map/ppermute | solution.py:93
  113.1 16.2 %collective-permute-start.23 = (bf16[8,12288]{1,0:T(8,128)(2,1)S(1)}, bf16[8,12288]{1,0:T(8,128)(2,1)S(1)}, u32[]{:S(2)}, u32[]{:S(2)}) collective-permute-start(bf16[8,12288]{1,0:T(8,128)(2,1)S(1)} %bitcast.76), channel_id=1, source_target_pairs={{0,2},{1,3},{2,0},{3,1},{4,6},{5,7},{6,4},{7,5},{8,10},{9,11},{10,... | collective-permute-start | bytes 589832 | tf_op jit(solution)/shard_map/ppermute | solution.py:93
  114.4 16.6 %collective-permute-start.22 = (bf16[8,12288]{1,0:T(8,128)(2,1)S(1)}, bf16[8,12288]{1,0:T(8,128)(2,1)S(1)}, u32[]{:S(2)}, u32[]{:S(2)}) collective-permute-start(bf16[8,12288]{1,0:T(8,128)(2,1)S(1)} %bitcast.77), channel_id=1, source_target_pairs={{0,1},{1,2},{2,3},{3,0},{4,5},{5,6},{6,7},{7,4},{8,9},{9,10},{10,1... | collective-permute-start | bytes 589832 | tf_op jit(solution)/shard_map/ppermute | solution.py:93
  117.2 36.3 %collective-permute-start.21 = (bf16[8,4,24,128]{3,2,1,0:T(8,128)(2,1)S(1)}, bf16[8,4,24,128]{3,2,1,0:T(8,128)(2,1)S(1)}, u32[]{:S(2)}, u32[]{:S(2)}) collective-permute-start(bf16[8,4,24,128]{3,2,1,0:T(8,128)(2,1)S(1)} %get-tuple-element.8), channel_id=1, source_target_pairs={{4,0},{8,4},{12,8},{16,12},{20,16},{24,20},{28,24},{5,1},{9,5},{13... | collective-permute-start | bytes 589832 | tf_op jit(solution)/shard_map/ppermute | solution.py:22
  127.7 28.2 %collective-permute-start.20 = (bf16[8,4,24,128]{3,2,1,0:T(8,128)(2,1)S(1)}, bf16[8,4,24,128]{3,2,1,0:T(8,128)(2,1)S(1)}, u32[]{:S(2)}, u32[]{:S(2)}) collective-permute-start(bf16[8,4,24,128]{3,2,1,0:T(8,128)(2,1)S(1)} %get-tuple-element.8), channel_id=1, source_target_pairs={{0,4},{4,8},{8,12},{12,16},{16,20},{20,24},{24,28},{1,5},{5,9},{9,... | collective-permute-start | bytes 589832 | tf_op jit(solution)/shard_map/ppermute | solution.py:21
  129.2 16.0 %collective-permute-start.58 = (bf16[8,12288]{1,0:T(8,128)(2,1)S(1)}, bf16[8,12288]{1,0:T(8,128)(2,1)S(1)}, u32[]{:S(2)}, u32[]{:S(2)}) collective-permute-start(bf16[8,12288]{1,0:T(8,128)(2,1)S(1)} %bitcast.83), channel_id=1, source_target_pairs={{0,3},{1,0},{2,1},{3,2},{4,7},{5,4},{6,5},{7,6},{8,11},{9,8},{10,9... | collective-permute-start | bytes 589832 | tf_op jit(solution)/shard_map/ppermute | solution.py:93
  129.3 17.3 %collective-permute-start.57 = (bf16[8,12288]{1,0:T(8,128)(2,1)S(1)}, bf16[8,12288]{1,0:T(8,128)(2,1)S(1)}, u32[]{:S(2)}, u32[]{:S(2)}) collective-permute-start(bf16[8,12288]{1,0:T(8,128)(2,1)S(1)} %bitcast.84), channel_id=1, source_target_pairs={{0,2},{1,3},{2,0},{3,1},{4,6},{5,7},{6,4},{7,5},{8,10},{9,11},{10,... | collective-permute-start | bytes 589832 | tf_op jit(solution)/shard_map/ppermute | solution.py:93
  131.0 18.6 %collective-permute-start.56 = (bf16[8,12288]{1,0:T(8,128)(2,1)S(1)}, bf16[8,12288]{1,0:T(8,128)(2,1)S(1)}, u32[]{:S(2)}, u32[]{:S(2)}) collective-permute-start(bf16[8,12288]{1,0:T(8,128)(2,1)S(1)} %bitcast.85), channel_id=1, source_target_pairs={{0,1},{1,2},{2,3},{3,0},{4,5},{5,6},{6,7},{7,4},{8,9},{9,10},{10,1... | collective-permute-start | bytes 589832 | tf_op jit(solution)/shard_map/ppermute | solution.py:93
  145.2 13.8 %collective-permute-start.55 = (bf16[8,4,24,128]{3,2,1,0:T(8,128)(2,1)S(1)}, bf16[8,4,24,128]{3,2,1,0:T(8,128)(2,1)S(1)}, u32[]{:S(2)}, u32[]{:S(2)}) collective-permute-start(bf16[8,4,24,128]{3,2,1,0:T(8,128)(2,1)S(1)} %get-tuple-element.18), channel_id=1, source_target_pairs={{4,0},{8,4},{12,8},{16,12},{20,16},{24,20},{28,24},{5,1},{9,5},{13... | collective-permute-start | bytes 589832 | tf_op jit(solution)/shard_map/ppermute | solution.py:22
  146.5 12.5 %collective-permute-start.54 = (bf16[8,4,24,128]{3,2,1,0:T(8,128)(2,1)S(1)}, bf16[8,4,24,128]{3,2,1,0:T(8,128)(2,1)S(1)}, u32[]{:S(2)}, u32[]{:S(2)}) collective-permute-start(bf16[8,4,24,128]{3,2,1,0:T(8,128)(2,1)S(1)} %get-tuple-element.18), channel_id=1, source_target_pairs={{0,4},{4,8},{8,12},{12,16},{16,20},{20,24},{24,28},{1,5},{5,9},{9,... | collective-permute-start | bytes 589832 | tf_op jit(solution)/shard_map/ppermute | solution.py:21
  149.6 3.8 %collective-permute-start.25 = (f32[256,32]{0,1:T(8,128)S(1)}, f32[256,32]{0,1:T(8,128)S(1)}, u32[]{:S(2)}, u32[]{:S(2)}) collective-permute-start(f32[256,32]{0,1:T(8,128)S(1)} %fusion.15), channel_id=1, source_target_pairs={{0,4},{4,0},{8,12},{12,8},{16,20},{20,16},{24,28},{28,24},{1,5},{5... | collective-permute-start | bytes 98312 | tf_op jit(solution)/shard_map/ppermute | solution.py:33
  153.6 4.3 %collective-permute-start.26 = (f32[256,32]{0,1:T(8,128)S(1)}, f32[256,32]{0,1:T(8,128)S(1)}, u32[]{:S(2)}, u32[]{:S(2)}) collective-permute-start(f32[256,32]{0,1:T(8,128)S(1)} %add.570), channel_id=1, source_target_pairs={{0,8},{4,12},{8,0},{12,4},{16,24},{20,28},{24,16},{28,20},{1,9},{5... | collective-permute-start | bytes 98312 | tf_op jit(solution)/shard_map/ppermute | solution.py:33
  156.0 4.0 %collective-permute-start.60 = (f32[256,32]{0,1:T(8,128)S(1)}, f32[256,32]{0,1:T(8,128)S(1)}, u32[]{:S(2)}, u32[]{:S(2)}) collective-permute-start(f32[256,32]{0,1:T(8,128)S(1)} %add.650), channel_id=1, source_target_pairs={{0,8},{4,12},{8,0},{12,4},{16,24},{20,28},{24,16},{28,20},{1,9},{5... | collective-permute-start | bytes 98312 | tf_op jit(solution)/shard_map/ppermute | solution.py:33
  157.9 4.1 %collective-permute-start.27 = (f32[256,32]{0,1:T(8,128)S(1)}, f32[256,32]{0,1:T(8,128)S(1)}, u32[]{:S(2)}, u32[]{:S(2)}) collective-permute-start(f32[256,32]{0,1:T(8,128)S(1)} %add.571), channel_id=1, source_target_pairs={{0,16},{4,20},{8,24},{12,28},{16,0},{20,4},{24,8},{28,12},{1,17},{... | collective-permute-start | bytes 98312 | tf_op jit(solution)/shard_map/ppermute | solution.py:33
  160.0 8.4 %collective-permute-start.61 = (f32[256,32]{0,1:T(8,128)S(1)}, f32[256,32]{0,1:T(8,128)S(1)}, u32[]{:S(2)}, u32[]{:S(2)}) collective-permute-start(f32[256,32]{0,1:T(8,128)S(1)} %add.651), channel_id=1, source_target_pairs={{0,16},{4,20},{8,24},{12,28},{16,0},{20,4},{24,8},{28,12},{1,17},{... | collective-permute-start | bytes 98312 | tf_op jit(solution)/shard_map/ppermute | solution.py:33
  164.1 10.3 %collective-permute-start.30 = (bf16[8,12288]{1,0:T(8,128)(2,1)S(1)}, bf16[8,12288]{1,0:T(8,128)(2,1)S(1)}, u32[]{:S(2)}, u32[]{:S(2)}) collective-permute-start(bf16[8,12288]{1,0:T(8,128)(2,1)S(1)} %get-tuple-element.31), channel_id=1, source_target_pairs={{3,0},{0,1},{1,2},{2,3},{7,4},{4,5},{5,6},{6,7},{11,8},{8,9},{9,10... | collective-permute-start | bytes 589832 | tf_op jit(solution)/shard_map/ppermute | solution.py:108
  164.2 18.0 %collective-permute-start.29 = (bf16[8,12288]{1,0:T(8,128)(2,1)S(1)}, bf16[8,12288]{1,0:T(8,128)(2,1)S(1)}, u32[]{:S(2)}, u32[]{:S(2)}) collective-permute-start(bf16[8,12288]{1,0:T(8,128)(2,1)S(1)} %get-tuple-element.32), channel_id=1, source_target_pairs={{2,0},{3,1},{0,2},{1,3},{6,4},{7,5},{4,6},{5,7},{10,8},{11,9},{8,1... | collective-permute-start | bytes 589832 | tf_op jit(solution)/shard_map/ppermute | solution.py:108
  168.4 24.6 %collective-permute-start.28 = (bf16[8,12288]{1,0:T(8,128)(2,1)S(1)}, bf16[8,12288]{1,0:T(8,128)(2,1)S(1)}, u32[]{:S(2)}, u32[]{:S(2)}) collective-permute-start(bf16[8,12288]{1,0:T(8,128)(2,1)S(1)} %get-tuple-element.30), channel_id=1, source_target_pairs={{1,0},{2,1},{3,2},{0,3},{5,4},{6,5},{7,6},{4,7},{9,8},{10,9},{11,1... | collective-permute-start | bytes 589832 | tf_op jit(solution)/shard_map/ppermute | solution.py:108
  170.5 32.1 %collective-permute-start.64 = (bf16[8,12288]{1,0:T(8,128)(2,1)S(1)}, bf16[8,12288]{1,0:T(8,128)(2,1)S(1)}, u32[]{:S(2)}, u32[]{:S(2)}) collective-permute-start(bf16[8,12288]{1,0:T(8,128)(2,1)S(1)} %get-tuple-element.36), channel_id=1, source_target_pairs={{3,0},{0,1},{1,2},{2,3},{7,4},{4,5},{5,6},{6,7},{11,8},{8,9},{9,10... | collective-permute-start | bytes 589832 | tf_op jit(solution)/shard_map/ppermute | solution.py:108
  172.5 30.0 %collective-permute-start.63 = (bf16[8,12288]{1,0:T(8,128)(2,1)S(1)}, bf16[8,12288]{1,0:T(8,128)(2,1)S(1)}, u32[]{:S(2)}, u32[]{:S(2)}) collective-permute-start(bf16[8,12288]{1,0:T(8,128)(2,1)S(1)} %get-tuple-element.37), channel_id=1, source_target_pairs={{2,0},{3,1},{0,2},{1,3},{6,4},{7,5},{4,6},{5,7},{10,8},{11,9},{8,1... | collective-permute-start | bytes 589832 | tf_op jit(solution)/shard_map/ppermute | solution.py:108
  174.4 28.2 %collective-permute-start.62 = (bf16[8,12288]{1,0:T(8,128)(2,1)S(1)}, bf16[8,12288]{1,0:T(8,128)(2,1)S(1)}, u32[]{:S(2)}, u32[]{:S(2)}) collective-permute-start(bf16[8,12288]{1,0:T(8,128)(2,1)S(1)} %get-tuple-element.35), channel_id=1, source_target_pairs={{1,0},{2,1},{3,2},{0,3},{5,4},{6,5},{7,6},{4,7},{9,8},{10,9},{11,1... | collective-permute-start | bytes 589832 | tf_op jit(solution)/shard_map/ppermute | solution.py:108
  (24 other events, 138.0 us)

commit v4 on v3

--- a/solution.py
+++ b/solution.py
@@ -33,6 +33,31 @@
         value = value + lax.ppermute(value, axis, pairs)
         stride *= 2
     return value
+
+
+def band_gather(block, peers):
+    blocks = [block] + [jnp.zeros_like(block) for _ in range(1, peers)]
+    rightward, leftward = block, block
+    for s in range(1, peers):
+        rightward = lax.ppermute(rightward, "band", [(i, i + 1) for i in range(s - 1, peers - 1)])
+        leftward = lax.ppermute(leftward, "band", [(i + 1, i) for i in range(peers - s)])
+        blocks[s] = blocks[s] + rightward
+        blocks[peers - s] = blocks[peers - s] + leftward
+    return blocks
+
+
+def band_reduce(terms, peers):
+    total = terms[0]
+    if peers == 1:
+        return total
+    carry_left = jnp.zeros(terms[0].shape, jnp.bfloat16)
+    carry_right = jnp.zeros(terms[0].shape, jnp.bfloat16)
+    for s in range(1, peers):
+        message = (terms[peers - s] + carry_left.astype(jnp.float32)).astype(jnp.bfloat16)
+        carry_left = lax.ppermute(message, "band", [(k, k - 1) for k in range(peers - s, peers)])
+        message = (terms[s] + carry_right.astype(jnp.float32)).astype(jnp.bfloat16)
+        carry_right = lax.ppermute(message, "band", [(k, k + 1) for k in range(s)])
+    return total + carry_left.astype(jnp.float32) + carry_right.astype(jnp.float32)
 
 
 def second_sum(padded, extent_x, extent_y, extent_z):
@@ -89,10 +114,7 @@
         padded = jnp.pad(padded, ((0, 0), (0, 0), (4, 4), (4, 4)))
         kinetic = -0.5 * second_sum(padded, width_x, width_y, width_z)
         rounded = direction.astype(jnp.bfloat16).reshape(local_bands, local_cells)
-        blocks = [rounded] + [
-            lax.ppermute(rounded, "band", [(i, (i + d) % band_count) for i in range(band_count)])
-            for d in range(1, band_count)
-        ]
+        blocks = band_gather(rounded, band_count)
         gathered = jnp.concatenate(blocks, axis=0)
         partial_margin = lax.dot_general(
             occupied_rows, gathered, (((1,), (1,)), ((), ())), preferred_element_type=jnp.float32
@@ -101,12 +123,10 @@
         scaled = (margins * weight_scale).astype(jnp.bfloat16)
         terms = lax.dot_general(
             scaled, occupied_rows, (((0,), (0,)), ((), ())), preferred_element_type=jnp.float32
-        ).astype(jnp.bfloat16)
-        projected = terms[:local_bands].astype(jnp.float32)
-        for d in range(1, band_count):
-            part = terms[d * local_bands : (d + 1) * local_bands]
-            back = lax.ppermute(part, "band", [((i + d) % band_count, i) for i in range(band_count)])
-            projected = projected + back.astype(jnp.float32)
+        )
+        projected = band_reduce(
+            [terms[d * local_bands : (d + 1) * local_bands] for d in range(band_count)], band_count
+        )
         applied = kinetic + potential_shift * direction + projected.reshape(direction.shape)
         curvature = grid_sum(inner_product(direction, applied), "grid")
         step_size = norm_now / curvature

time: 214 us -> 245 us (1.14)
  starting transfers between devices: 86.9 us -> 157 us
  waiting for transfers between devices: 96.9 us -> 54.3 us
    ppermute x24 -> x48, starting transfers between devices: 42.4 us -> 110 us  [the longest x12 37.9 us: band_reduce(): carry_right = lax.ppermute(message, 'band', [(k, k + 1) for k in range(s)])]
    ppermute x24 -> x48, waiting for transfers between devices: 61.7 us -> 24 us  [the longest x12 15.8 us: band_reduce(): lax.ppermute(message, 'band', [(k, k - 1) for k in range(peers - s, peers)])]
    ppermute x36, waiting for transfers between devices: 35.2 us -> 30.2 us  [grid_sum(): value = value + lax.ppermute(value, axis, pairs)]
  transfers between devices with their start and end apart: 68 -> 92, of which waited for: 30 -> 28; matrix products, arithmetic and copies ran while one was open for 10% -> 10% of each run, Pallas kernels for 0% -> 0%
where the time goes in v4:
time: 245 us; the launch traced here: 242 us
  starting transfers between devices  157 us (64%)
  waiting for transfers between devices  54.3 us (22%)
  matrix products  19.2 us (8%)
  other arithmetic  8.84 us (4%)
    ppermute x12, starting transfers between devices, band_reduce(): carry_right = lax.ppermute(message, 'band', [(k, k + 1) for k in range(s)])  37.9 us
    ppermute x12, starting transfers between devices, band_gather(): lax.ppermute(rightward, 'band', [(i, i + 1) for i in range(s - 1, peers -...  32.1 us
    ppermute x36, starting transfers between devices, grid_sum(): value = value + lax.ppermute(value, axis, pairs)  31 us
    ppermute x36, waiting for transfers between devices, grid_sum(): value = value + lax.ppermute(value, axis, pairs)  30.2 us
    ppermute x12, starting transfers between devices, band_gather(): lax.ppermute(leftward, 'band', [(i + 1, i) for i in range(peers - s)])  24.7 us
    ppermute x12, waiting for transfers between devices, band_reduce(): lax.ppermute(message, 'band', [(k, k - 1) for k in range(peers - s, peers)])  15.8 us
    ppermute x12, starting transfers between devices, band_reduce(): lax.ppermute(message, 'band', [(k, k - 1) for k in range(peers - s, peers)])  15.6 us
    dot_general x4, matrix products, chain(): lax.dot_general(occupied_rows, gathered, (((1,), (1,)), ((), ())), prefer...  11 us
  transfers between devices with their start and end apart: 92, of which 28 were waited for; matrix products, arithmetic and copies ran while one was open for 10% of the time, Pallas kernels for 0%

profile of v4, /device:TPU:8, one launch (start us, length us, event | category | flops | bytes accessed | tf_op | source)
XLA Modules:
  0.0 242.5 jit_solution(12828931715030749125)
XLA Ops:
  1.9 3.5 %collective-permute-start.5 = (bf16[8,12288]{1,0:T(8,128)(2,1)S(1)}, bf16[8,12288]{1,0:T(8,128)(2,1)S(1)}, u32[]{:S(2)}, u32[]{:S(2)}) collective-permute-start(bf16[8,12288]{1,0:T(8,128)(2,1)S(1)} %bitcast.86), channel_id=1, source_target_pairs={{0,1},{1,2},{2,3},{4,5},{5,6},{6,7},{8,9},{9,10},{10,11},{12,13},{... | collective-permute-start | bytes 589832 | tf_op jit(solution)/shard_map/ppermute | solution.py:42
  5.4 2.4 collective-permute-start.6
  7.9 3.5 %collective-permute-start.51 = (bf16[8,12288]{1,0:T(8,128)(2,1)S(1)}, bf16[8,12288]{1,0:T(8,128)(2,1)S(1)}, u32[]{:S(2)}, u32[]{:S(2)}) collective-permute-start(bf16[8,12288]{1,0:T(8,128)(2,1)S(1)} %bitcast.80), channel_id=1, source_target_pairs={{0,1},{1,2},{2,3},{4,5},{5,6},{6,7},{8,9},{9,10},{10,11},{12,13},{... | collective-permute-start | bytes 589832 | tf_op jit(solution)/shard_map/ppermute | solution.py:42
  11.3 2.4 collective-permute-start.52
  13.7 3.5 %collective-permute-start.9 = (bf16[8,12288]{1,0:T(8,128)(2,1)S(1)}, bf16[8,12288]{1,0:T(8,128)(2,1)S(1)}, u32[]{:S(2)}, u32[]{:S(2)}) collective-permute-start(bf16[8,12288]{1,0:T(8,128)(2,1)S(1)} %collective-permute-done.5), channel_id=1, source_target_pairs={{1,2},{2,3},{5,6},{6,7},{9,10},{10,11},{13,14},{14,15},{17,18},{18... | collective-permute-start | bytes 589832 | tf_op jit(solution)/shard_map/ppermute | solution.py:42
  20.5 3.9 %collective-permute-start.55 = (bf16[8,12288]{1,0:T(8,128)(2,1)S(1)}, bf16[8,12288]{1,0:T(8,128)(2,1)S(1)}, u32[]{:S(2)}, u32[]{:S(2)}) collective-permute-start(bf16[8,12288]{1,0:T(8,128)(2,1)S(1)} %collective-permute-done.51), channel_id=1, source_target_pairs={{1,2},{2,3},{5,6},{6,7},{9,10},{10,11},{13,14},{14,15},{17,18},{18... | collective-permute-start | bytes 589832 | tf_op jit(solution)/shard_map/ppermute | solution.py:42
  29.5 2.3 collective-permute-start.3
  31.8 2.2 collective-permute-done.53
  36.1 4.0 %collective-permute-start.54 = (bf16[8,12288]{1,0:T(8,128)(2,1)S(1)}, bf16[8,12288]{1,0:T(8,128)(2,1)S(1)}, u32[]{:S(2)}, u32[]{:S(2)}) collective-permute-start(bf16[8,12288]{1,0:T(8,128)(2,1)S(1)} %collective-permute-done.53), channel_id=1, source_target_pairs={{1,0},{5,4},{9,8},{13,12},{17,16},{21,20},{25,24},{29,28}} | collective-permute-start | bytes 589832 | tf_op jit(solution)/shard_map/ppermute | solution.py:43
  40.1 5.0 %fusion.16 = f32[256,32]{0,1:T(8,128)S(1)} fusion(bf16[32,8,96,128]{3,2,1,0:T(8,128)(2,1)} %bitcast.59, bf16[8,12288]{1,0:T(8,128)(2,1)S(1)} %add.613, bf16[8,12288]{1,0:T(8,128)(2,1)S(1)} %add.612, bf16[8,12288]{1,0:T(8,128)(2,1)S(1)} %add.611, bf16[8,12288]{1,0:T(8,128)(2,1)S(1)} %bitcast.88), kind=kOutput, calls=%fused_computation.80 | convolution fusion | flops 204472320 | bytes 7110656 | tf_op jit(solution)/shard_map/dot_general | solution.py:119
  47.1 2.1 collective-permute-start.11
  49.3 2.0 fusion.22
  59.5 2.0 fusion.12
  63.6 2.0 fusion.4
  70.8 6.5 %collective-permute-done.15 = bf16[8,12288]{1,0:T(8,128)(2,1)S(1)} collective-permute-done((bf16[8,12288]{1,0:T(8,128)(2,1)S(1)}, bf16[8,12288]{1,0:T(8,128)(2,1)S(1)}, u32[]{:S(2)}, u32[]{:S(2)}) %collective-permute-start.15) | collective-permute-done | bytes 196640 | tf_op jit(solution)/shard_map/ppermute | solution.py:57
  77.3 5.1 %collective-permute-start.18 = (bf16[8,12288]{1,0:T(8,128)(2,1)S(1)}, bf16[8,12288]{1,0:T(8,128)(2,1)S(1)}, u32[]{:S(2)}, u32[]{:S(2)}) collective-permute-start(bf16[8,12288]{1,0:T(8,128)(2,1)S(1)} %get-tuple-element.41), channel_id=1, source_target_pairs={{0,1},{1,2},{4,5},{5,6},{8,9},{9,10},{12,13},{13,14},{16,17},{17,1... | collective-permute-start | bytes 589832 | tf_op jit(solution)/shard_map/ppermute | solution.py:59
  84.5 3.9 %collective-permute-start.64 = (bf16[8,12288]{1,0:T(8,128)(2,1)S(1)}, bf16[8,12288]{1,0:T(8,128)(2,1)S(1)}, u32[]{:S(2)}, u32[]{:S(2)}) collective-permute-start(bf16[8,12288]{1,0:T(8,128)(2,1)S(1)} %get-tuple-element.37), channel_id=1, source_target_pairs={{0,1},{1,2},{4,5},{5,6},{8,9},{9,10},{12,13},{13,14},{16,17},{17,1... | collective-permute-start | bytes 589832 | tf_op jit(solution)/shard_map/ppermute | solution.py:59
  88.4 1.9 collective-permute-start.62
  90.4 4.0 %collective-permute-start.19 = (bf16[8,12288]{1,0:T(8,128)(2,1)S(1)}, bf16[8,12288]{1,0:T(8,128)(2,1)S(1)}, u32[]{:S(2)}, u32[]{:S(2)}) collective-permute-start(bf16[8,12288]{1,0:T(8,128)(2,1)S(1)} %add_convert_fusion.12), channel_id=1, source_target_pairs={{0,1},{1,2},{2,3},{4,5},{5,6},{6,7},{8,9},{9,10},{10,11},{12,13},{... | collective-permute-start | bytes 589832 | tf_op jit(solution)/shard_map/ppermute | solution.py:59
  94.5 3.3 %collective-permute-start.65 = (bf16[8,12288]{1,0:T(8,128)(2,1)S(1)}, bf16[8,12288]{1,0:T(8,128)(2,1)S(1)}, u32[]{:S(2)}, u32[]{:S(2)}) collective-permute-start(bf16[8,12288]{1,0:T(8,128)(2,1)S(1)} %add_convert_fusion.4), channel_id=1, source_target_pairs={{0,1},{1,2},{2,3},{4,5},{5,6},{6,7},{8,9},{9,10},{10,11},{12,13},{... | collective-permute-start | bytes 589832 | tf_op jit(solution)/shard_map/ppermute | solution.py:59
  98.4 3.7 %collective-permute-done.65 = bf16[8,12288]{1,0:T(8,128)(2,1)S(1)} collective-permute-done((bf16[8,12288]{1,0:T(8,128)(2,1)S(1)}, bf16[8,12288]{1,0:T(8,128)(2,1)S(1)}, u32[]{:S(2)}, u32[]{:S(2)}) %collective-permute-start.65) | collective-permute-done | bytes 196640 | tf_op jit(solution)/shard_map/ppermute | solution.py:59
  102.2 2.5 %multiply_reduce_fusion.6 = (f32[8]{0:T(128)S(1)}, f32[8]{0:T(128)S(1)}, f32[8]{0:T(128)S(1)}, f32[8]{0:T(128)S(1)}, f32[8,4,24,128]{3,2,1,0:T(8,128)S(1)}, /*index=5*/f32[8,4,24,128]{3,2,1,0:T(8,128)S(1)}) fusion(f32[16,4,24,128]{3,2,1,0:T(8,128)S(1)} %copy-done, f32[8,4,24,128]{3,0,2,1:T(8,128)S(1)} %bitcast.73, f32[8]{0:T(128)S(1)} %get-tuple-element.53, ...), kind=kLoop, calls=%fused_computation.320 | loop fusion | flops 9043936 | bytes 11846784 | tf_op jit(solution)/shard_map/reduce_sum | solution.py:89
  117.6 3.0 %collective-permute-done.24 = f32[8]{0:T(128)S(1)} collective-permute-done((f32[8]{0:T(128)S(1)}, f32[8]{0:T(128)S(1)}, u32[]{:S(2)}, u32[]{:S(2)}) %collective-permute-start.24) | collective-permute-done | bytes 64 | tf_op jit(solution)/shard_map/ppermute | solution.py:33
  121.2 2.9 %collective-permute-done.25 = f32[8]{0:T(128)S(1)} collective-permute-done((f32[8]{0:T(128)S(1)}, f32[8]{0:T(128)S(1)}, u32[]{:S(2)}, u32[]{:S(2)}) %collective-permute-start.25) | collective-permute-done | bytes 64 | tf_op jit(solution)/shard_map/ppermute | solution.py:33
  124.4 1.9 collective-permute-start.29
  126.4 3.9 %collective-permute-start.28 = (bf16[8,12288]{1,0:T(8,128)(2,1)S(1)}, bf16[8,12288]{1,0:T(8,128)(2,1)S(1)}, u32[]{:S(2)}, u32[]{:S(2)}) collective-permute-start(bf16[8,12288]{1,0:T(8,128)(2,1)S(1)} %bitcast.78), channel_id=1, source_target_pairs={{0,1},{1,2},{2,3},{4,5},{5,6},{6,7},{8,9},{9,10},{10,11},{12,13},{... | collective-permute-start | bytes 589832 | tf_op jit(solution)/shard_map/ppermute | solution.py:42
  132.0 3.0 %collective-permute-done.70 = f32[8]{0:T(128)S(1)} collective-permute-done((f32[8]{0:T(128)S(1)}, f32[8]{0:T(128)S(1)}, u32[]{:S(2)}, u32[]{:S(2)}) %collective-permute-start.70) | collective-permute-done | bytes 64 | tf_op jit(solution)/shard_map/ppermute | solution.py:33
  135.7 2.9 %collective-permute-done.71 = f32[8]{0:T(128)S(1)} collective-permute-done((f32[8]{0:T(128)S(1)}, f32[8]{0:T(128)S(1)}, u32[]{:S(2)}, u32[]{:S(2)}) %collective-permute-start.71) | collective-permute-done | bytes 64 | tf_op jit(solution)/shard_map/ppermute | solution.py:33
  138.8 3.6 %collective-permute-start.74 = (bf16[8,12288]{1,0:T(8,128)(2,1)S(1)}, bf16[8,12288]{1,0:T(8,128)(2,1)S(1)}, u32[]{:S(2)}, u32[]{:S(2)}) collective-permute-start(bf16[8,12288]{1,0:T(8,128)(2,1)S(1)} %bitcast.83), channel_id=1, source_target_pairs={{0,1},{1,2},{2,3},{4,5},{5,6},{6,7},{8,9},{9,10},{10,11},{12,13},{... | collective-permute-start | bytes 589832 | tf_op jit(solution)/shard_map/ppermute | solution.py:42
  142.4 2.3 collective-permute-start.75
  144.7 3.6 %collective-permute-start.32 = (bf16[8,12288]{1,0:T(8,128)(2,1)S(1)}, bf16[8,12288]{1,0:T(8,128)(2,1)S(1)}, u32[]{:S(2)}, u32[]{:S(2)}) collective-permute-start(bf16[8,12288]{1,0:T(8,128)(2,1)S(1)} %collective-permute-done.28), channel_id=1, source_target_pairs={{1,2},{2,3},{5,6},{6,7},{9,10},{10,11},{13,14},{14,15},{17,18},{18... | collective-permute-start | bytes 589832 | tf_op jit(solution)/shard_map/ppermute | solution.py:42
  150.2 3.9 %collective-permute-start.78 = (bf16[8,12288]{1,0:T(8,128)(2,1)S(1)}, bf16[8,12288]{1,0:T(8,128)(2,1)S(1)}, u32[]{:S(2)}, u32[]{:S(2)}) collective-permute-start(bf16[8,12288]{1,0:T(8,128)(2,1)S(1)} %collective-permute-done.74), channel_id=1, source_target_pairs={{1,2},{2,3},{5,6},{6,7},{9,10},{10,11},{13,14},{14,15},{17,18},{18... | collective-permute-start | bytes 589832 | tf_op jit(solution)/shard_map/ppermute | solution.py:42
  159.5 3.0 %collective-permute-start.26 = (bf16[8,4,24,128]{3,2,1,0:T(8,128)(2,1)S(1)}, bf16[8,4,24,128]{3,2,1,0:T(8,128)(2,1)S(1)}, u32[]{:S(2)}, u32[]{:S(2)}) collective-permute-start(bf16[8,4,24,128]{3,2,1,0:T(8,128)(2,1)S(1)} %get-tuple-element.8), channel_id=1, source_target_pairs={{0,4},{4,8},{8,12},{12,16},{16,20},{20,24},{24,28},{1,5},{5,9},{9,... | collective-permute-start | bytes 589832 | tf_op jit(solution)/shard_map/ppermute | solution.py:21
  166.3 2.0 fusion.19
  168.3 2.8 %collective-permute-start.72 = (bf16[8,4,24,128]{3,2,1,0:T(8,128)(2,1)S(1)}, bf16[8,4,24,128]{3,2,1,0:T(8,128)(2,1)S(1)}, u32[]{:S(2)}, u32[]{:S(2)}) collective-permute-start(bf16[8,4,24,128]{3,2,1,0:T(8,128)(2,1)S(1)} %get-tuple-element.18), channel_id=1, source_target_pairs={{0,4},{4,8},{8,12},{12,16},{16,20},{20,24},{24,28},{1,5},{5,9},{9,... | collective-permute-start | bytes 589832 | tf_op jit(solution)/shard_map/ppermute | solution.py:21
  172.5 2.0 fusion.25
  174.7 2.4 %collective-permute-start.35 = (f32[256,32]{0,1:T(8,128)S(1)}, f32[256,32]{0,1:T(8,128)S(1)}, u32[]{:S(2)}, u32[]{:S(2)}) collective-permute-start(f32[256,32]{0,1:T(8,128)S(1)} %add.659), channel_id=1, source_target_pairs={{0,8},{4,12},{8,0},{12,4},{16,24},{20,28},{24,16},{28,20},{1,9},{5... | collective-permute-start | bytes 98312 | tf_op jit(solution)/shard_map/ppermute | solution.py:33
  183.3 2.0 fusion.8
  187.6 2.0 fusion
  194.4 9.3 %collective-permute-done.38 = bf16[8,12288]{1,0:T(8,128)(2,1)S(1)} collective-permute-done((bf16[8,12288]{1,0:T(8,128)(2,1)S(1)}, bf16[8,12288]{1,0:T(8,128)(2,1)S(1)}, u32[]{:S(2)}, u32[]{:S(2)}) %collective-permute-start.38) | collective-permute-done | bytes 196640 | tf_op jit(solution)/shard_map/ppermute | solution.py:57
  203.8 4.6 %collective-permute-start.41 = (bf16[8,12288]{1,0:T(8,128)(2,1)S(1)}, bf16[8,12288]{1,0:T(8,128)(2,1)S(1)}, u32[]{:S(2)}, u32[]{:S(2)}) collective-permute-start(bf16[8,12288]{1,0:T(8,128)(2,1)S(1)} %get-tuple-element.29), channel_id=1, source_target_pairs={{0,1},{1,2},{4,5},{5,6},{8,9},{9,10},{12,13},{13,14},{16,17},{17,1... | collective-permute-start | bytes 589832 | tf_op jit(solution)/shard_map/ppermute | solution.py:59
  210.4 3.9 %collective-permute-start.87 = (bf16[8,12288]{1,0:T(8,128)(2,1)S(1)}, bf16[8,12288]{1,0:T(8,128)(2,1)S(1)}, u32[]{:S(2)}, u32[]{:S(2)}) collective-permute-start(bf16[8,12288]{1,0:T(8,128)(2,1)S(1)} %get-tuple-element.33), channel_id=1, source_target_pairs={{0,1},{1,2},{4,5},{5,6},{8,9},{9,10},{12,13},{13,14},{16,17},{17,1... | collective-permute-start | bytes 589832 | tf_op jit(solution)/shard_map/ppermute | solution.py:59
  214.3 1.9 collective-permute-start.85
  216.3 3.9 %collective-permute-start.42 = (bf16[8,12288]{1,0:T(8,128)(2,1)S(1)}, bf16[8,12288]{1,0:T(8,128)(2,1)S(1)}, u32[]{:S(2)}, u32[]{:S(2)}) collective-permute-start(bf16[8,12288]{1,0:T(8,128)(2,1)S(1)} %add_convert_fusion.8), channel_id=1, source_target_pairs={{0,1},{1,2},{2,3},{4,5},{5,6},{6,7},{8,9},{9,10},{10,11},{12,13},{... | collective-permute-start | bytes 589832 | tf_op jit(solution)/shard_map/ppermute | solution.py:59
  220.3 3.7 %collective-permute-start.88 = (bf16[8,12288]{1,0:T(8,128)(2,1)S(1)}, bf16[8,12288]{1,0:T(8,128)(2,1)S(1)}, u32[]{:S(2)}, u32[]{:S(2)}) collective-permute-start(bf16[8,12288]{1,0:T(8,128)(2,1)S(1)} %add_convert_fusion), channel_id=1, source_target_pairs={{0,1},{1,2},{2,3},{4,5},{5,6},{6,7},{8,9},{9,10},{10,11},{12,13},{... | collective-permute-start | bytes 589832 | tf_op jit(solution)/shard_map/ppermute | solution.py:59
  228.3 1.9 collective-permute-done.44
  235.5 1.9 collective-permute-done.90
  238.5 2.5 %collective-permute-done.91 = f32[8]{0:T(128)S(1)} collective-permute-done((f32[8]{0:T(128)S(1)}, f32[8]{0:T(128)S(1)}, u32[]{:S(2)}, u32[]{:S(2)}) %collective-permute-start.91) | collective-permute-done | bytes 64 | tf_op jit(solution)/shard_map/ppermute | solution.py:33
  (235 shorter events, 87.7 us)
Async XLA Ops:
  1.9 11.8 %collective-permute-start.5 = (bf16[8,12288]{1,0:T(8,128)(2,1)S(1)}, bf16[8,12288]{1,0:T(8,128)(2,1)S(1)}, u32[]{:S(2)}, u32[]{:S(2)}) collective-permute-start(bf16[8,12288]{1,0:T(8,128)(2,1)S(1)} %bitcast.86), channel_id=1, source_target_pairs={{0,1},{1,2},{2,3},{4,5},{5,6},{6,7},{8,9},{9,10},{10,11},{12,13},{... | collective-permute-start | bytes 589832 | tf_op jit(solution)/shard_map/ppermute | solution.py:42
  5.4 11.8 %collective-permute-start.6 = (bf16[8,12288]{1,0:T(8,128)(2,1)S(1)}, bf16[8,12288]{1,0:T(8,128)(2,1)S(1)}, u32[]{:S(2)}, u32[]{:S(2)}) collective-permute-start(bf16[8,12288]{1,0:T(8,128)(2,1)S(1)} %bitcast.87), channel_id=1, source_target_pairs={{1,0},{2,1},{3,2},{5,4},{6,5},{7,6},{9,8},{10,9},{11,10},{13,12},{... | collective-permute-start | bytes 589832 | tf_op jit(solution)/shard_map/ppermute | solution.py:43
  7.9 12.6 %collective-permute-start.51 = (bf16[8,12288]{1,0:T(8,128)(2,1)S(1)}, bf16[8,12288]{1,0:T(8,128)(2,1)S(1)}, u32[]{:S(2)}, u32[]{:S(2)}) collective-permute-start(bf16[8,12288]{1,0:T(8,128)(2,1)S(1)} %bitcast.80), channel_id=1, source_target_pairs={{0,1},{1,2},{2,3},{4,5},{5,6},{6,7},{8,9},{9,10},{10,11},{12,13},{... | collective-permute-start | bytes 589832 | tf_op jit(solution)/shard_map/ppermute | solution.py:42
  11.3 13.1 %collective-permute-start.52 = (bf16[8,12288]{1,0:T(8,128)(2,1)S(1)}, bf16[8,12288]{1,0:T(8,128)(2,1)S(1)}, u32[]{:S(2)}, u32[]{:S(2)}) collective-permute-start(bf16[8,12288]{1,0:T(8,128)(2,1)S(1)} %bitcast.81), channel_id=1, source_target_pairs={{1,0},{2,1},{3,2},{5,4},{6,5},{7,6},{9,8},{10,9},{11,10},{13,12},{... | collective-permute-start | bytes 589832 | tf_op jit(solution)/shard_map/ppermute | solution.py:43
  13.7 12.6 %collective-permute-start.9 = (bf16[8,12288]{1,0:T(8,128)(2,1)S(1)}, bf16[8,12288]{1,0:T(8,128)(2,1)S(1)}, u32[]{:S(2)}, u32[]{:S(2)}) collective-permute-start(bf16[8,12288]{1,0:T(8,128)(2,1)S(1)} %collective-permute-done.5), channel_id=1, source_target_pairs={{1,2},{2,3},{5,6},{6,7},{9,10},{10,11},{13,14},{14,15},{17,18},{18... | collective-permute-start | bytes 589832 | tf_op jit(solution)/shard_map/ppermute | solution.py:42
  17.2 9.8 %collective-permute-start.7 = (bf16[8,12288]{1,0:T(8,128)(2,1)S(1)}, bf16[8,12288]{1,0:T(8,128)(2,1)S(1)}, u32[]{:S(2)}, u32[]{:S(2)}) collective-permute-start(bf16[8,12288]{1,0:T(8,128)(2,1)S(1)} %collective-permute-done.6), channel_id=1, source_target_pairs={{1,0},{2,1},{5,4},{6,5},{9,8},{10,9},{13,12},{14,13},{17,16},{18,1... | collective-permute-start | bytes 589832 | tf_op jit(solution)/shard_map/ppermute | solution.py:43
  19.2 32.3 %collective-permute-start.4 = (bf16[8,4,24,128]{3,2,1,0:T(8,128)(2,1)S(1)}, bf16[8,4,24,128]{3,2,1,0:T(8,128)(2,1)S(1)}, u32[]{:S(2)}, u32[]{:S(2)}) collective-permute-start(bf16[8,4,24,128]{3,2,1,0:T(8,128)(2,1)S(1)} %get-tuple-element.49), channel_id=1, source_target_pairs={{4,0},{8,4},{12,8},{16,12},{20,16},{24,20},{28,24},{5,1},{9,5},{13... | collective-permute-start | bytes 589832 | tf_op jit(solution)/shard_map/ppermute | solution.py:22
  20.5 9.1 %collective-permute-start.55 = (bf16[8,12288]{1,0:T(8,128)(2,1)S(1)}, bf16[8,12288]{1,0:T(8,128)(2,1)S(1)}, u32[]{:S(2)}, u32[]{:S(2)}) collective-permute-start(bf16[8,12288]{1,0:T(8,128)(2,1)S(1)} %collective-permute-done.51), channel_id=1, source_target_pairs={{1,2},{2,3},{5,6},{6,7},{9,10},{10,11},{13,14},{14,15},{17,18},{18... | collective-permute-start | bytes 589832 | tf_op jit(solution)/shard_map/ppermute | solution.py:42
  24.4 9.5 %collective-permute-start.53 = (bf16[8,12288]{1,0:T(8,128)(2,1)S(1)}, bf16[8,12288]{1,0:T(8,128)(2,1)S(1)}, u32[]{:S(2)}, u32[]{:S(2)}) collective-permute-start(bf16[8,12288]{1,0:T(8,128)(2,1)S(1)} %collective-permute-done.52), channel_id=1, source_target_pairs={{1,0},{2,1},{5,4},{6,5},{9,8},{10,9},{13,12},{14,13},{17,16},{18,1... | collective-permute-start | bytes 589832 | tf_op jit(solution)/shard_map/ppermute | solution.py:43
  26.4 9.0 %collective-permute-start.10 = (bf16[8,12288]{1,0:T(8,128)(2,1)S(1)}, bf16[8,12288]{1,0:T(8,128)(2,1)S(1)}, u32[]{:S(2)}, u32[]{:S(2)}) collective-permute-start(bf16[8,12288]{1,0:T(8,128)(2,1)S(1)} %collective-permute-done.9), channel_id=1, source_target_pairs={{2,3},{6,7},{10,11},{14,15},{18,19},{22,23},{26,27},{30,31}} | collective-permute-start | bytes 589832 | tf_op jit(solution)/shard_map/ppermute | solution.py:42
  27.1 9.0 %collective-permute-start.8 = (bf16[8,12288]{1,0:T(8,128)(2,1)S(1)}, bf16[8,12288]{1,0:T(8,128)(2,1)S(1)}, u32[]{:S(2)}, u32[]{:S(2)}) collective-permute-start(bf16[8,12288]{1,0:T(8,128)(2,1)S(1)} %collective-permute-done.7), channel_id=1, source_target_pairs={{1,0},{5,4},{9,8},{13,12},{17,16},{21,20},{25,24},{29,28}} | collective-permute-start | bytes 589832 | tf_op jit(solution)/shard_map/ppermute | solution.py:43
  29.5 23.5 %collective-permute-start.3 = (bf16[8,4,24,128]{3,2,1,0:T(8,128)(2,1)S(1)}, bf16[8,4,24,128]{3,2,1,0:T(8,128)(2,1)S(1)}, u32[]{:S(2)}, u32[]{:S(2)}) collective-permute-start(bf16[8,4,24,128]{3,2,1,0:T(8,128)(2,1)S(1)} %get-tuple-element.49), channel_id=1, source_target_pairs={{0,4},{4,8},{8,12},{12,16},{16,20},{20,24},{24,28},{1,5},{5,9},{9,... | collective-permute-start | bytes 589832 | tf_op jit(solution)/shard_map/ppermute | solution.py:21
  34.0 23.1 %collective-permute-start.50 = (bf16[8,4,24,128]{3,2,1,0:T(8,128)(2,1)S(1)}, bf16[8,4,24,128]{3,2,1,0:T(8,128)(2,1)S(1)}, u32[]{:S(2)}, u32[]{:S(2)}) collective-permute-start(bf16[8,4,24,128]{3,2,1,0:T(8,128)(2,1)S(1)} %get-tuple-element.48), channel_id=1, source_target_pairs={{4,0},{8,4},{12,8},{16,12},{20,16},{24,20},{28,24},{5,1},{9,5},{13... | collective-permute-start | bytes 589832 | tf_op jit(solution)/shard_map/ppermute | solution.py:22
  35.3 9.8 %collective-permute-start.56 = (bf16[8,12288]{1,0:T(8,128)(2,1)S(1)}, bf16[8,12288]{1,0:T(8,128)(2,1)S(1)}, u32[]{:S(2)}, u32[]{:S(2)}) collective-permute-start(bf16[8,12288]{1,0:T(8,128)(2,1)S(1)} %collective-permute-done.55), channel_id=1, source_target_pairs={{2,3},{6,7},{10,11},{14,15},{18,19},{22,23},{26,27},{30,31}} | collective-permute-start | bytes 589832 | tf_op jit(solution)/shard_map/ppermute | solution.py:42
  36.1 11.0 %collective-permute-start.54 = (bf16[8,12288]{1,0:T(8,128)(2,1)S(1)}, bf16[8,12288]{1,0:T(8,128)(2,1)S(1)}, u32[]{:S(2)}, u32[]{:S(2)}) collective-permute-start(bf16[8,12288]{1,0:T(8,128)(2,1)S(1)} %collective-permute-done.53), channel_id=1, source_target_pairs={{1,0},{5,4},{9,8},{13,12},{17,16},{21,20},{25,24},{29,28}} | collective-permute-start | bytes 589832 | tf_op jit(solution)/shard_map/ppermute | solution.py:43
  45.1 11.9 %collective-permute-start.49 = (bf16[8,4,24,128]{3,2,1,0:T(8,128)(2,1)S(1)}, bf16[8,4,24,128]{3,2,1,0:T(8,128)(2,1)S(1)}, u32[]{:S(2)}, u32[]{:S(2)}) collective-permute-start(bf16[8,4,24,128]{3,2,1,0:T(8,128)(2,1)S(1)} %get-tuple-element.48), channel_id=1, source_target_pairs={{0,4},{4,8},{8,12},{12,16},{16,20},{20,24},{24,28},{1,5},{5,9},{9,... | collective-permute-start | bytes 589832 | tf_op jit(solution)/shard_map/ppermute | solution.py:21
  62.3 8.5 %collective-permute-start.17 = (bf16[8,12288]{1,0:T(8,128)(2,1)S(1)}, bf16[8,12288]{1,0:T(8,128)(2,1)S(1)}, u32[]{:S(2)}, u32[]{:S(2)}) collective-permute-start(bf16[8,12288]{1,0:T(8,128)(2,1)S(1)} %get-tuple-element.43), channel_id=1, source_target_pairs={{0,1},{4,5},{8,9},{12,13},{16,17},{20,21},{24,25},{28,29}} | collective-permute-start | bytes 589832 | tf_op jit(solution)/shard_map/ppermute | solution.py:59
  66.4 18.0 %collective-permute-start.63 = (bf16[8,12288]{1,0:T(8,128)(2,1)S(1)}, bf16[8,12288]{1,0:T(8,128)(2,1)S(1)}, u32[]{:S(2)}, u32[]{:S(2)}) collective-permute-start(bf16[8,12288]{1,0:T(8,128)(2,1)S(1)} %get-tuple-element.39), channel_id=1, source_target_pairs={{0,1},{4,5},{8,9},{12,13},{16,17},{20,21},{24,25},{28,29}} | collective-permute-start | bytes 589832 | tf_op jit(solution)/shard_map/ppermute | solution.py:59
  67.7 9.5 %collective-permute-start.15 = (bf16[8,12288]{1,0:T(8,128)(2,1)S(1)}, bf16[8,12288]{1,0:T(8,128)(2,1)S(1)}, u32[]{:S(2)}, u32[]{:S(2)}) collective-permute-start(bf16[8,12288]{1,0:T(8,128)(2,1)S(1)} %add_convert_fusion.15), channel_id=1, source_target_pairs={{2,1},{3,2},{6,5},{7,6},{10,9},{11,10},{14,13},{15,14},{18,17},{19... | collective-permute-start | bytes 589832 | tf_op jit(solution)/shard_map/ppermute | solution.py:57
  69.1 15.3 %collective-permute-start.61 = (bf16[8,12288]{1,0:T(8,128)(2,1)S(1)}, bf16[8,12288]{1,0:T(8,128)(2,1)S(1)}, u32[]{:S(2)}, u32[]{:S(2)}) collective-permute-start(bf16[8,12288]{1,0:T(8,128)(2,1)S(1)} %add_convert_fusion.7), channel_id=1, source_target_pairs={{2,1},{3,2},{6,5},{7,6},{10,9},{11,10},{14,13},{15,14},{18,17},{19... | collective-permute-start | bytes 589832 | tf_op jit(solution)/shard_map/ppermute | solution.py:57
  77.3 13.0 %collective-permute-start.18 = (bf16[8,12288]{1,0:T(8,128)(2,1)S(1)}, bf16[8,12288]{1,0:T(8,128)(2,1)S(1)}, u32[]{:S(2)}, u32[]{:S(2)}) collective-permute-start(bf16[8,12288]{1,0:T(8,128)(2,1)S(1)} %get-tuple-element.41), channel_id=1, source_target_pairs={{0,1},{1,2},{4,5},{5,6},{8,9},{9,10},{12,13},{13,14},{16,17},{17,1... | collective-permute-start | bytes 589832 | tf_op jit(solution)/shard_map/ppermute | solution.py:59
  82.4 15.4 %collective-permute-start.16 = (bf16[8,12288]{1,0:T(8,128)(2,1)S(1)}, bf16[8,12288]{1,0:T(8,128)(2,1)S(1)}, u32[]{:S(2)}, u32[]{:S(2)}) collective-permute-start(bf16[8,12288]{1,0:T(8,128)(2,1)S(1)} %get-tuple-element.40), channel_id=1, source_target_pairs={{1,0},{2,1},{3,2},{5,4},{6,5},{7,6},{9,8},{10,9},{11,10},{13,12},{... | collective-permute-start | bytes 589832 | tf_op jit(solution)/shard_map/ppermute | solution.py:57
  84.5 10.0 %collective-permute-start.64 = (bf16[8,12288]{1,0:T(8,128)(2,1)S(1)}, bf16[8,12288]{1,0:T(8,128)(2,1)S(1)}, u32[]{:S(2)}, u32[]{:S(2)}) collective-permute-start(bf16[8,12288]{1,0:T(8,128)(2,1)S(1)} %get-tuple-element.37), channel_id=1, source_target_pairs={{0,1},{1,2},{4,5},{5,6},{8,9},{9,10},{12,13},{13,14},{16,17},{17,1... | collective-permute-start | bytes 589832 | tf_op jit(solution)/shard_map/ppermute | solution.py:59
  88.4 10.0 %collective-permute-start.62 = (bf16[8,12288]{1,0:T(8,128)(2,1)S(1)}, bf16[8,12288]{1,0:T(8,128)(2,1)S(1)}, u32[]{:S(2)}, u32[]{:S(2)}) collective-permute-start(bf16[8,12288]{1,0:T(8,128)(2,1)S(1)} %get-tuple-element.36), channel_id=1, source_target_pairs={{1,0},{2,1},{3,2},{5,4},{6,5},{7,6},{9,8},{10,9},{11,10},{13,12},{... | collective-permute-start | bytes 589832 | tf_op jit(solution)/shard_map/ppermute | solution.py:57
  90.4 7.9 %collective-permute-start.19 = (bf16[8,12288]{1,0:T(8,128)(2,1)S(1)}, bf16[8,12288]{1,0:T(8,128)(2,1)S(1)}, u32[]{:S(2)}, u32[]{:S(2)}) collective-permute-start(bf16[8,12288]{1,0:T(8,128)(2,1)S(1)} %add_convert_fusion.12), channel_id=1, source_target_pairs={{0,1},{1,2},{2,3},{4,5},{5,6},{6,7},{8,9},{9,10},{10,11},{12,13},{... | collective-permute-start | bytes 589832 | tf_op jit(solution)/shard_map/ppermute | solution.py:59
  124.4 23.8 %collective-permute-start.29 = (bf16[8,12288]{1,0:T(8,128)(2,1)S(1)}, bf16[8,12288]{1,0:T(8,128)(2,1)S(1)}, u32[]{:S(2)}, u32[]{:S(2)}) collective-permute-start(bf16[8,12288]{1,0:T(8,128)(2,1)S(1)} %bitcast.77), channel_id=1, source_target_pairs={{1,0},{2,1},{3,2},{5,4},{6,5},{7,6},{9,8},{10,9},{11,10},{13,12},{... | collective-permute-start | bytes 589832 | tf_op jit(solution)/shard_map/ppermute | solution.py:43
  126.4 18.3 %collective-permute-start.28 = (bf16[8,12288]{1,0:T(8,128)(2,1)S(1)}, bf16[8,12288]{1,0:T(8,128)(2,1)S(1)}, u32[]{:S(2)}, u32[]{:S(2)}) collective-permute-start(bf16[8,12288]{1,0:T(8,128)(2,1)S(1)} %bitcast.78), channel_id=1, source_target_pairs={{0,1},{1,2},{2,3},{4,5},{5,6},{6,7},{8,9},{9,10},{10,11},{12,13},{... | collective-permute-start | bytes 589832 | tf_op jit(solution)/shard_map/ppermute | solution.py:42
  138.8 11.4 %collective-permute-start.74 = (bf16[8,12288]{1,0:T(8,128)(2,1)S(1)}, bf16[8,12288]{1,0:T(8,128)(2,1)S(1)}, u32[]{:S(2)}, u32[]{:S(2)}) collective-permute-start(bf16[8,12288]{1,0:T(8,128)(2,1)S(1)} %bitcast.83), channel_id=1, source_target_pairs={{0,1},{1,2},{2,3},{4,5},{5,6},{6,7},{8,9},{9,10},{10,11},{12,13},{... | collective-permute-start | bytes 589832 | tf_op jit(solution)/shard_map/ppermute | solution.py:42
  142.4 11.8 %collective-permute-start.75 = (bf16[8,12288]{1,0:T(8,128)(2,1)S(1)}, bf16[8,12288]{1,0:T(8,128)(2,1)S(1)}, u32[]{:S(2)}, u32[]{:S(2)}) collective-permute-start(bf16[8,12288]{1,0:T(8,128)(2,1)S(1)} %bitcast.84), channel_id=1, source_target_pairs={{1,0},{2,1},{3,2},{5,4},{6,5},{7,6},{9,8},{10,9},{11,10},{13,12},{... | collective-permute-start | bytes 589832 | tf_op jit(solution)/shard_map/ppermute | solution.py:43
  144.7 11.4 %collective-permute-start.32 = (bf16[8,12288]{1,0:T(8,128)(2,1)S(1)}, bf16[8,12288]{1,0:T(8,128)(2,1)S(1)}, u32[]{:S(2)}, u32[]{:S(2)}) collective-permute-start(bf16[8,12288]{1,0:T(8,128)(2,1)S(1)} %collective-permute-done.28), channel_id=1, source_target_pairs={{1,2},{2,3},{5,6},{6,7},{9,10},{10,11},{13,14},{14,15},{17,18},{18... | collective-permute-start | bytes 589832 | tf_op jit(solution)/shard_map/ppermute | solution.py:42
  148.3 8.5 %collective-permute-start.30 = (bf16[8,12288]{1,0:T(8,128)(2,1)S(1)}, bf16[8,12288]{1,0:T(8,128)(2,1)S(1)}, u32[]{:S(2)}, u32[]{:S(2)}) collective-permute-start(bf16[8,12288]{1,0:T(8,128)(2,1)S(1)} %collective-permute-done.29), channel_id=1, source_target_pairs={{1,0},{2,1},{5,4},{6,5},{9,8},{10,9},{13,12},{14,13},{17,16},{18,1... | collective-permute-start | bytes 589832 | tf_op jit(solution)/shard_map/ppermute | solution.py:43
  150.2 9.3 %collective-permute-start.78 = (bf16[8,12288]{1,0:T(8,128)(2,1)S(1)}, bf16[8,12288]{1,0:T(8,128)(2,1)S(1)}, u32[]{:S(2)}, u32[]{:S(2)}) collective-permute-start(bf16[8,12288]{1,0:T(8,128)(2,1)S(1)} %collective-permute-done.74), channel_id=1, source_target_pairs={{1,2},{2,3},{5,6},{6,7},{9,10},{10,11},{13,14},{14,15},{17,18},{18... | collective-permute-start | bytes 589832 | tf_op jit(solution)/shard_map/ppermute | solution.py:42
  154.2 8.4 %collective-permute-start.76 = (bf16[8,12288]{1,0:T(8,128)(2,1)S(1)}, bf16[8,12288]{1,0:T(8,128)(2,1)S(1)}, u32[]{:S(2)}, u32[]{:S(2)}) collective-permute-start(bf16[8,12288]{1,0:T(8,128)(2,1)S(1)} %collective-permute-done.75), channel_id=1, source_target_pairs={{1,0},{2,1},{5,4},{6,5},{9,8},{10,9},{13,12},{14,13},{17,16},{18,1... | collective-permute-start | bytes 589832 | tf_op jit(solution)/shard_map/ppermute | solution.py:43
  156.8 7.8 %collective-permute-start.31 = (bf16[8,12288]{1,0:T(8,128)(2,1)S(1)}, bf16[8,12288]{1,0:T(8,128)(2,1)S(1)}, u32[]{:S(2)}, u32[]{:S(2)}) collective-permute-start(bf16[8,12288]{1,0:T(8,128)(2,1)S(1)} %collective-permute-done.30), channel_id=1, source_target_pairs={{1,0},{5,4},{9,8},{13,12},{17,16},{21,20},{25,24},{29,28}} | collective-permute-start | bytes 589832 | tf_op jit(solution)/shard_map/ppermute | solution.py:43
  158.1 16.6 %collective-permute-start.27 = (bf16[8,4,24,128]{3,2,1,0:T(8,128)(2,1)S(1)}, bf16[8,4,24,128]{3,2,1,0:T(8,128)(2,1)S(1)}, u32[]{:S(2)}, u32[]{:S(2)}) collective-permute-start(bf16[8,4,24,128]{3,2,1,0:T(8,128)(2,1)S(1)} %get-tuple-element.8), channel_id=1, source_target_pairs={{4,0},{8,4},{12,8},{16,12},{20,16},{24,20},{28,24},{5,1},{9,5},{13... | collective-permute-start | bytes 589832 | tf_op jit(solution)/shard_map/ppermute | solution.py:22
  159.5 17.6 %collective-permute-start.26 = (bf16[8,4,24,128]{3,2,1,0:T(8,128)(2,1)S(1)}, bf16[8,4,24,128]{3,2,1,0:T(8,128)(2,1)S(1)}, u32[]{:S(2)}, u32[]{:S(2)}) collective-permute-start(bf16[8,4,24,128]{3,2,1,0:T(8,128)(2,1)S(1)} %get-tuple-element.8), channel_id=1, source_target_pairs={{0,4},{4,8},{8,12},{12,16},{16,20},{20,24},{24,28},{1,5},{5,9},{9,... | collective-permute-start | bytes 589832 | tf_op jit(solution)/shard_map/ppermute | solution.py:21
  162.5 18.0 %collective-permute-start.73 = (bf16[8,4,24,128]{3,2,1,0:T(8,128)(2,1)S(1)}, bf16[8,4,24,128]{3,2,1,0:T(8,128)(2,1)S(1)}, u32[]{:S(2)}, u32[]{:S(2)}) collective-permute-start(bf16[8,4,24,128]{3,2,1,0:T(8,128)(2,1)S(1)} %get-tuple-element.18), channel_id=1, source_target_pairs={{4,0},{8,4},{12,8},{16,12},{20,16},{24,20},{28,24},{5,1},{9,5},{13... | collective-permute-start | bytes 589832 | tf_op jit(solution)/shard_map/ppermute | solution.py:22
  168.3 12.2 %collective-permute-start.72 = (bf16[8,4,24,128]{3,2,1,0:T(8,128)(2,1)S(1)}, bf16[8,4,24,128]{3,2,1,0:T(8,128)(2,1)S(1)}, u32[]{:S(2)}, u32[]{:S(2)}) collective-permute-start(bf16[8,4,24,128]{3,2,1,0:T(8,128)(2,1)S(1)} %get-tuple-element.18), channel_id=1, source_target_pairs={{0,4},{4,8},{8,12},{12,16},{16,20},{20,24},{24,28},{1,5},{5,9},{9,... | collective-permute-start | bytes 589832 | tf_op jit(solution)/shard_map/ppermute | solution.py:21
  186.0 8.3 %collective-permute-start.40 = (bf16[8,12288]{1,0:T(8,128)(2,1)S(1)}, bf16[8,12288]{1,0:T(8,128)(2,1)S(1)}, u32[]{:S(2)}, u32[]{:S(2)}) collective-permute-start(bf16[8,12288]{1,0:T(8,128)(2,1)S(1)} %get-tuple-element.31), channel_id=1, source_target_pairs={{0,1},{4,5},{8,9},{12,13},{16,17},{20,21},{24,25},{28,29}} | collective-permute-start | bytes 589832 | tf_op jit(solution)/shard_map/ppermute | solution.py:59
  190.3 20.0 %collective-permute-start.86 = (bf16[8,12288]{1,0:T(8,128)(2,1)S(1)}, bf16[8,12288]{1,0:T(8,128)(2,1)S(1)}, u32[]{:S(2)}, u32[]{:S(2)}) collective-permute-start(bf16[8,12288]{1,0:T(8,128)(2,1)S(1)} %get-tuple-element.35), channel_id=1, source_target_pairs={{0,1},{4,5},{8,9},{12,13},{16,17},{20,21},{24,25},{28,29}} | collective-permute-start | bytes 589832 | tf_op jit(solution)/shard_map/ppermute | solution.py:59
  191.7 12.0 %collective-permute-start.38 = (bf16[8,12288]{1,0:T(8,128)(2,1)S(1)}, bf16[8,12288]{1,0:T(8,128)(2,1)S(1)}, u32[]{:S(2)}, u32[]{:S(2)}) collective-permute-start(bf16[8,12288]{1,0:T(8,128)(2,1)S(1)} %add_convert_fusion.11), channel_id=1, source_target_pairs={{2,1},{3,2},{6,5},{7,6},{10,9},{11,10},{14,13},{15,14},{18,17},{19... | collective-permute-start | bytes 589832 | tf_op jit(solution)/shard_map/ppermute | solution.py:57
  193.0 17.3 %collective-permute-start.84 = (bf16[8,12288]{1,0:T(8,128)(2,1)S(1)}, bf16[8,12288]{1,0:T(8,128)(2,1)S(1)}, u32[]{:S(2)}, u32[]{:S(2)}) collective-permute-start(bf16[8,12288]{1,0:T(8,128)(2,1)S(1)} %add_convert_fusion.3), channel_id=1, source_target_pairs={{2,1},{3,2},{6,5},{7,6},{10,9},{11,10},{14,13},{15,14},{18,17},{19... | collective-permute-start | bytes 589832 | tf_op jit(solution)/shard_map/ppermute | solution.py:57
  203.8 12.5 %collective-permute-start.41 = (bf16[8,12288]{1,0:T(8,128)(2,1)S(1)}, bf16[8,12288]{1,0:T(8,128)(2,1)S(1)}, u32[]{:S(2)}, u32[]{:S(2)}) collective-permute-start(bf16[8,12288]{1,0:T(8,128)(2,1)S(1)} %get-tuple-element.29), channel_id=1, source_target_pairs={{0,1},{1,2},{4,5},{5,6},{8,9},{9,10},{12,13},{13,14},{16,17},{17,1... | collective-permute-start | bytes 589832 | tf_op jit(solution)/shard_map/ppermute | solution.py:59
  208.4 15.7 %collective-permute-start.39 = (bf16[8,12288]{1,0:T(8,128)(2,1)S(1)}, bf16[8,12288]{1,0:T(8,128)(2,1)S(1)}, u32[]{:S(2)}, u32[]{:S(2)}) collective-permute-start(bf16[8,12288]{1,0:T(8,128)(2,1)S(1)} %get-tuple-element.28), channel_id=1, source_target_pairs={{1,0},{2,1},{3,2},{5,4},{6,5},{7,6},{9,8},{10,9},{11,10},{13,12},{... | collective-permute-start | bytes 589832 | tf_op jit(solution)/shard_map/ppermute | solution.py:57
  210.4 9.8 %collective-permute-start.87 = (bf16[8,12288]{1,0:T(8,128)(2,1)S(1)}, bf16[8,12288]{1,0:T(8,128)(2,1)S(1)}, u32[]{:S(2)}, u32[]{:S(2)}) collective-permute-start(bf16[8,12288]{1,0:T(8,128)(2,1)S(1)} %get-tuple-element.33), channel_id=1, source_target_pairs={{0,1},{1,2},{4,5},{5,6},{8,9},{9,10},{12,13},{13,14},{16,17},{17,1... | collective-permute-start | bytes 589832 | tf_op jit(solution)/shard_map/ppermute | solution.py:59
  214.3 17.0 %collective-permute-start.85 = (bf16[8,12288]{1,0:T(8,128)(2,1)S(1)}, bf16[8,12288]{1,0:T(8,128)(2,1)S(1)}, u32[]{:S(2)}, u32[]{:S(2)}) collective-permute-start(bf16[8,12288]{1,0:T(8,128)(2,1)S(1)} %get-tuple-element.32), channel_id=1, source_target_pairs={{1,0},{2,1},{3,2},{5,4},{6,5},{7,6},{9,8},{10,9},{11,10},{13,12},{... | collective-permute-start | bytes 589832 | tf_op jit(solution)/shard_map/ppermute | solution.py:57
  216.3 8.0 %collective-permute-start.42 = (bf16[8,12288]{1,0:T(8,128)(2,1)S(1)}, bf16[8,12288]{1,0:T(8,128)(2,1)S(1)}, u32[]{:S(2)}, u32[]{:S(2)}) collective-permute-start(bf16[8,12288]{1,0:T(8,128)(2,1)S(1)} %add_convert_fusion.8), channel_id=1, source_target_pairs={{0,1},{1,2},{2,3},{4,5},{5,6},{6,7},{8,9},{9,10},{10,11},{12,13},{... | collective-permute-start | bytes 589832 | tf_op jit(solution)/shard_map/ppermute | solution.py:59
  220.3 11.0 %collective-permute-start.88 = (bf16[8,12288]{1,0:T(8,128)(2,1)S(1)}, bf16[8,12288]{1,0:T(8,128)(2,1)S(1)}, u32[]{:S(2)}, u32[]{:S(2)}) collective-permute-start(bf16[8,12288]{1,0:T(8,128)(2,1)S(1)} %add_convert_fusion), channel_id=1, source_target_pairs={{0,1},{1,2},{2,3},{4,5},{5,6},{6,7},{8,9},{9,10},{10,11},{12,13},{... | collective-permute-start | bytes 589832 | tf_op jit(solution)/shard_map/ppermute | solution.py:59
  (49 other events, 243.7 us)

commit v5 on v3

--- a/solution.py
+++ b/solution.py
@@ -89,11 +89,9 @@
         padded = jnp.pad(padded, ((0, 0), (0, 0), (4, 4), (4, 4)))
         kinetic = -0.5 * second_sum(padded, width_x, width_y, width_z)
         rounded = direction.astype(jnp.bfloat16).reshape(local_bands, local_cells)
-        blocks = [rounded] + [
-            lax.ppermute(rounded, "band", [(i, (i + d) % band_count) for i in range(band_count)])
-            for d in range(1, band_count)
-        ]
-        gathered = jnp.concatenate(blocks, axis=0)
+        gathered = lax.all_to_all(
+            jnp.concatenate([rounded] * band_count, axis=0), "band", 0, 0, tiled=True
+        )
         partial_margin = lax.dot_general(
             occupied_rows, gathered, (((1,), (1,)), ((), ())), preferred_element_type=jnp.float32
         )
@@ -102,11 +100,8 @@
         terms = lax.dot_general(
             scaled, occupied_rows, (((0,), (0,)), ((), ())), preferred_element_type=jnp.float32
         ).astype(jnp.bfloat16)
-        projected = terms[:local_bands].astype(jnp.float32)
-        for d in range(1, band_count):
-            part = terms[d * local_bands : (d + 1) * local_bands]
-            back = lax.ppermute(part, "band", [((i + d) % band_count, i) for i in range(band_count)])
-            projected = projected + back.astype(jnp.float32)
+        received = lax.all_to_all(terms, "band", 0, 0, tiled=True).astype(jnp.float32)
+        projected = received.reshape(band_count, local_bands, local_cells).sum(axis=0)
         applied = kinetic + potential_shift * direction + projected.reshape(direction.shape)
         curvature = grid_sum(inner_product(direction, applied), "grid")
         step_size = norm_now / curvature

time: 214 us -> 239 us (1.12)
  matrix products: 19.1 us -> 39.6 us
  waiting for transfers between devices: 96.9 us -> 76.9 us
  starting transfers between devices: 86.9 us -> 101 us
  other arithmetic: 7.82 us -> 15.5 us
    ppermute x24 -> x0, waiting for transfers between devices: 61.7 us -> none  [the longest x12 42.4 us: chain(): lax.ppermute(part, 'band', [((i + d) % band_count, i) for i in range(band...]
    all_to_all x0 -> x8, starting transfers between devices: none -> 46.5 us  [the longest x4 25 us: chain(): lax.all_to_all(jnp.concatenate([rounded] * band_count, axis=0), 'band', 0...]
    ppermute x24 -> x0, starting transfers between devices: 42.4 us -> none  [the longest x12 25.9 us: chain(): lax.ppermute(rounded, 'band', [(i, (i + d) % band_count) for i in range(b...]
    all_to_all x0 -> x8, waiting for transfers between devices: none -> 25.1 us  [the longest x4 20.4 us: chain(): lax.all_to_all(jnp.concatenate([rounded] * band_count, axis=0), 'band', 0...]
    ppermute x36, waiting for transfers between devices: 35.2 us -> 50.2 us  [grid_sum(): value = value + lax.ppermute(value, axis, pairs)]
    dot_general x4, matrix products: 8.07 us -> 20 us  [chain(): lax.dot_general(scaled, occupied_rows, (((0,), (0,)), ((), ())), preferre...]
    dot_general x4, matrix products: 11.1 us -> 19.6 us  [chain(): lax.dot_general(occupied_rows, gathered, (((1,), (1,)), ((), ())), prefer...]
    ppermute x36, starting transfers between devices: 28.9 us -> 36.1 us  [grid_sum(): value = value + lax.ppermute(value, axis, pairs)]
  transfers between devices with their start and end apart: 68 -> 52, of which waited for: 30 -> 31; matrix products, arithmetic and copies ran while one was open for 10% -> 19% of each run, Pallas kernels for 0% -> 0%
where the time goes in v5:
time: 239 us; the launch traced here: 236 us
  starting transfers between devices  101 us (42%)
  waiting for transfers between devices  76.9 us (32%)
  matrix products  39.6 us (17%)
  other arithmetic  15.5 us (6%)
    ppermute x36, waiting for transfers between devices, grid_sum(): value = value + lax.ppermute(value, axis, pairs)  50.2 us
    ppermute x36, starting transfers between devices, grid_sum(): value = value + lax.ppermute(value, axis, pairs)  36.1 us
    all_to_all x4, starting transfers between devices, chain(): lax.all_to_all(jnp.concatenate([rounded] * band_count, axis=0), 'band', 0...  25 us
    all_to_all x4, starting transfers between devices, chain(): lax.all_to_all(terms, 'band', 0, 0, tiled=True).astype(jnp.float32)  21.5 us
    all_to_all x4, waiting for transfers between devices, chain(): lax.all_to_all(jnp.concatenate([rounded] * band_count, axis=0), 'band', 0...  20.4 us
    dot_general x4, matrix products, chain(): lax.dot_general(scaled, occupied_rows, (((0,), (0,)), ((), ())), preferre...  20 us
    dot_general x4, matrix products, chain(): lax.dot_general(occupied_rows, gathered, (((1,), (1,)), ((), ())), prefer...  19.6 us
    ppermute x4, starting transfers between devices, with_halo(): before = lax.ppermute(last, axis, up)  13.6 us
  transfers between devices with their start and end apart: 52, of which 31 were waited for; matrix products, arithmetic and copies ran while one was open for 19% of the time, Pallas kernels for 0%

profile of v5, /device:TPU:8, one launch (start us, length us, event | category | flops | bytes accessed | tf_op | source)
XLA Modules:
  0.0 236.4 jit_solution(2411040180289890567)
XLA Ops:
  2.8 5.3 %all-to-all-start = ((bf16[4,8,12288]{2,1,0:T(8,128)(2,1)}), bf16[4,8,12288]{2,1,0:T(8,128)(2,1)S(1)}, u32[]{:S(2)}, u32[]{:S(2)}) async-start(bf16[4,8,12288]{2,1,0:T(8,128)(2,1)} %maximum_bitcast_fusion), calls=%async_computation | async-start | bytes 1572864 | tf_op jit(solution)/shard_map/all_to_all | solution.py:92
  9.2 15.8 %all-to-all-done = bf16[4,8,12288]{2,1,0:T(8,128)(2,1)S(1)} async-done(((bf16[4,8,12288]{2,1,0:T(8,128)(2,1)}), bf16[4,8,12288]{2,1,0:T(8,128)(2,1)S(1)}, u32[]{:S(2)}, u32[]{:S(2)}) %all-to-all-start) | async-done | bytes 786464 | tf_op jit(solution)/shard_map/all_to_all | solution.py:92
  25.0 6.7 %all-to-all-start.4 = ((bf16[4,8,12288]{2,1,0:T(8,128)(2,1)}), bf16[4,8,12288]{2,1,0:T(8,128)(2,1)S(1)}, u32[]{:S(2)}, u32[]{:S(2)}) async-start(bf16[4,8,12288]{2,1,0:T(8,128)(2,1)} %maximum_bitcast_fusion.2), calls=%async_computation.4 | async-start | bytes 1572864 | tf_op jit(solution)/shard_map/all_to_all | solution.py:92
  31.7 5.0 %fusion.16 = f32[256,32]{0,1:T(8,128)S(1)} fusion(bf16[32,8,96,128]{3,2,1,0:T(8,128)(2,1)} %bitcast.95, bf16[4,8,12288]{2,1,0:T(8,128)(2,1)S(1)} %all-to-all-done), kind=kOutput, calls=%fused_computation.88 | convolution fusion | flops 201326592 | bytes 7110656 | tf_op jit(solution)/shard_map/dot_general | solution.py:95
  39.4 2.4 %collective-permute-done.6 = f32[256,32]{0,1:T(8,128)S(1)} collective-permute-done((f32[256,32]{0,1:T(8,128)S(1)}, f32[256,32]{0,1:T(8,128)S(1)}, u32[]{:S(2)}, u32[]{:S(2)}) %collective-permute-start.6) | collective-permute-done | bytes 32800 | tf_op jit(solution)/shard_map/ppermute | solution.py:33
  41.9 1.5 collective-permute-start.7
  43.4 2.4 %collective-permute-done.7 = f32[256,32]{0,1:T(8,128)S(1)} collective-permute-done((f32[256,32]{0,1:T(8,128)S(1)}, f32[256,32]{0,1:T(8,128)S(1)}, u32[]{:S(2)}, u32[]{:S(2)}) %collective-permute-start.7) | collective-permute-done | bytes 32800 | tf_op jit(solution)/shard_map/ppermute | solution.py:33
  45.8 2.9 %fusion = bf16[4,8,12288]{2,1,0:T(8,128)(2,1)} fusion(bf16[32,8,96,128]{3,2,1,0:T(8,128)(2,1)S(1)} %bitcast.102, f32[256,32]{0,1:T(8,128)S(1)} %add.496, f32[256,32]{0,1:T(8,128)S(1)} %collective-permute-done.7), kind=kOutput, calls=%fused_computation.68 | convolution fusion | flops 201744384 | bytes 7143424 | tf_op jit(solution)/shard_map/dot_general | solution.py:100
  48.7 6.1 %all-to-all-start.1 = ((bf16[4,8,12288]{2,1,0:T(8,128)(2,1)}), bf16[4,8,12288]{2,1,0:T(8,128)(2,1)S(1)}, u32[]{:S(2)}, u32[]{:S(2)}) async-start(bf16[4,8,12288]{2,1,0:T(8,128)(2,1)} %fusion), calls=%async_computation.1 | async-start | bytes 1572864 | tf_op jit(solution)/shard_map/all_to_all | solution.py:103
  54.8 4.8 %fusion.22 = f32[256,32]{0,1:T(8,128)S(1)} fusion(bf16[32,8,96,128]{3,2,1,0:T(8,128)(2,1)} %bitcast.96, bf16[4,8,12288]{2,1,0:T(8,128)(2,1)S(1)} %all-to-all-done.4), kind=kOutput, calls=%fused_computation.90 | convolution fusion | flops 201326592 | bytes 7110656 | tf_op jit(solution)/shard_map/dot_general | solution.py:95
  62.3 2.4 %collective-permute-done.28 = f32[256,32]{0,1:T(8,128)S(1)} collective-permute-done((f32[256,32]{0,1:T(8,128)S(1)}, f32[256,32]{0,1:T(8,128)S(1)}, u32[]{:S(2)}, u32[]{:S(2)}) %collective-permute-start.28) | collective-permute-done | bytes 32800 | tf_op jit(solution)/shard_map/ppermute | solution.py:33
  64.8 1.5 collective-permute-start.29
  66.3 2.4 %collective-permute-done.29 = f32[256,32]{0,1:T(8,128)S(1)} collective-permute-done((f32[256,32]{0,1:T(8,128)S(1)}, f32[256,32]{0,1:T(8,128)S(1)}, u32[]{:S(2)}, u32[]{:S(2)}) %collective-permute-start.29) | collective-permute-done | bytes 32800 | tf_op jit(solution)/shard_map/ppermute | solution.py:33
  68.7 5.7 %fusion.2 = bf16[4,8,12288]{2,1,0:T(8,128)(2,1)} fusion(bf16[32,8,96,128]{3,2,1,0:T(8,128)(2,1)} %bitcast.97, f32[256,32]{0,1:T(8,128)S(1)} %add.570, f32[256,32]{0,1:T(8,128)S(1)} %collective-permute-done.29), kind=kOutput, calls=%fused_computation.70 | convolution fusion | flops 201744384 | bytes 7143424 | tf_op jit(solution)/shard_map/dot_general | solution.py:100
  74.4 5.2 %all-to-all-start.5 = ((bf16[4,8,12288]{2,1,0:T(8,128)(2,1)}), bf16[4,8,12288]{2,1,0:T(8,128)(2,1)}, u32[]{:S(2)}, u32[]{:S(2)}) async-start(bf16[4,8,12288]{2,1,0:T(8,128)(2,1)} %fusion.2), calls=%async_computation.5 | async-start | bytes 1572864 | tf_op jit(solution)/shard_map/all_to_all | solution.py:103
  80.9 3.0 %collective-permute-start.3 = (bf16[8,4,24,128]{3,2,1,0:T(8,128)(2,1)S(1)}, bf16[8,4,24,128]{3,2,1,0:T(8,128)(2,1)S(1)}, u32[]{:S(2)}, u32[]{:S(2)}) collective-permute-start(bf16[8,4,24,128]{3,2,1,0:T(8,128)(2,1)S(1)} %get-tuple-element.33), channel_id=1, source_target_pairs={{0,4},{4,8},{8,12},{12,16},{16,20},{20,24},{24,28},{1,5},{5,9},{9,... | collective-permute-start | bytes 589832 | tf_op jit(solution)/shard_map/ppermute | solution.py:21
  85.2 3.8 %collective-permute-start.25 = (bf16[8,4,24,128]{3,2,1,0:T(8,128)(2,1)S(1)}, bf16[8,4,24,128]{3,2,1,0:T(8,128)(2,1)S(1)}, u32[]{:S(2)}, u32[]{:S(2)}) collective-permute-start(bf16[8,4,24,128]{3,2,1,0:T(8,128)(2,1)S(1)} %get-tuple-element.32), channel_id=1, source_target_pairs={{0,4},{4,8},{8,12},{12,16},{16,20},{20,24},{24,28},{1,5},{5,9},{9,... | collective-permute-start | bytes 589832 | tf_op jit(solution)/shard_map/ppermute | solution.py:21
  90.2 4.7 %all-to-all-done.5 = bf16[4,8,12288]{2,1,0:T(8,128)(2,1)} async-done(((bf16[4,8,12288]{2,1,0:T(8,128)(2,1)}), bf16[4,8,12288]{2,1,0:T(8,128)(2,1)}, u32[]{:S(2)}, u32[]{:S(2)}) %all-to-all-start.5) | async-done | bytes 786464 | tf_op jit(solution)/shard_map/all_to_all | solution.py:103
  96.3 2.4 %multiply_reduce_fusion.6 = (f32[8]{0:T(128)S(1)}, f32[8]{0:T(128)S(1)}, f32[8]{0:T(128)S(1)}, f32[8]{0:T(128)S(1)}, f32[8,4,24,128]{3,2,1,0:T(8,128)S(1)}, /*index=5*/f32[8,4,24,128]{3,2,1,0:T(8,128)S(1)}) fusion(f32[16,4,24,128]{3,2,1,0:T(8,128)S(1)} %copy-done.1, f32[8,4,24,128]{3,2,1,0:T(8,128)S(1)} %bitcast.107, f32[8]{0:T(128)S(1)} %get-tuple-element.37, ...), kind=kLoop, calls=%fused_computation.288 | loop fusion | flops 9043936 | bytes 11846784 | tf_op jit(solution)/shard_map/reduce_sum | solution.py:64
  104.0 2.9 %collective-permute-start.10 = (f32[8]{0:T(128)S(1)}, f32[8]{0:T(128)S(1)}, u32[]{:S(2)}, u32[]{:S(2)}) collective-permute-start(f32[8]{0:T(128)S(1)} %add.500), channel_id=1, source_target_pairs={{0,16},{4,20},{8,24},{12,28},{16,0},{20,4},{24,8},{28,12},{1,17},{... | collective-permute-start | bytes 104 | tf_op jit(solution)/shard_map/ppermute | solution.py:33
  107.0 1.9 collective-permute-start.32
  110.7 1.7 collective-permute-done.24
  112.7 3.3 %collective-permute-done.12 = f32[8]{0:T(128)S(1)} collective-permute-done((f32[8]{0:T(128)S(1)}, f32[8]{0:T(128)S(1)}, u32[]{:S(2)}, u32[]{:S(2)}) %collective-permute-start.12) | collective-permute-done | bytes 64 | tf_op jit(solution)/shard_map/ppermute | solution.py:33
  116.2 3.4 %collective-permute-done.13 = f32[8]{0:T(128)S(1)} collective-permute-done((f32[8]{0:T(128)S(1)}, f32[8]{0:T(128)S(1)}, u32[]{:S(2)}, u32[]{:S(2)}) %collective-permute-start.13) | collective-permute-done | bytes 64 | tf_op jit(solution)/shard_map/ppermute | solution.py:33
  121.4 5.5 %all-to-all-start.2 = ((bf16[4,8,12288]{2,1,0:T(8,128)(2,1)}), bf16[4,8,12288]{2,1,0:T(8,128)(2,1)S(1)}, u32[]{:S(2)}, u32[]{:S(2)}) async-start(bf16[4,8,12288]{2,1,0:T(8,128)(2,1)} %maximum_bitcast_fusion.1), calls=%async_computation.2 | async-start | bytes 1572864 | tf_op jit(solution)/shard_map/all_to_all | solution.py:92
  129.5 2.0 collective-permute-done.34
  132.5 2.6 %collective-permute-done.35 = f32[8]{0:T(128)S(1)} collective-permute-done((f32[8]{0:T(128)S(1)}, f32[8]{0:T(128)S(1)}, u32[]{:S(2)}, u32[]{:S(2)}) %collective-permute-start.35) | collective-permute-done | bytes 64 | tf_op jit(solution)/shard_map/ppermute | solution.py:33
  136.8 4.6 %all-to-all-done.2 = bf16[4,8,12288]{2,1,0:T(8,128)(2,1)S(1)} async-done(((bf16[4,8,12288]{2,1,0:T(8,128)(2,1)}), bf16[4,8,12288]{2,1,0:T(8,128)(2,1)S(1)}, u32[]{:S(2)}, u32[]{:S(2)}) %all-to-all-start.2) | async-done | bytes 786464 | tf_op jit(solution)/shard_map/all_to_all | solution.py:92
  141.4 7.5 %all-to-all-start.6 = ((bf16[4,8,12288]{2,1,0:T(8,128)(2,1)}), bf16[4,8,12288]{2,1,0:T(8,128)(2,1)}, u32[]{:S(2)}, u32[]{:S(2)}) async-start(bf16[4,8,12288]{2,1,0:T(8,128)(2,1)} %maximum_bitcast_fusion.3), calls=%async_computation.6 | async-start | bytes 1572864 | tf_op jit(solution)/shard_map/all_to_all | solution.py:92
  148.8 4.8 %fusion.19 = f32[256,32]{0,1:T(8,128)S(1)} fusion(bf16[32,8,96,128]{3,2,1,0:T(8,128)(2,1)} %bitcast.98, bf16[4,8,12288]{2,1,0:T(8,128)(2,1)S(1)} %all-to-all-done.2), kind=kOutput, calls=%fused_computation.89 | convolution fusion | flops 201326592 | bytes 7110656 | tf_op jit(solution)/shard_map/dot_general | solution.py:95
  156.4 2.4 %collective-permute-done.17 = f32[256,32]{0,1:T(8,128)S(1)} collective-permute-done((f32[256,32]{0,1:T(8,128)S(1)}, f32[256,32]{0,1:T(8,128)S(1)}, u32[]{:S(2)}, u32[]{:S(2)}) %collective-permute-start.17) | collective-permute-done | bytes 32800 | tf_op jit(solution)/shard_map/ppermute | solution.py:33
  159.8 3.0 %collective-permute-done.18 = f32[256,32]{0,1:T(8,128)S(1)} collective-permute-done((f32[256,32]{0,1:T(8,128)S(1)}, f32[256,32]{0,1:T(8,128)S(1)}, u32[]{:S(2)}, u32[]{:S(2)}) %collective-permute-start.18) | collective-permute-done | bytes 32800 | tf_op jit(solution)/shard_map/ppermute | solution.py:33
  162.7 5.7 %fusion.1 = bf16[4,8,12288]{2,1,0:T(8,128)(2,1)} fusion(bf16[32,8,96,128]{3,2,1,0:T(8,128)(2,1)} %bitcast.99, f32[256,32]{0,1:T(8,128)S(1)} %add.532, f32[256,32]{0,1:T(8,128)S(1)} %collective-permute-done.18), kind=kOutput, calls=%fused_computation.69 | convolution fusion | flops 201744384 | bytes 7143424 | tf_op jit(solution)/shard_map/dot_general | solution.py:100
  168.4 5.1 %all-to-all-start.3 = ((bf16[4,8,12288]{2,1,0:T(8,128)(2,1)}), bf16[4,8,12288]{2,1,0:T(8,128)(2,1)S(1)}, u32[]{:S(2)}, u32[]{:S(2)}) async-start(bf16[4,8,12288]{2,1,0:T(8,128)(2,1)} %fusion.1), calls=%async_computation.3 | async-start | bytes 1572864 | tf_op jit(solution)/shard_map/all_to_all | solution.py:103
  173.5 5.1 %fusion.25 = f32[256,32]{0,1:T(8,128)S(1)} fusion(bf16[32,8,96,128]{3,2,1,0:T(8,128)(2,1)} %bitcast.100, bf16[4,8,12288]{2,1,0:T(8,128)(2,1)} %all-to-all-done.6), kind=kOutput, calls=%fused_computation.91 | convolution fusion | flops 201326592 | bytes 7110656 | tf_op jit(solution)/shard_map/dot_general | solution.py:95
  181.3 2.4 %collective-permute-done.39 = f32[256,32]{0,1:T(8,128)S(1)} collective-permute-done((f32[256,32]{0,1:T(8,128)S(1)}, f32[256,32]{0,1:T(8,128)S(1)}, u32[]{:S(2)}, u32[]{:S(2)}) %collective-permute-start.39) | collective-permute-done | bytes 32800 | tf_op jit(solution)/shard_map/ppermute | solution.py:33
  184.7 3.0 %collective-permute-done.40 = f32[256,32]{0,1:T(8,128)S(1)} collective-permute-done((f32[256,32]{0,1:T(8,128)S(1)}, f32[256,32]{0,1:T(8,128)S(1)}, u32[]{:S(2)}, u32[]{:S(2)}) %collective-permute-start.40) | collective-permute-done | bytes 32800 | tf_op jit(solution)/shard_map/ppermute | solution.py:33
  187.7 5.7 %fusion.3 = bf16[4,8,12288]{2,1,0:T(8,128)(2,1)} fusion(bf16[32,8,96,128]{3,2,1,0:T(8,128)(2,1)} %bitcast.101, f32[256,32]{0,1:T(8,128)S(1)} %add.606, f32[256,32]{0,1:T(8,128)S(1)} %collective-permute-done.40), kind=kOutput, calls=%fused_computation.71 | convolution fusion | flops 201744384 | bytes 7143424 | tf_op jit(solution)/shard_map/dot_general | solution.py:100
  193.4 5.1 %all-to-all-start.7 = ((bf16[4,8,12288]{2,1,0:T(8,128)(2,1)}), bf16[4,8,12288]{2,1,0:T(8,128)(2,1)}, u32[]{:S(2)}, u32[]{:S(2)}) async-start(bf16[4,8,12288]{2,1,0:T(8,128)(2,1)} %fusion.3), calls=%async_computation.7 | async-start | bytes 1572864 | tf_op jit(solution)/shard_map/all_to_all | solution.py:103
  199.8 3.0 %collective-permute-start.14 = (bf16[8,4,24,128]{3,2,1,0:T(8,128)(2,1)S(1)}, bf16[8,4,24,128]{3,2,1,0:T(8,128)(2,1)S(1)}, u32[]{:S(2)}, u32[]{:S(2)}) collective-permute-start(bf16[8,4,24,128]{3,2,1,0:T(8,128)(2,1)S(1)} %get-tuple-element.8), channel_id=1, source_target_pairs={{0,4},{4,8},{8,12},{12,16},{16,20},{20,24},{24,28},{1,5},{5,9},{9,... | collective-permute-start | bytes 589832 | tf_op jit(solution)/shard_map/ppermute | solution.py:21
  204.1 3.6 %collective-permute-start.36 = (bf16[8,4,24,128]{3,2,1,0:T(8,128)(2,1)S(1)}, bf16[8,4,24,128]{3,2,1,0:T(8,128)(2,1)S(1)}, u32[]{:S(2)}, u32[]{:S(2)}) collective-permute-start(bf16[8,4,24,128]{3,2,1,0:T(8,128)(2,1)S(1)} %get-tuple-element.18), channel_id=1, source_target_pairs={{0,4},{4,8},{8,12},{12,16},{16,20},{20,24},{24,28},{1,5},{5,9},{9,... | collective-permute-start | bytes 589832 | tf_op jit(solution)/shard_map/ppermute | solution.py:21
  209.3 1.8 multiply_reduce_fusion.4
  211.1 3.4 %collective-permute-start.19 = (f32[8]{0:T(128)S(1)}, f32[8]{0:T(128)S(1)}, u32[]{:S(2)}, u32[]{:S(2)}) collective-permute-start(f32[8]{0:T(128)S(1)} %get-tuple-element.6), channel_id=1, source_target_pairs={{0,4},{4,0},{8,12},{12,8},{16,20},{20,16},{24,28},{28,24},{1,5},{5... | collective-permute-start | bytes 104 | tf_op jit(solution)/shard_map/ppermute | solution.py:33
  215.3 2.4 %collective-permute-start.20 = (f32[8]{0:T(128)S(1)}, f32[8]{0:T(128)S(1)}, u32[]{:S(2)}, u32[]{:S(2)}) collective-permute-start(f32[8]{0:T(128)S(1)} %add.535), channel_id=1, source_target_pairs={{0,8},{4,12},{8,0},{12,4},{16,24},{20,28},{24,16},{28,20},{1,9},{5... | collective-permute-start | bytes 104 | tf_op jit(solution)/shard_map/ppermute | solution.py:33
  217.7 1.5 collective-permute-done.20
  219.2 3.3 %collective-permute-start.21 = (f32[8]{0:T(128)S(1)}, f32[8]{0:T(128)S(1)}, u32[]{:S(2)}, u32[]{:S(2)}) collective-permute-start(f32[8]{0:T(128)S(1)} %add.536), channel_id=1, source_target_pairs={{0,16},{4,20},{8,24},{12,28},{16,0},{20,4},{24,8},{28,12},{1,17},{... | collective-permute-start | bytes 104 | tf_op jit(solution)/shard_map/ppermute | solution.py:33
  228.5 2.8 %collective-permute-done.42 = f32[8]{0:T(128)S(1)} collective-permute-done((f32[8]{0:T(128)S(1)}, f32[8]{0:T(128)S(1)}, u32[]{:S(2)}, u32[]{:S(2)}) %collective-permute-start.42) | collective-permute-done | bytes 64 | tf_op jit(solution)/shard_map/ppermute | solution.py:33
  231.3 2.0 collective-permute-start.43
  (150 shorter events, 49.6 us)
Async XLA Ops:
  2.8 22.2 %all-to-all-start = ((bf16[4,8,12288]{2,1,0:T(8,128)(2,1)}), bf16[4,8,12288]{2,1,0:T(8,128)(2,1)S(1)}, u32[]{:S(2)}, u32[]{:S(2)}) async-start(bf16[4,8,12288]{2,1,0:T(8,128)(2,1)} %maximum_bitcast_fusion), calls=%async_computation | async-start | bytes 1572864 | tf_op jit(solution)/shard_map/all_to_all | solution.py:92
  25.0 23.7 %all-to-all-start.4 = ((bf16[4,8,12288]{2,1,0:T(8,128)(2,1)}), bf16[4,8,12288]{2,1,0:T(8,128)(2,1)S(1)}, u32[]{:S(2)}, u32[]{:S(2)}) async-start(bf16[4,8,12288]{2,1,0:T(8,128)(2,1)} %maximum_bitcast_fusion.2), calls=%async_computation.4 | async-start | bytes 1572864 | tf_op jit(solution)/shard_map/all_to_all | solution.py:92
  36.7 1.3 collective-permute-start.5
  38.0 3.9 %collective-permute-start.6 = (f32[256,32]{0,1:T(8,128)S(1)}, f32[256,32]{0,1:T(8,128)S(1)}, u32[]{:S(2)}, u32[]{:S(2)}) collective-permute-start(f32[256,32]{0,1:T(8,128)S(1)} %add.495), channel_id=1, source_target_pairs={{0,8},{4,12},{8,0},{12,4},{16,24},{20,28},{24,16},{28,20},{1,9},{5... | collective-permute-start | bytes 98312 | tf_op jit(solution)/shard_map/ppermute | solution.py:33
  41.9 3.9 %collective-permute-start.7 = (f32[256,32]{0,1:T(8,128)S(1)}, f32[256,32]{0,1:T(8,128)S(1)}, u32[]{:S(2)}, u32[]{:S(2)}) collective-permute-start(f32[256,32]{0,1:T(8,128)S(1)} %add.496), channel_id=1, source_target_pairs={{0,16},{4,20},{8,24},{12,28},{16,0},{20,4},{24,8},{28,12},{1,17},{... | collective-permute-start | bytes 98312 | tf_op jit(solution)/shard_map/ppermute | solution.py:33
  48.7 25.7 %all-to-all-start.1 = ((bf16[4,8,12288]{2,1,0:T(8,128)(2,1)}), bf16[4,8,12288]{2,1,0:T(8,128)(2,1)S(1)}, u32[]{:S(2)}, u32[]{:S(2)}) async-start(bf16[4,8,12288]{2,1,0:T(8,128)(2,1)} %fusion), calls=%async_computation.1 | async-start | bytes 1572864 | tf_op jit(solution)/shard_map/all_to_all | solution.py:103
  59.6 1.3 collective-permute-start.27
  60.8 3.9 %collective-permute-start.28 = (f32[256,32]{0,1:T(8,128)S(1)}, f32[256,32]{0,1:T(8,128)S(1)}, u32[]{:S(2)}, u32[]{:S(2)}) collective-permute-start(f32[256,32]{0,1:T(8,128)S(1)} %add.569), channel_id=1, source_target_pairs={{0,8},{4,12},{8,0},{12,4},{16,24},{20,28},{24,16},{28,20},{1,9},{5... | collective-permute-start | bytes 98312 | tf_op jit(solution)/shard_map/ppermute | solution.py:33
  64.8 3.9 %collective-permute-start.29 = (f32[256,32]{0,1:T(8,128)S(1)}, f32[256,32]{0,1:T(8,128)S(1)}, u32[]{:S(2)}, u32[]{:S(2)}) collective-permute-start(f32[256,32]{0,1:T(8,128)S(1)} %add.570), channel_id=1, source_target_pairs={{0,16},{4,20},{8,24},{12,28},{16,0},{20,4},{24,8},{28,12},{1,17},{... | collective-permute-start | bytes 98312 | tf_op jit(solution)/shard_map/ppermute | solution.py:33
  74.4 20.5 %all-to-all-start.5 = ((bf16[4,8,12288]{2,1,0:T(8,128)(2,1)}), bf16[4,8,12288]{2,1,0:T(8,128)(2,1)}, u32[]{:S(2)}, u32[]{:S(2)}) async-start(bf16[4,8,12288]{2,1,0:T(8,128)(2,1)} %fusion.2), calls=%async_computation.5 | async-start | bytes 1572864 | tf_op jit(solution)/shard_map/all_to_all | solution.py:103
  79.6 9.6 %collective-permute-start.4 = (bf16[8,4,24,128]{3,2,1,0:T(8,128)(2,1)S(1)}, bf16[8,4,24,128]{3,2,1,0:T(8,128)(2,1)S(1)}, u32[]{:S(2)}, u32[]{:S(2)}) collective-permute-start(bf16[8,4,24,128]{3,2,1,0:T(8,128)(2,1)S(1)} %get-tuple-element.33), channel_id=1, source_target_pairs={{4,0},{8,4},{12,8},{16,12},{20,16},{24,20},{28,24},{5,1},{9,5},{13... | collective-permute-start | bytes 589832 | tf_op jit(solution)/shard_map/ppermute | solution.py:22
  80.9 8.3 %collective-permute-start.3 = (bf16[8,4,24,128]{3,2,1,0:T(8,128)(2,1)S(1)}, bf16[8,4,24,128]{3,2,1,0:T(8,128)(2,1)S(1)}, u32[]{:S(2)}, u32[]{:S(2)}) collective-permute-start(bf16[8,4,24,128]{3,2,1,0:T(8,128)(2,1)S(1)} %get-tuple-element.33), channel_id=1, source_target_pairs={{0,4},{4,8},{8,12},{12,16},{16,20},{20,24},{24,28},{1,5},{5,9},{9,... | collective-permute-start | bytes 589832 | tf_op jit(solution)/shard_map/ppermute | solution.py:21
  83.9 5.3 %collective-permute-start.26 = (bf16[8,4,24,128]{3,2,1,0:T(8,128)(2,1)S(1)}, bf16[8,4,24,128]{3,2,1,0:T(8,128)(2,1)S(1)}, u32[]{:S(2)}, u32[]{:S(2)}) collective-permute-start(bf16[8,4,24,128]{3,2,1,0:T(8,128)(2,1)S(1)} %get-tuple-element.32), channel_id=1, source_target_pairs={{4,0},{8,4},{12,8},{16,12},{20,16},{24,20},{28,24},{5,1},{9,5},{13... | collective-permute-start | bytes 589832 | tf_op jit(solution)/shard_map/ppermute | solution.py:22
  85.2 4.7 %collective-permute-start.25 = (bf16[8,4,24,128]{3,2,1,0:T(8,128)(2,1)S(1)}, bf16[8,4,24,128]{3,2,1,0:T(8,128)(2,1)S(1)}, u32[]{:S(2)}, u32[]{:S(2)}) collective-permute-start(bf16[8,4,24,128]{3,2,1,0:T(8,128)(2,1)S(1)} %get-tuple-element.32), channel_id=1, source_target_pairs={{0,4},{4,8},{8,12},{12,16},{16,20},{20,24},{24,28},{1,5},{5,9},{9,... | collective-permute-start | bytes 589832 | tf_op jit(solution)/shard_map/ppermute | solution.py:21
  98.8 2.6 %collective-permute-start = (f32[8]{0:T(128)S(1)}, f32[8]{0:T(128)S(1)}, u32[]{:S(2)}, u32[]{:S(2)}) collective-permute-start(f32[8]{0:T(128)S(1)} %get-tuple-element.5), channel_id=1, source_target_pairs={{0,4},{4,0},{8,12},{12,8},{16,20},{20,16},{24,28},{28,24},{1,5},{5... | collective-permute-start | bytes 104 | tf_op jit(solution)/shard_map/ppermute | solution.py:33
  99.3 2.7 %collective-permute-start.30 = (f32[8]{0:T(128)S(1)}, f32[8]{0:T(128)S(1)}, u32[]{:S(2)}, u32[]{:S(2)}) collective-permute-start(f32[8]{0:T(128)S(1)} %get-tuple-element.3), channel_id=1, source_target_pairs={{0,4},{4,0},{8,12},{12,8},{16,20},{20,16},{24,28},{28,24},{1,5},{5... | collective-permute-start | bytes 104 | tf_op jit(solution)/shard_map/ppermute | solution.py:33
  99.3 4.1 %collective-permute-start.22 = (f32[8]{0:T(128)S(1)}, f32[8]{0:T(128)S(1)}, u32[]{:S(2)}, u32[]{:S(2)}) collective-permute-start(f32[8]{0:T(128)S(1)} %get-tuple-element.4), channel_id=1, source_target_pairs={{0,4},{4,0},{8,12},{12,8},{16,20},{20,16},{24,28},{28,24},{1,5},{5... | collective-permute-start | bytes 104 | tf_op jit(solution)/shard_map/ppermute | solution.py:33
  99.9 4.1 %collective-permute-start.9 = (f32[8]{0:T(128)S(1)}, f32[8]{0:T(128)S(1)}, u32[]{:S(2)}, u32[]{:S(2)}) collective-permute-start(f32[8]{0:T(128)S(1)} %add.499), channel_id=1, source_target_pairs={{0,8},{4,12},{8,0},{12,4},{16,24},{20,28},{24,16},{28,20},{1,9},{5... | collective-permute-start | bytes 104 | tf_op jit(solution)/shard_map/ppermute | solution.py:33
  101.4 5.5 %collective-permute-start.1 = (f32[8]{0:T(128)S(1)}, f32[8]{0:T(128)S(1)}, u32[]{:S(2)}, u32[]{:S(2)}) collective-permute-start(f32[8]{0:T(128)S(1)} %add.464), channel_id=1, source_target_pairs={{0,8},{4,12},{8,0},{12,4},{16,24},{20,28},{24,16},{28,20},{1,9},{5... | collective-permute-start | bytes 104 | tf_op jit(solution)/shard_map/ppermute | solution.py:33
  101.9 5.0 %collective-permute-start.31 = (f32[8]{0:T(128)S(1)}, f32[8]{0:T(128)S(1)}, u32[]{:S(2)}, u32[]{:S(2)}) collective-permute-start(f32[8]{0:T(128)S(1)} %add.573), channel_id=1, source_target_pairs={{0,8},{4,12},{8,0},{12,4},{16,24},{20,28},{24,16},{28,20},{1,9},{5... | collective-permute-start | bytes 104 | tf_op jit(solution)/shard_map/ppermute | solution.py:33
  103.4 5.5 %collective-permute-start.23 = (f32[8]{0:T(128)S(1)}, f32[8]{0:T(128)S(1)}, u32[]{:S(2)}, u32[]{:S(2)}) collective-permute-start(f32[8]{0:T(128)S(1)} %add.539), channel_id=1, source_target_pairs={{0,8},{4,12},{8,0},{12,4},{16,24},{20,28},{24,16},{28,20},{1,9},{5... | collective-permute-start | bytes 104 | tf_op jit(solution)/shard_map/ppermute | solution.py:33
  104.0 5.1 %collective-permute-start.10 = (f32[8]{0:T(128)S(1)}, f32[8]{0:T(128)S(1)}, u32[]{:S(2)}, u32[]{:S(2)}) collective-permute-start(f32[8]{0:T(128)S(1)} %add.500), channel_id=1, source_target_pairs={{0,16},{4,20},{8,24},{12,28},{16,0},{20,4},{24,8},{28,12},{1,17},{... | collective-permute-start | bytes 104 | tf_op jit(solution)/shard_map/ppermute | solution.py:33
  106.9 3.5 %collective-permute-start.2 = (f32[8]{0:T(128)S(1)}, f32[8]{0:T(128)S(1)}, u32[]{:S(2)}, u32[]{:S(2)}) collective-permute-start(f32[8]{0:T(128)S(1)} %add.465), channel_id=1, source_target_pairs={{0,16},{4,20},{8,24},{12,28},{16,0},{20,4},{24,8},{28,12},{1,17},{... | collective-permute-start | bytes 104 | tf_op jit(solution)/shard_map/ppermute | solution.py:33
  107.0 3.8 %collective-permute-start.32 = (f32[8]{0:T(128)S(1)}, f32[8]{0:T(128)S(1)}, u32[]{:S(2)}, u32[]{:S(2)}) collective-permute-start(f32[8]{0:T(128)S(1)} %add.574), channel_id=1, source_target_pairs={{0,16},{4,20},{8,24},{12,28},{16,0},{20,4},{24,8},{28,12},{1,17},{... | collective-permute-start | bytes 104 | tf_op jit(solution)/shard_map/ppermute | solution.py:33
  108.9 3.5 %collective-permute-start.24 = (f32[8]{0:T(128)S(1)}, f32[8]{0:T(128)S(1)}, u32[]{:S(2)}, u32[]{:S(2)}) collective-permute-start(f32[8]{0:T(128)S(1)} %add.540), channel_id=1, source_target_pairs={{0,16},{4,20},{8,24},{12,28},{16,0},{20,4},{24,8},{28,12},{1,17},{... | collective-permute-start | bytes 104 | tf_op jit(solution)/shard_map/ppermute | solution.py:33
  110.7 1.8 collective-permute-start.11
  112.5 3.6 %collective-permute-start.12 = (f32[8]{0:T(128)S(1)}, f32[8]{0:T(128)S(1)}, u32[]{:S(2)}, u32[]{:S(2)}) collective-permute-start(f32[8]{0:T(128)S(1)} %add.502), channel_id=1, source_target_pairs={{0,8},{4,12},{8,0},{12,4},{16,24},{20,28},{24,16},{28,20},{1,9},{5... | collective-permute-start | bytes 104 | tf_op jit(solution)/shard_map/ppermute | solution.py:33
  116.1 3.5 %collective-permute-start.13 = (f32[8]{0:T(128)S(1)}, f32[8]{0:T(128)S(1)}, u32[]{:S(2)}, u32[]{:S(2)}) collective-permute-start(f32[8]{0:T(128)S(1)} %add.503), channel_id=1, source_target_pairs={{0,16},{4,20},{8,24},{12,28},{16,0},{20,4},{24,8},{28,12},{1,17},{... | collective-permute-start | bytes 104 | tf_op jit(solution)/shard_map/ppermute | solution.py:33
  121.4 19.9 %all-to-all-start.2 = ((bf16[4,8,12288]{2,1,0:T(8,128)(2,1)}), bf16[4,8,12288]{2,1,0:T(8,128)(2,1)S(1)}, u32[]{:S(2)}, u32[]{:S(2)}) async-start(bf16[4,8,12288]{2,1,0:T(8,128)(2,1)} %maximum_bitcast_fusion.1), calls=%async_computation.2 | async-start | bytes 1572864 | tf_op jit(solution)/shard_map/all_to_all | solution.py:92
  128.0 3.5 %collective-permute-start.34 = (f32[8]{0:T(128)S(1)}, f32[8]{0:T(128)S(1)}, u32[]{:S(2)}, u32[]{:S(2)}) collective-permute-start(f32[8]{0:T(128)S(1)} %add.576), channel_id=1, source_target_pairs={{0,8},{4,12},{8,0},{12,4},{16,24},{20,28},{24,16},{28,20},{1,9},{5... | collective-permute-start | bytes 104 | tf_op jit(solution)/shard_map/ppermute | solution.py:33
  131.6 3.5 %collective-permute-start.35 = (f32[8]{0:T(128)S(1)}, f32[8]{0:T(128)S(1)}, u32[]{:S(2)}, u32[]{:S(2)}) collective-permute-start(f32[8]{0:T(128)S(1)} %add.577), channel_id=1, source_target_pairs={{0,16},{4,20},{8,24},{12,28},{16,0},{20,4},{24,8},{28,12},{1,17},{... | collective-permute-start | bytes 104 | tf_op jit(solution)/shard_map/ppermute | solution.py:33
  141.4 27.0 %all-to-all-start.6 = ((bf16[4,8,12288]{2,1,0:T(8,128)(2,1)}), bf16[4,8,12288]{2,1,0:T(8,128)(2,1)}, u32[]{:S(2)}, u32[]{:S(2)}) async-start(bf16[4,8,12288]{2,1,0:T(8,128)(2,1)} %maximum_bitcast_fusion.3), calls=%async_computation.6 | async-start | bytes 1572864 | tf_op jit(solution)/shard_map/all_to_all | solution.py:92
  154.9 3.9 %collective-permute-start.17 = (f32[256,32]{0,1:T(8,128)S(1)}, f32[256,32]{0,1:T(8,128)S(1)}, u32[]{:S(2)}, u32[]{:S(2)}) collective-permute-start(f32[256,32]{0,1:T(8,128)S(1)} %add.531), channel_id=1, source_target_pairs={{0,8},{4,12},{8,0},{12,4},{16,24},{20,28},{24,16},{28,20},{1,9},{5... | collective-permute-start | bytes 98312 | tf_op jit(solution)/shard_map/ppermute | solution.py:33
  158.8 3.9 %collective-permute-start.18 = (f32[256,32]{0,1:T(8,128)S(1)}, f32[256,32]{0,1:T(8,128)S(1)}, u32[]{:S(2)}, u32[]{:S(2)}) collective-permute-start(f32[256,32]{0,1:T(8,128)S(1)} %add.532), channel_id=1, source_target_pairs={{0,16},{4,20},{8,24},{12,28},{16,0},{20,4},{24,8},{28,12},{1,17},{... | collective-permute-start | bytes 98312 | tf_op jit(solution)/shard_map/ppermute | solution.py:33
  168.4 25.0 %all-to-all-start.3 = ((bf16[4,8,12288]{2,1,0:T(8,128)(2,1)}), bf16[4,8,12288]{2,1,0:T(8,128)(2,1)S(1)}, u32[]{:S(2)}, u32[]{:S(2)}) async-start(bf16[4,8,12288]{2,1,0:T(8,128)(2,1)} %fusion.1), calls=%async_computation.3 | async-start | bytes 1572864 | tf_op jit(solution)/shard_map/all_to_all | solution.py:103
  178.6 1.3 collective-permute-start.38
  179.9 3.9 %collective-permute-start.39 = (f32[256,32]{0,1:T(8,128)S(1)}, f32[256,32]{0,1:T(8,128)S(1)}, u32[]{:S(2)}, u32[]{:S(2)}) collective-permute-start(f32[256,32]{0,1:T(8,128)S(1)} %add.605), channel_id=1, source_target_pairs={{0,8},{4,12},{8,0},{12,4},{16,24},{20,28},{24,16},{28,20},{1,9},{5... | collective-permute-start | bytes 98312 | tf_op jit(solution)/shard_map/ppermute | solution.py:33
  183.8 3.9 %collective-permute-start.40 = (f32[256,32]{0,1:T(8,128)S(1)}, f32[256,32]{0,1:T(8,128)S(1)}, u32[]{:S(2)}, u32[]{:S(2)}) collective-permute-start(f32[256,32]{0,1:T(8,128)S(1)} %add.606), channel_id=1, source_target_pairs={{0,16},{4,20},{8,24},{12,28},{16,0},{20,4},{24,8},{28,12},{1,17},{... | collective-permute-start | bytes 98312 | tf_op jit(solution)/shard_map/ppermute | solution.py:33
  193.4 30.7 %all-to-all-start.7 = ((bf16[4,8,12288]{2,1,0:T(8,128)(2,1)}), bf16[4,8,12288]{2,1,0:T(8,128)(2,1)}, u32[]{:S(2)}, u32[]{:S(2)}) async-start(bf16[4,8,12288]{2,1,0:T(8,128)(2,1)} %fusion.3), calls=%async_computation.7 | async-start | bytes 1572864 | tf_op jit(solution)/shard_map/all_to_all | solution.py:103
  198.5 9.3 %collective-permute-start.15 = (bf16[8,4,24,128]{3,2,1,0:T(8,128)(2,1)S(1)}, bf16[8,4,24,128]{3,2,1,0:T(8,128)(2,1)S(1)}, u32[]{:S(2)}, u32[]{:S(2)}) collective-permute-start(bf16[8,4,24,128]{3,2,1,0:T(8,128)(2,1)S(1)} %get-tuple-element.8), channel_id=1, source_target_pairs={{4,0},{8,4},{12,8},{16,12},{20,16},{24,20},{28,24},{5,1},{9,5},{13... | collective-permute-start | bytes 589832 | tf_op jit(solution)/shard_map/ppermute | solution.py:22
  199.8 8.0 %collective-permute-start.14 = (bf16[8,4,24,128]{3,2,1,0:T(8,128)(2,1)S(1)}, bf16[8,4,24,128]{3,2,1,0:T(8,128)(2,1)S(1)}, u32[]{:S(2)}, u32[]{:S(2)}) collective-permute-start(bf16[8,4,24,128]{3,2,1,0:T(8,128)(2,1)S(1)} %get-tuple-element.8), channel_id=1, source_target_pairs={{0,4},{4,8},{8,12},{12,16},{16,20},{20,24},{24,28},{1,5},{5,9},{9,... | collective-permute-start | bytes 589832 | tf_op jit(solution)/shard_map/ppermute | solution.py:21
  202.8 5.1 %collective-permute-start.37 = (bf16[8,4,24,128]{3,2,1,0:T(8,128)(2,1)S(1)}, bf16[8,4,24,128]{3,2,1,0:T(8,128)(2,1)S(1)}, u32[]{:S(2)}, u32[]{:S(2)}) collective-permute-start(bf16[8,4,24,128]{3,2,1,0:T(8,128)(2,1)S(1)} %get-tuple-element.18), channel_id=1, source_target_pairs={{4,0},{8,4},{12,8},{16,12},{20,16},{24,20},{28,24},{5,1},{9,5},{13... | collective-permute-start | bytes 589832 | tf_op jit(solution)/shard_map/ppermute | solution.py:22
  204.1 4.7 %collective-permute-start.36 = (bf16[8,4,24,128]{3,2,1,0:T(8,128)(2,1)S(1)}, bf16[8,4,24,128]{3,2,1,0:T(8,128)(2,1)S(1)}, u32[]{:S(2)}, u32[]{:S(2)}) collective-permute-start(bf16[8,4,24,128]{3,2,1,0:T(8,128)(2,1)S(1)} %get-tuple-element.18), channel_id=1, source_target_pairs={{0,4},{4,8},{8,12},{12,16},{16,20},{20,24},{24,28},{1,5},{5,9},{9,... | collective-permute-start | bytes 589832 | tf_op jit(solution)/shard_map/ppermute | solution.py:21
  211.1 4.2 %collective-permute-start.19 = (f32[8]{0:T(128)S(1)}, f32[8]{0:T(128)S(1)}, u32[]{:S(2)}, u32[]{:S(2)}) collective-permute-start(f32[8]{0:T(128)S(1)} %get-tuple-element.6), channel_id=1, source_target_pairs={{0,4},{4,0},{8,12},{12,8},{16,20},{20,16},{24,28},{28,24},{1,5},{5... | collective-permute-start | bytes 104 | tf_op jit(solution)/shard_map/ppermute | solution.py:33
  215.3 3.9 %collective-permute-start.20 = (f32[8]{0:T(128)S(1)}, f32[8]{0:T(128)S(1)}, u32[]{:S(2)}, u32[]{:S(2)}) collective-permute-start(f32[8]{0:T(128)S(1)} %add.535), channel_id=1, source_target_pairs={{0,8},{4,12},{8,0},{12,4},{16,24},{20,28},{24,16},{28,20},{1,9},{5... | collective-permute-start | bytes 104 | tf_op jit(solution)/shard_map/ppermute | solution.py:33
  219.2 4.8 %collective-permute-start.21 = (f32[8]{0:T(128)S(1)}, f32[8]{0:T(128)S(1)}, u32[]{:S(2)}, u32[]{:S(2)}) collective-permute-start(f32[8]{0:T(128)S(1)} %add.536), channel_id=1, source_target_pairs={{0,16},{4,20},{8,24},{12,28},{16,0},{20,4},{24,8},{28,12},{1,17},{... | collective-permute-start | bytes 104 | tf_op jit(solution)/shard_map/ppermute | solution.py:33
  227.8 3.5 %collective-permute-start.42 = (f32[8]{0:T(128)S(1)}, f32[8]{0:T(128)S(1)}, u32[]{:S(2)}, u32[]{:S(2)}) collective-permute-start(f32[8]{0:T(128)S(1)} %add.609), channel_id=1, source_target_pairs={{0,8},{4,12},{8,0},{12,4},{16,24},{20,28},{24,16},{28,20},{1,9},{5... | collective-permute-start | bytes 104 | tf_op jit(solution)/shard_map/ppermute | solution.py:33
  231.3 3.5 %collective-permute-start.43 = (f32[8]{0:T(128)S(1)}, f32[8]{0:T(128)S(1)}, u32[]{:S(2)}, u32[]{:S(2)}) collective-permute-start(f32[8]{0:T(128)S(1)} %add.610), channel_id=1, source_target_pairs={{0,16},{4,20},{8,24},{12,28},{16,0},{20,4},{24,8},{28,12},{1,17},{... | collective-permute-start | bytes 104 | tf_op jit(solution)/shard_map/ppermute | solution.py:33
  (17 other events, 162.4 us)

commit v6 on v3

--- a/solution.py
+++ b/solution.py
@@ -77,12 +77,13 @@
         local_occupied * band_count * local_cells * lax.axis_size("grid")
     )
     occupied_rows = occupied.reshape(local_occupied, local_cells)
-    potential_shift = potential[None] + shifts[:, None, None, None]
     solution = jnp.zeros_like(source_term)
     residual = source_term
     direction = source_term
     norm_now = grid_sum(inner_product(source_term, source_term), "grid")
     for iteration in range(ITERS):
+        own_potential, direction = lax.optimization_barrier((potential, direction))
+        potential_shift = own_potential[None] + shifts[:, None, None, None]
         padded = with_halo(direction.astype(jnp.bfloat16), (("grid", 1),), 4).astype(
             direction.dtype
         )

time: 214 us -> 212 us (level)
  waiting for transfers between devices: 96.9 us -> 85.4 us
  starting transfers between devices: 86.9 us -> 96 us
    ppermute x36, waiting for transfers between devices: 35.2 us -> 23 us  [grid_sum(): value = value + lax.ppermute(value, axis, pairs)]
    ppermute x36, starting transfers between devices: 28.9 us -> 33.2 us  [grid_sum(): value = value + lax.ppermute(value, axis, pairs)]
    ppermute x12, starting transfers between devices: 16.5 us -> 19.3 us  [chain(): lax.ppermute(part, 'band', [((i + d) % band_count, i) for i in range(band...]
    reduce_sum x4 -> x6, other arithmetic: 5.09 us -> 6.35 us  [inner_product(): return jnp.sum(first_field * second_field, axis=(1, 2, 3))]
  transfers between devices with their start and end apart: 68 -> 68, of which waited for: 30 -> 36; matrix products, arithmetic and copies ran while one was open for 10% -> 12% of each run, Pallas kernels for 0% -> 0%
where the time goes in v6:
time: 212 us
  starting transfers between devices  96 us (45%)
  waiting for transfers between devices  85.4 us (40%)
  matrix products  19.1 us (9%)
  other arithmetic  9.7 us (5%)
    ppermute x12, waiting for transfers between devices, chain(): lax.ppermute(part, 'band', [((i + d) % band_count, i) for i in range(band...  44.5 us
    ppermute x36, starting transfers between devices, grid_sum(): value = value + lax.ppermute(value, axis, pairs)  33.2 us
    ppermute x12, starting transfers between devices, chain(): lax.ppermute(rounded, 'band', [(i, (i + d) % band_count) for i in range(b...  26.3 us
    ppermute x36, waiting for transfers between devices, grid_sum(): value = value + lax.ppermute(value, axis, pairs)  23 us
    ppermute x12, starting transfers between devices, chain(): lax.ppermute(part, 'band', [((i + d) % band_count, i) for i in range(band...  19.3 us
    ppermute x12, waiting for transfers between devices, chain(): lax.ppermute(rounded, 'band', [(i, (i + d) % band_count) for i in range(b...  17.9 us
    ppermute x4, starting transfers between devices, with_halo(): before = lax.ppermute(last, axis, up)  12.1 us
    dot_general x4, matrix products, chain(): lax.dot_general(occupied_rows, gathered, (((1,), (1,)), ((), ())), prefer...  11 us
  transfers between devices with their start and end apart: 68, of which 36 were waited for; matrix products, arithmetic and copies ran while one was open for 12% of the time, Pallas kernels for 0%

profile of v6, /device:TPU:8, one launch (start us, length us, event | category | flops | bytes accessed | tf_op | source)
XLA Modules:
  0.0 212.0 jit_solution(10813321109090820124)
XLA Ops:
  2.1 3.0 %collective-permute-start.40 = (bf16[8,12288]{1,0:T(8,128)(2,1)S(1)}, bf16[8,12288]{1,0:T(8,128)(2,1)S(1)}, u32[]{:S(2)}, u32[]{:S(2)}) collective-permute-start(bf16[8,12288]{1,0:T(8,128)(2,1)S(1)} %bitcast.82), channel_id=1, source_target_pairs={{0,2},{1,3},{2,0},{3,1},{4,6},{5,7},{6,4},{7,5},{8,10},{9,11},{10,... | collective-permute-start | bytes 589832 | tf_op jit(solution)/shard_map/ppermute | solution.py:94
  5.2 2.5 %collective-permute-start.39 = (bf16[8,12288]{1,0:T(8,128)(2,1)S(1)}, bf16[8,12288]{1,0:T(8,128)(2,1)S(1)}, u32[]{:S(2)}, u32[]{:S(2)}) collective-permute-start(bf16[8,12288]{1,0:T(8,128)(2,1)S(1)} %bitcast.83), channel_id=1, source_target_pairs={{0,1},{1,2},{2,3},{3,0},{4,5},{5,6},{6,7},{7,4},{8,9},{9,10},{10,1... | collective-permute-start | bytes 589832 | tf_op jit(solution)/shard_map/ppermute | solution.py:94
  11.6 2.0 collective-permute-done.35
  15.2 2.0 collective-permute-done.1
  18.6 2.4 %collective-permute-start.5 = (bf16[8,12288]{1,0:T(8,128)(2,1)S(1)}, bf16[8,12288]{1,0:T(8,128)(2,1)S(1)}, u32[]{:S(2)}, u32[]{:S(2)}) collective-permute-start(bf16[8,12288]{1,0:T(8,128)(2,1)S(1)} %bitcast.79), channel_id=1, source_target_pairs={{0,1},{1,2},{2,3},{3,0},{4,5},{5,6},{6,7},{7,4},{8,9},{9,10},{10,1... | collective-permute-start | bytes 589832 | tf_op jit(solution)/shard_map/ppermute | solution.py:94
  22.3 8.8 %collective-permute-done.39 = bf16[8,12288]{1,0:T(8,128)(2,1)S(1)} collective-permute-done((bf16[8,12288]{1,0:T(8,128)(2,1)S(1)}, bf16[8,12288]{1,0:T(8,128)(2,1)S(1)}, u32[]{:S(2)}, u32[]{:S(2)}) %collective-permute-start.39) | collective-permute-done | bytes 196640 | tf_op jit(solution)/shard_map/ppermute | solution.py:94
  32.3 5.0 %fusion.18 = f32[256,32]{0,1:T(8,128)S(1)} fusion(bf16[32,8,96,128]{3,2,1,0:T(8,128)(2,1)} %bitcast.59, bf16[8,12288]{1,0:T(8,128)(2,1)S(1)} %collective-permute-done.41, bf16[8,12288]{1,0:T(8,128)(2,1)S(1)} %collective-permute-done.40, bf16[8,12288]{1,0:T(8,128)(2,1)S(1)} %collective-permute-done.39, bf16[8,12288]{1,0:T(8,128)(2,1)S(1)} %bitcast.84), kind=kOutput, calls=%fused_computation.82 | convolution fusion | flops 204472320 | bytes 7110656 | tf_op jit(solution)/shard_map/dot_general | solution.py:98
  38.7 4.8 %collective-permute-start.37 = (bf16[8,4,24,128]{3,2,1,0:T(8,128)(2,1)S(1)}, bf16[8,4,24,128]{3,2,1,0:T(8,128)(2,1)S(1)}, u32[]{:S(2)}, u32[]{:S(2)}) collective-permute-start(bf16[8,4,24,128]{3,2,1,0:T(8,128)(2,1)S(1)} %convert_element_type.121), channel_id=1, source_target_pairs={{0,4},{4,8},{8,12},{12,16},{16,20},{20,24},{24,28},{1,5},{5,9},{9,... | collective-permute-start | bytes 589832 | tf_op jit(solution)/shard_map/ppermute | solution.py:21
  43.4 1.8 collective-permute-start.42
  45.2 2.0 fusion.12
  47.3 1.6 collective-permute-start.36
  50.1 1.9 collective-permute-start.2
  53.8 2.1 collective-permute-start.44
  58.1 2.0 convolution_convert_fusion.1
  60.1 2.5 %collective-permute-start.47 = (bf16[8,12288]{1,0:T(8,128)(2,1)S(1)}, bf16[8,12288]{1,0:T(8,128)(2,1)S(1)}, u32[]{:S(2)}, u32[]{:S(2)}) collective-permute-start(bf16[8,12288]{1,0:T(8,128)(2,1)S(1)} %get-tuple-element.54), channel_id=1, source_target_pairs={{3,0},{0,1},{1,2},{2,3},{7,4},{4,5},{5,6},{6,7},{11,8},{8,9},{9,10... | collective-permute-start | bytes 589832 | tf_op jit(solution)/shard_map/ppermute | solution.py:109
  62.7 1.5 collective-permute-start.45
  64.2 2.0 convolution_convert_fusion.3
  66.3 8.8 %collective-permute-done.47 = bf16[8,12288]{1,0:T(8,128)(2,1)S(1)} collective-permute-done((bf16[8,12288]{1,0:T(8,128)(2,1)S(1)}, bf16[8,12288]{1,0:T(8,128)(2,1)S(1)}, u32[]{:S(2)}, u32[]{:S(2)}) %collective-permute-start.47) | collective-permute-done | bytes 196640 | tf_op jit(solution)/shard_map/ppermute | solution.py:109
  75.1 2.6 %collective-permute-start.13 = (bf16[8,12288]{1,0:T(8,128)(2,1)S(1)}, bf16[8,12288]{1,0:T(8,128)(2,1)S(1)}, u32[]{:S(2)}, u32[]{:S(2)}) collective-permute-start(bf16[8,12288]{1,0:T(8,128)(2,1)S(1)} %get-tuple-element.46), channel_id=1, source_target_pairs={{3,0},{0,1},{1,2},{2,3},{7,4},{4,5},{5,6},{6,7},{11,8},{8,9},{9,10... | collective-permute-start | bytes 589832 | tf_op jit(solution)/shard_map/ppermute | solution.py:109
  77.7 7.9 %collective-permute-done.46 = bf16[8,12288]{1,0:T(8,128)(2,1)S(1)} collective-permute-done((bf16[8,12288]{1,0:T(8,128)(2,1)S(1)}, bf16[8,12288]{1,0:T(8,128)(2,1)S(1)}, u32[]{:S(2)}, u32[]{:S(2)}) %collective-permute-start.46) | collective-permute-done | bytes 196640 | tf_op jit(solution)/shard_map/ppermute | solution.py:109
  85.6 3.5 %collective-permute-start.12 = (bf16[8,12288]{1,0:T(8,128)(2,1)S(1)}, bf16[8,12288]{1,0:T(8,128)(2,1)S(1)}, u32[]{:S(2)}, u32[]{:S(2)}) collective-permute-start(bf16[8,12288]{1,0:T(8,128)(2,1)S(1)} %get-tuple-element.47), channel_id=1, source_target_pairs={{2,0},{3,1},{0,2},{1,3},{6,4},{7,5},{4,6},{5,7},{10,8},{11,9},{8,1... | collective-permute-start | bytes 589832 | tf_op jit(solution)/shard_map/ppermute | solution.py:109
  90.5 4.2 %collective-permute-done.12 = bf16[8,12288]{1,0:T(8,128)(2,1)S(1)} collective-permute-done((bf16[8,12288]{1,0:T(8,128)(2,1)S(1)}, bf16[8,12288]{1,0:T(8,128)(2,1)S(1)}, u32[]{:S(2)}, u32[]{:S(2)}) %collective-permute-start.12) | collective-permute-done | bytes 196640 | tf_op jit(solution)/shard_map/ppermute | solution.py:109
  99.9 1.7 collective-permute-start.50
  103.4 1.7 collective-permute-done.16
  108.6 1.5 collective-permute-done.52
  114.0 3.2 %collective-permute-start.57 = (bf16[8,12288]{1,0:T(8,128)(2,1)S(1)}, bf16[8,12288]{1,0:T(8,128)(2,1)S(1)}, u32[]{:S(2)}, u32[]{:S(2)}) collective-permute-start(bf16[8,12288]{1,0:T(8,128)(2,1)S(1)} %bitcast.86), channel_id=1, source_target_pairs={{0,2},{1,3},{2,0},{3,1},{4,6},{5,7},{6,4},{7,5},{8,10},{9,11},{10,... | collective-permute-start | bytes 589832 | tf_op jit(solution)/shard_map/ppermute | solution.py:94
  117.2 2.8 %collective-permute-start.56 = (bf16[8,12288]{1,0:T(8,128)(2,1)S(1)}, bf16[8,12288]{1,0:T(8,128)(2,1)S(1)}, u32[]{:S(2)}, u32[]{:S(2)}) collective-permute-start(bf16[8,12288]{1,0:T(8,128)(2,1)S(1)} %bitcast.87), channel_id=1, source_target_pairs={{0,1},{1,2},{2,3},{3,0},{4,5},{5,6},{6,7},{7,4},{8,9},{9,10},{10,1... | collective-permute-start | bytes 589832 | tf_op jit(solution)/shard_map/ppermute | solution.py:94
  121.4 3.0 %collective-permute-start.54 = (bf16[8,4,24,128]{3,2,1,0:T(8,128)(2,1)S(1)}, bf16[8,4,24,128]{3,2,1,0:T(8,128)(2,1)S(1)}, u32[]{:S(2)}, u32[]{:S(2)}) collective-permute-start(bf16[8,4,24,128]{3,2,1,0:T(8,128)(2,1)S(1)} %convert_element_type.129), channel_id=1, source_target_pairs={{0,4},{4,8},{8,12},{12,16},{16,20},{20,24},{24,28},{1,5},{5,9},{9,... | collective-permute-start | bytes 589832 | tf_op jit(solution)/shard_map/ppermute | solution.py:21
  124.7 4.7 %collective-permute-done.58 = bf16[8,12288]{1,0:T(8,128)(2,1)S(1)} collective-permute-done((bf16[8,12288]{1,0:T(8,128)(2,1)S(1)}, bf16[8,12288]{1,0:T(8,128)(2,1)S(1)}, u32[]{:S(2)}, u32[]{:S(2)}) %collective-permute-start.58) | collective-permute-done | bytes 196640 | tf_op jit(solution)/shard_map/ppermute | solution.py:94
  130.4 8.3 %collective-permute-start.23 = (bf16[8,12288]{1,0:T(8,128)(2,1)S(1)}, bf16[8,12288]{1,0:T(8,128)(2,1)S(1)}, u32[]{:S(2)}, u32[]{:S(2)}) collective-permute-start(bf16[8,12288]{1,0:T(8,128)(2,1)S(1)} %bitcast.90), channel_id=1, source_target_pairs={{0,2},{1,3},{2,0},{3,1},{4,6},{5,7},{6,4},{7,5},{8,10},{9,11},{10,... | collective-permute-start | bytes 589832 | tf_op jit(solution)/shard_map/ppermute | solution.py:94
  139.5 2.5 %collective-permute-start.22 = (bf16[8,12288]{1,0:T(8,128)(2,1)S(1)}, bf16[8,12288]{1,0:T(8,128)(2,1)S(1)}, u32[]{:S(2)}, u32[]{:S(2)}) collective-permute-start(bf16[8,12288]{1,0:T(8,128)(2,1)S(1)} %bitcast.91), channel_id=1, source_target_pairs={{0,1},{1,2},{2,3},{3,0},{4,5},{5,6},{6,7},{7,4},{8,9},{9,10},{10,1... | collective-permute-start | bytes 589832 | tf_op jit(solution)/shard_map/ppermute | solution.py:94
  142.0 2.0 fusion.21
  144.0 2.5 %collective-permute-done.24 = bf16[8,12288]{1,0:T(8,128)(2,1)S(1)} collective-permute-done((bf16[8,12288]{1,0:T(8,128)(2,1)S(1)}, bf16[8,12288]{1,0:T(8,128)(2,1)S(1)}, u32[]{:S(2)}, u32[]{:S(2)}) %collective-permute-start.24) | collective-permute-done | bytes 196640 | tf_op jit(solution)/shard_map/ppermute | solution.py:94
  147.8 3.0 %collective-permute-start.20 = (bf16[8,4,24,128]{3,2,1,0:T(8,128)(2,1)S(1)}, bf16[8,4,24,128]{3,2,1,0:T(8,128)(2,1)S(1)}, u32[]{:S(2)}, u32[]{:S(2)}) collective-permute-start(bf16[8,4,24,128]{3,2,1,0:T(8,128)(2,1)S(1)} %convert_element_type.113), channel_id=1, source_target_pairs={{0,4},{4,8},{8,12},{12,16},{16,20},{20,24},{24,28},{1,5},{5,9},{9,... | collective-permute-start | bytes 589832 | tf_op jit(solution)/shard_map/ppermute | solution.py:21
  151.4 2.0 fusion.15
  153.6 1.7 collective-permute-start.60
  159.8 1.9 collective-permute-done.61
  161.7 2.0 convolution_convert_fusion
  164.2 4.2 %collective-permute-start.63 = (bf16[8,12288]{1,0:T(8,128)(2,1)S(1)}, bf16[8,12288]{1,0:T(8,128)(2,1)S(1)}, u32[]{:S(2)}, u32[]{:S(2)}) collective-permute-start(bf16[8,12288]{1,0:T(8,128)(2,1)S(1)} %get-tuple-element.51), channel_id=1, source_target_pairs={{2,0},{3,1},{0,2},{1,3},{6,4},{7,5},{4,6},{5,7},{10,8},{11,9},{8,1... | collective-permute-start | bytes 589832 | tf_op jit(solution)/shard_map/ppermute | solution.py:109
  168.3 2.0 convolution_convert_fusion.2
  170.4 2.1 collective-permute-start.30
  172.5 1.8 collective-permute-start.29
  175.7 14.3 %collective-permute-done.63 = bf16[8,12288]{1,0:T(8,128)(2,1)S(1)} collective-permute-done((bf16[8,12288]{1,0:T(8,128)(2,1)S(1)}, bf16[8,12288]{1,0:T(8,128)(2,1)S(1)}, u32[]{:S(2)}, u32[]{:S(2)}) %collective-permute-start.63) | collective-permute-done | bytes 196640 | tf_op jit(solution)/shard_map/ppermute | solution.py:109
  190.0 2.3 %collective-permute-done.62 = bf16[8,12288]{1,0:T(8,128)(2,1)S(1)} collective-permute-done((bf16[8,12288]{1,0:T(8,128)(2,1)S(1)}, bf16[8,12288]{1,0:T(8,128)(2,1)S(1)}, u32[]{:S(2)}, u32[]{:S(2)}) %collective-permute-start.62) | collective-permute-done | bytes 196640 | tf_op jit(solution)/shard_map/ppermute | solution.py:109
  194.2 2.7 %collective-permute-done.29 = bf16[8,12288]{1,0:T(8,128)(2,1)S(1)} collective-permute-done((bf16[8,12288]{1,0:T(8,128)(2,1)S(1)}, bf16[8,12288]{1,0:T(8,128)(2,1)S(1)}, u32[]{:S(2)}, u32[]{:S(2)}) %collective-permute-start.29) | collective-permute-done | bytes 196640 | tf_op jit(solution)/shard_map/ppermute | solution.py:109
  196.8 2.9 %collective-permute-done.28 = bf16[8,12288]{1,0:T(8,128)(2,1)S(1)} collective-permute-done((bf16[8,12288]{1,0:T(8,128)(2,1)S(1)}, bf16[8,12288]{1,0:T(8,128)(2,1)S(1)}, u32[]{:S(2)}, u32[]{:S(2)}) %collective-permute-start.28) | collective-permute-done | bytes 196640 | tf_op jit(solution)/shard_map/ppermute | solution.py:109
  201.1 1.8 collective-permute-start.66
  208.4 1.6 collective-permute-done.33
  (169 shorter events, 55.7 us)
Async XLA Ops:
  2.1 16.5 %collective-permute-start.41 = (bf16[8,12288]{1,0:T(8,128)(2,1)S(1)}, bf16[8,12288]{1,0:T(8,128)(2,1)S(1)}, u32[]{:S(2)}, u32[]{:S(2)}) collective-permute-start(bf16[8,12288]{1,0:T(8,128)(2,1)S(1)} %bitcast.81), channel_id=1, source_target_pairs={{0,3},{1,0},{2,1},{3,2},{4,7},{5,4},{6,5},{7,6},{8,11},{9,8},{10,9... | collective-permute-start | bytes 589832 | tf_op jit(solution)/shard_map/ppermute | solution.py:94
  2.1 18.8 %collective-permute-start.40 = (bf16[8,12288]{1,0:T(8,128)(2,1)S(1)}, bf16[8,12288]{1,0:T(8,128)(2,1)S(1)}, u32[]{:S(2)}, u32[]{:S(2)}) collective-permute-start(bf16[8,12288]{1,0:T(8,128)(2,1)S(1)} %bitcast.82), channel_id=1, source_target_pairs={{0,2},{1,3},{2,0},{3,1},{4,6},{5,7},{6,4},{7,5},{8,10},{9,11},{10,... | collective-permute-start | bytes 589832 | tf_op jit(solution)/shard_map/ppermute | solution.py:94
  5.2 25.9 %collective-permute-start.39 = (bf16[8,12288]{1,0:T(8,128)(2,1)S(1)}, bf16[8,12288]{1,0:T(8,128)(2,1)S(1)}, u32[]{:S(2)}, u32[]{:S(2)}) collective-permute-start(bf16[8,12288]{1,0:T(8,128)(2,1)S(1)} %bitcast.83), channel_id=1, source_target_pairs={{0,1},{1,2},{2,3},{3,0},{4,5},{5,6},{6,7},{7,4},{8,9},{9,10},{10,1... | collective-permute-start | bytes 589832 | tf_op jit(solution)/shard_map/ppermute | solution.py:94
  7.8 29.6 %collective-permute-start.7 = (bf16[8,12288]{1,0:T(8,128)(2,1)S(1)}, bf16[8,12288]{1,0:T(8,128)(2,1)S(1)}, u32[]{:S(2)}, u32[]{:S(2)}) collective-permute-start(bf16[8,12288]{1,0:T(8,128)(2,1)S(1)} %bitcast.77), channel_id=1, source_target_pairs={{0,3},{1,0},{2,1},{3,2},{4,7},{5,4},{6,5},{7,6},{8,11},{9,8},{10,9... | collective-permute-start | bytes 589832 | tf_op jit(solution)/shard_map/ppermute | solution.py:94
  17.2 21.4 %collective-permute-start.6 = (bf16[8,12288]{1,0:T(8,128)(2,1)S(1)}, bf16[8,12288]{1,0:T(8,128)(2,1)S(1)}, u32[]{:S(2)}, u32[]{:S(2)}) collective-permute-start(bf16[8,12288]{1,0:T(8,128)(2,1)S(1)} %bitcast.78), channel_id=1, source_target_pairs={{0,2},{1,3},{2,0},{3,1},{4,6},{5,7},{6,4},{7,5},{8,10},{9,11},{10,... | collective-permute-start | bytes 589832 | tf_op jit(solution)/shard_map/ppermute | solution.py:94
  18.6 24.8 %collective-permute-start.5 = (bf16[8,12288]{1,0:T(8,128)(2,1)S(1)}, bf16[8,12288]{1,0:T(8,128)(2,1)S(1)}, u32[]{:S(2)}, u32[]{:S(2)}) collective-permute-start(bf16[8,12288]{1,0:T(8,128)(2,1)S(1)} %bitcast.79), channel_id=1, source_target_pairs={{0,1},{1,2},{2,3},{3,0},{4,5},{5,6},{6,7},{7,4},{8,9},{9,10},{10,1... | collective-permute-start | bytes 589832 | tf_op jit(solution)/shard_map/ppermute | solution.py:94
  21.0 27.9 %collective-permute-start.4 = (bf16[8,4,24,128]{3,2,1,0:T(8,128)(2,1)S(1)}, bf16[8,4,24,128]{3,2,1,0:T(8,128)(2,1)S(1)}, u32[]{:S(2)}, u32[]{:S(2)}) collective-permute-start(bf16[8,4,24,128]{3,2,1,0:T(8,128)(2,1)S(1)} %convert_element_type.105), channel_id=1, source_target_pairs={{4,0},{8,4},{12,8},{16,12},{20,16},{24,20},{28,24},{5,1},{9,5},{13... | collective-permute-start | bytes 589832 | tf_op jit(solution)/shard_map/ppermute | solution.py:22
  31.0 17.9 %collective-permute-start.3 = (bf16[8,4,24,128]{3,2,1,0:T(8,128)(2,1)S(1)}, bf16[8,4,24,128]{3,2,1,0:T(8,128)(2,1)S(1)}, u32[]{:S(2)}, u32[]{:S(2)}) collective-permute-start(bf16[8,4,24,128]{3,2,1,0:T(8,128)(2,1)S(1)} %convert_element_type.105), channel_id=1, source_target_pairs={{0,4},{4,8},{8,12},{12,16},{16,20},{20,24},{24,28},{1,5},{5,9},{9,... | collective-permute-start | bytes 589832 | tf_op jit(solution)/shard_map/ppermute | solution.py:21
  37.4 16.5 %collective-permute-start.38 = (bf16[8,4,24,128]{3,2,1,0:T(8,128)(2,1)S(1)}, bf16[8,4,24,128]{3,2,1,0:T(8,128)(2,1)S(1)}, u32[]{:S(2)}, u32[]{:S(2)}) collective-permute-start(bf16[8,4,24,128]{3,2,1,0:T(8,128)(2,1)S(1)} %convert_element_type.121), channel_id=1, source_target_pairs={{4,0},{8,4},{12,8},{16,12},{20,16},{24,20},{28,24},{5,1},{9,5},{13... | collective-permute-start | bytes 589832 | tf_op jit(solution)/shard_map/ppermute | solution.py:22
  38.7 17.2 %collective-permute-start.37 = (bf16[8,4,24,128]{3,2,1,0:T(8,128)(2,1)S(1)}, bf16[8,4,24,128]{3,2,1,0:T(8,128)(2,1)S(1)}, u32[]{:S(2)}, u32[]{:S(2)}) collective-permute-start(bf16[8,4,24,128]{3,2,1,0:T(8,128)(2,1)S(1)} %convert_element_type.121), channel_id=1, source_target_pairs={{0,4},{4,8},{8,12},{12,16},{16,20},{20,24},{24,28},{1,5},{5,9},{9,... | collective-permute-start | bytes 589832 | tf_op jit(solution)/shard_map/ppermute | solution.py:21
  43.4 3.8 %collective-permute-start.42 = (f32[256,32]{0,1:T(8,128)S(1)}, f32[256,32]{0,1:T(8,128)S(1)}, u32[]{:S(2)}, u32[]{:S(2)}) collective-permute-start(f32[256,32]{0,1:T(8,128)S(1)} %fusion.18), channel_id=1, source_target_pairs={{0,4},{4,0},{8,12},{12,8},{16,20},{20,16},{24,28},{28,24},{1,5},{5... | collective-permute-start | bytes 98312 | tf_op jit(solution)/shard_map/ppermute | solution.py:33
  47.3 55.3 %collective-permute-start.36 = (f32[8]{0:T(128)S(1)}, f32[8]{0:T(128)S(1)}, u32[]{:S(2)}, u32[]{:S(2)}) collective-permute-start(f32[8]{0:T(128)S(1)} %add.608), channel_id=1, source_target_pairs={{0,16},{4,20},{8,24},{12,28},{16,0},{20,4},{24,8},{28,12},{1,17},{... | collective-permute-start | bytes 104 | tf_op jit(solution)/shard_map/ppermute | solution.py:33
  49.0 4.0 %collective-permute-start.43 = (f32[256,32]{0,1:T(8,128)S(1)}, f32[256,32]{0,1:T(8,128)S(1)}, u32[]{:S(2)}, u32[]{:S(2)}) collective-permute-start(f32[256,32]{0,1:T(8,128)S(1)} %add.638), channel_id=1, source_target_pairs={{0,8},{4,12},{8,0},{12,4},{16,24},{20,28},{24,16},{28,20},{1,9},{5... | collective-permute-start | bytes 98312 | tf_op jit(solution)/shard_map/ppermute | solution.py:33
  50.1 52.5 %collective-permute-start.2 = (f32[8]{0:T(128)S(1)}, f32[8]{0:T(128)S(1)}, u32[]{:S(2)}, u32[]{:S(2)}) collective-permute-start(f32[8]{0:T(128)S(1)} %add.525), channel_id=1, source_target_pairs={{0,16},{4,20},{8,24},{12,28},{16,0},{20,4},{24,8},{28,12},{1,17},{... | collective-permute-start | bytes 104 | tf_op jit(solution)/shard_map/ppermute | solution.py:33
  52.9 3.9 %collective-permute-start.9 = (f32[256,32]{0,1:T(8,128)S(1)}, f32[256,32]{0,1:T(8,128)S(1)}, u32[]{:S(2)}, u32[]{:S(2)}) collective-permute-start(f32[256,32]{0,1:T(8,128)S(1)} %add.555), channel_id=1, source_target_pairs={{0,8},{4,12},{8,0},{12,4},{16,24},{20,28},{24,16},{28,20},{1,9},{5... | collective-permute-start | bytes 98312 | tf_op jit(solution)/shard_map/ppermute | solution.py:33
  53.8 4.2 %collective-permute-start.44 = (f32[256,32]{0,1:T(8,128)S(1)}, f32[256,32]{0,1:T(8,128)S(1)}, u32[]{:S(2)}, u32[]{:S(2)}) collective-permute-start(f32[256,32]{0,1:T(8,128)S(1)} %add.639), channel_id=1, source_target_pairs={{0,16},{4,20},{8,24},{12,28},{16,0},{20,4},{24,8},{28,12},{1,17},{... | collective-permute-start | bytes 98312 | tf_op jit(solution)/shard_map/ppermute | solution.py:33
  56.9 5.8 %collective-permute-start.10 = (f32[256,32]{0,1:T(8,128)S(1)}, f32[256,32]{0,1:T(8,128)S(1)}, u32[]{:S(2)}, u32[]{:S(2)}) collective-permute-start(f32[256,32]{0,1:T(8,128)S(1)} %add.556), channel_id=1, source_target_pairs={{0,16},{4,20},{8,24},{12,28},{16,0},{20,4},{24,8},{28,12},{1,17},{... | collective-permute-start | bytes 98312 | tf_op jit(solution)/shard_map/ppermute | solution.py:33
  60.1 15.0 %collective-permute-start.47 = (bf16[8,12288]{1,0:T(8,128)(2,1)S(1)}, bf16[8,12288]{1,0:T(8,128)(2,1)S(1)}, u32[]{:S(2)}, u32[]{:S(2)}) collective-permute-start(bf16[8,12288]{1,0:T(8,128)(2,1)S(1)} %get-tuple-element.54), channel_id=1, source_target_pairs={{3,0},{0,1},{1,2},{2,3},{7,4},{4,5},{5,6},{6,7},{11,8},{8,9},{9,10... | collective-permute-start | bytes 589832 | tf_op jit(solution)/shard_map/ppermute | solution.py:109
  62.7 22.9 %collective-permute-start.46 = (bf16[8,12288]{1,0:T(8,128)(2,1)S(1)}, bf16[8,12288]{1,0:T(8,128)(2,1)S(1)}, u32[]{:S(2)}, u32[]{:S(2)}) collective-permute-start(bf16[8,12288]{1,0:T(8,128)(2,1)S(1)} %get-tuple-element.55), channel_id=1, source_target_pairs={{2,0},{3,1},{0,2},{1,3},{6,4},{7,5},{4,6},{5,7},{10,8},{11,9},{8,1... | collective-permute-start | bytes 589832 | tf_op jit(solution)/shard_map/ppermute | solution.py:109
  62.7 26.5 %collective-permute-start.45 = (bf16[8,12288]{1,0:T(8,128)(2,1)S(1)}, bf16[8,12288]{1,0:T(8,128)(2,1)S(1)}, u32[]{:S(2)}, u32[]{:S(2)}) collective-permute-start(bf16[8,12288]{1,0:T(8,128)(2,1)S(1)} %get-tuple-element.53), channel_id=1, source_target_pairs={{1,0},{2,1},{3,2},{0,3},{5,4},{6,5},{7,6},{4,7},{9,8},{10,9},{11,1... | collective-permute-start | bytes 589832 | tf_op jit(solution)/shard_map/ppermute | solution.py:109
  75.1 15.4 %collective-permute-start.13 = (bf16[8,12288]{1,0:T(8,128)(2,1)S(1)}, bf16[8,12288]{1,0:T(8,128)(2,1)S(1)}, u32[]{:S(2)}, u32[]{:S(2)}) collective-permute-start(bf16[8,12288]{1,0:T(8,128)(2,1)S(1)} %get-tuple-element.46), channel_id=1, source_target_pairs={{3,0},{0,1},{1,2},{2,3},{7,4},{4,5},{5,6},{6,7},{11,8},{8,9},{9,10... | collective-permute-start | bytes 589832 | tf_op jit(solution)/shard_map/ppermute | solution.py:109
  85.6 9.1 %collective-permute-start.12 = (bf16[8,12288]{1,0:T(8,128)(2,1)S(1)}, bf16[8,12288]{1,0:T(8,128)(2,1)S(1)}, u32[]{:S(2)}, u32[]{:S(2)}) collective-permute-start(bf16[8,12288]{1,0:T(8,128)(2,1)S(1)} %get-tuple-element.47), channel_id=1, source_target_pairs={{2,0},{3,1},{0,2},{1,3},{6,4},{7,5},{4,6},{5,7},{10,8},{11,9},{8,1... | collective-permute-start | bytes 589832 | tf_op jit(solution)/shard_map/ppermute | solution.py:109
  89.1 5.8 %collective-permute-start.11 = (bf16[8,12288]{1,0:T(8,128)(2,1)S(1)}, bf16[8,12288]{1,0:T(8,128)(2,1)S(1)}, u32[]{:S(2)}, u32[]{:S(2)}) collective-permute-start(bf16[8,12288]{1,0:T(8,128)(2,1)S(1)} %get-tuple-element.45), channel_id=1, source_target_pairs={{1,0},{2,1},{3,2},{0,3},{5,4},{6,5},{7,6},{4,7},{9,8},{10,9},{11,1... | collective-permute-start | bytes 589832 | tf_op jit(solution)/shard_map/ppermute | solution.py:109
  90.4 5.8 %collective-permute-start.48 = (f32[8]{0:T(128)S(1)}, f32[8]{0:T(128)S(1)}, u32[]{:S(2)}, u32[]{:S(2)}) collective-permute-start(f32[8]{0:T(128)S(1)} %get-tuple-element.38), channel_id=1, source_target_pairs={{0,4},{4,0},{8,12},{12,8},{16,20},{20,16},{24,28},{28,24},{1,5},{5... | collective-permute-start | bytes 104 | tf_op jit(solution)/shard_map/ppermute | solution.py:33
  97.8 3.8 %collective-permute-start.15 = (f32[8]{0:T(128)S(1)}, f32[8]{0:T(128)S(1)}, u32[]{:S(2)}, u32[]{:S(2)}) collective-permute-start(f32[8]{0:T(128)S(1)} %add.562), channel_id=1, source_target_pairs={{0,8},{4,12},{8,0},{12,4},{16,24},{20,28},{24,16},{28,20},{1,9},{5... | collective-permute-start | bytes 104 | tf_op jit(solution)/shard_map/ppermute | solution.py:33
  107.4 3.8 %collective-permute-start.18 = (f32[8]{0:T(128)S(1)}, f32[8]{0:T(128)S(1)}, u32[]{:S(2)}, u32[]{:S(2)}) collective-permute-start(f32[8]{0:T(128)S(1)} %add.565), channel_id=1, source_target_pairs={{0,8},{4,12},{8,0},{12,4},{16,24},{20,28},{24,16},{28,20},{1,9},{5... | collective-permute-start | bytes 104 | tf_op jit(solution)/shard_map/ppermute | solution.py:33
  111.2 10.2 %collective-permute-start.19 = (f32[8]{0:T(128)S(1)}, f32[8]{0:T(128)S(1)}, u32[]{:S(2)}, u32[]{:S(2)}) collective-permute-start(f32[8]{0:T(128)S(1)} %add.566), channel_id=1, source_target_pairs={{0,16},{4,20},{8,24},{12,28},{16,0},{20,4},{24,8},{28,12},{1,17},{... | collective-permute-start | bytes 104 | tf_op jit(solution)/shard_map/ppermute | solution.py:33
  113.9 15.4 %collective-permute-start.58 = (bf16[8,12288]{1,0:T(8,128)(2,1)S(1)}, bf16[8,12288]{1,0:T(8,128)(2,1)S(1)}, u32[]{:S(2)}, u32[]{:S(2)}) collective-permute-start(bf16[8,12288]{1,0:T(8,128)(2,1)S(1)} %bitcast.85), channel_id=1, source_target_pairs={{0,3},{1,0},{2,1},{3,2},{4,7},{5,4},{6,5},{7,6},{8,11},{9,8},{10,9... | collective-permute-start | bytes 589832 | tf_op jit(solution)/shard_map/ppermute | solution.py:94
  114.0 16.4 %collective-permute-start.57 = (bf16[8,12288]{1,0:T(8,128)(2,1)S(1)}, bf16[8,12288]{1,0:T(8,128)(2,1)S(1)}, u32[]{:S(2)}, u32[]{:S(2)}) collective-permute-start(bf16[8,12288]{1,0:T(8,128)(2,1)S(1)} %bitcast.86), channel_id=1, source_target_pairs={{0,2},{1,3},{2,0},{3,1},{4,6},{5,7},{6,4},{7,5},{8,10},{9,11},{10,... | collective-permute-start | bytes 589832 | tf_op jit(solution)/shard_map/ppermute | solution.py:94
  117.2 22.3 %collective-permute-start.56 = (bf16[8,12288]{1,0:T(8,128)(2,1)S(1)}, bf16[8,12288]{1,0:T(8,128)(2,1)S(1)}, u32[]{:S(2)}, u32[]{:S(2)}) collective-permute-start(bf16[8,12288]{1,0:T(8,128)(2,1)S(1)} %bitcast.87), channel_id=1, source_target_pairs={{0,1},{1,2},{2,3},{3,0},{4,5},{5,6},{6,7},{7,4},{8,9},{9,10},{10,1... | collective-permute-start | bytes 589832 | tf_op jit(solution)/shard_map/ppermute | solution.py:94
  120.1 33.5 %collective-permute-start.55 = (bf16[8,4,24,128]{3,2,1,0:T(8,128)(2,1)S(1)}, bf16[8,4,24,128]{3,2,1,0:T(8,128)(2,1)S(1)}, u32[]{:S(2)}, u32[]{:S(2)}) collective-permute-start(bf16[8,4,24,128]{3,2,1,0:T(8,128)(2,1)S(1)} %convert_element_type.129), channel_id=1, source_target_pairs={{4,0},{8,4},{12,8},{16,12},{20,16},{24,20},{28,24},{5,1},{9,5},{13... | collective-permute-start | bytes 589832 | tf_op jit(solution)/shard_map/ppermute | solution.py:22
  121.4 33.9 %collective-permute-start.54 = (bf16[8,4,24,128]{3,2,1,0:T(8,128)(2,1)S(1)}, bf16[8,4,24,128]{3,2,1,0:T(8,128)(2,1)S(1)}, u32[]{:S(2)}, u32[]{:S(2)}) collective-permute-start(bf16[8,4,24,128]{3,2,1,0:T(8,128)(2,1)S(1)} %convert_element_type.129), channel_id=1, source_target_pairs={{0,4},{4,8},{8,12},{12,16},{16,20},{20,24},{24,28},{1,5},{5,9},{9,... | collective-permute-start | bytes 589832 | tf_op jit(solution)/shard_map/ppermute | solution.py:21
  129.4 17.1 %collective-permute-start.24 = (bf16[8,12288]{1,0:T(8,128)(2,1)S(1)}, bf16[8,12288]{1,0:T(8,128)(2,1)S(1)}, u32[]{:S(2)}, u32[]{:S(2)}) collective-permute-start(bf16[8,12288]{1,0:T(8,128)(2,1)S(1)} %bitcast.89), channel_id=1, source_target_pairs={{0,3},{1,0},{2,1},{3,2},{4,7},{5,4},{6,5},{7,6},{8,11},{9,8},{10,9... | collective-permute-start | bytes 589832 | tf_op jit(solution)/shard_map/ppermute | solution.py:94
  130.4 17.4 %collective-permute-start.23 = (bf16[8,12288]{1,0:T(8,128)(2,1)S(1)}, bf16[8,12288]{1,0:T(8,128)(2,1)S(1)}, u32[]{:S(2)}, u32[]{:S(2)}) collective-permute-start(bf16[8,12288]{1,0:T(8,128)(2,1)S(1)} %bitcast.90), channel_id=1, source_target_pairs={{0,2},{1,3},{2,0},{3,1},{4,6},{5,7},{6,4},{7,5},{8,10},{9,11},{10,... | collective-permute-start | bytes 589832 | tf_op jit(solution)/shard_map/ppermute | solution.py:94
  139.5 11.4 %collective-permute-start.22 = (bf16[8,12288]{1,0:T(8,128)(2,1)S(1)}, bf16[8,12288]{1,0:T(8,128)(2,1)S(1)}, u32[]{:S(2)}, u32[]{:S(2)}) collective-permute-start(bf16[8,12288]{1,0:T(8,128)(2,1)S(1)} %bitcast.91), channel_id=1, source_target_pairs={{0,1},{1,2},{2,3},{3,0},{4,5},{5,6},{6,7},{7,4},{8,9},{9,10},{10,1... | collective-permute-start | bytes 589832 | tf_op jit(solution)/shard_map/ppermute | solution.py:94
  146.5 12.2 %collective-permute-start.21 = (bf16[8,4,24,128]{3,2,1,0:T(8,128)(2,1)S(1)}, bf16[8,4,24,128]{3,2,1,0:T(8,128)(2,1)S(1)}, u32[]{:S(2)}, u32[]{:S(2)}) collective-permute-start(bf16[8,4,24,128]{3,2,1,0:T(8,128)(2,1)S(1)} %convert_element_type.113), channel_id=1, source_target_pairs={{4,0},{8,4},{12,8},{16,12},{20,16},{24,20},{28,24},{5,1},{9,5},{13... | collective-permute-start | bytes 589832 | tf_op jit(solution)/shard_map/ppermute | solution.py:22
  147.8 10.9 %collective-permute-start.20 = (bf16[8,4,24,128]{3,2,1,0:T(8,128)(2,1)S(1)}, bf16[8,4,24,128]{3,2,1,0:T(8,128)(2,1)S(1)}, u32[]{:S(2)}, u32[]{:S(2)}) collective-permute-start(bf16[8,4,24,128]{3,2,1,0:T(8,128)(2,1)S(1)} %convert_element_type.113), channel_id=1, source_target_pairs={{0,4},{4,8},{8,12},{12,16},{16,20},{20,24},{24,28},{1,5},{5,9},{9,... | collective-permute-start | bytes 589832 | tf_op jit(solution)/shard_map/ppermute | solution.py:21
  153.6 4.0 %collective-permute-start.60 = (f32[256,32]{0,1:T(8,128)S(1)}, f32[256,32]{0,1:T(8,128)S(1)}, u32[]{:S(2)}, u32[]{:S(2)}) collective-permute-start(f32[256,32]{0,1:T(8,128)S(1)} %add.679), channel_id=1, source_target_pairs={{0,8},{4,12},{8,0},{12,4},{16,24},{20,28},{24,16},{28,20},{1,9},{5... | collective-permute-start | bytes 98312 | tf_op jit(solution)/shard_map/ppermute | solution.py:33
  155.3 4.0 %collective-permute-start.26 = (f32[256,32]{0,1:T(8,128)S(1)}, f32[256,32]{0,1:T(8,128)S(1)}, u32[]{:S(2)}, u32[]{:S(2)}) collective-permute-start(f32[256,32]{0,1:T(8,128)S(1)} %add.596), channel_id=1, source_target_pairs={{0,8},{4,12},{8,0},{12,4},{16,24},{20,28},{24,16},{28,20},{1,9},{5... | collective-permute-start | bytes 98312 | tf_op jit(solution)/shard_map/ppermute | solution.py:33
  157.6 4.1 %collective-permute-start.61 = (f32[256,32]{0,1:T(8,128)S(1)}, f32[256,32]{0,1:T(8,128)S(1)}, u32[]{:S(2)}, u32[]{:S(2)}) collective-permute-start(f32[256,32]{0,1:T(8,128)S(1)} %add.680), channel_id=1, source_target_pairs={{0,16},{4,20},{8,24},{12,28},{16,0},{20,4},{24,8},{28,12},{1,17},{... | collective-permute-start | bytes 98312 | tf_op jit(solution)/shard_map/ppermute | solution.py:33
  159.3 9.0 %collective-permute-start.27 = (f32[256,32]{0,1:T(8,128)S(1)}, f32[256,32]{0,1:T(8,128)S(1)}, u32[]{:S(2)}, u32[]{:S(2)}) collective-permute-start(f32[256,32]{0,1:T(8,128)S(1)} %add.597), channel_id=1, source_target_pairs={{0,16},{4,20},{8,24},{12,28},{16,0},{20,4},{24,8},{28,12},{1,17},{... | collective-permute-start | bytes 98312 | tf_op jit(solution)/shard_map/ppermute | solution.py:33
  163.8 11.2 %collective-permute-start.64 = (bf16[8,12288]{1,0:T(8,128)(2,1)S(1)}, bf16[8,12288]{1,0:T(8,128)(2,1)S(1)}, u32[]{:S(2)}, u32[]{:S(2)}) collective-permute-start(bf16[8,12288]{1,0:T(8,128)(2,1)S(1)} %get-tuple-element.50), channel_id=1, source_target_pairs={{3,0},{0,1},{1,2},{2,3},{7,4},{4,5},{5,6},{6,7},{11,8},{8,9},{9,10... | collective-permute-start | bytes 589832 | tf_op jit(solution)/shard_map/ppermute | solution.py:109
  164.2 25.8 %collective-permute-start.63 = (bf16[8,12288]{1,0:T(8,128)(2,1)S(1)}, bf16[8,12288]{1,0:T(8,128)(2,1)S(1)}, u32[]{:S(2)}, u32[]{:S(2)}) collective-permute-start(bf16[8,12288]{1,0:T(8,128)(2,1)S(1)} %get-tuple-element.51), channel_id=1, source_target_pairs={{2,0},{3,1},{0,2},{1,3},{6,4},{7,5},{4,6},{5,7},{10,8},{11,9},{8,1... | collective-permute-start | bytes 589832 | tf_op jit(solution)/shard_map/ppermute | solution.py:109
  168.3 23.9 %collective-permute-start.62 = (bf16[8,12288]{1,0:T(8,128)(2,1)S(1)}, bf16[8,12288]{1,0:T(8,128)(2,1)S(1)}, u32[]{:S(2)}, u32[]{:S(2)}) collective-permute-start(bf16[8,12288]{1,0:T(8,128)(2,1)S(1)} %get-tuple-element.49), channel_id=1, source_target_pairs={{1,0},{2,1},{3,2},{0,3},{5,4},{6,5},{7,6},{4,7},{9,8},{10,9},{11,1... | collective-permute-start | bytes 589832 | tf_op jit(solution)/shard_map/ppermute | solution.py:109
  170.4 23.8 %collective-permute-start.30 = (bf16[8,12288]{1,0:T(8,128)(2,1)S(1)}, bf16[8,12288]{1,0:T(8,128)(2,1)S(1)}, u32[]{:S(2)}, u32[]{:S(2)}) collective-permute-start(bf16[8,12288]{1,0:T(8,128)(2,1)S(1)} %get-tuple-element.41), channel_id=1, source_target_pairs={{3,0},{0,1},{1,2},{2,3},{7,4},{4,5},{5,6},{6,7},{11,8},{8,9},{9,10... | collective-permute-start | bytes 589832 | tf_op jit(solution)/shard_map/ppermute | solution.py:109
  172.5 24.4 %collective-permute-start.29 = (bf16[8,12288]{1,0:T(8,128)(2,1)S(1)}, bf16[8,12288]{1,0:T(8,128)(2,1)S(1)}, u32[]{:S(2)}, u32[]{:S(2)}) collective-permute-start(bf16[8,12288]{1,0:T(8,128)(2,1)S(1)} %get-tuple-element.42), channel_id=1, source_target_pairs={{2,0},{3,1},{0,2},{1,3},{6,4},{7,5},{4,6},{5,7},{10,8},{11,9},{8,1... | collective-permute-start | bytes 589832 | tf_op jit(solution)/shard_map/ppermute | solution.py:109
  175.0 24.7 %collective-permute-start.28 = (bf16[8,12288]{1,0:T(8,128)(2,1)S(1)}, bf16[8,12288]{1,0:T(8,128)(2,1)S(1)}, u32[]{:S(2)}, u32[]{:S(2)}) collective-permute-start(bf16[8,12288]{1,0:T(8,128)(2,1)S(1)} %get-tuple-element.40), channel_id=1, source_target_pairs={{1,0},{2,1},{3,2},{0,3},{5,4},{6,5},{7,6},{4,7},{9,8},{10,9},{11,1... | collective-permute-start | bytes 589832 | tf_op jit(solution)/shard_map/ppermute | solution.py:109
  193.5 7.5 %collective-permute-start.65 = (f32[8]{0:T(128)S(1)}, f32[8]{0:T(128)S(1)}, u32[]{:S(2)}, u32[]{:S(2)}) collective-permute-start(f32[8]{0:T(128)S(1)} %get-tuple-element.30), channel_id=1, source_target_pairs={{0,4},{4,0},{8,12},{12,8},{16,20},{20,16},{24,28},{28,24},{1,5},{5... | collective-permute-start | bytes 104 | tf_op jit(solution)/shard_map/ppermute | solution.py:33
  (25 other events, 150.2 us)

commit v7 on v6

--- a/solution.py
+++ b/solution.py
@@ -81,6 +81,8 @@
     residual = source_term
     direction = source_term
     norm_now = grid_sum(inner_product(source_term, source_term), "grid")
+    shift_pairs = [[(i, (i + d) % band_count) for i in range(band_count)] for d in range(1, band_count)]
+    previous_margins = None
     for iteration in range(ITERS):
         own_potential, direction = lax.optimization_barrier((potential, direction))
         potential_shift = own_potential[None] + shifts[:, None, None, None]
@@ -89,16 +91,17 @@
         )
         padded = jnp.pad(padded, ((0, 0), (0, 0), (4, 4), (4, 4)))
         kinetic = -0.5 * second_sum(padded, width_x, width_y, width_z)
-        rounded = direction.astype(jnp.bfloat16).reshape(local_bands, local_cells)
-        blocks = [rounded] + [
-            lax.ppermute(rounded, "band", [(i, (i + d) % band_count) for i in range(band_count)])
-            for d in range(1, band_count)
-        ]
+        fresh = direction if previous_margins is None else residual
+        rounded = fresh.astype(jnp.bfloat16).reshape(local_bands, local_cells)
+        blocks = [rounded] + [lax.ppermute(rounded, "band", pairs) for pairs in shift_pairs]
         gathered = jnp.concatenate(blocks, axis=0)
         partial_margin = lax.dot_general(
             occupied_rows, gathered, (((1,), (1,)), ((), ())), preferred_element_type=jnp.float32
         )
         margins = grid_sum(partial_margin, "grid")
+        if previous_margins is not None:
+            margins = margins + beta_all[None, :] * previous_margins
+        previous_margins = margins
         scaled = (margins * weight_scale).astype(jnp.bfloat16)
         terms = lax.dot_general(
             scaled, occupied_rows, (((0,), (0,)), ((), ())), preferred_element_type=jnp.float32
@@ -115,7 +118,9 @@
         residual = residual - expand(step_size) * applied
         if iteration + 1 < ITERS:
             norm_next = grid_sum(inner_product(residual, residual), "grid")
-            direction = residual + expand(norm_next / norm_now) * direction
+            beta = norm_next / norm_now
+            beta_all = jnp.concatenate([beta] + [lax.ppermute(beta, "band", pairs) for pairs in shift_pairs])
+            direction = residual + expand(beta) * direction
             norm_now = norm_next
     return (solution, residual)
 

time: 212 us -> 231 us (1.090)
  waiting for transfers between devices: 85.4 us -> 95.3 us
  starting transfers between devices: 96 us -> 105 us
    ppermute x36, waiting for transfers between devices: 23 us -> 30.4 us  [grid_sum(): value = value + lax.ppermute(value, axis, pairs)]
    ppermute x12 -> x18, starting transfers between devices: 26.3 us -> 33 us  [the longest x12 18.2 us: chain(): lax.ppermute(rounded, 'band', pairs)]
    ppermute x12, waiting for transfers between devices: 44.5 us -> 47.2 us  [chain(): lax.ppermute(part, 'band', [((i + d) % band_count, i) for i in range(band...]
    ppermute x36, starting transfers between devices: 33.2 us -> 35.5 us  [grid_sum(): value = value + lax.ppermute(value, axis, pairs)]
    ppermute x12 -> x18, waiting for transfers between devices: 17.9 us -> 17.7 us  [the longest x6 12.9 us: chain(): lax.ppermute(beta, 'band', pairs)]
    reduce_sum x6 -> x7, other arithmetic: 6.35 us -> 6.37 us  [inner_product(): return jnp.sum(first_field * second_field, axis=(1, 2, 3))]
  transfers between devices with their start and end apart: 68 -> 74, of which waited for: 36 -> 43; matrix products, arithmetic and copies ran while one was open for 12% -> 11% of each run, Pallas kernels for 0% -> 0%
where the time goes in v7:
time: 231 us
  starting transfers between devices  105 us (45%)
  waiting for transfers between devices  95.3 us (41%)
  matrix products  19.1 us (8%)
  other arithmetic  10.1 us (4%)
    ppermute x12, waiting for transfers between devices, chain(): lax.ppermute(part, 'band', [((i + d) % band_count, i) for i in range(band...  47.2 us
    ppermute x36, starting transfers between devices, grid_sum(): value = value + lax.ppermute(value, axis, pairs)  35.5 us
    ppermute x36, waiting for transfers between devices, grid_sum(): value = value + lax.ppermute(value, axis, pairs)  30.4 us
    ppermute x12, starting transfers between devices, chain(): lax.ppermute(rounded, 'band', pairs)  18.2 us
    ppermute x12, starting transfers between devices, chain(): lax.ppermute(part, 'band', [((i + d) % band_count, i) for i in range(band...  17.5 us
    ppermute x6, starting transfers between devices, chain(): lax.ppermute(beta, 'band', pairs)  14.8 us
    ppermute x4, starting transfers between devices, with_halo(): before = lax.ppermute(last, axis, up)  13.7 us
    ppermute x6, waiting for transfers between devices, chain(): lax.ppermute(beta, 'band', pairs)  12.9 us
  transfers between devices with their start and end apart: 74, of which 43 were waited for; matrix products, arithmetic and copies ran while one was open for 11% of the time, Pallas kernels for 0%

profile of v7, /device:TPU:8, one launch (start us, length us, event | category | flops | bytes accessed | tf_op | source)
XLA Modules:
  0.0 231.1 jit_solution(14227554796092757625)
XLA Ops:
  2.1 3.0 %collective-permute-start.6 = (bf16[8,12288]{1,0:T(8,128)(2,1)S(1)}, bf16[8,12288]{1,0:T(8,128)(2,1)S(1)}, u32[]{:S(2)}, u32[]{:S(2)}) collective-permute-start(bf16[8,12288]{1,0:T(8,128)(2,1)S(1)} %bitcast.90), channel_id=1, source_target_pairs={{0,2},{1,3},{2,0},{3,1},{4,6},{5,7},{6,4},{7,5},{8,10},{9,11},{10,... | collective-permute-start | bytes 589832 | tf_op jit(solution)/shard_map/ppermute | solution.py:96
  5.2 2.5 %collective-permute-start.5 = (bf16[8,12288]{1,0:T(8,128)(2,1)S(1)}, bf16[8,12288]{1,0:T(8,128)(2,1)S(1)}, u32[]{:S(2)}, u32[]{:S(2)}) collective-permute-start(bf16[8,12288]{1,0:T(8,128)(2,1)S(1)} %bitcast.91), channel_id=1, source_target_pairs={{0,1},{1,2},{2,3},{3,0},{4,5},{5,6},{6,7},{7,4},{8,9},{9,10},{10,1... | collective-permute-start | bytes 589832 | tf_op jit(solution)/shard_map/ppermute | solution.py:96
  13.6 2.0 collective-permute-done.38
  17.1 2.0 collective-permute-done.1
  22.0 2.4 %collective-permute-start.42 = (bf16[8,12288]{1,0:T(8,128)(2,1)S(1)}, bf16[8,12288]{1,0:T(8,128)(2,1)S(1)}, u32[]{:S(2)}, u32[]{:S(2)}) collective-permute-start(bf16[8,12288]{1,0:T(8,128)(2,1)S(1)} %bitcast.87), channel_id=1, source_target_pairs={{0,1},{1,2},{2,3},{3,0},{4,5},{5,6},{6,7},{7,4},{8,9},{9,10},{10,1... | collective-permute-start | bytes 589832 | tf_op jit(solution)/shard_map/ppermute | solution.py:96
  24.4 5.0 %fusion.12 = f32[256,32]{0,1:T(8,128)S(1)} fusion(bf16[32,8,96,128]{3,2,1,0:T(8,128)(2,1)} %bitcast.59, bf16[8,12288]{1,0:T(8,128)(2,1)S(1)} %collective-permute-done.7, bf16[8,12288]{1,0:T(8,128)(2,1)S(1)} %collective-permute-done.6, bf16[8,12288]{1,0:T(8,128)(2,1)S(1)} %collective-permute-done.5, bf16[8,12288]{1,0:T(8,128)(2,1)S(1)} %bitcast.92), kind=kOutput, calls=%fused_computation.80 | convolution fusion | flops 204472320 | bytes 7110656 | tf_op jit(solution)/shard_map/dot_general | solution.py:98
  30.7 4.7 %collective-permute-done.43 = bf16[8,12288]{1,0:T(8,128)(2,1)S(1)} collective-permute-done((bf16[8,12288]{1,0:T(8,128)(2,1)S(1)}, bf16[8,12288]{1,0:T(8,128)(2,1)S(1)}, u32[]{:S(2)}, u32[]{:S(2)}) %collective-permute-start.43) | collective-permute-done | bytes 196640 | tf_op jit(solution)/shard_map/ppermute | solution.py:96
  35.4 6.3 %collective-permute-start.40 = (bf16[8,4,24,128]{3,2,1,0:T(8,128)(2,1)S(1)}, bf16[8,4,24,128]{3,2,1,0:T(8,128)(2,1)S(1)}, u32[]{:S(2)}, u32[]{:S(2)}) collective-permute-start(bf16[8,4,24,128]{3,2,1,0:T(8,128)(2,1)S(1)} %convert_element_type.126), channel_id=1, source_target_pairs={{0,4},{4,8},{8,12},{12,16},{16,20},{20,24},{24,28},{1,5},{5,9},{9,... | collective-permute-start | bytes 589832 | tf_op jit(solution)/shard_map/ppermute | solution.py:21
  41.7 1.8 collective-permute-start.8
  43.5 2.0 fusion.18
  48.3 1.9 collective-permute-start.2
  52.0 2.1 collective-permute-start.10
  56.3 2.0 convolution_convert_fusion.3
  59.0 2.0 convolution_convert_fusion.1
  61.1 3.9 %collective-permute-start.49 = (bf16[8,12288]{1,0:T(8,128)(2,1)S(1)}, bf16[8,12288]{1,0:T(8,128)(2,1)S(1)}, u32[]{:S(2)}, u32[]{:S(2)}) collective-permute-start(bf16[8,12288]{1,0:T(8,128)(2,1)S(1)} %get-tuple-element.55), channel_id=1, source_target_pairs={{2,0},{3,1},{0,2},{1,3},{6,4},{7,5},{4,6},{5,7},{10,8},{11,9},{8,1... | collective-permute-start | bytes 589832 | tf_op jit(solution)/shard_map/ppermute | solution.py:112
  65.1 7.3 %collective-permute-done.50 = bf16[8,12288]{1,0:T(8,128)(2,1)S(1)} collective-permute-done((bf16[8,12288]{1,0:T(8,128)(2,1)S(1)}, bf16[8,12288]{1,0:T(8,128)(2,1)S(1)}, u32[]{:S(2)}, u32[]{:S(2)}) %collective-permute-start.50) | collective-permute-done | bytes 196640 | tf_op jit(solution)/shard_map/ppermute | solution.py:112
  72.4 3.0 %collective-permute-start.13 = (bf16[8,12288]{1,0:T(8,128)(2,1)S(1)}, bf16[8,12288]{1,0:T(8,128)(2,1)S(1)}, u32[]{:S(2)}, u32[]{:S(2)}) collective-permute-start(bf16[8,12288]{1,0:T(8,128)(2,1)S(1)} %get-tuple-element.46), channel_id=1, source_target_pairs={{3,0},{0,1},{1,2},{2,3},{7,4},{4,5},{5,6},{6,7},{11,8},{8,9},{9,10... | collective-permute-start | bytes 589832 | tf_op jit(solution)/shard_map/ppermute | solution.py:112
  75.4 7.7 %collective-permute-done.49 = bf16[8,12288]{1,0:T(8,128)(2,1)S(1)} collective-permute-done((bf16[8,12288]{1,0:T(8,128)(2,1)S(1)}, bf16[8,12288]{1,0:T(8,128)(2,1)S(1)}, u32[]{:S(2)}, u32[]{:S(2)}) %collective-permute-start.49) | collective-permute-done | bytes 196640 | tf_op jit(solution)/shard_map/ppermute | solution.py:112
  83.1 3.4 %collective-permute-start.12 = (bf16[8,12288]{1,0:T(8,128)(2,1)S(1)}, bf16[8,12288]{1,0:T(8,128)(2,1)S(1)}, u32[]{:S(2)}, u32[]{:S(2)}) collective-permute-start(bf16[8,12288]{1,0:T(8,128)(2,1)S(1)} %get-tuple-element.47), channel_id=1, source_target_pairs={{2,0},{3,1},{0,2},{1,3},{6,4},{7,5},{4,6},{5,7},{10,8},{11,9},{8,1... | collective-permute-start | bytes 589832 | tf_op jit(solution)/shard_map/ppermute | solution.py:112
  87.9 3.6 %collective-permute-done.13 = bf16[8,12288]{1,0:T(8,128)(2,1)S(1)} collective-permute-done((bf16[8,12288]{1,0:T(8,128)(2,1)S(1)}, bf16[8,12288]{1,0:T(8,128)(2,1)S(1)}, u32[]{:S(2)}, u32[]{:S(2)}) %collective-permute-start.13) | collective-permute-done | bytes 196640 | tf_op jit(solution)/shard_map/ppermute | solution.py:112
  91.5 2.3 collective-permute-done.12
  93.8 2.4 %collective-permute-done.11 = bf16[8,12288]{1,0:T(8,128)(2,1)S(1)} collective-permute-done((bf16[8,12288]{1,0:T(8,128)(2,1)S(1)}, bf16[8,12288]{1,0:T(8,128)(2,1)S(1)}, u32[]{:S(2)}, u32[]{:S(2)}) %collective-permute-start.11) | collective-permute-done | bytes 196640 | tf_op jit(solution)/shard_map/ppermute | solution.py:112
  107.7 2.5 %collective-permute-start.59 = (bf16[8,12288]{1,0:T(8,128)(2,1)S(1)}, bf16[8,12288]{1,0:T(8,128)(2,1)S(1)}, u32[]{:S(2)}, u32[]{:S(2)}) collective-permute-start(bf16[8,12288]{1,0:T(8,128)(2,1)S(1)} %bitcast.83), channel_id=1, source_target_pairs={{0,1},{1,2},{2,3},{3,0},{4,5},{5,6},{6,7},{7,4},{8,9},{9,10},{10,1... | collective-permute-start | bytes 589832 | tf_op jit(solution)/shard_map/ppermute | solution.py:96
  113.2 2.3 collective-permute-done.55
  116.7 2.3 collective-permute-done.18
  120.3 2.3 collective-permute-done.56
  124.0 2.1 collective-permute-done.19
  126.1 3.4 %collective-permute-start.67 = (f32[8]{0:T(128)S(1)}, f32[8]{0:T(128)S(1)}, u32[]{:S(2)}, u32[]{:S(2)}) collective-permute-start(f32[8]{0:T(128)S(1)} %get-tuple-element.34), channel_id=1, source_target_pairs={{0,3},{1,0},{2,1},{3,2},{4,7},{5,4},{6,5},{7,6},{8,11},{9,8},{10,9... | collective-permute-start | bytes 104 | tf_op jit(solution)/shard_map/ppermute | solution.py:122
  130.8 3.0 %collective-permute-start.66 = (f32[8]{0:T(128)S(1)}, f32[8]{0:T(128)S(1)}, u32[]{:S(2)}, u32[]{:S(2)}) collective-permute-start(f32[8]{0:T(128)S(1)} %get-tuple-element.34), channel_id=1, source_target_pairs={{0,2},{1,3},{2,0},{3,1},{4,6},{5,7},{6,4},{7,5},{8,10},{9,11},{10,... | collective-permute-start | bytes 104 | tf_op jit(solution)/shard_map/ppermute | solution.py:122
  136.1 3.0 %collective-permute-done.65 = f32[8]{0:T(128)S(1)} collective-permute-done((f32[8]{0:T(128)S(1)}, f32[8]{0:T(128)S(1)}, u32[]{:S(2)}, u32[]{:S(2)}) %collective-permute-start.65) | collective-permute-done | bytes 64 | tf_op jit(solution)/shard_map/ppermute | solution.py:122
  139.0 3.8 %collective-permute-start.30 = (f32[8]{0:T(128)S(1)}, f32[8]{0:T(128)S(1)}, u32[]{:S(2)}, u32[]{:S(2)}) collective-permute-start(f32[8]{0:T(128)S(1)} %get-tuple-element.24), channel_id=1, source_target_pairs={{0,3},{1,0},{2,1},{3,2},{4,7},{5,4},{6,5},{7,6},{8,11},{9,8},{10,9... | collective-permute-start | bytes 104 | tf_op jit(solution)/shard_map/ppermute | solution.py:122
  144.2 3.0 %collective-permute-start.29 = (f32[8]{0:T(128)S(1)}, f32[8]{0:T(128)S(1)}, u32[]{:S(2)}, u32[]{:S(2)}) collective-permute-start(f32[8]{0:T(128)S(1)} %get-tuple-element.24), channel_id=1, source_target_pairs={{0,2},{1,3},{2,0},{3,1},{4,6},{5,7},{6,4},{7,5},{8,10},{9,11},{10,... | collective-permute-start | bytes 104 | tf_op jit(solution)/shard_map/ppermute | solution.py:122
  149.5 4.6 %collective-permute-done.28 = f32[8]{0:T(128)S(1)} collective-permute-done((f32[8]{0:T(128)S(1)}, f32[8]{0:T(128)S(1)}, u32[]{:S(2)}, u32[]{:S(2)}) %collective-permute-start.28) | collective-permute-done | bytes 64 | tf_op jit(solution)/shard_map/ppermute | solution.py:122
  154.0 2.1 collective-permute-start.23
  156.3 3.1 %collective-permute-start.22 = (bf16[8,12288]{1,0:T(8,128)(2,1)S(1)}, bf16[8,12288]{1,0:T(8,128)(2,1)S(1)}, u32[]{:S(2)}, u32[]{:S(2)}) collective-permute-start(bf16[8,12288]{1,0:T(8,128)(2,1)S(1)} %bitcast.79), channel_id=1, source_target_pairs={{0,1},{1,2},{2,3},{3,0},{4,5},{5,6},{6,7},{7,4},{8,9},{9,10},{10,1... | collective-permute-start | bytes 589832 | tf_op jit(solution)/shard_map/ppermute | solution.py:96
  160.7 3.0 %collective-permute-start.57 = (bf16[8,4,24,128]{3,2,1,0:T(8,128)(2,1)S(1)}, bf16[8,4,24,128]{3,2,1,0:T(8,128)(2,1)S(1)}, u32[]{:S(2)}, u32[]{:S(2)}) collective-permute-start(bf16[8,4,24,128]{3,2,1,0:T(8,128)(2,1)S(1)} %convert_element_type.134), channel_id=1, source_target_pairs={{0,4},{4,8},{8,12},{12,16},{16,20},{20,24},{24,28},{1,5},{5,9},{9,... | collective-permute-start | bytes 589832 | tf_op jit(solution)/shard_map/ppermute | solution.py:21
  163.8 2.0 fusion.21
  167.1 3.0 %collective-permute-start.20 = (bf16[8,4,24,128]{3,2,1,0:T(8,128)(2,1)S(1)}, bf16[8,4,24,128]{3,2,1,0:T(8,128)(2,1)S(1)}, u32[]{:S(2)}, u32[]{:S(2)}) collective-permute-start(bf16[8,4,24,128]{3,2,1,0:T(8,128)(2,1)S(1)} %convert_element_type.117), channel_id=1, source_target_pairs={{0,4},{4,8},{8,12},{12,16},{16,20},{20,24},{24,28},{1,5},{5,9},{9,... | collective-permute-start | bytes 589832 | tf_op jit(solution)/shard_map/ppermute | solution.py:21
  171.9 2.0 fusion.15
  174.0 2.6 %collective-permute-start.63 = (f32[256,32]{0,1:T(8,128)S(1)}, f32[256,32]{0,1:T(8,128)S(1)}, u32[]{:S(2)}, u32[]{:S(2)}) collective-permute-start(f32[256,32]{0,1:T(8,128)S(1)} %add.686), channel_id=1, source_target_pairs={{0,8},{4,12},{8,0},{12,4},{16,24},{20,28},{24,16},{28,20},{1,9},{5... | collective-permute-start | bytes 98312 | tf_op jit(solution)/shard_map/ppermute | solution.py:33
  180.9 1.9 collective-permute-done.64
  182.8 2.0 convolution_convert_fusion
  188.1 2.0 convolution_convert_fusion.2
  190.8 3.3 %collective-permute-start.32 = (bf16[8,12288]{1,0:T(8,128)(2,1)S(1)}, bf16[8,12288]{1,0:T(8,128)(2,1)S(1)}, u32[]{:S(2)}, u32[]{:S(2)}) collective-permute-start(bf16[8,12288]{1,0:T(8,128)(2,1)S(1)} %get-tuple-element.42), channel_id=1, source_target_pairs={{2,0},{3,1},{0,2},{1,3},{6,4},{7,5},{4,6},{5,7},{10,8},{11,9},{8,1... | collective-permute-start | bytes 589832 | tf_op jit(solution)/shard_map/ppermute | solution.py:112
  194.1 3.0 %collective-permute-done.70 = bf16[8,12288]{1,0:T(8,128)(2,1)S(1)} collective-permute-done((bf16[8,12288]{1,0:T(8,128)(2,1)S(1)}, bf16[8,12288]{1,0:T(8,128)(2,1)S(1)}, u32[]{:S(2)}, u32[]{:S(2)}) %collective-permute-start.70) | collective-permute-done | bytes 196640 | tf_op jit(solution)/shard_map/ppermute | solution.py:112
  197.1 14.5 %collective-permute-done.69 = bf16[8,12288]{1,0:T(8,128)(2,1)S(1)} collective-permute-done((bf16[8,12288]{1,0:T(8,128)(2,1)S(1)}, bf16[8,12288]{1,0:T(8,128)(2,1)S(1)}, u32[]{:S(2)}, u32[]{:S(2)}) %collective-permute-start.69) | collective-permute-done | bytes 196640 | tf_op jit(solution)/shard_map/ppermute | solution.py:112
  213.0 2.7 %collective-permute-done.33 = bf16[8,12288]{1,0:T(8,128)(2,1)S(1)} collective-permute-done((bf16[8,12288]{1,0:T(8,128)(2,1)S(1)}, bf16[8,12288]{1,0:T(8,128)(2,1)S(1)}, u32[]{:S(2)}, u32[]{:S(2)}) %collective-permute-start.33) | collective-permute-done | bytes 196640 | tf_op jit(solution)/shard_map/ppermute | solution.py:112
  215.7 2.1 collective-permute-done.32
  (187 shorter events, 74.7 us)
Async XLA Ops:
  2.1 18.4 %collective-permute-start.7 = (bf16[8,12288]{1,0:T(8,128)(2,1)S(1)}, bf16[8,12288]{1,0:T(8,128)(2,1)S(1)}, u32[]{:S(2)}, u32[]{:S(2)}) collective-permute-start(bf16[8,12288]{1,0:T(8,128)(2,1)S(1)} %bitcast.89), channel_id=1, source_target_pairs={{0,3},{1,0},{2,1},{3,2},{4,7},{5,4},{6,5},{7,6},{8,11},{9,8},{10,9... | collective-permute-start | bytes 589832 | tf_op jit(solution)/shard_map/ppermute | solution.py:96
  2.1 18.4 %collective-permute-start.6 = (bf16[8,12288]{1,0:T(8,128)(2,1)S(1)}, bf16[8,12288]{1,0:T(8,128)(2,1)S(1)}, u32[]{:S(2)}, u32[]{:S(2)}) collective-permute-start(bf16[8,12288]{1,0:T(8,128)(2,1)S(1)} %bitcast.90), channel_id=1, source_target_pairs={{0,2},{1,3},{2,0},{3,1},{4,6},{5,7},{6,4},{7,5},{8,10},{9,11},{10,... | collective-permute-start | bytes 589832 | tf_op jit(solution)/shard_map/ppermute | solution.py:96
  5.2 16.9 %collective-permute-start.5 = (bf16[8,12288]{1,0:T(8,128)(2,1)S(1)}, bf16[8,12288]{1,0:T(8,128)(2,1)S(1)}, u32[]{:S(2)}, u32[]{:S(2)}) collective-permute-start(bf16[8,12288]{1,0:T(8,128)(2,1)S(1)} %bitcast.91), channel_id=1, source_target_pairs={{0,1},{1,2},{2,3},{3,0},{4,5},{5,6},{6,7},{7,4},{8,9},{9,10},{10,1... | collective-permute-start | bytes 589832 | tf_op jit(solution)/shard_map/ppermute | solution.py:96
  7.6 39.4 %collective-permute-start.4 = (bf16[8,4,24,128]{3,2,1,0:T(8,128)(2,1)S(1)}, bf16[8,4,24,128]{3,2,1,0:T(8,128)(2,1)S(1)}, u32[]{:S(2)}, u32[]{:S(2)}) collective-permute-start(bf16[8,4,24,128]{3,2,1,0:T(8,128)(2,1)S(1)} %convert_element_type.109), channel_id=1, source_target_pairs={{4,0},{8,4},{12,8},{16,12},{20,16},{24,20},{28,24},{5,1},{9,5},{13... | collective-permute-start | bytes 589832 | tf_op jit(solution)/shard_map/ppermute | solution.py:22
  19.2 28.0 %collective-permute-start.3 = (bf16[8,4,24,128]{3,2,1,0:T(8,128)(2,1)S(1)}, bf16[8,4,24,128]{3,2,1,0:T(8,128)(2,1)S(1)}, u32[]{:S(2)}, u32[]{:S(2)}) collective-permute-start(bf16[8,4,24,128]{3,2,1,0:T(8,128)(2,1)S(1)} %convert_element_type.109), channel_id=1, source_target_pairs={{0,4},{4,8},{8,12},{12,16},{16,20},{20,24},{24,28},{1,5},{5,9},{9,... | collective-permute-start | bytes 589832 | tf_op jit(solution)/shard_map/ppermute | solution.py:21
  20.5 8.9 %collective-permute-start.44 = (bf16[8,12288]{1,0:T(8,128)(2,1)S(1)}, bf16[8,12288]{1,0:T(8,128)(2,1)S(1)}, u32[]{:S(2)}, u32[]{:S(2)}) collective-permute-start(bf16[8,12288]{1,0:T(8,128)(2,1)S(1)} %bitcast.85), channel_id=1, source_target_pairs={{0,3},{1,0},{2,1},{3,2},{4,7},{5,4},{6,5},{7,6},{8,11},{9,8},{10,9... | collective-permute-start | bytes 589832 | tf_op jit(solution)/shard_map/ppermute | solution.py:96
  20.6 14.8 %collective-permute-start.43 = (bf16[8,12288]{1,0:T(8,128)(2,1)S(1)}, bf16[8,12288]{1,0:T(8,128)(2,1)S(1)}, u32[]{:S(2)}, u32[]{:S(2)}) collective-permute-start(bf16[8,12288]{1,0:T(8,128)(2,1)S(1)} %bitcast.86), channel_id=1, source_target_pairs={{0,2},{1,3},{2,0},{3,1},{4,6},{5,7},{6,4},{7,5},{8,10},{9,11},{10,... | collective-permute-start | bytes 589832 | tf_op jit(solution)/shard_map/ppermute | solution.py:96
  22.0 19.7 %collective-permute-start.42 = (bf16[8,12288]{1,0:T(8,128)(2,1)S(1)}, bf16[8,12288]{1,0:T(8,128)(2,1)S(1)}, u32[]{:S(2)}, u32[]{:S(2)}) collective-permute-start(bf16[8,12288]{1,0:T(8,128)(2,1)S(1)} %bitcast.87), channel_id=1, source_target_pairs={{0,1},{1,2},{2,3},{3,0},{4,5},{5,6},{6,7},{7,4},{8,9},{9,10},{10,1... | collective-permute-start | bytes 589832 | tf_op jit(solution)/shard_map/ppermute | solution.py:96
  29.4 22.7 %collective-permute-start.41 = (bf16[8,4,24,128]{3,2,1,0:T(8,128)(2,1)S(1)}, bf16[8,4,24,128]{3,2,1,0:T(8,128)(2,1)S(1)}, u32[]{:S(2)}, u32[]{:S(2)}) collective-permute-start(bf16[8,4,24,128]{3,2,1,0:T(8,128)(2,1)S(1)} %convert_element_type.126), channel_id=1, source_target_pairs={{4,0},{8,4},{12,8},{16,12},{20,16},{24,20},{28,24},{5,1},{9,5},{13... | collective-permute-start | bytes 589832 | tf_op jit(solution)/shard_map/ppermute | solution.py:22
  35.4 18.8 %collective-permute-start.40 = (bf16[8,4,24,128]{3,2,1,0:T(8,128)(2,1)S(1)}, bf16[8,4,24,128]{3,2,1,0:T(8,128)(2,1)S(1)}, u32[]{:S(2)}, u32[]{:S(2)}) collective-permute-start(bf16[8,4,24,128]{3,2,1,0:T(8,128)(2,1)S(1)} %convert_element_type.126), channel_id=1, source_target_pairs={{0,4},{4,8},{8,12},{12,16},{16,20},{20,24},{24,28},{1,5},{5,9},{9,... | collective-permute-start | bytes 589832 | tf_op jit(solution)/shard_map/ppermute | solution.py:21
  45.6 58.3 %collective-permute-start.39 = (f32[8]{0:T(128)S(1)}, f32[8]{0:T(128)S(1)}, u32[]{:S(2)}, u32[]{:S(2)}) collective-permute-start(f32[8]{0:T(128)S(1)} %add.615), channel_id=1, source_target_pairs={{0,16},{4,20},{8,24},{12,28},{16,0},{20,4},{24,8},{28,12},{1,17},{... | collective-permute-start | bytes 104 | tf_op jit(solution)/shard_map/ppermute | solution.py:33
  47.2 4.0 %collective-permute-start.9 = (f32[256,32]{0,1:T(8,128)S(1)}, f32[256,32]{0,1:T(8,128)S(1)}, u32[]{:S(2)}, u32[]{:S(2)}) collective-permute-start(f32[256,32]{0,1:T(8,128)S(1)} %add.561), channel_id=1, source_target_pairs={{0,8},{4,12},{8,0},{12,4},{16,24},{20,28},{24,16},{28,20},{1,9},{5... | collective-permute-start | bytes 98312 | tf_op jit(solution)/shard_map/ppermute | solution.py:33
  48.3 55.5 %collective-permute-start.2 = (f32[8]{0:T(128)S(1)}, f32[8]{0:T(128)S(1)}, u32[]{:S(2)}, u32[]{:S(2)}) collective-permute-start(f32[8]{0:T(128)S(1)} %add.531), channel_id=1, source_target_pairs={{0,16},{4,20},{8,24},{12,28},{16,0},{20,4},{24,8},{28,12},{1,17},{... | collective-permute-start | bytes 104 | tf_op jit(solution)/shard_map/ppermute | solution.py:33
  51.1 3.9 %collective-permute-start.46 = (f32[256,32]{0,1:T(8,128)S(1)}, f32[256,32]{0,1:T(8,128)S(1)}, u32[]{:S(2)}, u32[]{:S(2)}) collective-permute-start(f32[256,32]{0,1:T(8,128)S(1)} %add.645), channel_id=1, source_target_pairs={{0,8},{4,12},{8,0},{12,4},{16,24},{20,28},{24,16},{28,20},{1,9},{5... | collective-permute-start | bytes 98312 | tf_op jit(solution)/shard_map/ppermute | solution.py:33
  52.0 4.2 %collective-permute-start.10 = (f32[256,32]{0,1:T(8,128)S(1)}, f32[256,32]{0,1:T(8,128)S(1)}, u32[]{:S(2)}, u32[]{:S(2)}) collective-permute-start(f32[256,32]{0,1:T(8,128)S(1)} %add.562), channel_id=1, source_target_pairs={{0,16},{4,20},{8,24},{12,28},{16,0},{20,4},{24,8},{28,12},{1,17},{... | collective-permute-start | bytes 98312 | tf_op jit(solution)/shard_map/ppermute | solution.py:33
  61.0 11.4 %collective-permute-start.50 = (bf16[8,12288]{1,0:T(8,128)(2,1)S(1)}, bf16[8,12288]{1,0:T(8,128)(2,1)S(1)}, u32[]{:S(2)}, u32[]{:S(2)}) collective-permute-start(bf16[8,12288]{1,0:T(8,128)(2,1)S(1)} %get-tuple-element.54), channel_id=1, source_target_pairs={{3,0},{0,1},{1,2},{2,3},{7,4},{4,5},{5,6},{6,7},{11,8},{8,9},{9,10... | collective-permute-start | bytes 589832 | tf_op jit(solution)/shard_map/ppermute | solution.py:112
  61.1 21.9 %collective-permute-start.49 = (bf16[8,12288]{1,0:T(8,128)(2,1)S(1)}, bf16[8,12288]{1,0:T(8,128)(2,1)S(1)}, u32[]{:S(2)}, u32[]{:S(2)}) collective-permute-start(bf16[8,12288]{1,0:T(8,128)(2,1)S(1)} %get-tuple-element.55), channel_id=1, source_target_pairs={{2,0},{3,1},{0,2},{1,3},{6,4},{7,5},{4,6},{5,7},{10,8},{11,9},{8,1... | collective-permute-start | bytes 589832 | tf_op jit(solution)/shard_map/ppermute | solution.py:112
  65.1 21.6 %collective-permute-start.48 = (bf16[8,12288]{1,0:T(8,128)(2,1)S(1)}, bf16[8,12288]{1,0:T(8,128)(2,1)S(1)}, u32[]{:S(2)}, u32[]{:S(2)}) collective-permute-start(bf16[8,12288]{1,0:T(8,128)(2,1)S(1)} %get-tuple-element.53), channel_id=1, source_target_pairs={{1,0},{2,1},{3,2},{0,3},{5,4},{6,5},{7,6},{4,7},{9,8},{10,9},{11,1... | collective-permute-start | bytes 589832 | tf_op jit(solution)/shard_map/ppermute | solution.py:112
  72.4 19.1 %collective-permute-start.13 = (bf16[8,12288]{1,0:T(8,128)(2,1)S(1)}, bf16[8,12288]{1,0:T(8,128)(2,1)S(1)}, u32[]{:S(2)}, u32[]{:S(2)}) collective-permute-start(bf16[8,12288]{1,0:T(8,128)(2,1)S(1)} %get-tuple-element.46), channel_id=1, source_target_pairs={{3,0},{0,1},{1,2},{2,3},{7,4},{4,5},{5,6},{6,7},{11,8},{8,9},{9,10... | collective-permute-start | bytes 589832 | tf_op jit(solution)/shard_map/ppermute | solution.py:112
  83.1 10.7 %collective-permute-start.12 = (bf16[8,12288]{1,0:T(8,128)(2,1)S(1)}, bf16[8,12288]{1,0:T(8,128)(2,1)S(1)}, u32[]{:S(2)}, u32[]{:S(2)}) collective-permute-start(bf16[8,12288]{1,0:T(8,128)(2,1)S(1)} %get-tuple-element.47), channel_id=1, source_target_pairs={{2,0},{3,1},{0,2},{1,3},{6,4},{7,5},{4,6},{5,7},{10,8},{11,9},{8,1... | collective-permute-start | bytes 589832 | tf_op jit(solution)/shard_map/ppermute | solution.py:112
  86.6 9.6 %collective-permute-start.11 = (bf16[8,12288]{1,0:T(8,128)(2,1)S(1)}, bf16[8,12288]{1,0:T(8,128)(2,1)S(1)}, u32[]{:S(2)}, u32[]{:S(2)}) collective-permute-start(bf16[8,12288]{1,0:T(8,128)(2,1)S(1)} %get-tuple-element.45), channel_id=1, source_target_pairs={{1,0},{2,1},{3,2},{0,3},{5,4},{6,5},{7,6},{4,7},{9,8},{10,9},{11,1... | collective-permute-start | bytes 589832 | tf_op jit(solution)/shard_map/ppermute | solution.py:112
  91.5 6.1 %collective-permute-start.51 = (f32[8]{0:T(128)S(1)}, f32[8]{0:T(128)S(1)}, u32[]{:S(2)}, u32[]{:S(2)}) collective-permute-start(f32[8]{0:T(128)S(1)} %get-tuple-element.38), channel_id=1, source_target_pairs={{0,4},{4,0},{8,12},{12,8},{16,20},{20,16},{24,28},{28,24},{1,5},{5... | collective-permute-start | bytes 104 | tf_op jit(solution)/shard_map/ppermute | solution.py:33
  106.7 49.6 %collective-permute-start.61 = (bf16[8,12288]{1,0:T(8,128)(2,1)S(1)}, bf16[8,12288]{1,0:T(8,128)(2,1)S(1)}, u32[]{:S(2)}, u32[]{:S(2)}) collective-permute-start(bf16[8,12288]{1,0:T(8,128)(2,1)S(1)} %bitcast.81), channel_id=1, source_target_pairs={{0,3},{1,0},{2,1},{3,2},{4,7},{5,4},{6,5},{7,6},{8,11},{9,8},{10,9... | collective-permute-start | bytes 589832 | tf_op jit(solution)/shard_map/ppermute | solution.py:96
  106.8 52.7 %collective-permute-start.60 = (bf16[8,12288]{1,0:T(8,128)(2,1)S(1)}, bf16[8,12288]{1,0:T(8,128)(2,1)S(1)}, u32[]{:S(2)}, u32[]{:S(2)}) collective-permute-start(bf16[8,12288]{1,0:T(8,128)(2,1)S(1)} %bitcast.82), channel_id=1, source_target_pairs={{0,2},{1,3},{2,0},{3,1},{4,6},{5,7},{6,4},{7,5},{8,10},{9,11},{10,... | collective-permute-start | bytes 589832 | tf_op jit(solution)/shard_map/ppermute | solution.py:96
  107.7 53.0 %collective-permute-start.59 = (bf16[8,12288]{1,0:T(8,128)(2,1)S(1)}, bf16[8,12288]{1,0:T(8,128)(2,1)S(1)}, u32[]{:S(2)}, u32[]{:S(2)}) collective-permute-start(bf16[8,12288]{1,0:T(8,128)(2,1)S(1)} %bitcast.83), channel_id=1, source_target_pairs={{0,1},{1,2},{2,3},{3,0},{4,5},{5,6},{6,7},{7,4},{8,9},{9,10},{10,1... | collective-permute-start | bytes 589832 | tf_op jit(solution)/shard_map/ppermute | solution.py:96
  111.5 54.3 %collective-permute-start.24 = (bf16[8,12288]{1,0:T(8,128)(2,1)S(1)}, bf16[8,12288]{1,0:T(8,128)(2,1)S(1)}, u32[]{:S(2)}, u32[]{:S(2)}) collective-permute-start(bf16[8,12288]{1,0:T(8,128)(2,1)S(1)} %bitcast.77), channel_id=1, source_target_pairs={{0,3},{1,0},{2,1},{3,2},{4,7},{5,4},{6,5},{7,6},{8,11},{9,8},{10,9... | collective-permute-start | bytes 589832 | tf_op jit(solution)/shard_map/ppermute | solution.py:96
  126.1 4.7 %collective-permute-start.67 = (f32[8]{0:T(128)S(1)}, f32[8]{0:T(128)S(1)}, u32[]{:S(2)}, u32[]{:S(2)}) collective-permute-start(f32[8]{0:T(128)S(1)} %get-tuple-element.34), channel_id=1, source_target_pairs={{0,3},{1,0},{2,1},{3,2},{4,7},{5,4},{6,5},{7,6},{8,11},{9,8},{10,9... | collective-permute-start | bytes 104 | tf_op jit(solution)/shard_map/ppermute | solution.py:122
  130.8 4.5 %collective-permute-start.66 = (f32[8]{0:T(128)S(1)}, f32[8]{0:T(128)S(1)}, u32[]{:S(2)}, u32[]{:S(2)}) collective-permute-start(f32[8]{0:T(128)S(1)} %get-tuple-element.34), channel_id=1, source_target_pairs={{0,2},{1,3},{2,0},{3,1},{4,6},{5,7},{6,4},{7,5},{8,10},{9,11},{10,... | collective-permute-start | bytes 104 | tf_op jit(solution)/shard_map/ppermute | solution.py:122
  139.0 5.1 %collective-permute-start.30 = (f32[8]{0:T(128)S(1)}, f32[8]{0:T(128)S(1)}, u32[]{:S(2)}, u32[]{:S(2)}) collective-permute-start(f32[8]{0:T(128)S(1)} %get-tuple-element.24), channel_id=1, source_target_pairs={{0,3},{1,0},{2,1},{3,2},{4,7},{5,4},{6,5},{7,6},{8,11},{9,8},{10,9... | collective-permute-start | bytes 104 | tf_op jit(solution)/shard_map/ppermute | solution.py:122
  144.2 4.5 %collective-permute-start.29 = (f32[8]{0:T(128)S(1)}, f32[8]{0:T(128)S(1)}, u32[]{:S(2)}, u32[]{:S(2)}) collective-permute-start(f32[8]{0:T(128)S(1)} %get-tuple-element.24), channel_id=1, source_target_pairs={{0,2},{1,3},{2,0},{3,1},{4,6},{5,7},{6,4},{7,5},{8,10},{9,11},{10,... | collective-permute-start | bytes 104 | tf_op jit(solution)/shard_map/ppermute | solution.py:122
  148.7 5.4 %collective-permute-start.28 = (f32[8]{0:T(128)S(1)}, f32[8]{0:T(128)S(1)}, u32[]{:S(2)}, u32[]{:S(2)}) collective-permute-start(f32[8]{0:T(128)S(1)} %get-tuple-element.24), channel_id=1, source_target_pairs={{0,1},{1,2},{2,3},{3,0},{4,5},{5,6},{6,7},{7,4},{8,9},{9,10},{10,1... | collective-permute-start | bytes 104 | tf_op jit(solution)/shard_map/ppermute | solution.py:122
  154.0 13.1 %collective-permute-start.23 = (bf16[8,12288]{1,0:T(8,128)(2,1)S(1)}, bf16[8,12288]{1,0:T(8,128)(2,1)S(1)}, u32[]{:S(2)}, u32[]{:S(2)}) collective-permute-start(bf16[8,12288]{1,0:T(8,128)(2,1)S(1)} %bitcast.78), channel_id=1, source_target_pairs={{0,2},{1,3},{2,0},{3,1},{4,6},{5,7},{6,4},{7,5},{8,10},{9,11},{10,... | collective-permute-start | bytes 589832 | tf_op jit(solution)/shard_map/ppermute | solution.py:96
  156.3 13.9 %collective-permute-start.22 = (bf16[8,12288]{1,0:T(8,128)(2,1)S(1)}, bf16[8,12288]{1,0:T(8,128)(2,1)S(1)}, u32[]{:S(2)}, u32[]{:S(2)}) collective-permute-start(bf16[8,12288]{1,0:T(8,128)(2,1)S(1)} %bitcast.79), channel_id=1, source_target_pairs={{0,1},{1,2},{2,3},{3,0},{4,5},{5,6},{6,7},{7,4},{8,9},{9,10},{10,1... | collective-permute-start | bytes 589832 | tf_op jit(solution)/shard_map/ppermute | solution.py:96
  159.4 14.6 %collective-permute-start.58 = (bf16[8,4,24,128]{3,2,1,0:T(8,128)(2,1)S(1)}, bf16[8,4,24,128]{3,2,1,0:T(8,128)(2,1)S(1)}, u32[]{:S(2)}, u32[]{:S(2)}) collective-permute-start(bf16[8,4,24,128]{3,2,1,0:T(8,128)(2,1)S(1)} %convert_element_type.134), channel_id=1, source_target_pairs={{4,0},{8,4},{12,8},{16,12},{20,16},{24,20},{28,24},{5,1},{9,5},{13... | collective-permute-start | bytes 589832 | tf_op jit(solution)/shard_map/ppermute | solution.py:22
  160.7 15.9 %collective-permute-start.57 = (bf16[8,4,24,128]{3,2,1,0:T(8,128)(2,1)S(1)}, bf16[8,4,24,128]{3,2,1,0:T(8,128)(2,1)S(1)}, u32[]{:S(2)}, u32[]{:S(2)}) collective-permute-start(bf16[8,4,24,128]{3,2,1,0:T(8,128)(2,1)S(1)} %convert_element_type.134), channel_id=1, source_target_pairs={{0,4},{4,8},{8,12},{12,16},{16,20},{20,24},{24,28},{1,5},{5,9},{9,... | collective-permute-start | bytes 589832 | tf_op jit(solution)/shard_map/ppermute | solution.py:21
  165.8 13.9 %collective-permute-start.21 = (bf16[8,4,24,128]{3,2,1,0:T(8,128)(2,1)S(1)}, bf16[8,4,24,128]{3,2,1,0:T(8,128)(2,1)S(1)}, u32[]{:S(2)}, u32[]{:S(2)}) collective-permute-start(bf16[8,4,24,128]{3,2,1,0:T(8,128)(2,1)S(1)} %convert_element_type.117), channel_id=1, source_target_pairs={{4,0},{8,4},{12,8},{16,12},{20,16},{24,20},{28,24},{5,1},{9,5},{13... | collective-permute-start | bytes 589832 | tf_op jit(solution)/shard_map/ppermute | solution.py:22
  167.1 12.6 %collective-permute-start.20 = (bf16[8,4,24,128]{3,2,1,0:T(8,128)(2,1)S(1)}, bf16[8,4,24,128]{3,2,1,0:T(8,128)(2,1)S(1)}, u32[]{:S(2)}, u32[]{:S(2)}) collective-permute-start(bf16[8,4,24,128]{3,2,1,0:T(8,128)(2,1)S(1)} %convert_element_type.117), channel_id=1, source_target_pairs={{0,4},{4,8},{8,12},{12,16},{16,20},{20,24},{24,28},{1,5},{5,9},{9,... | collective-permute-start | bytes 589832 | tf_op jit(solution)/shard_map/ppermute | solution.py:21
  174.0 4.7 %collective-permute-start.63 = (f32[256,32]{0,1:T(8,128)S(1)}, f32[256,32]{0,1:T(8,128)S(1)}, u32[]{:S(2)}, u32[]{:S(2)}) collective-permute-start(f32[256,32]{0,1:T(8,128)S(1)} %add.686), channel_id=1, source_target_pairs={{0,8},{4,12},{8,0},{12,4},{16,24},{20,28},{24,16},{28,20},{1,9},{5... | collective-permute-start | bytes 98312 | tf_op jit(solution)/shard_map/ppermute | solution.py:33
  176.8 4.0 %collective-permute-start.26 = (f32[256,32]{0,1:T(8,128)S(1)}, f32[256,32]{0,1:T(8,128)S(1)}, u32[]{:S(2)}, u32[]{:S(2)}) collective-permute-start(f32[256,32]{0,1:T(8,128)S(1)} %add.602), channel_id=1, source_target_pairs={{0,8},{4,12},{8,0},{12,4},{16,24},{20,28},{24,16},{28,20},{1,9},{5... | collective-permute-start | bytes 98312 | tf_op jit(solution)/shard_map/ppermute | solution.py:33
  178.7 4.1 %collective-permute-start.64 = (f32[256,32]{0,1:T(8,128)S(1)}, f32[256,32]{0,1:T(8,128)S(1)}, u32[]{:S(2)}, u32[]{:S(2)}) collective-permute-start(f32[256,32]{0,1:T(8,128)S(1)} %add.687), channel_id=1, source_target_pairs={{0,16},{4,20},{8,24},{12,28},{16,0},{20,4},{24,8},{28,12},{1,17},{... | collective-permute-start | bytes 98312 | tf_op jit(solution)/shard_map/ppermute | solution.py:33
  180.8 7.3 %collective-permute-start.27 = (f32[256,32]{0,1:T(8,128)S(1)}, f32[256,32]{0,1:T(8,128)S(1)}, u32[]{:S(2)}, u32[]{:S(2)}) collective-permute-start(f32[256,32]{0,1:T(8,128)S(1)} %add.603), channel_id=1, source_target_pairs={{0,16},{4,20},{8,24},{12,28},{16,0},{20,4},{24,8},{28,12},{1,17},{... | collective-permute-start | bytes 98312 | tf_op jit(solution)/shard_map/ppermute | solution.py:33
  184.9 12.2 %collective-permute-start.70 = (bf16[8,12288]{1,0:T(8,128)(2,1)S(1)}, bf16[8,12288]{1,0:T(8,128)(2,1)S(1)}, u32[]{:S(2)}, u32[]{:S(2)}) collective-permute-start(bf16[8,12288]{1,0:T(8,128)(2,1)S(1)} %get-tuple-element.50), channel_id=1, source_target_pairs={{3,0},{0,1},{1,2},{2,3},{7,4},{4,5},{5,6},{6,7},{11,8},{8,9},{9,10... | collective-permute-start | bytes 589832 | tf_op jit(solution)/shard_map/ppermute | solution.py:112
  185.2 26.4 %collective-permute-start.69 = (bf16[8,12288]{1,0:T(8,128)(2,1)S(1)}, bf16[8,12288]{1,0:T(8,128)(2,1)S(1)}, u32[]{:S(2)}, u32[]{:S(2)}) collective-permute-start(bf16[8,12288]{1,0:T(8,128)(2,1)S(1)} %get-tuple-element.51), channel_id=1, source_target_pairs={{2,0},{3,1},{0,2},{1,3},{6,4},{7,5},{4,6},{5,7},{10,8},{11,9},{8,1... | collective-permute-start | bytes 589832 | tf_op jit(solution)/shard_map/ppermute | solution.py:112
  186.4 25.2 %collective-permute-start.68 = (bf16[8,12288]{1,0:T(8,128)(2,1)S(1)}, bf16[8,12288]{1,0:T(8,128)(2,1)S(1)}, u32[]{:S(2)}, u32[]{:S(2)}) collective-permute-start(bf16[8,12288]{1,0:T(8,128)(2,1)S(1)} %get-tuple-element.49), channel_id=1, source_target_pairs={{1,0},{2,1},{3,2},{0,3},{5,4},{6,5},{7,6},{4,7},{9,8},{10,9},{11,1... | collective-permute-start | bytes 589832 | tf_op jit(solution)/shard_map/ppermute | solution.py:112
  190.2 25.5 %collective-permute-start.33 = (bf16[8,12288]{1,0:T(8,128)(2,1)S(1)}, bf16[8,12288]{1,0:T(8,128)(2,1)S(1)}, u32[]{:S(2)}, u32[]{:S(2)}) collective-permute-start(bf16[8,12288]{1,0:T(8,128)(2,1)S(1)} %get-tuple-element.41), channel_id=1, source_target_pairs={{3,0},{0,1},{1,2},{2,3},{7,4},{4,5},{5,6},{6,7},{11,8},{8,9},{9,10... | collective-permute-start | bytes 589832 | tf_op jit(solution)/shard_map/ppermute | solution.py:112
  190.8 27.0 %collective-permute-start.32 = (bf16[8,12288]{1,0:T(8,128)(2,1)S(1)}, bf16[8,12288]{1,0:T(8,128)(2,1)S(1)}, u32[]{:S(2)}, u32[]{:S(2)}) collective-permute-start(bf16[8,12288]{1,0:T(8,128)(2,1)S(1)} %get-tuple-element.42), channel_id=1, source_target_pairs={{2,0},{3,1},{0,2},{1,3},{6,4},{7,5},{4,6},{5,7},{10,8},{11,9},{8,1... | collective-permute-start | bytes 589832 | tf_op jit(solution)/shard_map/ppermute | solution.py:112
  197.1 22.1 %collective-permute-start.31 = (bf16[8,12288]{1,0:T(8,128)(2,1)S(1)}, bf16[8,12288]{1,0:T(8,128)(2,1)S(1)}, u32[]{:S(2)}, u32[]{:S(2)}) collective-permute-start(bf16[8,12288]{1,0:T(8,128)(2,1)S(1)} %get-tuple-element.40), channel_id=1, source_target_pairs={{1,0},{2,1},{3,2},{0,3},{5,4},{6,5},{7,6},{4,7},{9,8},{10,9},{11,1... | collective-permute-start | bytes 589832 | tf_op jit(solution)/shard_map/ppermute | solution.py:112
  212.9 7.7 %collective-permute-start.71 = (f32[8]{0:T(128)S(1)}, f32[8]{0:T(128)S(1)}, u32[]{:S(2)}, u32[]{:S(2)}) collective-permute-start(f32[8]{0:T(128)S(1)} %get-tuple-element.30), channel_id=1, source_target_pairs={{0,4},{4,0},{8,12},{12,8},{16,20},{20,16},{24,28},{28,24},{1,5},{5... | collective-permute-start | bytes 104 | tf_op jit(solution)/shard_map/ppermute | solution.py:33
  (31 other events, 184.1 us)

commit v8 on v6

--- a/solution.py
+++ b/solution.py
@@ -68,7 +68,7 @@
     return vector[:, None, None, None]
 
 
-def chain(occupied, potential, shifts, source_term):
+def chain(occupied, potential, shifts, source_term, after):
     local_bands, width_x, width_y, width_z = source_term.shape
     local_occupied = occupied.shape[0]
     band_count = lax.axis_size("band")
@@ -81,6 +81,7 @@
     residual = source_term
     direction = source_term
     norm_now = grid_sum(inner_product(source_term, source_term), "grid")
+    arrivals = []
     for iteration in range(ITERS):
         own_potential, direction = lax.optimization_barrier((potential, direction))
         potential_shift = own_potential[None] + shifts[:, None, None, None]
@@ -89,12 +90,15 @@
         )
         padded = jnp.pad(padded, ((0, 0), (0, 0), (4, 4), (4, 4)))
         kinetic = -0.5 * second_sum(padded, width_x, width_y, width_z)
+        if after is not None:
+            direction, _ = lax.optimization_barrier((direction, after[iteration]))
         rounded = direction.astype(jnp.bfloat16).reshape(local_bands, local_cells)
         blocks = [rounded] + [
             lax.ppermute(rounded, "band", [(i, (i + d) % band_count) for i in range(band_count)])
             for d in range(1, band_count)
         ]
         gathered = jnp.concatenate(blocks, axis=0)
+        arrivals.append(gathered)
         partial_margin = lax.dot_general(
             occupied_rows, gathered, (((1,), (1,)), ((), ())), preferred_element_type=jnp.float32
         )
@@ -117,16 +121,24 @@
             norm_next = grid_sum(inner_product(residual, residual), "grid")
             direction = residual + expand(norm_next / norm_now) * direction
             norm_now = norm_next
-    return (solution, residual)
+    return (solution, residual, arrivals)
 
 
 def body(occupied, potential, shifts, source_term):
     pieces = 2 if source_term.shape[0] % 2 == 0 else 1
     width = source_term.shape[0] // pieces
-    results = [
-        chain(occupied, potential, shifts[k * width : (k + 1) * width], source_term[k * width : (k + 1) * width])
-        for k in range(pieces)
-    ]
+    results = []
+    after = None
+    for k in range(pieces):
+        result = chain(
+            occupied,
+            potential,
+            shifts[k * width : (k + 1) * width],
+            source_term[k * width : (k + 1) * width],
+            after,
+        )
+        after = result[2]
+        results.append(result)
     return tuple(jnp.concatenate([r[i] for r in results], axis=0) for i in range(2))
 
 

time: 212 us -> 224 us (1.057)
  waiting for transfers between devices: 85.4 us -> 115 us
  starting transfers between devices: 96 us -> 78.1 us
    ppermute x12, waiting for transfers between devices: 17.9 us -> 39.1 us  [chain(): lax.ppermute(rounded, 'band', [(i, (i + d) % band_count) for i in range(b...]
    ppermute x36, waiting for transfers between devices: 23 us -> 38.8 us  [grid_sum(): value = value + lax.ppermute(value, axis, pairs)]
    ppermute x12, starting transfers between devices: 26.3 us -> 17.7 us  [chain(): lax.ppermute(rounded, 'band', [(i, (i + d) % band_count) for i in range(b...]
    ppermute x12, waiting for transfers between devices: 44.5 us -> 37.3 us  [chain(): lax.ppermute(part, 'band', [((i + d) % band_count, i) for i in range(band...]
    ppermute x12, starting transfers between devices: 19.3 us -> 15.5 us  [chain(): lax.ppermute(part, 'band', [((i + d) % band_count, i) for i in range(band...]
    ppermute x36, starting transfers between devices: 33.2 us -> 29.3 us  [grid_sum(): value = value + lax.ppermute(value, axis, pairs)]
  transfers between devices with their start and end apart: 68 -> 68, of which waited for: 36 -> 38; matrix products, arithmetic and copies ran while one was open for 12% -> 9% of each run, Pallas kernels for 0% -> 0%
where the time goes in v8:
time: 224 us
  waiting for transfers between devices  115 us (51%)
  starting transfers between devices  78.1 us (35%)
  matrix products  19.1 us (9%)
  other arithmetic  9.75 us (4%)
    ppermute x12, waiting for transfers between devices, chain(): lax.ppermute(rounded, 'band', [(i, (i + d) % band_count) for i in range(b...  39.1 us
    ppermute x36, waiting for transfers between devices, grid_sum(): value = value + lax.ppermute(value, axis, pairs)  38.8 us
    ppermute x12, waiting for transfers between devices, chain(): lax.ppermute(part, 'band', [((i + d) % band_count, i) for i in range(band...  37.3 us
    ppermute x36, starting transfers between devices, grid_sum(): value = value + lax.ppermute(value, axis, pairs)  29.3 us
    ppermute x12, starting transfers between devices, chain(): lax.ppermute(rounded, 'band', [(i, (i + d) % band_count) for i in range(b...  17.7 us
    ppermute x12, starting transfers between devices, chain(): lax.ppermute(part, 'band', [((i + d) % band_count, i) for i in range(band...  15.5 us
    dot_general x4, matrix products, chain(): lax.dot_general(occupied_rows, gathered, (((1,), (1,)), ((), ())), prefer...  11 us
    ppermute x4, starting transfers between devices, with_halo(): before = lax.ppermute(last, axis, up)  10.4 us
  transfers between devices with their start and end apart: 68, of which 38 were waited for; matrix products, arithmetic and copies ran while one was open for 9% of the time, Pallas kernels for 0%

profile of v8, /device:TPU:8, one launch (start us, length us, event | category | flops | bytes accessed | tf_op | source)
XLA Modules:
  0.0 224.2 jit_solution(3479885194320797520)
XLA Ops:
  4.8 1.9 collective-permute-start.7
  6.8 10.6 %collective-permute-done.5 = bf16[8,12288]{1,0:T(8,128)(2,1)S(1)} collective-permute-done((bf16[8,12288]{1,0:T(8,128)(2,1)S(1)}, bf16[8,12288]{1,0:T(8,128)(2,1)S(1)}, u32[]{:S(2)}, u32[]{:S(2)}) %collective-permute-start.5) | collective-permute-done | bytes 196640 | tf_op jit(solution)/shard_map/ppermute | solution.py:97
  17.4 3.0 %collective-permute-done.6 = bf16[8,12288]{1,0:T(8,128)(2,1)S(1)} collective-permute-done((bf16[8,12288]{1,0:T(8,128)(2,1)S(1)}, bf16[8,12288]{1,0:T(8,128)(2,1)S(1)}, u32[]{:S(2)}, u32[]{:S(2)}) %collective-permute-start.6) | collective-permute-done | bytes 196640 | tf_op jit(solution)/shard_map/ppermute | solution.py:97
  20.5 1.8 collective-permute-done.7
  22.3 5.0 %fusion.12 = f32[256,32]{0,1:T(8,128)S(1)} fusion(bf16[32,12288]{1,0:T(8,128)(2,1)S(1)} %constant_dynamic-update-slice_fusion, bf16[32,8,96,128]{3,2,1,0:T(8,128)(2,1)} %bitcast.65), kind=kOutput, calls=%fused_computation.80 | convolution fusion | flops 201326592 | bytes 7110656 | tf_op jit(solution)/shard_map/dot_general | solution.py:102
  31.3 3.0 %collective-permute-start.3 = (bf16[8,4,24,128]{3,2,1,0:T(8,128)(2,1)S(1)}, bf16[8,4,24,128]{3,2,1,0:T(8,128)(2,1)S(1)}, u32[]{:S(2)}, u32[]{:S(2)}) collective-permute-start(bf16[8,4,24,128]{3,2,1,0:T(8,128)(2,1)S(1)} %convert_element_type.109), channel_id=1, source_target_pairs={{0,4},{4,8},{8,12},{12,16},{16,20},{20,24},{24,28},{1,5},{5,9},{9,... | collective-permute-start | bytes 589832 | tf_op jit(solution)/shard_map/ppermute | solution.py:21
  41.6 1.7 collective-permute-start.40
  43.3 2.8 %collective-permute-start.39 = (bf16[8,12288]{1,0:T(8,128)(2,1)S(1)}, bf16[8,12288]{1,0:T(8,128)(2,1)S(1)}, u32[]{:S(2)}, u32[]{:S(2)}) collective-permute-start(bf16[8,12288]{1,0:T(8,128)(2,1)S(1)} %bitcast.94), channel_id=1, source_target_pairs={{0,1},{1,2},{2,3},{3,0},{4,5},{5,6},{6,7},{7,4},{8,9},{9,10},{10,1... | collective-permute-start | bytes 589832 | tf_op jit(solution)/shard_map/ppermute | solution.py:97
  46.2 2.0 convolution_convert_fusion.3
  48.2 9.4 %collective-permute-done.41 = bf16[8,12288]{1,0:T(8,128)(2,1)S(1)} collective-permute-done((bf16[8,12288]{1,0:T(8,128)(2,1)S(1)}, bf16[8,12288]{1,0:T(8,128)(2,1)S(1)}, u32[]{:S(2)}, u32[]{:S(2)}) %collective-permute-start.41) | collective-permute-done | bytes 196640 | tf_op jit(solution)/shard_map/ppermute | solution.py:97
  58.9 3.0 %collective-permute-start.37 = (bf16[8,4,24,128]{3,2,1,0:T(8,128)(2,1)S(1)}, bf16[8,4,24,128]{3,2,1,0:T(8,128)(2,1)S(1)}, u32[]{:S(2)}, u32[]{:S(2)}) collective-permute-start(bf16[8,4,24,128]{3,2,1,0:T(8,128)(2,1)S(1)} %convert_element_type.125), channel_id=1, source_target_pairs={{0,4},{4,8},{8,12},{12,16},{16,20},{20,24},{24,28},{1,5},{5,9},{9,... | collective-permute-start | bytes 589832 | tf_op jit(solution)/shard_map/ppermute | solution.py:21
  62.0 2.0 fusion.18
  65.4 4.0 %collective-permute-start.12 = (bf16[8,12288]{1,0:T(8,128)(2,1)S(1)}, bf16[8,12288]{1,0:T(8,128)(2,1)S(1)}, u32[]{:S(2)}, u32[]{:S(2)}) collective-permute-start(bf16[8,12288]{1,0:T(8,128)(2,1)S(1)} %get-tuple-element.54), channel_id=1, source_target_pairs={{2,0},{3,1},{0,2},{1,3},{6,4},{7,5},{4,6},{5,7},{10,8},{11,9},{8,1... | collective-permute-start | bytes 589832 | tf_op jit(solution)/shard_map/ppermute | solution.py:113
  71.4 2.7 %collective-permute-done.43 = f32[256,32]{0,1:T(8,128)S(1)} collective-permute-done((f32[256,32]{0,1:T(8,128)S(1)}, f32[256,32]{0,1:T(8,128)S(1)}, u32[]{:S(2)}, u32[]{:S(2)}) %collective-permute-start.43) | collective-permute-done | bytes 32800 | tf_op jit(solution)/shard_map/ppermute | solution.py:33
  75.6 7.1 %collective-permute-done.12 = bf16[8,12288]{1,0:T(8,128)(2,1)S(1)} collective-permute-done((bf16[8,12288]{1,0:T(8,128)(2,1)S(1)}, bf16[8,12288]{1,0:T(8,128)(2,1)S(1)}, u32[]{:S(2)}, u32[]{:S(2)}) %collective-permute-start.12) | collective-permute-done | bytes 196640 | tf_op jit(solution)/shard_map/ppermute | solution.py:113
  82.7 3.4 %collective-permute-done.11 = bf16[8,12288]{1,0:T(8,128)(2,1)S(1)} collective-permute-done((bf16[8,12288]{1,0:T(8,128)(2,1)S(1)}, bf16[8,12288]{1,0:T(8,128)(2,1)S(1)}, u32[]{:S(2)}, u32[]{:S(2)}) %collective-permute-start.11) | collective-permute-done | bytes 196640 | tf_op jit(solution)/shard_map/ppermute | solution.py:113
  86.2 2.0 convolution_convert_fusion.1
  94.4 1.9 collective-permute-done.15
  98.3 6.5 %collective-permute-done.46 = bf16[8,12288]{1,0:T(8,128)(2,1)S(1)} collective-permute-done((bf16[8,12288]{1,0:T(8,128)(2,1)S(1)}, bf16[8,12288]{1,0:T(8,128)(2,1)S(1)}, u32[]{:S(2)}, u32[]{:S(2)}) %collective-permute-start.46) | collective-permute-done | bytes 196640 | tf_op jit(solution)/shard_map/ppermute | solution.py:113
  109.5 2.0 collective-permute-done.49
  112.8 2.2 collective-permute-done.50
  122.1 3.1 %collective-permute-done.19 = f32[8]{0:T(128)S(1)} collective-permute-done((f32[8]{0:T(128)S(1)}, f32[8]{0:T(128)S(1)}, u32[]{:S(2)}, u32[]{:S(2)}) %collective-permute-start.19) | collective-permute-done | bytes 64 | tf_op jit(solution)/shard_map/ppermute | solution.py:33
  125.6 2.8 %collective-permute-start.23 = (bf16[8,12288]{1,0:T(8,128)(2,1)S(1)}, bf16[8,12288]{1,0:T(8,128)(2,1)S(1)}, u32[]{:S(2)}, u32[]{:S(2)}) collective-permute-start(bf16[8,12288]{1,0:T(8,128)(2,1)S(1)} %bitcast.90), channel_id=1, source_target_pairs={{0,2},{1,3},{2,0},{3,1},{4,6},{5,7},{6,4},{7,5},{8,10},{9,11},{10,... | collective-permute-start | bytes 589832 | tf_op jit(solution)/shard_map/ppermute | solution.py:97
  128.4 1.9 collective-permute-start.24
  131.8 3.0 %collective-permute-start.54 = (bf16[8,4,24,128]{3,2,1,0:T(8,128)(2,1)S(1)}, bf16[8,4,24,128]{3,2,1,0:T(8,128)(2,1)S(1)}, u32[]{:S(2)}, u32[]{:S(2)}) collective-permute-start(bf16[8,4,24,128]{3,2,1,0:T(8,128)(2,1)S(1)} %convert_element_type.134), channel_id=1, source_target_pairs={{0,4},{4,8},{8,12},{12,16},{16,20},{20,24},{24,28},{1,5},{5,9},{9,... | collective-permute-start | bytes 589832 | tf_op jit(solution)/shard_map/ppermute | solution.py:21
  134.9 3.9 %collective-permute-done.22 = bf16[8,12288]{1,0:T(8,128)(2,1)S(1)} collective-permute-done((bf16[8,12288]{1,0:T(8,128)(2,1)S(1)}, bf16[8,12288]{1,0:T(8,128)(2,1)S(1)}, u32[]{:S(2)}, u32[]{:S(2)}) %collective-permute-start.22) | collective-permute-done | bytes 196640 | tf_op jit(solution)/shard_map/ppermute | solution.py:97
  138.8 2.1 collective-permute-done.23
  140.9 2.8 %collective-permute-done.24 = bf16[8,12288]{1,0:T(8,128)(2,1)S(1)} collective-permute-done((bf16[8,12288]{1,0:T(8,128)(2,1)S(1)}, bf16[8,12288]{1,0:T(8,128)(2,1)S(1)}, u32[]{:S(2)}, u32[]{:S(2)}) %collective-permute-start.24) | collective-permute-done | bytes 196640 | tf_op jit(solution)/shard_map/ppermute | solution.py:97
  143.7 2.0 fusion.15
  146.9 2.5 %collective-permute-start.56 = (bf16[8,12288]{1,0:T(8,128)(2,1)S(1)}, bf16[8,12288]{1,0:T(8,128)(2,1)S(1)}, u32[]{:S(2)}, u32[]{:S(2)}) collective-permute-start(bf16[8,12288]{1,0:T(8,128)(2,1)S(1)} %bitcast.87), channel_id=1, source_target_pairs={{0,1},{1,2},{2,3},{3,0},{4,5},{5,6},{6,7},{7,4},{8,9},{9,10},{10,1... | collective-permute-start | bytes 589832 | tf_op jit(solution)/shard_map/ppermute | solution.py:97
  150.8 2.0 collective-permute-start.26
  152.8 4.2 %collective-permute-done.26 = f32[256,32]{0,1:T(8,128)S(1)} collective-permute-done((f32[256,32]{0,1:T(8,128)S(1)}, f32[256,32]{0,1:T(8,128)S(1)}, u32[]{:S(2)}, u32[]{:S(2)}) %collective-permute-start.26) | collective-permute-done | bytes 32800 | tf_op jit(solution)/shard_map/ppermute | solution.py:33
  158.3 3.7 %collective-permute-done.58 = bf16[8,12288]{1,0:T(8,128)(2,1)S(1)} collective-permute-done((bf16[8,12288]{1,0:T(8,128)(2,1)S(1)}, bf16[8,12288]{1,0:T(8,128)(2,1)S(1)}, u32[]{:S(2)}, u32[]{:S(2)}) %collective-permute-start.58) | collective-permute-done | bytes 196640 | tf_op jit(solution)/shard_map/ppermute | solution.py:97
  162.4 1.7 collective-permute-done.56
  164.1 2.0 fusion.21
  168.0 2.0 convolution_convert_fusion.2
  171.9 2.5 %collective-permute-start.30 = (bf16[8,12288]{1,0:T(8,128)(2,1)S(1)}, bf16[8,12288]{1,0:T(8,128)(2,1)S(1)}, u32[]{:S(2)}, u32[]{:S(2)}) collective-permute-start(bf16[8,12288]{1,0:T(8,128)(2,1)S(1)} %get-tuple-element.45), channel_id=1, source_target_pairs={{3,0},{0,1},{1,2},{2,3},{7,4},{4,5},{5,6},{6,7},{11,8},{8,9},{9,10... | collective-permute-start | bytes 589832 | tf_op jit(solution)/shard_map/ppermute | solution.py:113
  174.4 2.9 %collective-permute-start.29 = (bf16[8,12288]{1,0:T(8,128)(2,1)S(1)}, bf16[8,12288]{1,0:T(8,128)(2,1)S(1)}, u32[]{:S(2)}, u32[]{:S(2)}) collective-permute-start(bf16[8,12288]{1,0:T(8,128)(2,1)S(1)} %get-tuple-element.46), channel_id=1, source_target_pairs={{2,0},{3,1},{0,2},{1,3},{6,4},{7,5},{4,6},{5,7},{10,8},{11,9},{8,1... | collective-permute-start | bytes 589832 | tf_op jit(solution)/shard_map/ppermute | solution.py:113
  177.3 2.0 convolution_convert_fusion
  179.4 2.1 collective-permute-start.64
  181.5 1.8 collective-permute-start.63
  183.3 3.9 %collective-permute-done.30 = bf16[8,12288]{1,0:T(8,128)(2,1)S(1)} collective-permute-done((bf16[8,12288]{1,0:T(8,128)(2,1)S(1)}, bf16[8,12288]{1,0:T(8,128)(2,1)S(1)}, u32[]{:S(2)}, u32[]{:S(2)}) %collective-permute-start.30) | collective-permute-done | bytes 196640 | tf_op jit(solution)/shard_map/ppermute | solution.py:113
  187.1 13.4 %collective-permute-done.29 = bf16[8,12288]{1,0:T(8,128)(2,1)S(1)} collective-permute-done((bf16[8,12288]{1,0:T(8,128)(2,1)S(1)}, bf16[8,12288]{1,0:T(8,128)(2,1)S(1)}, u32[]{:S(2)}, u32[]{:S(2)}) %collective-permute-start.29) | collective-permute-done | bytes 196640 | tf_op jit(solution)/shard_map/ppermute | solution.py:113
  200.6 2.3 %collective-permute-done.28 = bf16[8,12288]{1,0:T(8,128)(2,1)S(1)} collective-permute-done((bf16[8,12288]{1,0:T(8,128)(2,1)S(1)}, bf16[8,12288]{1,0:T(8,128)(2,1)S(1)}, u32[]{:S(2)}, u32[]{:S(2)}) %collective-permute-start.28) | collective-permute-done | bytes 196640 | tf_op jit(solution)/shard_map/ppermute | solution.py:113
  206.2 2.6 %collective-permute-done.32 = f32[8]{0:T(128)S(1)} collective-permute-done((f32[8]{0:T(128)S(1)}, f32[8]{0:T(128)S(1)}, u32[]{:S(2)}, u32[]{:S(2)}) %collective-permute-start.32) | collective-permute-done | bytes 64 | tf_op jit(solution)/shard_map/ppermute | solution.py:33
  209.8 2.6 %collective-permute-done.33 = f32[8]{0:T(128)S(1)} collective-permute-done((f32[8]{0:T(128)S(1)}, f32[8]{0:T(128)S(1)}, u32[]{:S(2)}, u32[]{:S(2)}) %collective-permute-start.33) | collective-permute-done | bytes 64 | tf_op jit(solution)/shard_map/ppermute | solution.py:33
  216.0 2.6 %collective-permute-done.66 = f32[8]{0:T(128)S(1)} collective-permute-done((f32[8]{0:T(128)S(1)}, f32[8]{0:T(128)S(1)}, u32[]{:S(2)}, u32[]{:S(2)}) %collective-permute-start.66) | collective-permute-done | bytes 64 | tf_op jit(solution)/shard_map/ppermute | solution.py:33
  219.5 2.6 %collective-permute-done.67 = f32[8]{0:T(128)S(1)} collective-permute-done((f32[8]{0:T(128)S(1)}, f32[8]{0:T(128)S(1)}, u32[]{:S(2)}, u32[]{:S(2)}) %collective-permute-start.67) | collective-permute-done | bytes 64 | tf_op jit(solution)/shard_map/ppermute | solution.py:33
  (179 shorter events, 63.5 us)
Async XLA Ops:
  2.1 15.4 %collective-permute-start.5 = (bf16[8,12288]{1,0:T(8,128)(2,1)S(1)}, bf16[8,12288]{1,0:T(8,128)(2,1)S(1)}, u32[]{:S(2)}, u32[]{:S(2)}) collective-permute-start(bf16[8,12288]{1,0:T(8,128)(2,1)S(1)} %bitcast.96), channel_id=1, source_target_pairs={{0,1},{1,2},{2,3},{3,0},{4,5},{5,6},{6,7},{7,4},{8,9},{9,10},{10,1... | collective-permute-start | bytes 589832 | tf_op jit(solution)/shard_map/ppermute | solution.py:97
  3.7 16.8 %collective-permute-start.6 = (bf16[8,12288]{1,0:T(8,128)(2,1)S(1)}, bf16[8,12288]{1,0:T(8,128)(2,1)S(1)}, u32[]{:S(2)}, u32[]{:S(2)}) collective-permute-start(bf16[8,12288]{1,0:T(8,128)(2,1)S(1)} %bitcast.97), channel_id=1, source_target_pairs={{0,2},{1,3},{2,0},{3,1},{4,6},{5,7},{6,4},{7,5},{8,10},{9,11},{10,... | collective-permute-start | bytes 589832 | tf_op jit(solution)/shard_map/ppermute | solution.py:97
  4.8 17.5 %collective-permute-start.7 = (bf16[8,12288]{1,0:T(8,128)(2,1)S(1)}, bf16[8,12288]{1,0:T(8,128)(2,1)S(1)}, u32[]{:S(2)}, u32[]{:S(2)}) collective-permute-start(bf16[8,12288]{1,0:T(8,128)(2,1)S(1)} %bitcast.98), channel_id=1, source_target_pairs={{0,3},{1,0},{2,1},{3,2},{4,7},{5,4},{6,5},{7,6},{8,11},{9,8},{10,9... | collective-permute-start | bytes 589832 | tf_op jit(solution)/shard_map/ppermute | solution.py:97
  28.6 7.1 %collective-permute-start.9 = (f32[256,32]{0,1:T(8,128)S(1)}, f32[256,32]{0,1:T(8,128)S(1)}, u32[]{:S(2)}, u32[]{:S(2)}) collective-permute-start(f32[256,32]{0,1:T(8,128)S(1)} %add.555), channel_id=1, source_target_pairs={{0,8},{4,12},{8,0},{12,4},{16,24},{20,28},{24,16},{28,20},{1,9},{5... | collective-permute-start | bytes 98312 | tf_op jit(solution)/shard_map/ppermute | solution.py:33
  30.0 35.3 %collective-permute-start.4 = (bf16[8,4,24,128]{3,2,1,0:T(8,128)(2,1)S(1)}, bf16[8,4,24,128]{3,2,1,0:T(8,128)(2,1)S(1)}, u32[]{:S(2)}, u32[]{:S(2)}) collective-permute-start(bf16[8,4,24,128]{3,2,1,0:T(8,128)(2,1)S(1)} %convert_element_type.109), channel_id=1, source_target_pairs={{4,0},{8,4},{12,8},{16,12},{20,16},{24,20},{28,24},{5,1},{9,5},{13... | collective-permute-start | bytes 589832 | tf_op jit(solution)/shard_map/ppermute | solution.py:22
  31.3 34.1 %collective-permute-start.3 = (bf16[8,4,24,128]{3,2,1,0:T(8,128)(2,1)S(1)}, bf16[8,4,24,128]{3,2,1,0:T(8,128)(2,1)S(1)}, u32[]{:S(2)}, u32[]{:S(2)}) collective-permute-start(bf16[8,4,24,128]{3,2,1,0:T(8,128)(2,1)S(1)} %convert_element_type.109), channel_id=1, source_target_pairs={{0,4},{4,8},{8,12},{12,16},{16,20},{20,24},{24,28},{1,5},{5,9},{9,... | collective-permute-start | bytes 589832 | tf_op jit(solution)/shard_map/ppermute | solution.py:21
  35.6 7.7 %collective-permute-start.10 = (f32[256,32]{0,1:T(8,128)S(1)}, f32[256,32]{0,1:T(8,128)S(1)}, u32[]{:S(2)}, u32[]{:S(2)}) collective-permute-start(f32[256,32]{0,1:T(8,128)S(1)} %add.556), channel_id=1, source_target_pairs={{0,16},{4,20},{8,24},{12,28},{16,0},{20,4},{24,8},{28,12},{1,17},{... | collective-permute-start | bytes 98312 | tf_op jit(solution)/shard_map/ppermute | solution.py:33
  37.3 3.6 %collective-permute-start.35 = (f32[8]{0:T(128)S(1)}, f32[8]{0:T(128)S(1)}, u32[]{:S(2)}, u32[]{:S(2)}) collective-permute-start(f32[8]{0:T(128)S(1)} %add.607), channel_id=1, source_target_pairs={{0,8},{4,12},{8,0},{12,4},{16,24},{20,28},{24,16},{28,20},{1,9},{5... | collective-permute-start | bytes 104 | tf_op jit(solution)/shard_map/ppermute | solution.py:33
  37.9 3.5 %collective-permute-start.1 = (f32[8]{0:T(128)S(1)}, f32[8]{0:T(128)S(1)}, u32[]{:S(2)}, u32[]{:S(2)}) collective-permute-start(f32[8]{0:T(128)S(1)} %add.524), channel_id=1, source_target_pairs={{0,8},{4,12},{8,0},{12,4},{16,24},{20,28},{24,16},{28,20},{1,9},{5... | collective-permute-start | bytes 104 | tf_op jit(solution)/shard_map/ppermute | solution.py:33
  41.5 16.1 %collective-permute-start.41 = (bf16[8,12288]{1,0:T(8,128)(2,1)S(1)}, bf16[8,12288]{1,0:T(8,128)(2,1)S(1)}, u32[]{:S(2)}, u32[]{:S(2)}) collective-permute-start(bf16[8,12288]{1,0:T(8,128)(2,1)S(1)} %bitcast.92), channel_id=1, source_target_pairs={{0,3},{1,0},{2,1},{3,2},{4,7},{5,4},{6,5},{7,6},{8,11},{9,8},{10,9... | collective-permute-start | bytes 589832 | tf_op jit(solution)/shard_map/ppermute | solution.py:97
  41.6 17.3 %collective-permute-start.40 = (bf16[8,12288]{1,0:T(8,128)(2,1)S(1)}, bf16[8,12288]{1,0:T(8,128)(2,1)S(1)}, u32[]{:S(2)}, u32[]{:S(2)}) collective-permute-start(bf16[8,12288]{1,0:T(8,128)(2,1)S(1)} %bitcast.93), channel_id=1, source_target_pairs={{0,2},{1,3},{2,0},{3,1},{4,6},{5,7},{6,4},{7,5},{8,10},{9,11},{10,... | collective-permute-start | bytes 589832 | tf_op jit(solution)/shard_map/ppermute | solution.py:97
  43.3 18.7 %collective-permute-start.39 = (bf16[8,12288]{1,0:T(8,128)(2,1)S(1)}, bf16[8,12288]{1,0:T(8,128)(2,1)S(1)}, u32[]{:S(2)}, u32[]{:S(2)}) collective-permute-start(bf16[8,12288]{1,0:T(8,128)(2,1)S(1)} %bitcast.94), channel_id=1, source_target_pairs={{0,1},{1,2},{2,3},{3,0},{4,5},{5,6},{6,7},{7,4},{8,9},{9,10},{10,1... | collective-permute-start | bytes 589832 | tf_op jit(solution)/shard_map/ppermute | solution.py:97
  57.6 11.9 %collective-permute-start.38 = (bf16[8,4,24,128]{3,2,1,0:T(8,128)(2,1)S(1)}, bf16[8,4,24,128]{3,2,1,0:T(8,128)(2,1)S(1)}, u32[]{:S(2)}, u32[]{:S(2)}) collective-permute-start(bf16[8,4,24,128]{3,2,1,0:T(8,128)(2,1)S(1)} %convert_element_type.125), channel_id=1, source_target_pairs={{4,0},{8,4},{12,8},{16,12},{20,16},{24,20},{28,24},{5,1},{9,5},{13... | collective-permute-start | bytes 589832 | tf_op jit(solution)/shard_map/ppermute | solution.py:22
  58.9 11.3 %collective-permute-start.37 = (bf16[8,4,24,128]{3,2,1,0:T(8,128)(2,1)S(1)}, bf16[8,4,24,128]{3,2,1,0:T(8,128)(2,1)S(1)}, u32[]{:S(2)}, u32[]{:S(2)}) collective-permute-start(bf16[8,4,24,128]{3,2,1,0:T(8,128)(2,1)S(1)} %convert_element_type.125), channel_id=1, source_target_pairs={{0,4},{4,8},{8,12},{12,16},{16,20},{20,24},{24,28},{1,5},{5,9},{9,... | collective-permute-start | bytes 589832 | tf_op jit(solution)/shard_map/ppermute | solution.py:21
  64.0 5.4 %collective-permute-start.42 = (f32[256,32]{0,1:T(8,128)S(1)}, f32[256,32]{0,1:T(8,128)S(1)}, u32[]{:S(2)}, u32[]{:S(2)}) collective-permute-start(f32[256,32]{0,1:T(8,128)S(1)} %fusion.18), channel_id=1, source_target_pairs={{0,4},{4,0},{8,12},{12,8},{16,20},{20,16},{24,28},{28,24},{1,5},{5... | collective-permute-start | bytes 98312 | tf_op jit(solution)/shard_map/ppermute | solution.py:33
  65.3 10.2 %collective-permute-start.13 = (bf16[8,12288]{1,0:T(8,128)(2,1)S(1)}, bf16[8,12288]{1,0:T(8,128)(2,1)S(1)}, u32[]{:S(2)}, u32[]{:S(2)}) collective-permute-start(bf16[8,12288]{1,0:T(8,128)(2,1)S(1)} %get-tuple-element.53), channel_id=1, source_target_pairs={{3,0},{0,1},{1,2},{2,3},{7,4},{4,5},{5,6},{6,7},{11,8},{8,9},{9,10... | collective-permute-start | bytes 589832 | tf_op jit(solution)/shard_map/ppermute | solution.py:113
  65.4 17.2 %collective-permute-start.12 = (bf16[8,12288]{1,0:T(8,128)(2,1)S(1)}, bf16[8,12288]{1,0:T(8,128)(2,1)S(1)}, u32[]{:S(2)}, u32[]{:S(2)}) collective-permute-start(bf16[8,12288]{1,0:T(8,128)(2,1)S(1)} %get-tuple-element.54), channel_id=1, source_target_pairs={{2,0},{3,1},{0,2},{1,3},{6,4},{7,5},{4,6},{5,7},{10,8},{11,9},{8,1... | collective-permute-start | bytes 589832 | tf_op jit(solution)/shard_map/ppermute | solution.py:113
  69.4 16.7 %collective-permute-start.11 = (bf16[8,12288]{1,0:T(8,128)(2,1)S(1)}, bf16[8,12288]{1,0:T(8,128)(2,1)S(1)}, u32[]{:S(2)}, u32[]{:S(2)}) collective-permute-start(bf16[8,12288]{1,0:T(8,128)(2,1)S(1)} %get-tuple-element.52), channel_id=1, source_target_pairs={{1,0},{2,1},{3,2},{0,3},{5,4},{6,5},{7,6},{4,7},{9,8},{10,9},{11,1... | collective-permute-start | bytes 589832 | tf_op jit(solution)/shard_map/ppermute | solution.py:113
  69.5 43.3 %collective-permute-start.36 = (f32[8]{0:T(128)S(1)}, f32[8]{0:T(128)S(1)}, u32[]{:S(2)}, u32[]{:S(2)}) collective-permute-start(f32[8]{0:T(128)S(1)} %add.608), channel_id=1, source_target_pairs={{0,16},{4,20},{8,24},{12,28},{16,0},{20,4},{24,8},{28,12},{1,17},{... | collective-permute-start | bytes 104 | tf_op jit(solution)/shard_map/ppermute | solution.py:33
  70.2 3.9 %collective-permute-start.43 = (f32[256,32]{0,1:T(8,128)S(1)}, f32[256,32]{0,1:T(8,128)S(1)}, u32[]{:S(2)}, u32[]{:S(2)}) collective-permute-start(f32[256,32]{0,1:T(8,128)S(1)} %add.638), channel_id=1, source_target_pairs={{0,8},{4,12},{8,0},{12,4},{16,24},{20,28},{24,16},{28,20},{1,9},{5... | collective-permute-start | bytes 98312 | tf_op jit(solution)/shard_map/ppermute | solution.py:33
  74.1 12.1 %collective-permute-start.44 = (f32[256,32]{0,1:T(8,128)S(1)}, f32[256,32]{0,1:T(8,128)S(1)}, u32[]{:S(2)}, u32[]{:S(2)}) collective-permute-start(f32[256,32]{0,1:T(8,128)S(1)} %add.639), channel_id=1, source_target_pairs={{0,16},{4,20},{8,24},{12,28},{16,0},{20,4},{24,8},{28,12},{1,17},{... | collective-permute-start | bytes 98312 | tf_op jit(solution)/shard_map/ppermute | solution.py:33
  88.3 8.9 %collective-permute-start.47 = (bf16[8,12288]{1,0:T(8,128)(2,1)S(1)}, bf16[8,12288]{1,0:T(8,128)(2,1)S(1)}, u32[]{:S(2)}, u32[]{:S(2)}) collective-permute-start(bf16[8,12288]{1,0:T(8,128)(2,1)S(1)} %get-tuple-element.58), channel_id=1, source_target_pairs={{3,0},{0,1},{1,2},{2,3},{7,4},{4,5},{5,6},{6,7},{11,8},{8,9},{9,10... | collective-permute-start | bytes 589832 | tf_op jit(solution)/shard_map/ppermute | solution.py:113
  88.3 16.4 %collective-permute-start.46 = (bf16[8,12288]{1,0:T(8,128)(2,1)S(1)}, bf16[8,12288]{1,0:T(8,128)(2,1)S(1)}, u32[]{:S(2)}, u32[]{:S(2)}) collective-permute-start(bf16[8,12288]{1,0:T(8,128)(2,1)S(1)} %get-tuple-element.59), channel_id=1, source_target_pairs={{2,0},{3,1},{0,2},{1,3},{6,4},{7,5},{4,6},{5,7},{10,8},{11,9},{8,1... | collective-permute-start | bytes 589832 | tf_op jit(solution)/shard_map/ppermute | solution.py:113
  88.9 16.6 %collective-permute-start.45 = (bf16[8,12288]{1,0:T(8,128)(2,1)S(1)}, bf16[8,12288]{1,0:T(8,128)(2,1)S(1)}, u32[]{:S(2)}, u32[]{:S(2)}) collective-permute-start(bf16[8,12288]{1,0:T(8,128)(2,1)S(1)} %get-tuple-element.57), channel_id=1, source_target_pairs={{1,0},{2,1},{3,2},{0,3},{5,4},{6,5},{7,6},{4,7},{9,8},{10,9},{11,1... | collective-permute-start | bytes 589832 | tf_op jit(solution)/shard_map/ppermute | solution.py:113
  96.3 16.5 %collective-permute-start.2 = (f32[8]{0:T(128)S(1)}, f32[8]{0:T(128)S(1)}, u32[]{:S(2)}, u32[]{:S(2)}) collective-permute-start(f32[8]{0:T(128)S(1)} %add.525), channel_id=1, source_target_pairs={{0,16},{4,20},{8,24},{12,28},{16,0},{20,4},{24,8},{28,12},{1,17},{... | collective-permute-start | bytes 104 | tf_op jit(solution)/shard_map/ppermute | solution.py:33
  97.2 15.6 %collective-permute-start.16 = (f32[8]{0:T(128)S(1)}, f32[8]{0:T(128)S(1)}, u32[]{:S(2)}, u32[]{:S(2)}) collective-permute-start(f32[8]{0:T(128)S(1)} %add.563), channel_id=1, source_target_pairs={{0,16},{4,20},{8,24},{12,28},{16,0},{20,4},{24,8},{28,12},{1,17},{... | collective-permute-start | bytes 104 | tf_op jit(solution)/shard_map/ppermute | solution.py:33
  118.1 3.5 %collective-permute-start.18 = (f32[8]{0:T(128)S(1)}, f32[8]{0:T(128)S(1)}, u32[]{:S(2)}, u32[]{:S(2)}) collective-permute-start(f32[8]{0:T(128)S(1)} %add.565), channel_id=1, source_target_pairs={{0,8},{4,12},{8,0},{12,4},{16,24},{20,28},{24,16},{28,20},{1,9},{5... | collective-permute-start | bytes 104 | tf_op jit(solution)/shard_map/ppermute | solution.py:33
  120.1 10.3 %collective-permute-start.53 = (f32[8]{0:T(128)S(1)}, f32[8]{0:T(128)S(1)}, u32[]{:S(2)}, u32[]{:S(2)}) collective-permute-start(f32[8]{0:T(128)S(1)} %add.649), channel_id=1, source_target_pairs={{0,16},{4,20},{8,24},{12,28},{16,0},{20,4},{24,8},{28,12},{1,17},{... | collective-permute-start | bytes 104 | tf_op jit(solution)/shard_map/ppermute | solution.py:33
  125.5 13.3 %collective-permute-start.22 = (bf16[8,12288]{1,0:T(8,128)(2,1)S(1)}, bf16[8,12288]{1,0:T(8,128)(2,1)S(1)}, u32[]{:S(2)}, u32[]{:S(2)}) collective-permute-start(bf16[8,12288]{1,0:T(8,128)(2,1)S(1)} %bitcast.89), channel_id=1, source_target_pairs={{0,1},{1,2},{2,3},{3,0},{4,5},{5,6},{6,7},{7,4},{8,9},{9,10},{10,1... | collective-permute-start | bytes 589832 | tf_op jit(solution)/shard_map/ppermute | solution.py:97
  125.6 15.3 %collective-permute-start.23 = (bf16[8,12288]{1,0:T(8,128)(2,1)S(1)}, bf16[8,12288]{1,0:T(8,128)(2,1)S(1)}, u32[]{:S(2)}, u32[]{:S(2)}) collective-permute-start(bf16[8,12288]{1,0:T(8,128)(2,1)S(1)} %bitcast.90), channel_id=1, source_target_pairs={{0,2},{1,3},{2,0},{3,1},{4,6},{5,7},{6,4},{7,5},{8,10},{9,11},{10,... | collective-permute-start | bytes 589832 | tf_op jit(solution)/shard_map/ppermute | solution.py:97
  128.4 15.3 %collective-permute-start.24 = (bf16[8,12288]{1,0:T(8,128)(2,1)S(1)}, bf16[8,12288]{1,0:T(8,128)(2,1)S(1)}, u32[]{:S(2)}, u32[]{:S(2)}) collective-permute-start(bf16[8,12288]{1,0:T(8,128)(2,1)S(1)} %bitcast.91), channel_id=1, source_target_pairs={{0,3},{1,0},{2,1},{3,2},{4,7},{5,4},{6,5},{7,6},{8,11},{9,8},{10,9... | collective-permute-start | bytes 589832 | tf_op jit(solution)/shard_map/ppermute | solution.py:97
  130.5 19.0 %collective-permute-start.55 = (bf16[8,4,24,128]{3,2,1,0:T(8,128)(2,1)S(1)}, bf16[8,4,24,128]{3,2,1,0:T(8,128)(2,1)S(1)}, u32[]{:S(2)}, u32[]{:S(2)}) collective-permute-start(bf16[8,4,24,128]{3,2,1,0:T(8,128)(2,1)S(1)} %convert_element_type.134), channel_id=1, source_target_pairs={{4,0},{8,4},{12,8},{16,12},{20,16},{24,20},{28,24},{5,1},{9,5},{13... | collective-permute-start | bytes 589832 | tf_op jit(solution)/shard_map/ppermute | solution.py:22
  131.8 19.0 %collective-permute-start.54 = (bf16[8,4,24,128]{3,2,1,0:T(8,128)(2,1)S(1)}, bf16[8,4,24,128]{3,2,1,0:T(8,128)(2,1)S(1)}, u32[]{:S(2)}, u32[]{:S(2)}) collective-permute-start(bf16[8,4,24,128]{3,2,1,0:T(8,128)(2,1)S(1)} %convert_element_type.134), channel_id=1, source_target_pairs={{0,4},{4,8},{8,12},{12,16},{16,20},{20,24},{24,28},{1,5},{5,9},{9,... | collective-permute-start | bytes 589832 | tf_op jit(solution)/shard_map/ppermute | solution.py:21
  145.9 16.2 %collective-permute-start.58 = (bf16[8,12288]{1,0:T(8,128)(2,1)S(1)}, bf16[8,12288]{1,0:T(8,128)(2,1)S(1)}, u32[]{:S(2)}, u32[]{:S(2)}) collective-permute-start(bf16[8,12288]{1,0:T(8,128)(2,1)S(1)} %bitcast.85), channel_id=1, source_target_pairs={{0,3},{1,0},{2,1},{3,2},{4,7},{5,4},{6,5},{7,6},{8,11},{9,8},{10,9... | collective-permute-start | bytes 589832 | tf_op jit(solution)/shard_map/ppermute | solution.py:97
  145.9 16.5 %collective-permute-start.57 = (bf16[8,12288]{1,0:T(8,128)(2,1)S(1)}, bf16[8,12288]{1,0:T(8,128)(2,1)S(1)}, u32[]{:S(2)}, u32[]{:S(2)}) collective-permute-start(bf16[8,12288]{1,0:T(8,128)(2,1)S(1)} %bitcast.86), channel_id=1, source_target_pairs={{0,2},{1,3},{2,0},{3,1},{4,6},{5,7},{6,4},{7,5},{8,10},{9,11},{10,... | collective-permute-start | bytes 589832 | tf_op jit(solution)/shard_map/ppermute | solution.py:97
  146.9 17.2 %collective-permute-start.56 = (bf16[8,12288]{1,0:T(8,128)(2,1)S(1)}, bf16[8,12288]{1,0:T(8,128)(2,1)S(1)}, u32[]{:S(2)}, u32[]{:S(2)}) collective-permute-start(bf16[8,12288]{1,0:T(8,128)(2,1)S(1)} %bitcast.87), channel_id=1, source_target_pairs={{0,1},{1,2},{2,3},{3,0},{4,5},{5,6},{6,7},{7,4},{8,9},{9,10},{10,1... | collective-permute-start | bytes 589832 | tf_op jit(solution)/shard_map/ppermute | solution.py:97
  149.5 16.7 %collective-permute-start.21 = (bf16[8,4,24,128]{3,2,1,0:T(8,128)(2,1)S(1)}, bf16[8,4,24,128]{3,2,1,0:T(8,128)(2,1)S(1)}, u32[]{:S(2)}, u32[]{:S(2)}) collective-permute-start(bf16[8,4,24,128]{3,2,1,0:T(8,128)(2,1)S(1)} %convert_element_type.117), channel_id=1, source_target_pairs={{4,0},{8,4},{12,8},{16,12},{20,16},{24,20},{28,24},{5,1},{9,5},{13... | collective-permute-start | bytes 589832 | tf_op jit(solution)/shard_map/ppermute | solution.py:22
  150.8 6.2 %collective-permute-start.26 = (f32[256,32]{0,1:T(8,128)S(1)}, f32[256,32]{0,1:T(8,128)S(1)}, u32[]{:S(2)}, u32[]{:S(2)}) collective-permute-start(f32[256,32]{0,1:T(8,128)S(1)} %add.596), channel_id=1, source_target_pairs={{0,8},{4,12},{8,0},{12,4},{16,24},{20,28},{24,16},{28,20},{1,9},{5... | collective-permute-start | bytes 98312 | tf_op jit(solution)/shard_map/ppermute | solution.py:33
  157.0 9.2 %collective-permute-start.20 = (bf16[8,4,24,128]{3,2,1,0:T(8,128)(2,1)S(1)}, bf16[8,4,24,128]{3,2,1,0:T(8,128)(2,1)S(1)}, u32[]{:S(2)}, u32[]{:S(2)}) collective-permute-start(bf16[8,4,24,128]{3,2,1,0:T(8,128)(2,1)S(1)} %convert_element_type.117), channel_id=1, source_target_pairs={{0,4},{4,8},{8,12},{12,16},{16,20},{20,24},{24,28},{1,5},{5,9},{9,... | collective-permute-start | bytes 589832 | tf_op jit(solution)/shard_map/ppermute | solution.py:21
  162.0 5.9 %collective-permute-start.27 = (f32[256,32]{0,1:T(8,128)S(1)}, f32[256,32]{0,1:T(8,128)S(1)}, u32[]{:S(2)}, u32[]{:S(2)}) collective-permute-start(f32[256,32]{0,1:T(8,128)S(1)} %add.597), channel_id=1, source_target_pairs={{0,16},{4,20},{8,24},{12,28},{16,0},{20,4},{24,8},{28,12},{1,17},{... | collective-permute-start | bytes 98312 | tf_op jit(solution)/shard_map/ppermute | solution.py:33
  167.4 3.9 %collective-permute-start.60 = (f32[256,32]{0,1:T(8,128)S(1)}, f32[256,32]{0,1:T(8,128)S(1)}, u32[]{:S(2)}, u32[]{:S(2)}) collective-permute-start(f32[256,32]{0,1:T(8,128)S(1)} %add.679), channel_id=1, source_target_pairs={{0,8},{4,12},{8,0},{12,4},{16,24},{20,28},{24,16},{28,20},{1,9},{5... | collective-permute-start | bytes 98312 | tf_op jit(solution)/shard_map/ppermute | solution.py:33
  171.3 6.0 %collective-permute-start.61 = (f32[256,32]{0,1:T(8,128)S(1)}, f32[256,32]{0,1:T(8,128)S(1)}, u32[]{:S(2)}, u32[]{:S(2)}) collective-permute-start(f32[256,32]{0,1:T(8,128)S(1)} %add.680), channel_id=1, source_target_pairs={{0,16},{4,20},{8,24},{12,28},{16,0},{20,4},{24,8},{28,12},{1,17},{... | collective-permute-start | bytes 98312 | tf_op jit(solution)/shard_map/ppermute | solution.py:33
  171.9 15.3 %collective-permute-start.30 = (bf16[8,12288]{1,0:T(8,128)(2,1)S(1)}, bf16[8,12288]{1,0:T(8,128)(2,1)S(1)}, u32[]{:S(2)}, u32[]{:S(2)}) collective-permute-start(bf16[8,12288]{1,0:T(8,128)(2,1)S(1)} %get-tuple-element.45), channel_id=1, source_target_pairs={{3,0},{0,1},{1,2},{2,3},{7,4},{4,5},{5,6},{6,7},{11,8},{8,9},{9,10... | collective-permute-start | bytes 589832 | tf_op jit(solution)/shard_map/ppermute | solution.py:113
  174.4 26.2 %collective-permute-start.29 = (bf16[8,12288]{1,0:T(8,128)(2,1)S(1)}, bf16[8,12288]{1,0:T(8,128)(2,1)S(1)}, u32[]{:S(2)}, u32[]{:S(2)}) collective-permute-start(bf16[8,12288]{1,0:T(8,128)(2,1)S(1)} %get-tuple-element.46), channel_id=1, source_target_pairs={{2,0},{3,1},{0,2},{1,3},{6,4},{7,5},{4,6},{5,7},{10,8},{11,9},{8,1... | collective-permute-start | bytes 589832 | tf_op jit(solution)/shard_map/ppermute | solution.py:113
  177.3 25.5 %collective-permute-start.28 = (bf16[8,12288]{1,0:T(8,128)(2,1)S(1)}, bf16[8,12288]{1,0:T(8,128)(2,1)S(1)}, u32[]{:S(2)}, u32[]{:S(2)}) collective-permute-start(bf16[8,12288]{1,0:T(8,128)(2,1)S(1)} %get-tuple-element.44), channel_id=1, source_target_pairs={{1,0},{2,1},{3,2},{0,3},{5,4},{6,5},{7,6},{4,7},{9,8},{10,9},{11,1... | collective-permute-start | bytes 589832 | tf_op jit(solution)/shard_map/ppermute | solution.py:113
  179.4 33.1 %collective-permute-start.64 = (bf16[8,12288]{1,0:T(8,128)(2,1)S(1)}, bf16[8,12288]{1,0:T(8,128)(2,1)S(1)}, u32[]{:S(2)}, u32[]{:S(2)}) collective-permute-start(bf16[8,12288]{1,0:T(8,128)(2,1)S(1)} %get-tuple-element.48), channel_id=1, source_target_pairs={{3,0},{0,1},{1,2},{2,3},{7,4},{4,5},{5,6},{6,7},{11,8},{8,9},{9,10... | collective-permute-start | bytes 589832 | tf_op jit(solution)/shard_map/ppermute | solution.py:113
  181.5 31.1 %collective-permute-start.63 = (bf16[8,12288]{1,0:T(8,128)(2,1)S(1)}, bf16[8,12288]{1,0:T(8,128)(2,1)S(1)}, u32[]{:S(2)}, u32[]{:S(2)}) collective-permute-start(bf16[8,12288]{1,0:T(8,128)(2,1)S(1)} %get-tuple-element.49), channel_id=1, source_target_pairs={{2,0},{3,1},{0,2},{1,3},{6,4},{7,5},{4,6},{5,7},{10,8},{11,9},{8,1... | collective-permute-start | bytes 589832 | tf_op jit(solution)/shard_map/ppermute | solution.py:113
  187.1 25.4 %collective-permute-start.62 = (bf16[8,12288]{1,0:T(8,128)(2,1)S(1)}, bf16[8,12288]{1,0:T(8,128)(2,1)S(1)}, u32[]{:S(2)}, u32[]{:S(2)}) collective-permute-start(bf16[8,12288]{1,0:T(8,128)(2,1)S(1)} %get-tuple-element.47), channel_id=1, source_target_pairs={{1,0},{2,1},{3,2},{0,3},{5,4},{6,5},{7,6},{4,7},{9,8},{10,9},{11,1... | collective-permute-start | bytes 589832 | tf_op jit(solution)/shard_map/ppermute | solution.py:113
  (25 other events, 146.0 us)

commit v9 on v1

--- a/solution.py
+++ b/solution.py
@@ -89,22 +89,48 @@
         padded = jnp.pad(padded, ((0, 0), (0, 0), (4, 4), (4, 4)))
         kinetic = -0.5 * second_sum(padded, width_x, width_y, width_z)
         rounded = direction.astype(jnp.bfloat16).reshape(local_bands, local_cells)
-        partial_margin = lax.dot_general(
-            occupied_rows,
-            lax.all_gather(rounded, "band", axis=0, tiled=True),
-            (((1,), (1,)), ((), ())),
-            preferred_element_type=jnp.float32,
+        halves = 2 if local_bands % 2 == 0 else 1
+        half = local_bands // halves
+        partial_margin = jnp.concatenate(
+            [
+                lax.dot_general(
+                    occupied_rows,
+                    jnp.concatenate(
+                        [rounded[h * half : (h + 1) * half]]
+                        + [
+                            lax.ppermute(
+                                rounded[h * half : (h + 1) * half],
+                                "band",
+                                [(i, (i + d) % band_count) for i in range(band_count)],
+                            )
+                            for d in range(1, band_count)
+                        ],
+                        axis=0,
+                    ),
+                    (((1,), (1,)), ((), ())),
+                    preferred_element_type=jnp.float32,
+                )
+                for h in range(halves)
+            ],
+            axis=1,
         )
         margins = grid_sum(partial_margin, "grid")
         scaled = (margins * weight_scale).astype(jnp.bfloat16)
-        projected = lax.psum_scatter(
-            lax.dot_general(
-                scaled, occupied_rows, (((0,), (0,)), ((), ())), preferred_element_type=jnp.float32
-            ).astype(jnp.bfloat16),
-            "band",
-            scatter_dimension=0,
-            tiled=True,
-        ).astype(jnp.float32)
+        pieces = []
+        for h in range(halves):
+            terms = lax.dot_general(
+                scaled[:, h * band_count * half : (h + 1) * band_count * half],
+                occupied_rows,
+                (((0,), (0,)), ((), ())),
+                preferred_element_type=jnp.float32,
+            ).astype(jnp.bfloat16)
+            piece = terms[:half].astype(jnp.float32)
+            for d in range(1, band_count):
+                part = terms[d * half : (d + 1) * half]
+                back = lax.ppermute(part, "band", [((i + d) % band_count, i) for i in range(band_count)])
+                piece = piece + back.astype(jnp.float32)
+            pieces.append(piece)
+        projected = jnp.concatenate(pieces, axis=0)
         applied = kinetic + potential_shift * direction + projected.reshape(direction.shape)
         curvature = grid_sum(inner_product(direction, applied), "grid")
         step_size = norm_now / curvature

time: 241 us -> 220 us (0.913)
  waiting for transfers between devices: 161 us -> 131 us
  starting transfers between devices: 27 us -> 53.1 us
  between operations: 14 us -> 1.04 us
  other arithmetic: 13.4 us -> 9.2 us
    ppermute x0 -> x24, waiting for transfers between devices: none -> 103 us  [the longest x12 55.2 us: body(): lax.ppermute(part, 'band', [((i + d) % band_count, i) for i in range(band...]
    all_gather x2 -> x0, waiting for transfers between devices: 73 us -> none  [body(): lax.all_gather(rounded, 'band', axis=0, tiled=True)]
    reduce_scatter x2 -> x0, waiting for transfers between devices: 56.5 us -> none  [body(): lax.psum_scatter(lax.dot_general(scaled, occupied_rows, (((0,), (0,)), ((...]
    ppermute x0 -> x24, starting transfers between devices: none -> 32.2 us  [the longest x12 16.4 us: body(): lax.ppermute(rounded[h * half:(h + 1) * half], 'band', [(i, (i + d) % ban...]
    ppermute x18, starting transfers between devices: 17.8 us -> 12.2 us  [grid_sum(): value = value + lax.ppermute(value, axis, pairs)]
    ppermute x2, waiting for transfers between devices: 2.59 us -> 0.01 us  [with_halo(): before = lax.ppermute(last, axis, up)]
    dot_general x4 -> x8, matrix products: 20.5 us -> 19.1 us  [the longest x4 11 us: body(): lax.dot_general(occupied_rows, jnp.concatenate([rounded[h * half:(h + 1)...]
  transfers between devices with their start and end apart: 26 -> 46, of which waited for: 22 -> 34; matrix products, arithmetic and copies ran while one was open for 0% -> 7% of each run, Pallas kernels for 0% -> 0%
where the time goes in v9:
time: 220 us; the launch traced here: 215 us
  waiting for transfers between devices  131 us (60%)
  starting transfers between devices  53.1 us (24%)
  matrix products  19.1 us (9%)
  other arithmetic  9.2 us (4%)
    ppermute x12, waiting for transfers between devices, body(): lax.ppermute(part, 'band', [((i + d) % band_count, i) for i in range(band...  55.2 us
    ppermute x12, waiting for transfers between devices, body(): lax.ppermute(rounded[h * half:(h + 1) * half], 'band', [(i, (i + d) % ban...  48.3 us
    ppermute x18, waiting for transfers between devices, grid_sum(): value = value + lax.ppermute(value, axis, pairs)  27.5 us
    ppermute x12, starting transfers between devices, body(): lax.ppermute(rounded[h * half:(h + 1) * half], 'band', [(i, (i + d) % ban...  16.4 us
    ppermute x12, starting transfers between devices, body(): lax.ppermute(part, 'band', [((i + d) % band_count, i) for i in range(band...  15.9 us
    ppermute x18, starting transfers between devices, grid_sum(): value = value + lax.ppermute(value, axis, pairs)  12.2 us
    dot_general x4, matrix products, body(): lax.dot_general(occupied_rows, jnp.concatenate([rounded[h * half:(h + 1)...  11 us
    dot_general x4, matrix products, body(): lax.dot_general(scaled[:, h * band_count * half:(h + 1) * band_count * ha...  8.11 us
  transfers between devices with their start and end apart: 46, of which 34 were waited for; matrix products, arithmetic and copies ran while one was open for 7% of the time, Pallas kernels for 0%

profile of v9, /device:TPU:8, one launch (start us, length us, event | category | flops | bytes accessed | tf_op | source)
XLA Modules:
  0.0 215.2 jit_solution(3430300674162020398)
XLA Ops:
  2.2 3.0 %collective-permute-start.9 = (bf16[8,12288]{1,0:T(8,128)(2,1)S(1)}, bf16[8,12288]{1,0:T(8,128)(2,1)S(1)}, u32[]{:S(2)}, u32[]{:S(2)}) collective-permute-start(bf16[8,12288]{1,0:T(8,128)(2,1)S(1)} %bitcast.80), channel_id=1, source_target_pairs={{0,2},{1,3},{2,0},{3,1},{4,6},{5,7},{6,4},{7,5},{8,10},{9,11},{10,... | collective-permute-start | bytes 589832 | tf_op jit(solution)/shard_map/ppermute | solution.py:101
  5.2 2.5 %collective-permute-start.8 = (bf16[8,12288]{1,0:T(8,128)(2,1)S(1)}, bf16[8,12288]{1,0:T(8,128)(2,1)S(1)}, u32[]{:S(2)}, u32[]{:S(2)}) collective-permute-start(bf16[8,12288]{1,0:T(8,128)(2,1)S(1)} %bitcast.81), channel_id=1, source_target_pairs={{0,1},{1,2},{2,3},{3,0},{4,5},{5,6},{6,7},{7,4},{8,9},{9,10},{10,1... | collective-permute-start | bytes 589832 | tf_op jit(solution)/shard_map/ppermute | solution.py:101
  11.7 7.6 %collective-permute-done.9 = bf16[8,12288]{1,0:T(8,128)(2,1)S(1)} collective-permute-done((bf16[8,12288]{1,0:T(8,128)(2,1)S(1)}, bf16[8,12288]{1,0:T(8,128)(2,1)S(1)}, u32[]{:S(2)}, u32[]{:S(2)}) %collective-permute-start.9) | collective-permute-done | bytes 196640 | tf_op jit(solution)/shard_map/ppermute | solution.py:101
  19.2 11.9 %collective-permute-done.8 = bf16[8,12288]{1,0:T(8,128)(2,1)S(1)} collective-permute-done((bf16[8,12288]{1,0:T(8,128)(2,1)S(1)}, bf16[8,12288]{1,0:T(8,128)(2,1)S(1)}, u32[]{:S(2)}, u32[]{:S(2)}) %collective-permute-start.8) | collective-permute-done | bytes 196640 | tf_op jit(solution)/shard_map/ppermute | solution.py:101
  31.1 5.0 %fusion.15 = f32[256,32]{0,1:T(8,128)S(1)} fusion(bf16[32,8,96,128]{3,2,1,0:T(8,128)(2,1)} %bitcast.63, bf16[8,12288]{1,0:T(8,128)(2,1)S(1)} %collective-permute-done.10, bf16[8,12288]{1,0:T(8,128)(2,1)S(1)} %collective-permute-done.9, bf16[8,12288]{1,0:T(8,128)(2,1)S(1)} %collective-permute-done.8, bf16[8,12288]{1,0:T(8,128)(2,1)S(1)} %bitcast.82), kind=kOutput, calls=%fused_computation.53 | convolution fusion | flops 204472320 | bytes 7110656 | tf_op jit(solution)/shard_map/dot_general | solution.py:96
  36.1 2.5 %collective-permute-done.5 = bf16[8,12288]{1,0:T(8,128)(2,1)S(1)} collective-permute-done((bf16[8,12288]{1,0:T(8,128)(2,1)S(1)}, bf16[8,12288]{1,0:T(8,128)(2,1)S(1)}, u32[]{:S(2)}, u32[]{:S(2)}) %collective-permute-start.5) | collective-permute-done | bytes 196640 | tf_op jit(solution)/shard_map/ppermute | solution.py:101
  38.7 2.0 fusion.12
  42.0 1.6 collective-permute-start.12
  43.6 2.8 %collective-permute-done.12 = f32[256,64]{0,1:T(8,128)S(1)} collective-permute-done((f32[256,64]{0,1:T(8,128)S(1)}, f32[256,64]{0,1:T(8,128)S(1)}, u32[]{:S(2)}, u32[]{:S(2)}) %collective-permute-start.12) | collective-permute-done | bytes 65568 | tf_op jit(solution)/shard_map/ppermute | solution.py:33
  46.4 1.6 collective-permute-start.13
  49.3 3.1 %collective-permute-start.3 = (bf16[16,4,24,128]{3,2,1,0:T(8,128)(2,1)S(1)}, bf16[16,4,24,128]{3,2,1,0:T(8,128)(2,1)S(1)}, u32[]{:S(2)}, u32[]{:S(2)}) collective-permute-start(bf16[16,4,24,128]{3,2,1,0:T(8,128)(2,1)S(1)} %convert_element_type.83), channel_id=1, source_target_pairs={{0,4},{4,8},{8,12},{12,16},{16,20},{20,24},{24,28},{1,5},{5,9},{9,... | collective-permute-start | bytes 1179656 | tf_op jit(solution)/shard_map/ppermute | solution.py:21
  52.4 2.0 convolution_convert_fusion.2
  54.4 2.0 convolution_convert_fusion.3
  60.5 2.1 collective-permute-start.14
  62.8 1.7 collective-permute-done.17
  64.4 1.7 collective-permute-start.15
  66.2 1.7 collective-permute-done.19
  67.9 11.7 %collective-permute-done.18 = bf16[8,12288]{1,0:T(8,128)(2,1)S(1)} collective-permute-done((bf16[8,12288]{1,0:T(8,128)(2,1)S(1)}, bf16[8,12288]{1,0:T(8,128)(2,1)S(1)}, u32[]{:S(2)}, u32[]{:S(2)}) %collective-permute-start.18) | collective-permute-done | bytes 196640 | tf_op jit(solution)/shard_map/ppermute | solution.py:130
  79.7 10.1 %collective-permute-done.14 = bf16[8,12288]{1,0:T(8,128)(2,1)S(1)} collective-permute-done((bf16[8,12288]{1,0:T(8,128)(2,1)S(1)}, bf16[8,12288]{1,0:T(8,128)(2,1)S(1)}, u32[]{:S(2)}, u32[]{:S(2)}) %collective-permute-start.14) | collective-permute-done | bytes 196640 | tf_op jit(solution)/shard_map/ppermute | solution.py:130
  89.8 2.5 %collective-permute-done.15 = bf16[8,12288]{1,0:T(8,128)(2,1)S(1)} collective-permute-done((bf16[8,12288]{1,0:T(8,128)(2,1)S(1)}, bf16[8,12288]{1,0:T(8,128)(2,1)S(1)}, u32[]{:S(2)}, u32[]{:S(2)}) %collective-permute-start.15) | collective-permute-done | bytes 196640 | tf_op jit(solution)/shard_map/ppermute | solution.py:130
  93.5 2.4 %multiply_reduce_fusion.2 = (f32[16]{0:T(128)S(1)}, f32[16]{0:T(128)S(1)}, f32[16,4,24,128]{3,2,1,0:T(8,128)S(1)}) fusion(f32[16,4,24,128]{3,2,1,0:T(8,128)S(1)} %copy-done, f32[16,4,24,128]{3,2,1,0:T(8,128)S(1)} %bitcast.73, f32[16]{0:T(128)S(1)} %copy-done.2, f32[4,24,128]{2,1,0:T(8,128)S(1)} %copy-done.1, f32[16,12,24,128]{3,2,1,0:T(8,128)S(1)} %maximum_convert_fusion), kind=kLoop, calls=%fused_computation.178 | loop fusion | flops 9043936 | bytes 11846272 | tf_op jit(solution)/shard_map/reduce_sum | solution.py:64
  107.7 2.9 %collective-permute-done.24 = f32[16]{0:T(128)S(1)} collective-permute-done((f32[16]{0:T(128)S(1)}, f32[16]{0:T(128)S(1)}, u32[]{:S(2)}, u32[]{:S(2)}) %collective-permute-start.24) | collective-permute-done | bytes 96 | tf_op jit(solution)/shard_map/ppermute | solution.py:33
  111.2 2.9 %collective-permute-done.25 = f32[16]{0:T(128)S(1)} collective-permute-done((f32[16]{0:T(128)S(1)}, f32[16]{0:T(128)S(1)}, u32[]{:S(2)}, u32[]{:S(2)}) %collective-permute-start.25) | collective-permute-done | bytes 96 | tf_op jit(solution)/shard_map/ppermute | solution.py:33
  114.6 3.5 %collective-permute-start.33 = (bf16[8,12288]{1,0:T(8,128)(2,1)S(1)}, bf16[8,12288]{1,0:T(8,128)(2,1)S(1)}, u32[]{:S(2)}, u32[]{:S(2)}) collective-permute-start(bf16[8,12288]{1,0:T(8,128)(2,1)S(1)} %bitcast.83), channel_id=1, source_target_pairs={{0,3},{1,0},{2,1},{3,2},{4,7},{5,4},{6,5},{7,6},{8,11},{9,8},{10,9... | collective-permute-start | bytes 589832 | tf_op jit(solution)/shard_map/ppermute | solution.py:101
  118.1 2.8 %collective-permute-start.31 = (bf16[8,12288]{1,0:T(8,128)(2,1)S(1)}, bf16[8,12288]{1,0:T(8,128)(2,1)S(1)}, u32[]{:S(2)}, u32[]{:S(2)}) collective-permute-start(bf16[8,12288]{1,0:T(8,128)(2,1)S(1)} %bitcast.85), channel_id=1, source_target_pairs={{0,1},{1,2},{2,3},{3,0},{4,5},{5,6},{6,7},{7,4},{8,9},{9,10},{10,1... | collective-permute-start | bytes 589832 | tf_op jit(solution)/shard_map/ppermute | solution.py:101
  121.1 2.0 collective-permute-start.29
  123.1 4.6 %collective-permute-done.33 = bf16[8,12288]{1,0:T(8,128)(2,1)S(1)} collective-permute-done((bf16[8,12288]{1,0:T(8,128)(2,1)S(1)}, bf16[8,12288]{1,0:T(8,128)(2,1)S(1)}, u32[]{:S(2)}, u32[]{:S(2)}) %collective-permute-start.33) | collective-permute-done | bytes 196640 | tf_op jit(solution)/shard_map/ppermute | solution.py:101
  127.7 4.8 %collective-permute-done.32 = bf16[8,12288]{1,0:T(8,128)(2,1)S(1)} collective-permute-done((bf16[8,12288]{1,0:T(8,128)(2,1)S(1)}, bf16[8,12288]{1,0:T(8,128)(2,1)S(1)}, u32[]{:S(2)}, u32[]{:S(2)}) %collective-permute-start.32) | collective-permute-done | bytes 196640 | tf_op jit(solution)/shard_map/ppermute | solution.py:101
  132.5 9.9 %collective-permute-done.31 = bf16[8,12288]{1,0:T(8,128)(2,1)S(1)} collective-permute-done((bf16[8,12288]{1,0:T(8,128)(2,1)S(1)}, bf16[8,12288]{1,0:T(8,128)(2,1)S(1)}, u32[]{:S(2)}, u32[]{:S(2)}) %collective-permute-start.31) | collective-permute-done | bytes 196640 | tf_op jit(solution)/shard_map/ppermute | solution.py:101
  142.4 2.0 fusion.21
  144.4 2.3 %collective-permute-done.30 = bf16[8,12288]{1,0:T(8,128)(2,1)S(1)} collective-permute-done((bf16[8,12288]{1,0:T(8,128)(2,1)S(1)}, bf16[8,12288]{1,0:T(8,128)(2,1)S(1)}, u32[]{:S(2)}, u32[]{:S(2)}) %collective-permute-start.30) | collective-permute-done | bytes 196640 | tf_op jit(solution)/shard_map/ppermute | solution.py:101
  146.7 3.1 %collective-permute-done.28 = bf16[8,12288]{1,0:T(8,128)(2,1)S(1)} collective-permute-done((bf16[8,12288]{1,0:T(8,128)(2,1)S(1)}, bf16[8,12288]{1,0:T(8,128)(2,1)S(1)}, u32[]{:S(2)}, u32[]{:S(2)}) %collective-permute-start.28) | collective-permute-done | bytes 196640 | tf_op jit(solution)/shard_map/ppermute | solution.py:101
  149.9 2.0 fusion.18
  154.0 3.6 %collective-permute-done.35 = f32[256,64]{0,1:T(8,128)S(1)} collective-permute-done((f32[256,64]{0,1:T(8,128)S(1)}, f32[256,64]{0,1:T(8,128)S(1)}, u32[]{:S(2)}, u32[]{:S(2)}) %collective-permute-start.35) | collective-permute-done | bytes 65568 | tf_op jit(solution)/shard_map/ppermute | solution.py:33
  159.6 3.1 %collective-permute-start.26 = (bf16[16,4,24,128]{3,2,1,0:T(8,128)(2,1)S(1)}, bf16[16,4,24,128]{3,2,1,0:T(8,128)(2,1)S(1)}, u32[]{:S(2)}, u32[]{:S(2)}) collective-permute-start(bf16[16,4,24,128]{3,2,1,0:T(8,128)(2,1)S(1)} %get-tuple-element.6), channel_id=1, source_target_pairs={{0,4},{4,8},{8,12},{12,16},{16,20},{20,24},{24,28},{1,5},{5,9},{9,... | collective-permute-start | bytes 1179656 | tf_op jit(solution)/shard_map/ppermute | solution.py:21
  162.7 2.0 convolution_convert_fusion
  164.7 2.0 convolution_convert_fusion.1
  170.9 2.0 collective-permute-start.37
  173.2 1.6 collective-permute-done.40
  174.8 1.9 collective-permute-start.38
  176.7 1.7 collective-permute-done.42
  178.4 11.6 %collective-permute-done.41 = bf16[8,12288]{1,0:T(8,128)(2,1)S(1)} collective-permute-done((bf16[8,12288]{1,0:T(8,128)(2,1)S(1)}, bf16[8,12288]{1,0:T(8,128)(2,1)S(1)}, u32[]{:S(2)}, u32[]{:S(2)}) %collective-permute-start.41) | collective-permute-done | bytes 196640 | tf_op jit(solution)/shard_map/ppermute | solution.py:130
  190.1 10.0 %collective-permute-done.37 = bf16[8,12288]{1,0:T(8,128)(2,1)S(1)} collective-permute-done((bf16[8,12288]{1,0:T(8,128)(2,1)S(1)}, bf16[8,12288]{1,0:T(8,128)(2,1)S(1)}, u32[]{:S(2)}, u32[]{:S(2)}) %collective-permute-start.37) | collective-permute-done | bytes 196640 | tf_op jit(solution)/shard_map/ppermute | solution.py:130
  200.1 2.5 %collective-permute-done.38 = bf16[8,12288]{1,0:T(8,128)(2,1)S(1)} collective-permute-done((bf16[8,12288]{1,0:T(8,128)(2,1)S(1)}, bf16[8,12288]{1,0:T(8,128)(2,1)S(1)}, u32[]{:S(2)}, u32[]{:S(2)}) %collective-permute-start.38) | collective-permute-done | bytes 196640 | tf_op jit(solution)/shard_map/ppermute | solution.py:130
  203.0 2.4 %multiply_reduce_fusion = (f32[16]{0:T(128)S(1)}, f32[16,4,24,128]{3,2,1,0:T(8,128)S(1)}) fusion(f32[16,4,24,128]{3,2,1,0:T(8,128)S(1)} %get-tuple-element.7, f32[16,4,24,128]{3,2,1,0:T(8,128)S(1)} %bitcast.74, f32[16]{0:T(128)S(1)} %copy-done.2, f32[4,24,128]{2,1,0:T(8,128)S(1)} %copy-done.1, f32[16,12,24,128]{3,2,1,0:T(8,128)S(1)} %maximum_convert_fusion.1), kind=kLoop, calls=%fused_computation.174 | loop fusion | flops 8650736 | bytes 11846208 | tf_op jit(solution)/shard_map/reduce_sum | solution.py:64
  207.9 2.2 %collective-permute-done.44 = f32[16]{0:T(128)S(1)} collective-permute-done((f32[16]{0:T(128)S(1)}, f32[16]{0:T(128)S(1)}, u32[]{:S(2)}, u32[]{:S(2)}) %collective-permute-start.44) | collective-permute-done | bytes 96 | tf_op jit(solution)/shard_map/ppermute | solution.py:33
  210.8 2.8 %collective-permute-done.45 = f32[16]{0:T(128)S(1)} collective-permute-done((f32[16]{0:T(128)S(1)}, f32[16]{0:T(128)S(1)}, u32[]{:S(2)}, u32[]{:S(2)}) %collective-permute-start.45) | collective-permute-done | bytes 96 | tf_op jit(solution)/shard_map/ppermute | solution.py:33
  213.7 1.6 multiply_subtract_fusion
  (108 shorter events, 38.8 us)
Async XLA Ops:
  0.6 38.0 %slice-start = ((s8[6291456]{0:T(1024)(128)(4,1)}), s8[4194304]{0:T(1024)(128)(4,1)S(1)}, s32[]{:S(2)}) async-start(s8[6291456]{0:T(1024)(128)(4,1)} %bitcast.64), calls=%async_computation | async-start | bytes 8388608
  2.1 8.7 %collective-permute-start.10 = (bf16[8,12288]{1,0:T(8,128)(2,1)S(1)}, bf16[8,12288]{1,0:T(8,128)(2,1)S(1)}, u32[]{:S(2)}, u32[]{:S(2)}) collective-permute-start(bf16[8,12288]{1,0:T(8,128)(2,1)S(1)} %bitcast.79), channel_id=1, source_target_pairs={{0,3},{1,0},{2,1},{3,2},{4,7},{5,4},{6,5},{7,6},{8,11},{9,8},{10,9... | collective-permute-start | bytes 589832 | tf_op jit(solution)/shard_map/ppermute | solution.py:101
  2.2 17.1 %collective-permute-start.9 = (bf16[8,12288]{1,0:T(8,128)(2,1)S(1)}, bf16[8,12288]{1,0:T(8,128)(2,1)S(1)}, u32[]{:S(2)}, u32[]{:S(2)}) collective-permute-start(bf16[8,12288]{1,0:T(8,128)(2,1)S(1)} %bitcast.80), channel_id=1, source_target_pairs={{0,2},{1,3},{2,0},{3,1},{4,6},{5,7},{6,4},{7,5},{8,10},{9,11},{10,... | collective-permute-start | bytes 589832 | tf_op jit(solution)/shard_map/ppermute | solution.py:101
  5.2 25.9 %collective-permute-start.8 = (bf16[8,12288]{1,0:T(8,128)(2,1)S(1)}, bf16[8,12288]{1,0:T(8,128)(2,1)S(1)}, u32[]{:S(2)}, u32[]{:S(2)}) collective-permute-start(bf16[8,12288]{1,0:T(8,128)(2,1)S(1)} %bitcast.81), channel_id=1, source_target_pairs={{0,1},{1,2},{2,3},{3,0},{4,5},{5,6},{6,7},{7,4},{8,9},{9,10},{10,1... | collective-permute-start | bytes 589832 | tf_op jit(solution)/shard_map/ppermute | solution.py:101
  7.8 28.4 %collective-permute-start.7 = (bf16[8,12288]{1,0:T(8,128)(2,1)S(1)}, bf16[8,12288]{1,0:T(8,128)(2,1)S(1)}, u32[]{:S(2)}, u32[]{:S(2)}) collective-permute-start(bf16[8,12288]{1,0:T(8,128)(2,1)S(1)} %bitcast.87), channel_id=1, source_target_pairs={{0,3},{1,0},{2,1},{3,2},{4,7},{5,4},{6,5},{7,6},{8,11},{9,8},{10,9... | collective-permute-start | bytes 589832 | tf_op jit(solution)/shard_map/ppermute | solution.py:101
  7.8 28.3 %collective-permute-start.6 = (bf16[8,12288]{1,0:T(8,128)(2,1)S(1)}, bf16[8,12288]{1,0:T(8,128)(2,1)S(1)}, u32[]{:S(2)}, u32[]{:S(2)}) collective-permute-start(bf16[8,12288]{1,0:T(8,128)(2,1)S(1)} %bitcast.88), channel_id=1, source_target_pairs={{0,2},{1,3},{2,0},{3,1},{4,6},{5,7},{6,4},{7,5},{8,10},{9,11},{10,... | collective-permute-start | bytes 589832 | tf_op jit(solution)/shard_map/ppermute | solution.py:101
  10.8 27.8 %collective-permute-start.5 = (bf16[8,12288]{1,0:T(8,128)(2,1)S(1)}, bf16[8,12288]{1,0:T(8,128)(2,1)S(1)}, u32[]{:S(2)}, u32[]{:S(2)}) collective-permute-start(bf16[8,12288]{1,0:T(8,128)(2,1)S(1)} %bitcast.89), channel_id=1, source_target_pairs={{0,1},{1,2},{2,3},{3,0},{4,5},{5,6},{6,7},{7,4},{8,9},{9,10},{10,1... | collective-permute-start | bytes 589832 | tf_op jit(solution)/shard_map/ppermute | solution.py:101
  31.1 7.6 %slice-start.1 = ((s8[6291456]{0:T(1024)(128)(4,1)}), s8[2097152]{0:T(1024)(128)(4,1)S(1)}, s32[]{:S(2)}) async-start(s8[6291456]{0:T(1024)(128)(4,1)} %bitcast.64), calls=%async_computation.1 | async-start | bytes 4194304
  40.7 1.3 collective-permute-start.11
  42.0 4.3 %collective-permute-start.12 = (f32[256,64]{0,1:T(8,128)S(1)}, f32[256,64]{0,1:T(8,128)S(1)}, u32[]{:S(2)}, u32[]{:S(2)}) collective-permute-start(f32[256,64]{0,1:T(8,128)S(1)} %fusion.137), channel_id=1, source_target_pairs={{0,8},{4,12},{8,0},{12,4},{16,24},{20,28},{24,16},{28,20},{1,9},{5... | collective-permute-start | bytes 196616 | tf_op jit(solution)/shard_map/ppermute | solution.py:33
  46.4 5.9 %collective-permute-start.13 = (f32[256,64]{0,1:T(8,128)S(1)}, f32[256,64]{0,1:T(8,128)S(1)}, u32[]{:S(2)}, u32[]{:S(2)}) collective-permute-start(f32[256,64]{0,1:T(8,128)S(1)} %add.301), channel_id=1, source_target_pairs={{0,16},{4,20},{8,24},{12,28},{16,0},{20,4},{24,8},{28,12},{1,17},{... | collective-permute-start | bytes 196616 | tf_op jit(solution)/shard_map/ppermute | solution.py:33
  48.0 12.5 %collective-permute-start.4 = (bf16[16,4,24,128]{3,2,1,0:T(8,128)(2,1)S(1)}, bf16[16,4,24,128]{3,2,1,0:T(8,128)(2,1)S(1)}, u32[]{:S(2)}, u32[]{:S(2)}) collective-permute-start(bf16[16,4,24,128]{3,2,1,0:T(8,128)(2,1)S(1)} %convert_element_type.83), channel_id=1, source_target_pairs={{4,0},{8,4},{12,8},{16,12},{20,16},{24,20},{28,24},{5,1},{9,5},{13... | collective-permute-start | bytes 1179656 | tf_op jit(solution)/shard_map/ppermute | solution.py:22
  49.3 13.3 %collective-permute-start.3 = (bf16[16,4,24,128]{3,2,1,0:T(8,128)(2,1)S(1)}, bf16[16,4,24,128]{3,2,1,0:T(8,128)(2,1)S(1)}, u32[]{:S(2)}, u32[]{:S(2)}) collective-permute-start(bf16[16,4,24,128]{3,2,1,0:T(8,128)(2,1)S(1)} %convert_element_type.83), channel_id=1, source_target_pairs={{0,4},{4,8},{8,12},{12,16},{16,20},{20,24},{24,28},{1,5},{5,9},{9,... | collective-permute-start | bytes 1179656 | tf_op jit(solution)/shard_map/ppermute | solution.py:21
  56.5 8.0 %collective-permute-start.17 = (bf16[8,12288]{1,0:T(8,128)(2,1)S(1)}, bf16[8,12288]{1,0:T(8,128)(2,1)S(1)}, u32[]{:S(2)}, u32[]{:S(2)}) collective-permute-start(bf16[8,12288]{1,0:T(8,128)(2,1)S(1)} %get-tuple-element.24), channel_id=1, source_target_pairs={{1,0},{2,1},{3,2},{0,3},{5,4},{6,5},{7,6},{4,7},{9,8},{10,9},{11,1... | collective-permute-start | bytes 589832 | tf_op jit(solution)/shard_map/ppermute | solution.py:130
  57.6 10.3 %collective-permute-start.19 = (bf16[8,12288]{1,0:T(8,128)(2,1)S(1)}, bf16[8,12288]{1,0:T(8,128)(2,1)S(1)}, u32[]{:S(2)}, u32[]{:S(2)}) collective-permute-start(bf16[8,12288]{1,0:T(8,128)(2,1)S(1)} %get-tuple-element.25), channel_id=1, source_target_pairs={{3,0},{0,1},{1,2},{2,3},{7,4},{4,5},{5,6},{6,7},{11,8},{8,9},{9,10... | collective-permute-start | bytes 589832 | tf_op jit(solution)/shard_map/ppermute | solution.py:130
  59.1 20.5 %collective-permute-start.18 = (bf16[8,12288]{1,0:T(8,128)(2,1)S(1)}, bf16[8,12288]{1,0:T(8,128)(2,1)S(1)}, u32[]{:S(2)}, u32[]{:S(2)}) collective-permute-start(bf16[8,12288]{1,0:T(8,128)(2,1)S(1)} %get-tuple-element.26), channel_id=1, source_target_pairs={{2,0},{3,1},{0,2},{1,3},{6,4},{7,5},{4,6},{5,7},{10,8},{11,9},{8,1... | collective-permute-start | bytes 589832 | tf_op jit(solution)/shard_map/ppermute | solution.py:130
  60.5 29.2 %collective-permute-start.14 = (bf16[8,12288]{1,0:T(8,128)(2,1)S(1)}, bf16[8,12288]{1,0:T(8,128)(2,1)S(1)}, u32[]{:S(2)}, u32[]{:S(2)}) collective-permute-start(bf16[8,12288]{1,0:T(8,128)(2,1)S(1)} %get-tuple-element.21), channel_id=1, source_target_pairs={{1,0},{2,1},{3,2},{0,3},{5,4},{6,5},{7,6},{4,7},{9,8},{10,9},{11,1... | collective-permute-start | bytes 589832 | tf_op jit(solution)/shard_map/ppermute | solution.py:130
  62.6 27.2 %collective-permute-start.16 = (bf16[8,12288]{1,0:T(8,128)(2,1)S(1)}, bf16[8,12288]{1,0:T(8,128)(2,1)S(1)}, u32[]{:S(2)}, u32[]{:S(2)}) collective-permute-start(bf16[8,12288]{1,0:T(8,128)(2,1)S(1)} %get-tuple-element.22), channel_id=1, source_target_pairs={{3,0},{0,1},{1,2},{2,3},{7,4},{4,5},{5,6},{6,7},{11,8},{8,9},{9,10... | collective-permute-start | bytes 589832 | tf_op jit(solution)/shard_map/ppermute | solution.py:130
  64.4 27.8 %collective-permute-start.15 = (bf16[8,12288]{1,0:T(8,128)(2,1)S(1)}, bf16[8,12288]{1,0:T(8,128)(2,1)S(1)}, u32[]{:S(2)}, u32[]{:S(2)}) collective-permute-start(bf16[8,12288]{1,0:T(8,128)(2,1)S(1)} %get-tuple-element.23), channel_id=1, source_target_pairs={{2,0},{3,1},{0,2},{1,3},{6,4},{7,5},{4,6},{5,7},{10,8},{11,9},{8,1... | collective-permute-start | bytes 589832 | tf_op jit(solution)/shard_map/ppermute | solution.py:130
  95.9 1.2 collective-permute-start.20
  96.1 2.4 %collective-permute-start = (f32[16]{0:T(128)S(1)}, f32[16]{0:T(128)S(1)}, u32[]{:S(2)}, u32[]{:S(2)}) collective-permute-start(f32[16]{0:T(128)S(1)} %get-tuple-element.3), channel_id=1, source_target_pairs={{0,4},{4,0},{8,12},{12,8},{16,20},{20,16},{24,28},{28,24},{1,5},{5... | collective-permute-start | bytes 200 | tf_op jit(solution)/shard_map/ppermute | solution.py:33
  97.1 3.5 %collective-permute-start.21 = (f32[16]{0:T(128)S(1)}, f32[16]{0:T(128)S(1)}, u32[]{:S(2)}, u32[]{:S(2)}) collective-permute-start(f32[16]{0:T(128)S(1)} %add.310), channel_id=1, source_target_pairs={{0,8},{4,12},{8,0},{12,4},{16,24},{20,28},{24,16},{28,20},{1,9},{5... | collective-permute-start | bytes 200 | tf_op jit(solution)/shard_map/ppermute | solution.py:33
  98.5 3.5 %collective-permute-start.1 = (f32[16]{0:T(128)S(1)}, f32[16]{0:T(128)S(1)}, u32[]{:S(2)}, u32[]{:S(2)}) collective-permute-start(f32[16]{0:T(128)S(1)} %add.269), channel_id=1, source_target_pairs={{0,8},{4,12},{8,0},{12,4},{16,24},{20,28},{24,16},{28,20},{1,9},{5... | collective-permute-start | bytes 200 | tf_op jit(solution)/shard_map/ppermute | solution.py:33
  100.6 3.5 %collective-permute-start.22 = (f32[16]{0:T(128)S(1)}, f32[16]{0:T(128)S(1)}, u32[]{:S(2)}, u32[]{:S(2)}) collective-permute-start(f32[16]{0:T(128)S(1)} %add.311), channel_id=1, source_target_pairs={{0,16},{4,20},{8,24},{12,28},{16,0},{20,4},{24,8},{28,12},{1,17},{... | collective-permute-start | bytes 200 | tf_op jit(solution)/shard_map/ppermute | solution.py:33
  102.0 3.5 %collective-permute-start.2 = (f32[16]{0:T(128)S(1)}, f32[16]{0:T(128)S(1)}, u32[]{:S(2)}, u32[]{:S(2)}) collective-permute-start(f32[16]{0:T(128)S(1)} %add.270), channel_id=1, source_target_pairs={{0,16},{4,20},{8,24},{12,28},{16,0},{20,4},{24,8},{28,12},{1,17},{... | collective-permute-start | bytes 200 | tf_op jit(solution)/shard_map/ppermute | solution.py:33
  105.9 1.2 collective-permute-start.23
  107.0 3.5 %collective-permute-start.24 = (f32[16]{0:T(128)S(1)}, f32[16]{0:T(128)S(1)}, u32[]{:S(2)}, u32[]{:S(2)}) collective-permute-start(f32[16]{0:T(128)S(1)} %add.313), channel_id=1, source_target_pairs={{0,8},{4,12},{8,0},{12,4},{16,24},{20,28},{24,16},{28,20},{1,9},{5... | collective-permute-start | bytes 200 | tf_op jit(solution)/shard_map/ppermute | solution.py:33
  110.6 3.5 %collective-permute-start.25 = (f32[16]{0:T(128)S(1)}, f32[16]{0:T(128)S(1)}, u32[]{:S(2)}, u32[]{:S(2)}) collective-permute-start(f32[16]{0:T(128)S(1)} %add.314), channel_id=1, source_target_pairs={{0,16},{4,20},{8,24},{12,28},{16,0},{20,4},{24,8},{28,12},{1,17},{... | collective-permute-start | bytes 200 | tf_op jit(solution)/shard_map/ppermute | solution.py:33
  114.6 13.1 %collective-permute-start.33 = (bf16[8,12288]{1,0:T(8,128)(2,1)S(1)}, bf16[8,12288]{1,0:T(8,128)(2,1)S(1)}, u32[]{:S(2)}, u32[]{:S(2)}) collective-permute-start(bf16[8,12288]{1,0:T(8,128)(2,1)S(1)} %bitcast.83), channel_id=1, source_target_pairs={{0,3},{1,0},{2,1},{3,2},{4,7},{5,4},{6,5},{7,6},{8,11},{9,8},{10,9... | collective-permute-start | bytes 589832 | tf_op jit(solution)/shard_map/ppermute | solution.py:101
  118.0 14.5 %collective-permute-start.32 = (bf16[8,12288]{1,0:T(8,128)(2,1)S(1)}, bf16[8,12288]{1,0:T(8,128)(2,1)S(1)}, u32[]{:S(2)}, u32[]{:S(2)}) collective-permute-start(bf16[8,12288]{1,0:T(8,128)(2,1)S(1)} %bitcast.84), channel_id=1, source_target_pairs={{0,2},{1,3},{2,0},{3,1},{4,6},{5,7},{6,4},{7,5},{8,10},{9,11},{10,... | collective-permute-start | bytes 589832 | tf_op jit(solution)/shard_map/ppermute | solution.py:101
  118.1 24.3 %collective-permute-start.31 = (bf16[8,12288]{1,0:T(8,128)(2,1)S(1)}, bf16[8,12288]{1,0:T(8,128)(2,1)S(1)}, u32[]{:S(2)}, u32[]{:S(2)}) collective-permute-start(bf16[8,12288]{1,0:T(8,128)(2,1)S(1)} %bitcast.85), channel_id=1, source_target_pairs={{0,1},{1,2},{2,3},{3,0},{4,5},{5,6},{6,7},{7,4},{8,9},{9,10},{10,1... | collective-permute-start | bytes 589832 | tf_op jit(solution)/shard_map/ppermute | solution.py:101
  121.0 25.7 %collective-permute-start.30 = (bf16[8,12288]{1,0:T(8,128)(2,1)S(1)}, bf16[8,12288]{1,0:T(8,128)(2,1)S(1)}, u32[]{:S(2)}, u32[]{:S(2)}) collective-permute-start(bf16[8,12288]{1,0:T(8,128)(2,1)S(1)} %bitcast.91), channel_id=1, source_target_pairs={{0,3},{1,0},{2,1},{3,2},{4,7},{5,4},{6,5},{7,6},{8,11},{9,8},{10,9... | collective-permute-start | bytes 589832 | tf_op jit(solution)/shard_map/ppermute | solution.py:101
  121.1 25.7 %collective-permute-start.29 = (bf16[8,12288]{1,0:T(8,128)(2,1)S(1)}, bf16[8,12288]{1,0:T(8,128)(2,1)S(1)}, u32[]{:S(2)}, u32[]{:S(2)}) collective-permute-start(bf16[8,12288]{1,0:T(8,128)(2,1)S(1)} %bitcast.92), channel_id=1, source_target_pairs={{0,2},{1,3},{2,0},{3,1},{4,6},{5,7},{6,4},{7,5},{8,10},{9,11},{10,... | collective-permute-start | bytes 589832 | tf_op jit(solution)/shard_map/ppermute | solution.py:101
  127.7 22.2 %collective-permute-start.28 = (bf16[8,12288]{1,0:T(8,128)(2,1)S(1)}, bf16[8,12288]{1,0:T(8,128)(2,1)S(1)}, u32[]{:S(2)}, u32[]{:S(2)}) collective-permute-start(bf16[8,12288]{1,0:T(8,128)(2,1)S(1)} %bitcast.93), channel_id=1, source_target_pairs={{0,1},{1,2},{2,3},{3,0},{4,5},{5,6},{6,7},{7,4},{8,9},{9,10},{10,1... | collective-permute-start | bytes 589832 | tf_op jit(solution)/shard_map/ppermute | solution.py:101
  151.9 1.3 collective-permute-start.34
  153.2 4.3 %collective-permute-start.35 = (f32[256,64]{0,1:T(8,128)S(1)}, f32[256,64]{0,1:T(8,128)S(1)}, u32[]{:S(2)}, u32[]{:S(2)}) collective-permute-start(f32[256,64]{0,1:T(8,128)S(1)} %fusion.136), channel_id=1, source_target_pairs={{0,8},{4,12},{8,0},{12,4},{16,24},{20,28},{24,16},{28,20},{1,9},{5... | collective-permute-start | bytes 196616 | tf_op jit(solution)/shard_map/ppermute | solution.py:33
  157.6 5.1 %collective-permute-start.36 = (f32[256,64]{0,1:T(8,128)S(1)}, f32[256,64]{0,1:T(8,128)S(1)}, u32[]{:S(2)}, u32[]{:S(2)}) collective-permute-start(f32[256,64]{0,1:T(8,128)S(1)} %add.343), channel_id=1, source_target_pairs={{0,16},{4,20},{8,24},{12,28},{16,0},{20,4},{24,8},{28,12},{1,17},{... | collective-permute-start | bytes 196616 | tf_op jit(solution)/shard_map/ppermute | solution.py:33
  158.3 12.6 %collective-permute-start.27 = (bf16[16,4,24,128]{3,2,1,0:T(8,128)(2,1)S(1)}, bf16[16,4,24,128]{3,2,1,0:T(8,128)(2,1)S(1)}, u32[]{:S(2)}, u32[]{:S(2)}) collective-permute-start(bf16[16,4,24,128]{3,2,1,0:T(8,128)(2,1)S(1)} %get-tuple-element.6), channel_id=1, source_target_pairs={{4,0},{8,4},{12,8},{16,12},{20,16},{24,20},{28,24},{5,1},{9,5},{13... | collective-permute-start | bytes 1179656 | tf_op jit(solution)/shard_map/ppermute | solution.py:22
  159.6 13.3 %collective-permute-start.26 = (bf16[16,4,24,128]{3,2,1,0:T(8,128)(2,1)S(1)}, bf16[16,4,24,128]{3,2,1,0:T(8,128)(2,1)S(1)}, u32[]{:S(2)}, u32[]{:S(2)}) collective-permute-start(bf16[16,4,24,128]{3,2,1,0:T(8,128)(2,1)S(1)} %get-tuple-element.6), channel_id=1, source_target_pairs={{0,4},{4,8},{8,12},{12,16},{16,20},{20,24},{24,28},{1,5},{5,9},{9,... | collective-permute-start | bytes 1179656 | tf_op jit(solution)/shard_map/ppermute | solution.py:21
  166.8 8.0 %collective-permute-start.40 = (bf16[8,12288]{1,0:T(8,128)(2,1)S(1)}, bf16[8,12288]{1,0:T(8,128)(2,1)S(1)}, u32[]{:S(2)}, u32[]{:S(2)}) collective-permute-start(bf16[8,12288]{1,0:T(8,128)(2,1)S(1)} %get-tuple-element.18), channel_id=1, source_target_pairs={{1,0},{2,1},{3,2},{0,3},{5,4},{6,5},{7,6},{4,7},{9,8},{10,9},{11,1... | collective-permute-start | bytes 589832 | tf_op jit(solution)/shard_map/ppermute | solution.py:130
  168.2 10.2 %collective-permute-start.42 = (bf16[8,12288]{1,0:T(8,128)(2,1)S(1)}, bf16[8,12288]{1,0:T(8,128)(2,1)S(1)}, u32[]{:S(2)}, u32[]{:S(2)}) collective-permute-start(bf16[8,12288]{1,0:T(8,128)(2,1)S(1)} %get-tuple-element.19), channel_id=1, source_target_pairs={{3,0},{0,1},{1,2},{2,3},{7,4},{4,5},{5,6},{6,7},{11,8},{8,9},{9,10... | collective-permute-start | bytes 589832 | tf_op jit(solution)/shard_map/ppermute | solution.py:130
  169.6 20.4 %collective-permute-start.41 = (bf16[8,12288]{1,0:T(8,128)(2,1)S(1)}, bf16[8,12288]{1,0:T(8,128)(2,1)S(1)}, u32[]{:S(2)}, u32[]{:S(2)}) collective-permute-start(bf16[8,12288]{1,0:T(8,128)(2,1)S(1)} %get-tuple-element.20), channel_id=1, source_target_pairs={{2,0},{3,1},{0,2},{1,3},{6,4},{7,5},{4,6},{5,7},{10,8},{11,9},{8,1... | collective-permute-start | bytes 589832 | tf_op jit(solution)/shard_map/ppermute | solution.py:130
  170.9 29.2 %collective-permute-start.37 = (bf16[8,12288]{1,0:T(8,128)(2,1)S(1)}, bf16[8,12288]{1,0:T(8,128)(2,1)S(1)}, u32[]{:S(2)}, u32[]{:S(2)}) collective-permute-start(bf16[8,12288]{1,0:T(8,128)(2,1)S(1)} %get-tuple-element.15), channel_id=1, source_target_pairs={{1,0},{2,1},{3,2},{0,3},{5,4},{6,5},{7,6},{4,7},{9,8},{10,9},{11,1... | collective-permute-start | bytes 589832 | tf_op jit(solution)/shard_map/ppermute | solution.py:130
  172.9 27.2 %collective-permute-start.39 = (bf16[8,12288]{1,0:T(8,128)(2,1)S(1)}, bf16[8,12288]{1,0:T(8,128)(2,1)S(1)}, u32[]{:S(2)}, u32[]{:S(2)}) collective-permute-start(bf16[8,12288]{1,0:T(8,128)(2,1)S(1)} %get-tuple-element.16), channel_id=1, source_target_pairs={{3,0},{0,1},{1,2},{2,3},{7,4},{4,5},{5,6},{6,7},{11,8},{8,9},{9,10... | collective-permute-start | bytes 589832 | tf_op jit(solution)/shard_map/ppermute | solution.py:130
  174.8 27.9 %collective-permute-start.38 = (bf16[8,12288]{1,0:T(8,128)(2,1)S(1)}, bf16[8,12288]{1,0:T(8,128)(2,1)S(1)}, u32[]{:S(2)}, u32[]{:S(2)}) collective-permute-start(bf16[8,12288]{1,0:T(8,128)(2,1)S(1)} %get-tuple-element.17), channel_id=1, source_target_pairs={{2,0},{3,1},{0,2},{1,3},{6,4},{7,5},{4,6},{5,7},{10,8},{11,9},{8,1... | collective-permute-start | bytes 589832 | tf_op jit(solution)/shard_map/ppermute | solution.py:130
  205.4 1.2 collective-permute-start.43
  206.6 3.5 %collective-permute-start.44 = (f32[16]{0:T(128)S(1)}, f32[16]{0:T(128)S(1)}, u32[]{:S(2)}, u32[]{:S(2)}) collective-permute-start(f32[16]{0:T(128)S(1)} %add.352), channel_id=1, source_target_pairs={{0,8},{4,12},{8,0},{12,4},{16,24},{20,28},{24,16},{28,20},{1,9},{5... | collective-permute-start | bytes 200 | tf_op jit(solution)/shard_map/ppermute | solution.py:33
  210.1 3.5 %collective-permute-start.45 = (f32[16]{0:T(128)S(1)}, f32[16]{0:T(128)S(1)}, u32[]{:S(2)}, u32[]{:S(2)}) collective-permute-start(f32[16]{0:T(128)S(1)} %add.353), channel_id=1, source_target_pairs={{0,16},{4,20},{8,24},{12,28},{16,0},{20,4},{24,8},{28,12},{1,17},{... | collective-permute-start | bytes 200 | tf_op jit(solution)/shard_map/ppermute | solution.py:33
  (3 other events, 3.4 us)

commit v10 on v1

--- a/solution.py
+++ b/solution.py
@@ -69,7 +69,7 @@
 
 
 def body(occupied, potential, shifts, source_term):
-    local_bands, width_x, width_y, width_z = source_term.shape
+    total_bands, width_x, width_y, width_z = source_term.shape
     local_occupied = occupied.shape[0]
     band_count = lax.axis_size("band")
     local_cells = width_x * width_y * width_z
@@ -77,44 +77,51 @@
         local_occupied * band_count * local_cells * lax.axis_size("grid")
     )
     occupied_rows = occupied.reshape(local_occupied, local_cells)
-    potential_shift = potential[None] + shifts[:, None, None, None]
-    solution = jnp.zeros_like(source_term)
-    residual = source_term
-    direction = source_term
-    norm_now = grid_sum(inner_product(source_term, source_term), "grid")
+    pieces = 2 if total_bands % 2 == 0 else 1
+    local_bands = total_bands // pieces
+    spans = [slice(k * local_bands, (k + 1) * local_bands) for k in range(pieces)]
+    norm_all = grid_sum(inner_product(source_term, source_term), "grid")
+    solution = [jnp.zeros_like(source_term[span]) for span in spans]
+    residual = [source_term[span] for span in spans]
+    direction = [source_term[span] for span in spans]
+    norm_now = [norm_all[span] for span in spans]
     for iteration in range(ITERS):
-        padded = with_halo(direction.astype(jnp.bfloat16), (("grid", 1),), 4).astype(
-            direction.dtype
-        )
+        whole = jnp.concatenate(direction, axis=0) if pieces > 1 else direction[0]
+        padded = with_halo(whole.astype(jnp.bfloat16), (("grid", 1),), 4).astype(whole.dtype)
         padded = jnp.pad(padded, ((0, 0), (0, 0), (4, 4), (4, 4)))
-        kinetic = -0.5 * second_sum(padded, width_x, width_y, width_z)
-        rounded = direction.astype(jnp.bfloat16).reshape(local_bands, local_cells)
-        partial_margin = lax.dot_general(
-            occupied_rows,
-            lax.all_gather(rounded, "band", axis=0, tiled=True),
-            (((1,), (1,)), ((), ())),
-            preferred_element_type=jnp.float32,
-        )
-        margins = grid_sum(partial_margin, "grid")
-        scaled = (margins * weight_scale).astype(jnp.bfloat16)
-        projected = lax.psum_scatter(
-            lax.dot_general(
+        kinetic_all = -0.5 * second_sum(padded, width_x, width_y, width_z)
+        for k, span in enumerate(spans):
+            own_potential, current = lax.optimization_barrier((potential, direction[k]))
+            potential_shift = own_potential[None] + shifts[span][:, None, None, None]
+            rounded = current.astype(jnp.bfloat16).reshape(local_bands, local_cells)
+            blocks = [rounded] + [
+                lax.ppermute(rounded, "band", [(i, (i + d) % band_count) for i in range(band_count)])
+                for d in range(1, band_count)
+            ]
+            gathered = jnp.concatenate(blocks, axis=0)
+            partial_margin = lax.dot_general(
+                occupied_rows, gathered, (((1,), (1,)), ((), ())), preferred_element_type=jnp.float32
+            )
+            margins = grid_sum(partial_margin, "grid")
+            scaled = (margins * weight_scale).astype(jnp.bfloat16)
+            terms = lax.dot_general(
                 scaled, occupied_rows, (((0,), (0,)), ((), ())), preferred_element_type=jnp.float32
-            ).astype(jnp.bfloat16),
-            "band",
-            scatter_dimension=0,
-            tiled=True,
-        ).astype(jnp.float32)
-        applied = kinetic + potential_shift * direction + projected.reshape(direction.shape)
-        curvature = grid_sum(inner_product(direction, applied), "grid")
-        step_size = norm_now / curvature
-        solution = solution + expand(step_size) * direction
-        residual = residual - expand(step_size) * applied
-        if iteration + 1 < ITERS:
-            norm_next = grid_sum(inner_product(residual, residual), "grid")
-            direction = residual + expand(norm_next / norm_now) * direction
-            norm_now = norm_next
-    return (solution, residual)
+            ).astype(jnp.bfloat16)
+            projected = terms[:local_bands].astype(jnp.float32)
+            for d in range(1, band_count):
+                part = terms[d * local_bands : (d + 1) * local_bands]
+                back = lax.ppermute(part, "band", [((i + d) % band_count, i) for i in range(band_count)])
+                projected = projected + back.astype(jnp.float32)
+            applied = kinetic_all[span] + potential_shift * current + projected.reshape(current.shape)
+            curvature = grid_sum(inner_product(current, applied), "grid")
+            step_size = norm_now[k] / curvature
+            solution[k] = solution[k] + expand(step_size) * current
+            residual[k] = residual[k] - expand(step_size) * applied
+            if iteration + 1 < ITERS:
+                norm_next = grid_sum(inner_product(residual[k], residual[k]), "grid")
+                direction[k] = residual[k] + expand(norm_next / norm_now[k]) * current
+                norm_now[k] = norm_next
+    return (jnp.concatenate(solution, axis=0), jnp.concatenate(residual, axis=0))
 
 
 def solution(mesh):

time: 241 us -> 216 us (0.90); the launches traced: 238 us -> 216 us
  waiting for transfers between devices: 161 us -> 118 us
  starting transfers between devices: 27 us -> 66.9 us
  between operations: 14 us -> 1.12 us
  other arithmetic: 13.4 us -> 8.82 us
    ppermute x0 -> x24, waiting for transfers between devices: none -> 95.7 us  [the longest x12 48.7 us: body(): lax.ppermute(rounded, 'band', [(i, (i + d) % band_count) for i in range(b...]
    all_gather x2 -> x0, waiting for transfers between devices: 73 us -> none  [body(): lax.all_gather(rounded, 'band', axis=0, tiled=True)]
    reduce_scatter x2 -> x0, waiting for transfers between devices: 56.5 us -> none  [body(): lax.psum_scatter(lax.dot_general(scaled, occupied_rows, (((0,), (0,)), ((...]
    ppermute x0 -> x24, starting transfers between devices: none -> 33.5 us  [the longest x12 18.9 us: body(): lax.ppermute(part, 'band', [((i + d) % band_count, i) for i in range(band...]
    ppermute x18 -> x33, starting transfers between devices: 17.8 us -> 26.5 us  [grid_sum(): value = value + lax.ppermute(value, axis, pairs)]
    ppermute x18 -> x33, waiting for transfers between devices: 28.3 us -> 22.6 us  [grid_sum(): value = value + lax.ppermute(value, axis, pairs)]
    reduce_sum x3 -> x4, other arithmetic: 6.73 us -> 1.52 us  [inner_product(): return jnp.sum(first_field * second_field, axis=(1, 2, 3))]
    mul x0 -> x2, other arithmetic: none -> 3.64 us  [body(): kinetic_all = -0.5 * second_sum(padded, width_x, width_y, width_z)]
  transfers between devices with their start and end apart: 26 -> 61, of which waited for: 22 -> 38; matrix products, arithmetic and copies ran while one was open for 0% -> 11% of each run, Pallas kernels for 0% -> 0%
where the time goes in v10:
time: 216 us
  waiting for transfers between devices  118 us (55%)
  starting transfers between devices  66.9 us (31%)
  matrix products  19.1 us (9%)
  other arithmetic  8.82 us (4%)
    ppermute x12, waiting for transfers between devices, body(): lax.ppermute(rounded, 'band', [(i, (i + d) % band_count) for i in range(b...  48.7 us
    ppermute x12, waiting for transfers between devices, body(): lax.ppermute(part, 'band', [((i + d) % band_count, i) for i in range(band...  47 us
    ppermute x33, starting transfers between devices, grid_sum(): value = value + lax.ppermute(value, axis, pairs)  26.5 us
    ppermute x33, waiting for transfers between devices, grid_sum(): value = value + lax.ppermute(value, axis, pairs)  22.6 us
    ppermute x12, starting transfers between devices, body(): lax.ppermute(part, 'band', [((i + d) % band_count, i) for i in range(band...  18.9 us
    ppermute x12, starting transfers between devices, body(): lax.ppermute(rounded, 'band', [(i, (i + d) % band_count) for i in range(b...  14.6 us
    dot_general x4, matrix products, body(): lax.dot_general(occupied_rows, gathered, (((1,), (1,)), ((), ())), prefer...  11 us
    dot_general x4, matrix products, body(): lax.dot_general(scaled, occupied_rows, (((0,), (0,)), ((), ())), preferre...  8.07 us
  transfers between devices with their start and end apart: 61, of which 38 were waited for; matrix products, arithmetic and copies ran while one was open for 11% of the time, Pallas kernels for 0%

profile of v10, /device:TPU:8, one launch (start us, length us, event | category | flops | bytes accessed | tf_op | source)
XLA Modules:
  0.0 216.0 jit_solution(18381104507843416651)
XLA Ops:
  2.0 3.0 %collective-permute-start.6 = (bf16[8,12288]{1,0:T(8,128)(2,1)S(1)}, bf16[8,12288]{1,0:T(8,128)(2,1)S(1)}, u32[]{:S(2)}, u32[]{:S(2)}) collective-permute-start(bf16[8,12288]{1,0:T(8,128)(2,1)S(1)} %bitcast.90), channel_id=1, source_target_pairs={{0,2},{1,3},{2,0},{3,1},{4,6},{5,7},{6,4},{7,5},{8,10},{9,11},{10,... | collective-permute-start | bytes 589832 | tf_op jit(solution)/shard_map/ppermute | solution.py:98
  5.0 2.5 %collective-permute-start.5 = (bf16[8,12288]{1,0:T(8,128)(2,1)S(1)}, bf16[8,12288]{1,0:T(8,128)(2,1)S(1)}, u32[]{:S(2)}, u32[]{:S(2)}) collective-permute-start(bf16[8,12288]{1,0:T(8,128)(2,1)S(1)} %bitcast.91), channel_id=1, source_target_pairs={{0,1},{1,2},{2,3},{3,0},{4,5},{5,6},{6,7},{7,4},{8,9},{9,10},{10,1... | collective-permute-start | bytes 589832 | tf_op jit(solution)/shard_map/ppermute | solution.py:98
  11.5 7.5 %collective-permute-done.6 = bf16[8,12288]{1,0:T(8,128)(2,1)S(1)} collective-permute-done((bf16[8,12288]{1,0:T(8,128)(2,1)S(1)}, bf16[8,12288]{1,0:T(8,128)(2,1)S(1)}, u32[]{:S(2)}, u32[]{:S(2)}) %collective-permute-start.6) | collective-permute-done | bytes 196640 | tf_op jit(solution)/shard_map/ppermute | solution.py:98
  19.1 11.9 %collective-permute-done.5 = bf16[8,12288]{1,0:T(8,128)(2,1)S(1)} collective-permute-done((bf16[8,12288]{1,0:T(8,128)(2,1)S(1)}, bf16[8,12288]{1,0:T(8,128)(2,1)S(1)}, u32[]{:S(2)}, u32[]{:S(2)}) %collective-permute-start.5) | collective-permute-done | bytes 196640 | tf_op jit(solution)/shard_map/ppermute | solution.py:98
  30.9 4.9 %fusion.12 = f32[256,32]{0,1:T(8,128)S(1)} fusion(bf16[32,8,96,128]{3,2,1,0:T(8,128)(2,1)} %bitcast.59, bf16[8,12288]{1,0:T(8,128)(2,1)S(1)} %collective-permute-done.7, bf16[8,12288]{1,0:T(8,128)(2,1)S(1)} %collective-permute-done.6, bf16[8,12288]{1,0:T(8,128)(2,1)S(1)} %collective-permute-done.5, bf16[8,12288]{1,0:T(8,128)(2,1)S(1)} %bitcast.92), kind=kOutput, calls=%fused_computation.50 | convolution fusion | flops 204472320 | bytes 7110656 | tf_op jit(solution)/shard_map/dot_general | solution.py:102
  36.0 2.5 %collective-permute-done.20 = bf16[8,12288]{1,0:T(8,128)(2,1)S(1)} collective-permute-done((bf16[8,12288]{1,0:T(8,128)(2,1)S(1)}, bf16[8,12288]{1,0:T(8,128)(2,1)S(1)}, u32[]{:S(2)}, u32[]{:S(2)}) %collective-permute-start.20) | collective-permute-done | bytes 196640 | tf_op jit(solution)/shard_map/ppermute | solution.py:98
  38.5 2.0 fusion.15
  40.6 1.6 collective-permute-start.9
  43.9 2.6 %collective-permute-start.1 = (f32[16]{0:T(128)S(1)}, f32[16]{0:T(128)S(1)}, u32[]{:S(2)}, u32[]{:S(2)}) collective-permute-start(f32[16]{0:T(128)S(1)} %add.367), channel_id=1, source_target_pairs={{0,8},{4,12},{8,0},{12,4},{16,24},{20,28},{24,16},{28,20},{1,9},{5... | collective-permute-start | bytes 200 | tf_op jit(solution)/shard_map/ppermute | solution.py:33
  47.8 4.3 %collective-permute-done.1 = f32[16]{0:T(128)S(1)} collective-permute-done((f32[16]{0:T(128)S(1)}, f32[16]{0:T(128)S(1)}, u32[]{:S(2)}, u32[]{:S(2)}) %collective-permute-start.1) | collective-permute-done | bytes 96 | tf_op jit(solution)/shard_map/ppermute | solution.py:33
  55.7 2.0 collective-permute-done.24
  58.9 2.0 convolution_convert_fusion.3
  61.0 2.5 %collective-permute-start.13 = (bf16[8,12288]{1,0:T(8,128)(2,1)S(1)}, bf16[8,12288]{1,0:T(8,128)(2,1)S(1)}, u32[]{:S(2)}, u32[]{:S(2)}) collective-permute-start(bf16[8,12288]{1,0:T(8,128)(2,1)S(1)} %get-tuple-element.47), channel_id=1, source_target_pairs={{3,0},{0,1},{1,2},{2,3},{7,4},{4,5},{5,6},{6,7},{11,8},{8,9},{9,10... | collective-permute-start | bytes 589832 | tf_op jit(solution)/shard_map/ppermute | solution.py:113
  65.1 2.0 convolution_convert_fusion.2
  68.7 3.7 %collective-permute-start.27 = (bf16[8,12288]{1,0:T(8,128)(2,1)S(1)}, bf16[8,12288]{1,0:T(8,128)(2,1)S(1)}, u32[]{:S(2)}, u32[]{:S(2)}) collective-permute-start(bf16[8,12288]{1,0:T(8,128)(2,1)S(1)} %get-tuple-element.53), channel_id=1, source_target_pairs={{2,0},{3,1},{0,2},{1,3},{6,4},{7,5},{4,6},{5,7},{10,8},{11,9},{8,1... | collective-permute-start | bytes 589832 | tf_op jit(solution)/shard_map/ppermute | solution.py:113
  72.6 1.8 fusion.125
  74.4 2.4 %collective-permute-done.13 = bf16[8,12288]{1,0:T(8,128)(2,1)S(1)} collective-permute-done((bf16[8,12288]{1,0:T(8,128)(2,1)S(1)}, bf16[8,12288]{1,0:T(8,128)(2,1)S(1)}, u32[]{:S(2)}, u32[]{:S(2)}) %collective-permute-start.13) | collective-permute-done | bytes 196640 | tf_op jit(solution)/shard_map/ppermute | solution.py:113
  76.9 11.6 %collective-permute-done.12 = bf16[8,12288]{1,0:T(8,128)(2,1)S(1)} collective-permute-done((bf16[8,12288]{1,0:T(8,128)(2,1)S(1)}, bf16[8,12288]{1,0:T(8,128)(2,1)S(1)}, u32[]{:S(2)}, u32[]{:S(2)}) %collective-permute-start.12) | collective-permute-done | bytes 196640 | tf_op jit(solution)/shard_map/ppermute | solution.py:113
  88.6 4.1 %collective-permute-done.28 = bf16[8,12288]{1,0:T(8,128)(2,1)S(1)} collective-permute-done((bf16[8,12288]{1,0:T(8,128)(2,1)S(1)}, bf16[8,12288]{1,0:T(8,128)(2,1)S(1)}, u32[]{:S(2)}, u32[]{:S(2)}) %collective-permute-start.28) | collective-permute-done | bytes 196640 | tf_op jit(solution)/shard_map/ppermute | solution.py:113
  92.7 2.6 %collective-permute-done.27 = bf16[8,12288]{1,0:T(8,128)(2,1)S(1)} collective-permute-done((bf16[8,12288]{1,0:T(8,128)(2,1)S(1)}, bf16[8,12288]{1,0:T(8,128)(2,1)S(1)}, u32[]{:S(2)}, u32[]{:S(2)}) %collective-permute-start.27) | collective-permute-done | bytes 196640 | tf_op jit(solution)/shard_map/ppermute | solution.py:113
  98.1 1.9 collective-permute-start.15
  101.7 1.7 collective-permute-start.16
  105.2 1.9 collective-permute-done.31
  109.1 1.7 collective-permute-start.33
  112.7 1.7 collective-permute-start.34
  116.7 2.2 %collective-permute-start.38 = (bf16[8,12288]{1,0:T(8,128)(2,1)S(1)}, bf16[8,12288]{1,0:T(8,128)(2,1)S(1)}, u32[]{:S(2)}, u32[]{:S(2)}) collective-permute-start(bf16[8,12288]{1,0:T(8,128)(2,1)S(1)} %bitcast.94), channel_id=1, source_target_pairs={{0,2},{1,3},{2,0},{3,1},{4,6},{5,7},{6,4},{7,5},{8,10},{9,11},{10,... | collective-permute-start | bytes 589832 | tf_op jit(solution)/shard_map/ppermute | solution.py:98
  118.9 2.8 %collective-permute-start.37 = (bf16[8,12288]{1,0:T(8,128)(2,1)S(1)}, bf16[8,12288]{1,0:T(8,128)(2,1)S(1)}, u32[]{:S(2)}, u32[]{:S(2)}) collective-permute-start(bf16[8,12288]{1,0:T(8,128)(2,1)S(1)} %bitcast.95), channel_id=1, source_target_pairs={{0,1},{1,2},{2,3},{3,0},{4,5},{5,6},{6,7},{7,4},{8,9},{9,10},{10,1... | collective-permute-start | bytes 589832 | tf_op jit(solution)/shard_map/ppermute | solution.py:98
  123.4 8.4 %collective-permute-done.39 = bf16[8,12288]{1,0:T(8,128)(2,1)S(1)} collective-permute-done((bf16[8,12288]{1,0:T(8,128)(2,1)S(1)}, bf16[8,12288]{1,0:T(8,128)(2,1)S(1)}, u32[]{:S(2)}, u32[]{:S(2)}) %collective-permute-start.39) | collective-permute-done | bytes 196640 | tf_op jit(solution)/shard_map/ppermute | solution.py:98
  131.8 1.5 collective-permute-done.38
  133.3 9.9 %collective-permute-done.37 = bf16[8,12288]{1,0:T(8,128)(2,1)S(1)} collective-permute-done((bf16[8,12288]{1,0:T(8,128)(2,1)S(1)}, bf16[8,12288]{1,0:T(8,128)(2,1)S(1)}, u32[]{:S(2)}, u32[]{:S(2)}) %collective-permute-start.37) | collective-permute-done | bytes 196640 | tf_op jit(solution)/shard_map/ppermute | solution.py:98
  143.3 2.0 fusion.18
  145.3 3.9 %collective-permute-done.51 = bf16[8,12288]{1,0:T(8,128)(2,1)S(1)} collective-permute-done((bf16[8,12288]{1,0:T(8,128)(2,1)S(1)}, bf16[8,12288]{1,0:T(8,128)(2,1)S(1)}, u32[]{:S(2)}, u32[]{:S(2)}) %collective-permute-start.51) | collective-permute-done | bytes 196640 | tf_op jit(solution)/shard_map/ppermute | solution.py:98
  150.7 2.0 fusion.21
  159.6 3.1 %collective-permute-start.35 = (bf16[16,4,24,128]{3,2,1,0:T(8,128)(2,1)S(1)}, bf16[16,4,24,128]{3,2,1,0:T(8,128)(2,1)S(1)}, u32[]{:S(2)}, u32[]{:S(2)}) collective-permute-start(bf16[16,4,24,128]{3,2,1,0:T(8,128)(2,1)S(1)} %pad_maximum_fusion.2), channel_id=1, source_target_pairs={{0,4},{4,8},{8,12},{12,16},{16,20},{20,24},{24,28},{1,5},{5,9},{9,... | collective-permute-start | bytes 1179656 | tf_op jit(solution)/shard_map/ppermute | solution.py:21
  163.3 2.0 convolution_convert_fusion.1
  165.3 2.5 %collective-permute-start.45 = (bf16[8,12288]{1,0:T(8,128)(2,1)S(1)}, bf16[8,12288]{1,0:T(8,128)(2,1)S(1)}, u32[]{:S(2)}, u32[]{:S(2)}) collective-permute-start(bf16[8,12288]{1,0:T(8,128)(2,1)S(1)} %get-tuple-element.42), channel_id=1, source_target_pairs={{3,0},{0,1},{1,2},{2,3},{7,4},{4,5},{5,6},{6,7},{11,8},{8,9},{9,10... | collective-permute-start | bytes 589832 | tf_op jit(solution)/shard_map/ppermute | solution.py:113
  167.9 1.9 collective-permute-start.44
  169.8 2.0 convolution_convert_fusion
  171.9 2.3 %collective-permute-start.57 = (bf16[8,12288]{1,0:T(8,128)(2,1)S(1)}, bf16[8,12288]{1,0:T(8,128)(2,1)S(1)}, u32[]{:S(2)}, u32[]{:S(2)}) collective-permute-start(bf16[8,12288]{1,0:T(8,128)(2,1)S(1)} %get-tuple-element.39), channel_id=1, source_target_pairs={{3,0},{0,1},{1,2},{2,3},{7,4},{4,5},{5,6},{6,7},{11,8},{8,9},{9,10... | collective-permute-start | bytes 589832 | tf_op jit(solution)/shard_map/ppermute | solution.py:113
  174.2 2.8 %collective-permute-start.56 = (bf16[8,12288]{1,0:T(8,128)(2,1)S(1)}, bf16[8,12288]{1,0:T(8,128)(2,1)S(1)}, u32[]{:S(2)}, u32[]{:S(2)}) collective-permute-start(bf16[8,12288]{1,0:T(8,128)(2,1)S(1)} %get-tuple-element.40), channel_id=1, source_target_pairs={{2,0},{3,1},{0,2},{1,3},{6,4},{7,5},{4,6},{5,7},{10,8},{11,9},{8,1... | collective-permute-start | bytes 589832 | tf_op jit(solution)/shard_map/ppermute | solution.py:113
  177.2 1.8 fusion.124
  179.0 2.6 %collective-permute-done.45 = bf16[8,12288]{1,0:T(8,128)(2,1)S(1)} collective-permute-done((bf16[8,12288]{1,0:T(8,128)(2,1)S(1)}, bf16[8,12288]{1,0:T(8,128)(2,1)S(1)}, u32[]{:S(2)}, u32[]{:S(2)}) %collective-permute-start.45) | collective-permute-done | bytes 196640 | tf_op jit(solution)/shard_map/ppermute | solution.py:113
  181.6 12.7 %collective-permute-done.44 = bf16[8,12288]{1,0:T(8,128)(2,1)S(1)} collective-permute-done((bf16[8,12288]{1,0:T(8,128)(2,1)S(1)}, bf16[8,12288]{1,0:T(8,128)(2,1)S(1)}, u32[]{:S(2)}, u32[]{:S(2)}) %collective-permute-start.44) | collective-permute-done | bytes 196640 | tf_op jit(solution)/shard_map/ppermute | solution.py:113
  194.3 1.6 collective-permute-done.43
  195.9 2.5 %collective-permute-done.57 = bf16[8,12288]{1,0:T(8,128)(2,1)S(1)} collective-permute-done((bf16[8,12288]{1,0:T(8,128)(2,1)S(1)}, bf16[8,12288]{1,0:T(8,128)(2,1)S(1)}, u32[]{:S(2)}, u32[]{:S(2)}) %collective-permute-start.57) | collective-permute-done | bytes 196640 | tf_op jit(solution)/shard_map/ppermute | solution.py:113
  198.5 4.1 %collective-permute-done.56 = bf16[8,12288]{1,0:T(8,128)(2,1)S(1)} collective-permute-done((bf16[8,12288]{1,0:T(8,128)(2,1)S(1)}, bf16[8,12288]{1,0:T(8,128)(2,1)S(1)}, u32[]{:S(2)}, u32[]{:S(2)}) %collective-permute-start.56) | collective-permute-done | bytes 196640 | tf_op jit(solution)/shard_map/ppermute | solution.py:113
  202.6 1.6 collective-permute-done.55
  206.2 1.6 collective-permute-start.59
  (151 shorter events, 50.4 us)
Async XLA Ops:
  1.9 8.7 %collective-permute-start.7 = (bf16[8,12288]{1,0:T(8,128)(2,1)S(1)}, bf16[8,12288]{1,0:T(8,128)(2,1)S(1)}, u32[]{:S(2)}, u32[]{:S(2)}) collective-permute-start(bf16[8,12288]{1,0:T(8,128)(2,1)S(1)} %bitcast.89), channel_id=1, source_target_pairs={{0,3},{1,0},{2,1},{3,2},{4,7},{5,4},{6,5},{7,6},{8,11},{9,8},{10,9... | collective-permute-start | bytes 589832 | tf_op jit(solution)/shard_map/ppermute | solution.py:98
  2.0 17.1 %collective-permute-start.6 = (bf16[8,12288]{1,0:T(8,128)(2,1)S(1)}, bf16[8,12288]{1,0:T(8,128)(2,1)S(1)}, u32[]{:S(2)}, u32[]{:S(2)}) collective-permute-start(bf16[8,12288]{1,0:T(8,128)(2,1)S(1)} %bitcast.90), channel_id=1, source_target_pairs={{0,2},{1,3},{2,0},{3,1},{4,6},{5,7},{6,4},{7,5},{8,10},{9,11},{10,... | collective-permute-start | bytes 589832 | tf_op jit(solution)/shard_map/ppermute | solution.py:98
  5.0 25.9 %collective-permute-start.5 = (bf16[8,12288]{1,0:T(8,128)(2,1)S(1)}, bf16[8,12288]{1,0:T(8,128)(2,1)S(1)}, u32[]{:S(2)}, u32[]{:S(2)}) collective-permute-start(bf16[8,12288]{1,0:T(8,128)(2,1)S(1)} %bitcast.91), channel_id=1, source_target_pairs={{0,1},{1,2},{2,3},{3,0},{4,5},{5,6},{6,7},{7,4},{8,9},{9,10},{10,1... | collective-permute-start | bytes 589832 | tf_op jit(solution)/shard_map/ppermute | solution.py:98
  7.6 28.4 %collective-permute-start.22 = (bf16[8,12288]{1,0:T(8,128)(2,1)S(1)}, bf16[8,12288]{1,0:T(8,128)(2,1)S(1)}, u32[]{:S(2)}, u32[]{:S(2)}) collective-permute-start(bf16[8,12288]{1,0:T(8,128)(2,1)S(1)} %bitcast.81), channel_id=1, source_target_pairs={{0,3},{1,0},{2,1},{3,2},{4,7},{5,4},{6,5},{7,6},{8,11},{9,8},{10,9... | collective-permute-start | bytes 589832 | tf_op jit(solution)/shard_map/ppermute | solution.py:98
  7.7 28.3 %collective-permute-start.21 = (bf16[8,12288]{1,0:T(8,128)(2,1)S(1)}, bf16[8,12288]{1,0:T(8,128)(2,1)S(1)}, u32[]{:S(2)}, u32[]{:S(2)}) collective-permute-start(bf16[8,12288]{1,0:T(8,128)(2,1)S(1)} %bitcast.82), channel_id=1, source_target_pairs={{0,2},{1,3},{2,0},{3,1},{4,6},{5,7},{6,4},{7,5},{8,10},{9,11},{10,... | collective-permute-start | bytes 589832 | tf_op jit(solution)/shard_map/ppermute | solution.py:98
  10.6 27.8 %collective-permute-start.20 = (bf16[8,12288]{1,0:T(8,128)(2,1)S(1)}, bf16[8,12288]{1,0:T(8,128)(2,1)S(1)}, u32[]{:S(2)}, u32[]{:S(2)}) collective-permute-start(bf16[8,12288]{1,0:T(8,128)(2,1)S(1)} %bitcast.83), channel_id=1, source_target_pairs={{0,1},{1,2},{2,3},{3,0},{4,5},{5,6},{6,7},{7,4},{8,9},{9,10},{10,1... | collective-permute-start | bytes 589832 | tf_op jit(solution)/shard_map/ppermute | solution.py:98
  35.9 4.6 %collective-permute-start.8 = (f32[256,32]{0,1:T(8,128)S(1)}, f32[256,32]{0,1:T(8,128)S(1)}, u32[]{:S(2)}, u32[]{:S(2)}) collective-permute-start(f32[256,32]{0,1:T(8,128)S(1)} %fusion.12), channel_id=1, source_target_pairs={{0,4},{4,0},{8,12},{12,8},{16,20},{20,16},{24,28},{28,24},{1,5},{5... | collective-permute-start | bytes 98312 | tf_op jit(solution)/shard_map/ppermute | solution.py:33
  40.5 13.2 %collective-permute-start.23 = (f32[256,32]{0,1:T(8,128)S(1)}, f32[256,32]{0,1:T(8,128)S(1)}, u32[]{:S(2)}, u32[]{:S(2)}) collective-permute-start(f32[256,32]{0,1:T(8,128)S(1)} %fusion.15), channel_id=1, source_target_pairs={{0,4},{4,0},{8,12},{12,8},{16,20},{20,16},{24,28},{28,24},{1,5},{5... | collective-permute-start | bytes 98312 | tf_op jit(solution)/shard_map/ppermute | solution.py:33
  40.6 14.4 %collective-permute-start.9 = (f32[256,32]{0,1:T(8,128)S(1)}, f32[256,32]{0,1:T(8,128)S(1)}, u32[]{:S(2)}, u32[]{:S(2)}) collective-permute-start(f32[256,32]{0,1:T(8,128)S(1)} %add.398), channel_id=1, source_target_pairs={{0,8},{4,12},{8,0},{12,4},{16,24},{20,28},{24,16},{28,20},{1,9},{5... | collective-permute-start | bytes 98312 | tf_op jit(solution)/shard_map/ppermute | solution.py:33
  42.6 24.5 %collective-permute-start.4 = (bf16[16,4,24,128]{3,2,1,0:T(8,128)(2,1)S(1)}, bf16[16,4,24,128]{3,2,1,0:T(8,128)(2,1)S(1)}, u32[]{:S(2)}, u32[]{:S(2)}) collective-permute-start(bf16[16,4,24,128]{3,2,1,0:T(8,128)(2,1)S(1)} %get-tuple-element.45), channel_id=1, source_target_pairs={{4,0},{8,4},{12,8},{16,12},{20,16},{24,20},{28,24},{5,1},{9,5},{13... | collective-permute-start | bytes 1179656 | tf_op jit(solution)/shard_map/ppermute | solution.py:22
  43.9 8.2 %collective-permute-start.1 = (f32[16]{0:T(128)S(1)}, f32[16]{0:T(128)S(1)}, u32[]{:S(2)}, u32[]{:S(2)}) collective-permute-start(f32[16]{0:T(128)S(1)} %add.367), channel_id=1, source_target_pairs={{0,8},{4,12},{8,0},{12,4},{16,24},{20,28},{24,16},{28,20},{1,9},{5... | collective-permute-start | bytes 200 | tf_op jit(solution)/shard_map/ppermute | solution.py:33
  46.5 22.2 %collective-permute-start.3 = (bf16[16,4,24,128]{3,2,1,0:T(8,128)(2,1)S(1)}, bf16[16,4,24,128]{3,2,1,0:T(8,128)(2,1)S(1)}, u32[]{:S(2)}, u32[]{:S(2)}) collective-permute-start(bf16[16,4,24,128]{3,2,1,0:T(8,128)(2,1)S(1)} %get-tuple-element.45), channel_id=1, source_target_pairs={{0,4},{4,8},{8,12},{12,16},{16,20},{20,24},{24,28},{1,5},{5,9},{9,... | collective-permute-start | bytes 1179656 | tf_op jit(solution)/shard_map/ppermute | solution.py:21
  52.1 3.5 %collective-permute-start.2 = (f32[16]{0:T(128)S(1)}, f32[16]{0:T(128)S(1)}, u32[]{:S(2)}, u32[]{:S(2)}) collective-permute-start(f32[16]{0:T(128)S(1)} %add.368), channel_id=1, source_target_pairs={{0,16},{4,20},{8,24},{12,28},{16,0},{20,4},{24,8},{28,12},{1,17},{... | collective-permute-start | bytes 200 | tf_op jit(solution)/shard_map/ppermute | solution.py:33
  53.7 4.0 %collective-permute-start.24 = (f32[256,32]{0,1:T(8,128)S(1)}, f32[256,32]{0,1:T(8,128)S(1)}, u32[]{:S(2)}, u32[]{:S(2)}) collective-permute-start(f32[256,32]{0,1:T(8,128)S(1)} %add.416), channel_id=1, source_target_pairs={{0,8},{4,12},{8,0},{12,4},{16,24},{20,28},{24,16},{28,20},{1,9},{5... | collective-permute-start | bytes 98312 | tf_op jit(solution)/shard_map/ppermute | solution.py:33
  54.9 4.0 %collective-permute-start.10 = (f32[256,32]{0,1:T(8,128)S(1)}, f32[256,32]{0,1:T(8,128)S(1)}, u32[]{:S(2)}, u32[]{:S(2)}) collective-permute-start(f32[256,32]{0,1:T(8,128)S(1)} %add.399), channel_id=1, source_target_pairs={{0,16},{4,20},{8,24},{12,28},{16,0},{20,4},{24,8},{28,12},{1,17},{... | collective-permute-start | bytes 98312 | tf_op jit(solution)/shard_map/ppermute | solution.py:33
  57.7 6.9 %collective-permute-start.25 = (f32[256,32]{0,1:T(8,128)S(1)}, f32[256,32]{0,1:T(8,128)S(1)}, u32[]{:S(2)}, u32[]{:S(2)}) collective-permute-start(f32[256,32]{0,1:T(8,128)S(1)} %add.417), channel_id=1, source_target_pairs={{0,16},{4,20},{8,24},{12,28},{16,0},{20,4},{24,8},{28,12},{1,17},{... | collective-permute-start | bytes 98312 | tf_op jit(solution)/shard_map/ppermute | solution.py:33
  61.0 15.9 %collective-permute-start.13 = (bf16[8,12288]{1,0:T(8,128)(2,1)S(1)}, bf16[8,12288]{1,0:T(8,128)(2,1)S(1)}, u32[]{:S(2)}, u32[]{:S(2)}) collective-permute-start(bf16[8,12288]{1,0:T(8,128)(2,1)S(1)} %get-tuple-element.47), channel_id=1, source_target_pairs={{3,0},{0,1},{1,2},{2,3},{7,4},{4,5},{5,6},{6,7},{11,8},{8,9},{9,10... | collective-permute-start | bytes 589832 | tf_op jit(solution)/shard_map/ppermute | solution.py:113
  63.5 24.9 %collective-permute-start.12 = (bf16[8,12288]{1,0:T(8,128)(2,1)S(1)}, bf16[8,12288]{1,0:T(8,128)(2,1)S(1)}, u32[]{:S(2)}, u32[]{:S(2)}) collective-permute-start(bf16[8,12288]{1,0:T(8,128)(2,1)S(1)} %get-tuple-element.48), channel_id=1, source_target_pairs={{2,0},{3,1},{0,2},{1,3},{6,4},{7,5},{4,6},{5,7},{10,8},{11,9},{8,1... | collective-permute-start | bytes 589832 | tf_op jit(solution)/shard_map/ppermute | solution.py:113
  64.5 23.9 %collective-permute-start.11 = (bf16[8,12288]{1,0:T(8,128)(2,1)S(1)}, bf16[8,12288]{1,0:T(8,128)(2,1)S(1)}, u32[]{:S(2)}, u32[]{:S(2)}) collective-permute-start(bf16[8,12288]{1,0:T(8,128)(2,1)S(1)} %get-tuple-element.46), channel_id=1, source_target_pairs={{1,0},{2,1},{3,2},{0,3},{5,4},{6,5},{7,6},{4,7},{9,8},{10,9},{11,1... | collective-permute-start | bytes 589832 | tf_op jit(solution)/shard_map/ppermute | solution.py:113
  67.1 25.5 %collective-permute-start.28 = (bf16[8,12288]{1,0:T(8,128)(2,1)S(1)}, bf16[8,12288]{1,0:T(8,128)(2,1)S(1)}, u32[]{:S(2)}, u32[]{:S(2)}) collective-permute-start(bf16[8,12288]{1,0:T(8,128)(2,1)S(1)} %get-tuple-element.52), channel_id=1, source_target_pairs={{3,0},{0,1},{1,2},{2,3},{7,4},{4,5},{5,6},{6,7},{11,8},{8,9},{9,10... | collective-permute-start | bytes 589832 | tf_op jit(solution)/shard_map/ppermute | solution.py:113
  68.7 26.5 %collective-permute-start.27 = (bf16[8,12288]{1,0:T(8,128)(2,1)S(1)}, bf16[8,12288]{1,0:T(8,128)(2,1)S(1)}, u32[]{:S(2)}, u32[]{:S(2)}) collective-permute-start(bf16[8,12288]{1,0:T(8,128)(2,1)S(1)} %get-tuple-element.53), channel_id=1, source_target_pairs={{2,0},{3,1},{0,2},{1,3},{6,4},{7,5},{4,6},{5,7},{10,8},{11,9},{8,1... | collective-permute-start | bytes 589832 | tf_op jit(solution)/shard_map/ppermute | solution.py:113
  76.9 19.6 %collective-permute-start.26 = (bf16[8,12288]{1,0:T(8,128)(2,1)S(1)}, bf16[8,12288]{1,0:T(8,128)(2,1)S(1)}, u32[]{:S(2)}, u32[]{:S(2)}) collective-permute-start(bf16[8,12288]{1,0:T(8,128)(2,1)S(1)} %get-tuple-element.51), channel_id=1, source_target_pairs={{1,0},{2,1},{3,2},{0,3},{5,4},{6,5},{7,6},{4,7},{9,8},{10,9},{11,1... | collective-permute-start | bytes 589832 | tf_op jit(solution)/shard_map/ppermute | solution.py:113
  98.1 3.5 %collective-permute-start.15 = (f32[8]{0:T(128)S(1)}, f32[8]{0:T(128)S(1)}, u32[]{:S(2)}, u32[]{:S(2)}) collective-permute-start(f32[8]{0:T(128)S(1)} %add.405), channel_id=1, source_target_pairs={{0,8},{4,12},{8,0},{12,4},{16,24},{20,28},{24,16},{28,20},{1,9},{5... | collective-permute-start | bytes 104 | tf_op jit(solution)/shard_map/ppermute | solution.py:33
  100.0 3.5 %collective-permute-start.30 = (f32[8]{0:T(128)S(1)}, f32[8]{0:T(128)S(1)}, u32[]{:S(2)}, u32[]{:S(2)}) collective-permute-start(f32[8]{0:T(128)S(1)} %add.423), channel_id=1, source_target_pairs={{0,8},{4,12},{8,0},{12,4},{16,24},{20,28},{24,16},{28,20},{1,9},{5... | collective-permute-start | bytes 104 | tf_op jit(solution)/shard_map/ppermute | solution.py:33
  101.7 3.5 %collective-permute-start.16 = (f32[8]{0:T(128)S(1)}, f32[8]{0:T(128)S(1)}, u32[]{:S(2)}, u32[]{:S(2)}) collective-permute-start(f32[8]{0:T(128)S(1)} %add.406), channel_id=1, source_target_pairs={{0,16},{4,20},{8,24},{12,28},{16,0},{20,4},{24,8},{28,12},{1,17},{... | collective-permute-start | bytes 104 | tf_op jit(solution)/shard_map/ppermute | solution.py:33
  109.1 3.5 %collective-permute-start.33 = (f32[8]{0:T(128)S(1)}, f32[8]{0:T(128)S(1)}, u32[]{:S(2)}, u32[]{:S(2)}) collective-permute-start(f32[8]{0:T(128)S(1)} %add.426), channel_id=1, source_target_pairs={{0,8},{4,12},{8,0},{12,4},{16,24},{20,28},{24,16},{28,20},{1,9},{5... | collective-permute-start | bytes 104 | tf_op jit(solution)/shard_map/ppermute | solution.py:33
  116.6 15.2 %collective-permute-start.39 = (bf16[8,12288]{1,0:T(8,128)(2,1)S(1)}, bf16[8,12288]{1,0:T(8,128)(2,1)S(1)}, u32[]{:S(2)}, u32[]{:S(2)}) collective-permute-start(bf16[8,12288]{1,0:T(8,128)(2,1)S(1)} %bitcast.93), channel_id=1, source_target_pairs={{0,3},{1,0},{2,1},{3,2},{4,7},{5,4},{6,5},{7,6},{8,11},{9,8},{10,9... | collective-permute-start | bytes 589832 | tf_op jit(solution)/shard_map/ppermute | solution.py:98
  116.7 16.7 %collective-permute-start.38 = (bf16[8,12288]{1,0:T(8,128)(2,1)S(1)}, bf16[8,12288]{1,0:T(8,128)(2,1)S(1)}, u32[]{:S(2)}, u32[]{:S(2)}) collective-permute-start(bf16[8,12288]{1,0:T(8,128)(2,1)S(1)} %bitcast.94), channel_id=1, source_target_pairs={{0,2},{1,3},{2,0},{3,1},{4,6},{5,7},{6,4},{7,5},{8,10},{9,11},{10,... | collective-permute-start | bytes 589832 | tf_op jit(solution)/shard_map/ppermute | solution.py:98
  118.9 24.4 %collective-permute-start.37 = (bf16[8,12288]{1,0:T(8,128)(2,1)S(1)}, bf16[8,12288]{1,0:T(8,128)(2,1)S(1)}, u32[]{:S(2)}, u32[]{:S(2)}) collective-permute-start(bf16[8,12288]{1,0:T(8,128)(2,1)S(1)} %bitcast.95), channel_id=1, source_target_pairs={{0,1},{1,2},{2,3},{3,0},{4,5},{5,6},{6,7},{7,4},{8,9},{9,10},{10,1... | collective-permute-start | bytes 589832 | tf_op jit(solution)/shard_map/ppermute | solution.py:98
  121.9 27.3 %collective-permute-start.51 = (bf16[8,12288]{1,0:T(8,128)(2,1)S(1)}, bf16[8,12288]{1,0:T(8,128)(2,1)S(1)}, u32[]{:S(2)}, u32[]{:S(2)}) collective-permute-start(bf16[8,12288]{1,0:T(8,128)(2,1)S(1)} %bitcast.85), channel_id=1, source_target_pairs={{0,3},{1,0},{2,1},{3,2},{4,7},{5,4},{6,5},{7,6},{8,11},{9,8},{10,9... | collective-permute-start | bytes 589832 | tf_op jit(solution)/shard_map/ppermute | solution.py:98
  121.9 27.3 %collective-permute-start.50 = (bf16[8,12288]{1,0:T(8,128)(2,1)S(1)}, bf16[8,12288]{1,0:T(8,128)(2,1)S(1)}, u32[]{:S(2)}, u32[]{:S(2)}) collective-permute-start(bf16[8,12288]{1,0:T(8,128)(2,1)S(1)} %bitcast.86), channel_id=1, source_target_pairs={{0,2},{1,3},{2,0},{3,1},{4,6},{5,7},{6,4},{7,5},{8,10},{9,11},{10,... | collective-permute-start | bytes 589832 | tf_op jit(solution)/shard_map/ppermute | solution.py:98
  131.8 18.9 %collective-permute-start.49 = (bf16[8,12288]{1,0:T(8,128)(2,1)S(1)}, bf16[8,12288]{1,0:T(8,128)(2,1)S(1)}, u32[]{:S(2)}, u32[]{:S(2)}) collective-permute-start(bf16[8,12288]{1,0:T(8,128)(2,1)S(1)} %bitcast.87), channel_id=1, source_target_pairs={{0,1},{1,2},{2,3},{3,0},{4,5},{5,6},{6,7},{7,4},{8,9},{9,10},{10,1... | collective-permute-start | bytes 589832 | tf_op jit(solution)/shard_map/ppermute | solution.py:98
  145.3 7.5 %collective-permute-start.40 = (f32[256,32]{0,1:T(8,128)S(1)}, f32[256,32]{0,1:T(8,128)S(1)}, u32[]{:S(2)}, u32[]{:S(2)}) collective-permute-start(f32[256,32]{0,1:T(8,128)S(1)} %fusion.18), channel_id=1, source_target_pairs={{0,4},{4,0},{8,12},{12,8},{16,20},{20,16},{24,28},{28,24},{1,5},{5... | collective-permute-start | bytes 98312 | tf_op jit(solution)/shard_map/ppermute | solution.py:33
  152.8 4.0 %collective-permute-start.41 = (f32[256,32]{0,1:T(8,128)S(1)}, f32[256,32]{0,1:T(8,128)S(1)}, u32[]{:S(2)}, u32[]{:S(2)}) collective-permute-start(f32[256,32]{0,1:T(8,128)S(1)} %add.457), channel_id=1, source_target_pairs={{0,8},{4,12},{8,0},{12,4},{16,24},{20,28},{24,16},{28,20},{1,9},{5... | collective-permute-start | bytes 98312 | tf_op jit(solution)/shard_map/ppermute | solution.py:33
  154.3 8.4 %collective-permute-start.53 = (f32[256,32]{0,1:T(8,128)S(1)}, f32[256,32]{0,1:T(8,128)S(1)}, u32[]{:S(2)}, u32[]{:S(2)}) collective-permute-start(f32[256,32]{0,1:T(8,128)S(1)} %add.471), channel_id=1, source_target_pairs={{0,8},{4,12},{8,0},{12,4},{16,24},{20,28},{24,16},{28,20},{1,9},{5... | collective-permute-start | bytes 98312 | tf_op jit(solution)/shard_map/ppermute | solution.py:33
  156.8 6.5 %collective-permute-start.42 = (f32[256,32]{0,1:T(8,128)S(1)}, f32[256,32]{0,1:T(8,128)S(1)}, u32[]{:S(2)}, u32[]{:S(2)}) collective-permute-start(f32[256,32]{0,1:T(8,128)S(1)} %add.458), channel_id=1, source_target_pairs={{0,16},{4,20},{8,24},{12,28},{16,0},{20,4},{24,8},{28,12},{1,17},{... | collective-permute-start | bytes 98312 | tf_op jit(solution)/shard_map/ppermute | solution.py:33
  158.3 13.6 %collective-permute-start.36 = (bf16[16,4,24,128]{3,2,1,0:T(8,128)(2,1)S(1)}, bf16[16,4,24,128]{3,2,1,0:T(8,128)(2,1)S(1)}, u32[]{:S(2)}, u32[]{:S(2)}) collective-permute-start(bf16[16,4,24,128]{3,2,1,0:T(8,128)(2,1)S(1)} %pad_maximum_fusion.2), channel_id=1, source_target_pairs={{4,0},{8,4},{12,8},{16,12},{20,16},{24,20},{28,24},{5,1},{9,5},{13... | collective-permute-start | bytes 1179656 | tf_op jit(solution)/shard_map/ppermute | solution.py:22
  159.6 14.6 %collective-permute-start.35 = (bf16[16,4,24,128]{3,2,1,0:T(8,128)(2,1)S(1)}, bf16[16,4,24,128]{3,2,1,0:T(8,128)(2,1)S(1)}, u32[]{:S(2)}, u32[]{:S(2)}) collective-permute-start(bf16[16,4,24,128]{3,2,1,0:T(8,128)(2,1)S(1)} %pad_maximum_fusion.2), channel_id=1, source_target_pairs={{0,4},{4,8},{8,12},{12,16},{16,20},{20,24},{24,28},{1,5},{5,9},{9,... | collective-permute-start | bytes 1179656 | tf_op jit(solution)/shard_map/ppermute | solution.py:21
  162.7 7.1 %collective-permute-start.54 = (f32[256,32]{0,1:T(8,128)S(1)}, f32[256,32]{0,1:T(8,128)S(1)}, u32[]{:S(2)}, u32[]{:S(2)}) collective-permute-start(f32[256,32]{0,1:T(8,128)S(1)} %add.472), channel_id=1, source_target_pairs={{0,16},{4,20},{8,24},{12,28},{16,0},{20,4},{24,8},{28,12},{1,17},{... | collective-permute-start | bytes 98312 | tf_op jit(solution)/shard_map/ppermute | solution.py:33
  165.3 16.3 %collective-permute-start.45 = (bf16[8,12288]{1,0:T(8,128)(2,1)S(1)}, bf16[8,12288]{1,0:T(8,128)(2,1)S(1)}, u32[]{:S(2)}, u32[]{:S(2)}) collective-permute-start(bf16[8,12288]{1,0:T(8,128)(2,1)S(1)} %get-tuple-element.42), channel_id=1, source_target_pairs={{3,0},{0,1},{1,2},{2,3},{7,4},{4,5},{5,6},{6,7},{11,8},{8,9},{9,10... | collective-permute-start | bytes 589832 | tf_op jit(solution)/shard_map/ppermute | solution.py:113
  167.9 26.4 %collective-permute-start.44 = (bf16[8,12288]{1,0:T(8,128)(2,1)S(1)}, bf16[8,12288]{1,0:T(8,128)(2,1)S(1)}, u32[]{:S(2)}, u32[]{:S(2)}) collective-permute-start(bf16[8,12288]{1,0:T(8,128)(2,1)S(1)} %get-tuple-element.43), channel_id=1, source_target_pairs={{2,0},{3,1},{0,2},{1,3},{6,4},{7,5},{4,6},{5,7},{10,8},{11,9},{8,1... | collective-permute-start | bytes 589832 | tf_op jit(solution)/shard_map/ppermute | solution.py:113
  169.8 26.0 %collective-permute-start.43 = (bf16[8,12288]{1,0:T(8,128)(2,1)S(1)}, bf16[8,12288]{1,0:T(8,128)(2,1)S(1)}, u32[]{:S(2)}, u32[]{:S(2)}) collective-permute-start(bf16[8,12288]{1,0:T(8,128)(2,1)S(1)} %get-tuple-element.41), channel_id=1, source_target_pairs={{1,0},{2,1},{3,2},{0,3},{5,4},{6,5},{7,6},{4,7},{9,8},{10,9},{11,1... | collective-permute-start | bytes 589832 | tf_op jit(solution)/shard_map/ppermute | solution.py:113
  171.9 26.6 %collective-permute-start.57 = (bf16[8,12288]{1,0:T(8,128)(2,1)S(1)}, bf16[8,12288]{1,0:T(8,128)(2,1)S(1)}, u32[]{:S(2)}, u32[]{:S(2)}) collective-permute-start(bf16[8,12288]{1,0:T(8,128)(2,1)S(1)} %get-tuple-element.39), channel_id=1, source_target_pairs={{3,0},{0,1},{1,2},{2,3},{7,4},{4,5},{5,6},{6,7},{11,8},{8,9},{9,10... | collective-permute-start | bytes 589832 | tf_op jit(solution)/shard_map/ppermute | solution.py:113
  174.2 28.4 %collective-permute-start.56 = (bf16[8,12288]{1,0:T(8,128)(2,1)S(1)}, bf16[8,12288]{1,0:T(8,128)(2,1)S(1)}, u32[]{:S(2)}, u32[]{:S(2)}) collective-permute-start(bf16[8,12288]{1,0:T(8,128)(2,1)S(1)} %get-tuple-element.40), channel_id=1, source_target_pairs={{2,0},{3,1},{0,2},{1,3},{6,4},{7,5},{4,6},{5,7},{10,8},{11,9},{8,1... | collective-permute-start | bytes 589832 | tf_op jit(solution)/shard_map/ppermute | solution.py:113
  181.6 22.5 %collective-permute-start.55 = (bf16[8,12288]{1,0:T(8,128)(2,1)S(1)}, bf16[8,12288]{1,0:T(8,128)(2,1)S(1)}, u32[]{:S(2)}, u32[]{:S(2)}) collective-permute-start(bf16[8,12288]{1,0:T(8,128)(2,1)S(1)} %get-tuple-element.38), channel_id=1, source_target_pairs={{1,0},{2,1},{3,2},{0,3},{5,4},{6,5},{7,6},{4,7},{9,8},{10,9},{11,1... | collective-permute-start | bytes 589832 | tf_op jit(solution)/shard_map/ppermute | solution.py:113
  205.8 3.5 %collective-permute-start.47 = (f32[8]{0:T(128)S(1)}, f32[8]{0:T(128)S(1)}, u32[]{:S(2)}, u32[]{:S(2)}) collective-permute-start(f32[8]{0:T(128)S(1)} %add.464), channel_id=1, source_target_pairs={{0,8},{4,12},{8,0},{12,4},{16,24},{20,28},{24,16},{28,20},{1,9},{5... | collective-permute-start | bytes 104 | tf_op jit(solution)/shard_map/ppermute | solution.py:33
  206.2 3.8 %collective-permute-start.59 = (f32[8]{0:T(128)S(1)}, f32[8]{0:T(128)S(1)}, u32[]{:S(2)}, u32[]{:S(2)}) collective-permute-start(f32[8]{0:T(128)S(1)} %add.478), channel_id=1, source_target_pairs={{0,8},{4,12},{8,0},{12,4},{16,24},{20,28},{24,16},{28,20},{1,9},{5... | collective-permute-start | bytes 104 | tf_op jit(solution)/shard_map/ppermute | solution.py:33
  210.0 3.5 %collective-permute-start.60 = (f32[8]{0:T(128)S(1)}, f32[8]{0:T(128)S(1)}, u32[]{:S(2)}, u32[]{:S(2)}) collective-permute-start(f32[8]{0:T(128)S(1)} %add.479), channel_id=1, source_target_pairs={{0,16},{4,20},{8,24},{12,28},{16,0},{20,4},{24,8},{28,12},{1,17},{... | collective-permute-start | bytes 104 | tf_op jit(solution)/shard_map/ppermute | solution.py:33
  (18 other events, 122.0 us)

commit v11 on v6

--- a/solution.py
+++ b/solution.py
@@ -90,10 +90,12 @@
         padded = jnp.pad(padded, ((0, 0), (0, 0), (4, 4), (4, 4)))
         kinetic = -0.5 * second_sum(padded, width_x, width_y, width_z)
         rounded = direction.astype(jnp.bfloat16).reshape(local_bands, local_cells)
-        blocks = [rounded] + [
-            lax.ppermute(rounded, "band", [(i, (i + d) % band_count) for i in range(band_count)])
-            for d in range(1, band_count)
-        ]
+        order = sorted(range(1, band_count), key=lambda d: (min(d, band_count - d), -d))
+        arrived = {
+            d: lax.ppermute(rounded, "band", [(i, (i + d) % band_count) for i in range(band_count)])
+            for d in order
+        }
+        blocks = [rounded] + [arrived[d] for d in range(1, band_count)]
         gathered = jnp.concatenate(blocks, axis=0)
         partial_margin = lax.dot_general(
             occupied_rows, gathered, (((1,), (1,)), ((), ())), preferred_element_type=jnp.float32
@@ -104,7 +106,7 @@
             scaled, occupied_rows, (((0,), (0,)), ((), ())), preferred_element_type=jnp.float32
         ).astype(jnp.bfloat16)
         projected = terms[:local_bands].astype(jnp.float32)
-        for d in range(1, band_count):
+        for d in order:
             part = terms[d * local_bands : (d + 1) * local_bands]
             back = lax.ppermute(part, "band", [((i + d) % band_count, i) for i in range(band_count)])
             projected = projected + back.astype(jnp.float32)

time: 212 us -> 211 us (level)
  starting transfers between devices: 96 us -> 90.4 us
  waiting for transfers between devices: 85.4 us -> 89.3 us
    ppermute x12, starting transfers between devices: 26.3 us -> 19.9 us  [chain(): lax.ppermute(rounded, 'band', [(i, (i + d) % band_count) for i in range(b...]
    ppermute x12, waiting for transfers between devices: 17.9 us -> 22.7 us  [chain(): lax.ppermute(rounded, 'band', [(i, (i + d) % band_count) for i in range(b...]
  transfers between devices with their start and end apart: 68 -> 68, of which waited for: 36 -> 33; matrix products, arithmetic and copies ran while one was open for 12% -> 12% of each run, Pallas kernels for 0% -> 0%
where the time goes in v11:
time: 211 us; the launch traced here: 210 us
  starting transfers between devices  90.4 us (43%)
  waiting for transfers between devices  89.3 us (42%)
  matrix products  19.1 us (9%)
  other arithmetic  9.7 us (5%)
    ppermute x12, waiting for transfers between devices, chain(): lax.ppermute(part, 'band', [((i + d) % band_count, i) for i in range(band...  43.5 us
    ppermute x36, starting transfers between devices, grid_sum(): value = value + lax.ppermute(value, axis, pairs)  33 us
    ppermute x36, waiting for transfers between devices, grid_sum(): value = value + lax.ppermute(value, axis, pairs)  23.1 us
    ppermute x12, waiting for transfers between devices, chain(): lax.ppermute(rounded, 'band', [(i, (i + d) % band_count) for i in range(b...  22.7 us
    ppermute x12, starting transfers between devices, chain(): lax.ppermute(part, 'band', [((i + d) % band_count, i) for i in range(band...  20.2 us
    ppermute x12, starting transfers between devices, chain(): lax.ppermute(rounded, 'band', [(i, (i + d) % band_count) for i in range(b...  19.9 us
    ppermute x4, starting transfers between devices, with_halo(): before = lax.ppermute(last, axis, up)  12.1 us
    dot_general x4, matrix products, chain(): lax.dot_general(occupied_rows, gathered, (((1,), (1,)), ((), ())), prefer...  11 us
  transfers between devices with their start and end apart: 68, of which 33 were waited for; matrix products, arithmetic and copies ran while one was open for 12% of the time, Pallas kernels for 0%

profile of v11, /device:TPU:8, one launch (start us, length us, event | category | flops | bytes accessed | tf_op | source)
XLA Modules:
  0.0 210.3 jit_solution(15688238946014728930)
XLA Ops:
  2.1 3.0 %collective-permute-start.40 = (bf16[8,12288]{1,0:T(8,128)(2,1)S(1)}, bf16[8,12288]{1,0:T(8,128)(2,1)S(1)}, u32[]{:S(2)}, u32[]{:S(2)}) collective-permute-start(bf16[8,12288]{1,0:T(8,128)(2,1)S(1)} %bitcast.82), channel_id=1, source_target_pairs={{0,2},{1,3},{2,0},{3,1},{4,6},{5,7},{6,4},{7,5},{8,10},{9,11},{10,... | collective-permute-start | bytes 589832 | tf_op jit(solution)/shard_map/ppermute | solution.py:95
  5.2 2.5 %collective-permute-start.39 = (bf16[8,12288]{1,0:T(8,128)(2,1)S(1)}, bf16[8,12288]{1,0:T(8,128)(2,1)S(1)}, u32[]{:S(2)}, u32[]{:S(2)}) collective-permute-start(bf16[8,12288]{1,0:T(8,128)(2,1)S(1)} %bitcast.83), channel_id=1, source_target_pairs={{0,1},{1,2},{2,3},{3,0},{4,5},{5,6},{6,7},{7,4},{8,9},{9,10},{10,1... | collective-permute-start | bytes 589832 | tf_op jit(solution)/shard_map/ppermute | solution.py:95
  10.1 1.5 collective-permute-start.35
  11.6 2.0 collective-permute-done.35
  13.7 1.5 collective-permute-start.1
  15.2 2.0 collective-permute-done.1
  18.6 2.4 %collective-permute-start.5 = (bf16[8,12288]{1,0:T(8,128)(2,1)S(1)}, bf16[8,12288]{1,0:T(8,128)(2,1)S(1)}, u32[]{:S(2)}, u32[]{:S(2)}) collective-permute-start(bf16[8,12288]{1,0:T(8,128)(2,1)S(1)} %bitcast.79), channel_id=1, source_target_pairs={{0,1},{1,2},{2,3},{3,0},{4,5},{5,6},{6,7},{7,4},{8,9},{9,10},{10,1... | collective-permute-start | bytes 589832 | tf_op jit(solution)/shard_map/ppermute | solution.py:95
  22.3 8.8 %collective-permute-done.39 = bf16[8,12288]{1,0:T(8,128)(2,1)S(1)} collective-permute-done((bf16[8,12288]{1,0:T(8,128)(2,1)S(1)}, bf16[8,12288]{1,0:T(8,128)(2,1)S(1)}, u32[]{:S(2)}, u32[]{:S(2)}) %collective-permute-start.39) | collective-permute-done | bytes 196640 | tf_op jit(solution)/shard_map/ppermute | solution.py:95
  32.3 5.0 %fusion.18 = f32[256,32]{0,1:T(8,128)S(1)} fusion(bf16[32,8,96,128]{3,2,1,0:T(8,128)(2,1)} %bitcast.59, bf16[8,12288]{1,0:T(8,128)(2,1)S(1)} %collective-permute-done.41, bf16[8,12288]{1,0:T(8,128)(2,1)S(1)} %collective-permute-done.40, bf16[8,12288]{1,0:T(8,128)(2,1)S(1)} %collective-permute-done.39, bf16[8,12288]{1,0:T(8,128)(2,1)S(1)} %bitcast.84), kind=kOutput, calls=%fused_computation.82 | convolution fusion | flops 204472320 | bytes 7110656 | tf_op jit(solution)/shard_map/dot_general | solution.py:100
  38.7 4.8 %collective-permute-start.37 = (bf16[8,4,24,128]{3,2,1,0:T(8,128)(2,1)S(1)}, bf16[8,4,24,128]{3,2,1,0:T(8,128)(2,1)S(1)}, u32[]{:S(2)}, u32[]{:S(2)}) collective-permute-start(bf16[8,4,24,128]{3,2,1,0:T(8,128)(2,1)S(1)} %convert_element_type.121), channel_id=1, source_target_pairs={{0,4},{4,8},{8,12},{12,16},{16,20},{20,24},{24,28},{1,5},{5,9},{9,... | collective-permute-start | bytes 589832 | tf_op jit(solution)/shard_map/ppermute | solution.py:21
  43.4 1.8 collective-permute-start.42
  45.2 2.0 fusion.12
  47.3 1.6 collective-permute-start.36
  50.1 1.9 collective-permute-start.2
  53.8 2.1 collective-permute-start.44
  58.1 2.0 convolution_convert_fusion.1
  60.3 3.9 %collective-permute-start.46 = (bf16[8,12288]{1,0:T(8,128)(2,1)S(1)}, bf16[8,12288]{1,0:T(8,128)(2,1)S(1)}, u32[]{:S(2)}, u32[]{:S(2)}) collective-permute-start(bf16[8,12288]{1,0:T(8,128)(2,1)S(1)} %get-tuple-element.55), channel_id=1, source_target_pairs={{1,0},{2,1},{3,2},{0,3},{5,4},{6,5},{7,6},{4,7},{9,8},{10,9},{11,1... | collective-permute-start | bytes 589832 | tf_op jit(solution)/shard_map/ppermute | solution.py:111
  64.1 2.0 convolution_convert_fusion.3
  66.2 7.2 %collective-permute-done.47 = bf16[8,12288]{1,0:T(8,128)(2,1)S(1)} collective-permute-done((bf16[8,12288]{1,0:T(8,128)(2,1)S(1)}, bf16[8,12288]{1,0:T(8,128)(2,1)S(1)}, u32[]{:S(2)}, u32[]{:S(2)}) %collective-permute-start.47) | collective-permute-done | bytes 196640 | tf_op jit(solution)/shard_map/ppermute | solution.py:111
  73.4 3.5 %collective-permute-start.13 = (bf16[8,12288]{1,0:T(8,128)(2,1)S(1)}, bf16[8,12288]{1,0:T(8,128)(2,1)S(1)}, u32[]{:S(2)}, u32[]{:S(2)}) collective-permute-start(bf16[8,12288]{1,0:T(8,128)(2,1)S(1)} %get-tuple-element.46), channel_id=1, source_target_pairs={{2,0},{3,1},{0,2},{1,3},{6,4},{7,5},{4,6},{5,7},{10,8},{11,9},{8,1... | collective-permute-start | bytes 589832 | tf_op jit(solution)/shard_map/ppermute | solution.py:111
  76.9 6.3 %collective-permute-done.46 = bf16[8,12288]{1,0:T(8,128)(2,1)S(1)} collective-permute-done((bf16[8,12288]{1,0:T(8,128)(2,1)S(1)}, bf16[8,12288]{1,0:T(8,128)(2,1)S(1)}, u32[]{:S(2)}, u32[]{:S(2)}) %collective-permute-start.46) | collective-permute-done | bytes 196640 | tf_op jit(solution)/shard_map/ppermute | solution.py:111
  83.2 2.8 %collective-permute-done.45 = bf16[8,12288]{1,0:T(8,128)(2,1)S(1)} collective-permute-done((bf16[8,12288]{1,0:T(8,128)(2,1)S(1)}, bf16[8,12288]{1,0:T(8,128)(2,1)S(1)}, u32[]{:S(2)}, u32[]{:S(2)}) %collective-permute-start.45) | collective-permute-done | bytes 196640 | tf_op jit(solution)/shard_map/ppermute | solution.py:111
  86.0 2.5 %collective-permute-start.11 = (bf16[8,12288]{1,0:T(8,128)(2,1)S(1)}, bf16[8,12288]{1,0:T(8,128)(2,1)S(1)}, u32[]{:S(2)}, u32[]{:S(2)}) collective-permute-start(bf16[8,12288]{1,0:T(8,128)(2,1)S(1)} %get-tuple-element.45), channel_id=1, source_target_pairs={{3,0},{0,1},{1,2},{2,3},{7,4},{4,5},{5,6},{6,7},{11,8},{8,9},{9,10... | collective-permute-start | bytes 589832 | tf_op jit(solution)/shard_map/ppermute | solution.py:111
  90.2 5.2 %collective-permute-done.12 = bf16[8,12288]{1,0:T(8,128)(2,1)S(1)} collective-permute-done((bf16[8,12288]{1,0:T(8,128)(2,1)S(1)}, bf16[8,12288]{1,0:T(8,128)(2,1)S(1)}, u32[]{:S(2)}, u32[]{:S(2)}) %collective-permute-start.12) | collective-permute-done | bytes 196640 | tf_op jit(solution)/shard_map/ppermute | solution.py:111
  96.8 1.5 collective-permute-start.49
  100.4 1.7 collective-permute-start.50
  104.0 1.7 collective-permute-done.16
  109.2 1.5 collective-permute-done.52
  112.8 1.5 collective-permute-done.53
  118.8 3.0 %collective-permute-start.54 = (bf16[8,4,24,128]{3,2,1,0:T(8,128)(2,1)S(1)}, bf16[8,4,24,128]{3,2,1,0:T(8,128)(2,1)S(1)}, u32[]{:S(2)}, u32[]{:S(2)}) collective-permute-start(bf16[8,4,24,128]{3,2,1,0:T(8,128)(2,1)S(1)} %convert_element_type.129), channel_id=1, source_target_pairs={{0,4},{4,8},{8,12},{12,16},{16,20},{20,24},{24,28},{1,5},{5,9},{9,... | collective-permute-start | bytes 589832 | tf_op jit(solution)/shard_map/ppermute | solution.py:21
  122.1 8.0 %collective-permute-done.58 = bf16[8,12288]{1,0:T(8,128)(2,1)S(1)} collective-permute-done((bf16[8,12288]{1,0:T(8,128)(2,1)S(1)}, bf16[8,12288]{1,0:T(8,128)(2,1)S(1)}, u32[]{:S(2)}, u32[]{:S(2)}) %collective-permute-start.58) | collective-permute-done | bytes 196640 | tf_op jit(solution)/shard_map/ppermute | solution.py:95
  131.1 5.9 %collective-permute-done.56 = bf16[8,12288]{1,0:T(8,128)(2,1)S(1)} collective-permute-done((bf16[8,12288]{1,0:T(8,128)(2,1)S(1)}, bf16[8,12288]{1,0:T(8,128)(2,1)S(1)}, u32[]{:S(2)}, u32[]{:S(2)}) %collective-permute-start.56) | collective-permute-done | bytes 196640 | tf_op jit(solution)/shard_map/ppermute | solution.py:95
  137.0 6.5 %collective-permute-start.22 = (bf16[8,12288]{1,0:T(8,128)(2,1)S(1)}, bf16[8,12288]{1,0:T(8,128)(2,1)S(1)}, u32[]{:S(2)}, u32[]{:S(2)}) collective-permute-start(bf16[8,12288]{1,0:T(8,128)(2,1)S(1)} %bitcast.91), channel_id=1, source_target_pairs={{0,1},{1,2},{2,3},{3,0},{4,5},{5,6},{6,7},{7,4},{8,9},{9,10},{10,1... | collective-permute-start | bytes 589832 | tf_op jit(solution)/shard_map/ppermute | solution.py:95
  143.6 2.0 fusion.21
  146.9 3.0 %collective-permute-start.20 = (bf16[8,4,24,128]{3,2,1,0:T(8,128)(2,1)S(1)}, bf16[8,4,24,128]{3,2,1,0:T(8,128)(2,1)S(1)}, u32[]{:S(2)}, u32[]{:S(2)}) collective-permute-start(bf16[8,4,24,128]{3,2,1,0:T(8,128)(2,1)S(1)} %convert_element_type.113), channel_id=1, source_target_pairs={{0,4},{4,8},{8,12},{12,16},{16,20},{20,24},{24,28},{1,5},{5,9},{9,... | collective-permute-start | bytes 589832 | tf_op jit(solution)/shard_map/ppermute | solution.py:21
  150.1 2.0 fusion.15
  152.7 1.7 collective-permute-start.60
  158.9 1.9 collective-permute-done.61
  160.8 2.0 convolution_convert_fusion
  163.8 2.1 collective-permute-start.63
  167.3 2.0 convolution_convert_fusion.2
  169.4 2.4 %collective-permute-start.30 = (bf16[8,12288]{1,0:T(8,128)(2,1)S(1)}, bf16[8,12288]{1,0:T(8,128)(2,1)S(1)}, u32[]{:S(2)}, u32[]{:S(2)}) collective-permute-start(bf16[8,12288]{1,0:T(8,128)(2,1)S(1)} %get-tuple-element.41), channel_id=1, source_target_pairs={{2,0},{3,1},{0,2},{1,3},{6,4},{7,5},{4,6},{5,7},{10,8},{11,9},{8,1... | collective-permute-start | bytes 589832 | tf_op jit(solution)/shard_map/ppermute | solution.py:111
  172.9 5.4 %collective-permute-done.64 = bf16[8,12288]{1,0:T(8,128)(2,1)S(1)} collective-permute-done((bf16[8,12288]{1,0:T(8,128)(2,1)S(1)}, bf16[8,12288]{1,0:T(8,128)(2,1)S(1)}, u32[]{:S(2)}, u32[]{:S(2)}) %collective-permute-start.64) | collective-permute-done | bytes 196640 | tf_op jit(solution)/shard_map/ppermute | solution.py:111
  178.4 2.2 %collective-permute-start.28 = (bf16[8,12288]{1,0:T(8,128)(2,1)S(1)}, bf16[8,12288]{1,0:T(8,128)(2,1)S(1)}, u32[]{:S(2)}, u32[]{:S(2)}) collective-permute-start(bf16[8,12288]{1,0:T(8,128)(2,1)S(1)} %get-tuple-element.40), channel_id=1, source_target_pairs={{3,0},{0,1},{1,2},{2,3},{7,4},{4,5},{5,6},{6,7},{11,8},{8,9},{9,10... | collective-permute-start | bytes 589832 | tf_op jit(solution)/shard_map/ppermute | solution.py:111
  180.6 10.6 %collective-permute-done.63 = bf16[8,12288]{1,0:T(8,128)(2,1)S(1)} collective-permute-done((bf16[8,12288]{1,0:T(8,128)(2,1)S(1)}, bf16[8,12288]{1,0:T(8,128)(2,1)S(1)}, u32[]{:S(2)}, u32[]{:S(2)}) %collective-permute-start.63) | collective-permute-done | bytes 196640 | tf_op jit(solution)/shard_map/ppermute | solution.py:111
  193.6 4.4 %collective-permute-done.29 = bf16[8,12288]{1,0:T(8,128)(2,1)S(1)} collective-permute-done((bf16[8,12288]{1,0:T(8,128)(2,1)S(1)}, bf16[8,12288]{1,0:T(8,128)(2,1)S(1)}, u32[]{:S(2)}, u32[]{:S(2)}) %collective-permute-start.29) | collective-permute-done | bytes 196640 | tf_op jit(solution)/shard_map/ppermute | solution.py:111
  199.4 1.7 collective-permute-start.66
  206.7 1.5 collective-permute-done.33
  (169 shorter events, 54.4 us)
Async XLA Ops:
  2.1 16.5 %collective-permute-start.41 = (bf16[8,12288]{1,0:T(8,128)(2,1)S(1)}, bf16[8,12288]{1,0:T(8,128)(2,1)S(1)}, u32[]{:S(2)}, u32[]{:S(2)}) collective-permute-start(bf16[8,12288]{1,0:T(8,128)(2,1)S(1)} %bitcast.81), channel_id=1, source_target_pairs={{0,3},{1,0},{2,1},{3,2},{4,7},{5,4},{6,5},{7,6},{8,11},{9,8},{10,9... | collective-permute-start | bytes 589832 | tf_op jit(solution)/shard_map/ppermute | solution.py:95
  2.1 18.8 %collective-permute-start.40 = (bf16[8,12288]{1,0:T(8,128)(2,1)S(1)}, bf16[8,12288]{1,0:T(8,128)(2,1)S(1)}, u32[]{:S(2)}, u32[]{:S(2)}) collective-permute-start(bf16[8,12288]{1,0:T(8,128)(2,1)S(1)} %bitcast.82), channel_id=1, source_target_pairs={{0,2},{1,3},{2,0},{3,1},{4,6},{5,7},{6,4},{7,5},{8,10},{9,11},{10,... | collective-permute-start | bytes 589832 | tf_op jit(solution)/shard_map/ppermute | solution.py:95
  5.2 25.9 %collective-permute-start.39 = (bf16[8,12288]{1,0:T(8,128)(2,1)S(1)}, bf16[8,12288]{1,0:T(8,128)(2,1)S(1)}, u32[]{:S(2)}, u32[]{:S(2)}) collective-permute-start(bf16[8,12288]{1,0:T(8,128)(2,1)S(1)} %bitcast.83), channel_id=1, source_target_pairs={{0,1},{1,2},{2,3},{3,0},{4,5},{5,6},{6,7},{7,4},{8,9},{9,10},{10,1... | collective-permute-start | bytes 589832 | tf_op jit(solution)/shard_map/ppermute | solution.py:95
  7.8 29.6 %collective-permute-start.7 = (bf16[8,12288]{1,0:T(8,128)(2,1)S(1)}, bf16[8,12288]{1,0:T(8,128)(2,1)S(1)}, u32[]{:S(2)}, u32[]{:S(2)}) collective-permute-start(bf16[8,12288]{1,0:T(8,128)(2,1)S(1)} %bitcast.77), channel_id=1, source_target_pairs={{0,3},{1,0},{2,1},{3,2},{4,7},{5,4},{6,5},{7,6},{8,11},{9,8},{10,9... | collective-permute-start | bytes 589832 | tf_op jit(solution)/shard_map/ppermute | solution.py:95
  17.2 21.4 %collective-permute-start.6 = (bf16[8,12288]{1,0:T(8,128)(2,1)S(1)}, bf16[8,12288]{1,0:T(8,128)(2,1)S(1)}, u32[]{:S(2)}, u32[]{:S(2)}) collective-permute-start(bf16[8,12288]{1,0:T(8,128)(2,1)S(1)} %bitcast.78), channel_id=1, source_target_pairs={{0,2},{1,3},{2,0},{3,1},{4,6},{5,7},{6,4},{7,5},{8,10},{9,11},{10,... | collective-permute-start | bytes 589832 | tf_op jit(solution)/shard_map/ppermute | solution.py:95
  18.6 24.8 %collective-permute-start.5 = (bf16[8,12288]{1,0:T(8,128)(2,1)S(1)}, bf16[8,12288]{1,0:T(8,128)(2,1)S(1)}, u32[]{:S(2)}, u32[]{:S(2)}) collective-permute-start(bf16[8,12288]{1,0:T(8,128)(2,1)S(1)} %bitcast.79), channel_id=1, source_target_pairs={{0,1},{1,2},{2,3},{3,0},{4,5},{5,6},{6,7},{7,4},{8,9},{9,10},{10,1... | collective-permute-start | bytes 589832 | tf_op jit(solution)/shard_map/ppermute | solution.py:95
  21.0 27.9 %collective-permute-start.4 = (bf16[8,4,24,128]{3,2,1,0:T(8,128)(2,1)S(1)}, bf16[8,4,24,128]{3,2,1,0:T(8,128)(2,1)S(1)}, u32[]{:S(2)}, u32[]{:S(2)}) collective-permute-start(bf16[8,4,24,128]{3,2,1,0:T(8,128)(2,1)S(1)} %convert_element_type.105), channel_id=1, source_target_pairs={{4,0},{8,4},{12,8},{16,12},{20,16},{24,20},{28,24},{5,1},{9,5},{13... | collective-permute-start | bytes 589832 | tf_op jit(solution)/shard_map/ppermute | solution.py:22
  31.0 17.9 %collective-permute-start.3 = (bf16[8,4,24,128]{3,2,1,0:T(8,128)(2,1)S(1)}, bf16[8,4,24,128]{3,2,1,0:T(8,128)(2,1)S(1)}, u32[]{:S(2)}, u32[]{:S(2)}) collective-permute-start(bf16[8,4,24,128]{3,2,1,0:T(8,128)(2,1)S(1)} %convert_element_type.105), channel_id=1, source_target_pairs={{0,4},{4,8},{8,12},{12,16},{16,20},{20,24},{24,28},{1,5},{5,9},{9,... | collective-permute-start | bytes 589832 | tf_op jit(solution)/shard_map/ppermute | solution.py:21
  37.4 16.5 %collective-permute-start.38 = (bf16[8,4,24,128]{3,2,1,0:T(8,128)(2,1)S(1)}, bf16[8,4,24,128]{3,2,1,0:T(8,128)(2,1)S(1)}, u32[]{:S(2)}, u32[]{:S(2)}) collective-permute-start(bf16[8,4,24,128]{3,2,1,0:T(8,128)(2,1)S(1)} %convert_element_type.121), channel_id=1, source_target_pairs={{4,0},{8,4},{12,8},{16,12},{20,16},{24,20},{28,24},{5,1},{9,5},{13... | collective-permute-start | bytes 589832 | tf_op jit(solution)/shard_map/ppermute | solution.py:22
  38.7 17.2 %collective-permute-start.37 = (bf16[8,4,24,128]{3,2,1,0:T(8,128)(2,1)S(1)}, bf16[8,4,24,128]{3,2,1,0:T(8,128)(2,1)S(1)}, u32[]{:S(2)}, u32[]{:S(2)}) collective-permute-start(bf16[8,4,24,128]{3,2,1,0:T(8,128)(2,1)S(1)} %convert_element_type.121), channel_id=1, source_target_pairs={{0,4},{4,8},{8,12},{12,16},{16,20},{20,24},{24,28},{1,5},{5,9},{9,... | collective-permute-start | bytes 589832 | tf_op jit(solution)/shard_map/ppermute | solution.py:21
  43.4 3.8 %collective-permute-start.42 = (f32[256,32]{0,1:T(8,128)S(1)}, f32[256,32]{0,1:T(8,128)S(1)}, u32[]{:S(2)}, u32[]{:S(2)}) collective-permute-start(f32[256,32]{0,1:T(8,128)S(1)} %fusion.18), channel_id=1, source_target_pairs={{0,4},{4,0},{8,12},{12,8},{16,20},{20,16},{24,28},{28,24},{1,5},{5... | collective-permute-start | bytes 98312 | tf_op jit(solution)/shard_map/ppermute | solution.py:33
  47.3 55.9 %collective-permute-start.36 = (f32[8]{0:T(128)S(1)}, f32[8]{0:T(128)S(1)}, u32[]{:S(2)}, u32[]{:S(2)}) collective-permute-start(f32[8]{0:T(128)S(1)} %add.608), channel_id=1, source_target_pairs={{0,16},{4,20},{8,24},{12,28},{16,0},{20,4},{24,8},{28,12},{1,17},{... | collective-permute-start | bytes 104 | tf_op jit(solution)/shard_map/ppermute | solution.py:33
  49.0 4.0 %collective-permute-start.43 = (f32[256,32]{0,1:T(8,128)S(1)}, f32[256,32]{0,1:T(8,128)S(1)}, u32[]{:S(2)}, u32[]{:S(2)}) collective-permute-start(f32[256,32]{0,1:T(8,128)S(1)} %add.638), channel_id=1, source_target_pairs={{0,8},{4,12},{8,0},{12,4},{16,24},{20,28},{24,16},{28,20},{1,9},{5... | collective-permute-start | bytes 98312 | tf_op jit(solution)/shard_map/ppermute | solution.py:33
  50.1 53.0 %collective-permute-start.2 = (f32[8]{0:T(128)S(1)}, f32[8]{0:T(128)S(1)}, u32[]{:S(2)}, u32[]{:S(2)}) collective-permute-start(f32[8]{0:T(128)S(1)} %add.525), channel_id=1, source_target_pairs={{0,16},{4,20},{8,24},{12,28},{16,0},{20,4},{24,8},{28,12},{1,17},{... | collective-permute-start | bytes 104 | tf_op jit(solution)/shard_map/ppermute | solution.py:33
  52.9 3.9 %collective-permute-start.9 = (f32[256,32]{0,1:T(8,128)S(1)}, f32[256,32]{0,1:T(8,128)S(1)}, u32[]{:S(2)}, u32[]{:S(2)}) collective-permute-start(f32[256,32]{0,1:T(8,128)S(1)} %add.555), channel_id=1, source_target_pairs={{0,8},{4,12},{8,0},{12,4},{16,24},{20,28},{24,16},{28,20},{1,9},{5... | collective-permute-start | bytes 98312 | tf_op jit(solution)/shard_map/ppermute | solution.py:33
  53.8 4.2 %collective-permute-start.44 = (f32[256,32]{0,1:T(8,128)S(1)}, f32[256,32]{0,1:T(8,128)S(1)}, u32[]{:S(2)}, u32[]{:S(2)}) collective-permute-start(f32[256,32]{0,1:T(8,128)S(1)} %add.639), channel_id=1, source_target_pairs={{0,16},{4,20},{8,24},{12,28},{16,0},{20,4},{24,8},{28,12},{1,17},{... | collective-permute-start | bytes 98312 | tf_op jit(solution)/shard_map/ppermute | solution.py:33
  56.9 7.3 %collective-permute-start.10 = (f32[256,32]{0,1:T(8,128)S(1)}, f32[256,32]{0,1:T(8,128)S(1)}, u32[]{:S(2)}, u32[]{:S(2)}) collective-permute-start(f32[256,32]{0,1:T(8,128)S(1)} %add.556), channel_id=1, source_target_pairs={{0,16},{4,20},{8,24},{12,28},{16,0},{20,4},{24,8},{28,12},{1,17},{... | collective-permute-start | bytes 98312 | tf_op jit(solution)/shard_map/ppermute | solution.py:33
  60.1 13.3 %collective-permute-start.47 = (bf16[8,12288]{1,0:T(8,128)(2,1)S(1)}, bf16[8,12288]{1,0:T(8,128)(2,1)S(1)}, u32[]{:S(2)}, u32[]{:S(2)}) collective-permute-start(bf16[8,12288]{1,0:T(8,128)(2,1)S(1)} %get-tuple-element.54), channel_id=1, source_target_pairs={{2,0},{3,1},{0,2},{1,3},{6,4},{7,5},{4,6},{5,7},{10,8},{11,9},{8,1... | collective-permute-start | bytes 589832 | tf_op jit(solution)/shard_map/ppermute | solution.py:111
  60.3 23.0 %collective-permute-start.46 = (bf16[8,12288]{1,0:T(8,128)(2,1)S(1)}, bf16[8,12288]{1,0:T(8,128)(2,1)S(1)}, u32[]{:S(2)}, u32[]{:S(2)}) collective-permute-start(bf16[8,12288]{1,0:T(8,128)(2,1)S(1)} %get-tuple-element.55), channel_id=1, source_target_pairs={{1,0},{2,1},{3,2},{0,3},{5,4},{6,5},{7,6},{4,7},{9,8},{10,9},{11,1... | collective-permute-start | bytes 589832 | tf_op jit(solution)/shard_map/ppermute | solution.py:111
  64.1 21.9 %collective-permute-start.45 = (bf16[8,12288]{1,0:T(8,128)(2,1)S(1)}, bf16[8,12288]{1,0:T(8,128)(2,1)S(1)}, u32[]{:S(2)}, u32[]{:S(2)}) collective-permute-start(bf16[8,12288]{1,0:T(8,128)(2,1)S(1)} %get-tuple-element.53), channel_id=1, source_target_pairs={{3,0},{0,1},{1,2},{2,3},{7,4},{4,5},{5,6},{6,7},{11,8},{8,9},{9,10... | collective-permute-start | bytes 589832 | tf_op jit(solution)/shard_map/ppermute | solution.py:111
  73.4 16.8 %collective-permute-start.13 = (bf16[8,12288]{1,0:T(8,128)(2,1)S(1)}, bf16[8,12288]{1,0:T(8,128)(2,1)S(1)}, u32[]{:S(2)}, u32[]{:S(2)}) collective-permute-start(bf16[8,12288]{1,0:T(8,128)(2,1)S(1)} %get-tuple-element.46), channel_id=1, source_target_pairs={{2,0},{3,1},{0,2},{1,3},{6,4},{7,5},{4,6},{5,7},{10,8},{11,9},{8,1... | collective-permute-start | bytes 589832 | tf_op jit(solution)/shard_map/ppermute | solution.py:111
  83.2 12.2 %collective-permute-start.12 = (bf16[8,12288]{1,0:T(8,128)(2,1)S(1)}, bf16[8,12288]{1,0:T(8,128)(2,1)S(1)}, u32[]{:S(2)}, u32[]{:S(2)}) collective-permute-start(bf16[8,12288]{1,0:T(8,128)(2,1)S(1)} %get-tuple-element.47), channel_id=1, source_target_pairs={{1,0},{2,1},{3,2},{0,3},{5,4},{6,5},{7,6},{4,7},{9,8},{10,9},{11,1... | collective-permute-start | bytes 589832 | tf_op jit(solution)/shard_map/ppermute | solution.py:111
  86.0 9.4 %collective-permute-start.11 = (bf16[8,12288]{1,0:T(8,128)(2,1)S(1)}, bf16[8,12288]{1,0:T(8,128)(2,1)S(1)}, u32[]{:S(2)}, u32[]{:S(2)}) collective-permute-start(bf16[8,12288]{1,0:T(8,128)(2,1)S(1)} %get-tuple-element.45), channel_id=1, source_target_pairs={{3,0},{0,1},{1,2},{2,3},{7,4},{4,5},{5,6},{6,7},{11,8},{8,9},{9,10... | collective-permute-start | bytes 589832 | tf_op jit(solution)/shard_map/ppermute | solution.py:111
  90.2 6.6 %collective-permute-start.48 = (f32[8]{0:T(128)S(1)}, f32[8]{0:T(128)S(1)}, u32[]{:S(2)}, u32[]{:S(2)}) collective-permute-start(f32[8]{0:T(128)S(1)} %get-tuple-element.38), channel_id=1, source_target_pairs={{0,4},{4,0},{8,12},{12,8},{16,20},{20,16},{24,28},{28,24},{1,5},{5... | collective-permute-start | bytes 104 | tf_op jit(solution)/shard_map/ppermute | solution.py:33
  98.3 3.8 %collective-permute-start.15 = (f32[8]{0:T(128)S(1)}, f32[8]{0:T(128)S(1)}, u32[]{:S(2)}, u32[]{:S(2)}) collective-permute-start(f32[8]{0:T(128)S(1)} %add.562), channel_id=1, source_target_pairs={{0,8},{4,12},{8,0},{12,4},{16,24},{20,28},{24,16},{28,20},{1,9},{5... | collective-permute-start | bytes 104 | tf_op jit(solution)/shard_map/ppermute | solution.py:33
  107.9 3.8 %collective-permute-start.18 = (f32[8]{0:T(128)S(1)}, f32[8]{0:T(128)S(1)}, u32[]{:S(2)}, u32[]{:S(2)}) collective-permute-start(f32[8]{0:T(128)S(1)} %add.565), channel_id=1, source_target_pairs={{0,8},{4,12},{8,0},{12,4},{16,24},{20,28},{24,16},{28,20},{1,9},{5... | collective-permute-start | bytes 104 | tf_op jit(solution)/shard_map/ppermute | solution.py:33
  111.7 7.1 %collective-permute-start.19 = (f32[8]{0:T(128)S(1)}, f32[8]{0:T(128)S(1)}, u32[]{:S(2)}, u32[]{:S(2)}) collective-permute-start(f32[8]{0:T(128)S(1)} %add.566), channel_id=1, source_target_pairs={{0,16},{4,20},{8,24},{12,28},{16,0},{20,4},{24,8},{28,12},{1,17},{... | collective-permute-start | bytes 104 | tf_op jit(solution)/shard_map/ppermute | solution.py:33
  114.5 15.6 %collective-permute-start.58 = (bf16[8,12288]{1,0:T(8,128)(2,1)S(1)}, bf16[8,12288]{1,0:T(8,128)(2,1)S(1)}, u32[]{:S(2)}, u32[]{:S(2)}) collective-permute-start(bf16[8,12288]{1,0:T(8,128)(2,1)S(1)} %bitcast.85), channel_id=1, source_target_pairs={{0,3},{1,0},{2,1},{3,2},{4,7},{5,4},{6,5},{7,6},{8,11},{9,8},{10,9... | collective-permute-start | bytes 589832 | tf_op jit(solution)/shard_map/ppermute | solution.py:95
  116.0 14.1 %collective-permute-start.57 = (bf16[8,12288]{1,0:T(8,128)(2,1)S(1)}, bf16[8,12288]{1,0:T(8,128)(2,1)S(1)}, u32[]{:S(2)}, u32[]{:S(2)}) collective-permute-start(bf16[8,12288]{1,0:T(8,128)(2,1)S(1)} %bitcast.86), channel_id=1, source_target_pairs={{0,2},{1,3},{2,0},{3,1},{4,6},{5,7},{6,4},{7,5},{8,10},{9,11},{10,... | collective-permute-start | bytes 589832 | tf_op jit(solution)/shard_map/ppermute | solution.py:95
  116.1 21.0 %collective-permute-start.56 = (bf16[8,12288]{1,0:T(8,128)(2,1)S(1)}, bf16[8,12288]{1,0:T(8,128)(2,1)S(1)}, u32[]{:S(2)}, u32[]{:S(2)}) collective-permute-start(bf16[8,12288]{1,0:T(8,128)(2,1)S(1)} %bitcast.87), channel_id=1, source_target_pairs={{0,1},{1,2},{2,3},{3,0},{4,5},{5,6},{6,7},{7,4},{8,9},{9,10},{10,1... | collective-permute-start | bytes 589832 | tf_op jit(solution)/shard_map/ppermute | solution.py:95
  117.5 35.1 %collective-permute-start.55 = (bf16[8,4,24,128]{3,2,1,0:T(8,128)(2,1)S(1)}, bf16[8,4,24,128]{3,2,1,0:T(8,128)(2,1)S(1)}, u32[]{:S(2)}, u32[]{:S(2)}) collective-permute-start(bf16[8,4,24,128]{3,2,1,0:T(8,128)(2,1)S(1)} %convert_element_type.129), channel_id=1, source_target_pairs={{4,0},{8,4},{12,8},{16,12},{20,16},{24,20},{28,24},{5,1},{9,5},{13... | collective-permute-start | bytes 589832 | tf_op jit(solution)/shard_map/ppermute | solution.py:22
  118.8 35.5 %collective-permute-start.54 = (bf16[8,4,24,128]{3,2,1,0:T(8,128)(2,1)S(1)}, bf16[8,4,24,128]{3,2,1,0:T(8,128)(2,1)S(1)}, u32[]{:S(2)}, u32[]{:S(2)}) collective-permute-start(bf16[8,4,24,128]{3,2,1,0:T(8,128)(2,1)S(1)} %convert_element_type.129), channel_id=1, source_target_pairs={{0,4},{4,8},{8,12},{12,16},{16,20},{20,24},{24,28},{1,5},{5,9},{9,... | collective-permute-start | bytes 589832 | tf_op jit(solution)/shard_map/ppermute | solution.py:21
  130.1 15.5 %collective-permute-start.24 = (bf16[8,12288]{1,0:T(8,128)(2,1)S(1)}, bf16[8,12288]{1,0:T(8,128)(2,1)S(1)}, u32[]{:S(2)}, u32[]{:S(2)}) collective-permute-start(bf16[8,12288]{1,0:T(8,128)(2,1)S(1)} %bitcast.89), channel_id=1, source_target_pairs={{0,3},{1,0},{2,1},{3,2},{4,7},{5,4},{6,5},{7,6},{8,11},{9,8},{10,9... | collective-permute-start | bytes 589832 | tf_op jit(solution)/shard_map/ppermute | solution.py:95
  130.1 16.8 %collective-permute-start.23 = (bf16[8,12288]{1,0:T(8,128)(2,1)S(1)}, bf16[8,12288]{1,0:T(8,128)(2,1)S(1)}, u32[]{:S(2)}, u32[]{:S(2)}) collective-permute-start(bf16[8,12288]{1,0:T(8,128)(2,1)S(1)} %bitcast.90), channel_id=1, source_target_pairs={{0,2},{1,3},{2,0},{3,1},{4,6},{5,7},{6,4},{7,5},{8,10},{9,11},{10,... | collective-permute-start | bytes 589832 | tf_op jit(solution)/shard_map/ppermute | solution.py:95
  137.0 12.9 %collective-permute-start.22 = (bf16[8,12288]{1,0:T(8,128)(2,1)S(1)}, bf16[8,12288]{1,0:T(8,128)(2,1)S(1)}, u32[]{:S(2)}, u32[]{:S(2)}) collective-permute-start(bf16[8,12288]{1,0:T(8,128)(2,1)S(1)} %bitcast.91), channel_id=1, source_target_pairs={{0,1},{1,2},{2,3},{3,0},{4,5},{5,6},{6,7},{7,4},{8,9},{9,10},{10,1... | collective-permute-start | bytes 589832 | tf_op jit(solution)/shard_map/ppermute | solution.py:95
  145.6 12.2 %collective-permute-start.21 = (bf16[8,4,24,128]{3,2,1,0:T(8,128)(2,1)S(1)}, bf16[8,4,24,128]{3,2,1,0:T(8,128)(2,1)S(1)}, u32[]{:S(2)}, u32[]{:S(2)}) collective-permute-start(bf16[8,4,24,128]{3,2,1,0:T(8,128)(2,1)S(1)} %convert_element_type.113), channel_id=1, source_target_pairs={{4,0},{8,4},{12,8},{16,12},{20,16},{24,20},{28,24},{5,1},{9,5},{13... | collective-permute-start | bytes 589832 | tf_op jit(solution)/shard_map/ppermute | solution.py:22
  146.9 10.9 %collective-permute-start.20 = (bf16[8,4,24,128]{3,2,1,0:T(8,128)(2,1)S(1)}, bf16[8,4,24,128]{3,2,1,0:T(8,128)(2,1)S(1)}, u32[]{:S(2)}, u32[]{:S(2)}) collective-permute-start(bf16[8,4,24,128]{3,2,1,0:T(8,128)(2,1)S(1)} %convert_element_type.113), channel_id=1, source_target_pairs={{0,4},{4,8},{8,12},{12,16},{16,20},{20,24},{24,28},{1,5},{5,9},{9,... | collective-permute-start | bytes 589832 | tf_op jit(solution)/shard_map/ppermute | solution.py:21
  152.7 4.0 %collective-permute-start.60 = (f32[256,32]{0,1:T(8,128)S(1)}, f32[256,32]{0,1:T(8,128)S(1)}, u32[]{:S(2)}, u32[]{:S(2)}) collective-permute-start(f32[256,32]{0,1:T(8,128)S(1)} %add.679), channel_id=1, source_target_pairs={{0,8},{4,12},{8,0},{12,4},{16,24},{20,28},{24,16},{28,20},{1,9},{5... | collective-permute-start | bytes 98312 | tf_op jit(solution)/shard_map/ppermute | solution.py:33
  154.4 4.0 %collective-permute-start.26 = (f32[256,32]{0,1:T(8,128)S(1)}, f32[256,32]{0,1:T(8,128)S(1)}, u32[]{:S(2)}, u32[]{:S(2)}) collective-permute-start(f32[256,32]{0,1:T(8,128)S(1)} %add.596), channel_id=1, source_target_pairs={{0,8},{4,12},{8,0},{12,4},{16,24},{20,28},{24,16},{28,20},{1,9},{5... | collective-permute-start | bytes 98312 | tf_op jit(solution)/shard_map/ppermute | solution.py:33
  156.6 4.1 %collective-permute-start.61 = (f32[256,32]{0,1:T(8,128)S(1)}, f32[256,32]{0,1:T(8,128)S(1)}, u32[]{:S(2)}, u32[]{:S(2)}) collective-permute-start(f32[256,32]{0,1:T(8,128)S(1)} %add.680), channel_id=1, source_target_pairs={{0,16},{4,20},{8,24},{12,28},{16,0},{20,4},{24,8},{28,12},{1,17},{... | collective-permute-start | bytes 98312 | tf_op jit(solution)/shard_map/ppermute | solution.py:33
  158.4 8.9 %collective-permute-start.27 = (f32[256,32]{0,1:T(8,128)S(1)}, f32[256,32]{0,1:T(8,128)S(1)}, u32[]{:S(2)}, u32[]{:S(2)}) collective-permute-start(f32[256,32]{0,1:T(8,128)S(1)} %add.597), channel_id=1, source_target_pairs={{0,16},{4,20},{8,24},{12,28},{16,0},{20,4},{24,8},{28,12},{1,17},{... | collective-permute-start | bytes 98312 | tf_op jit(solution)/shard_map/ppermute | solution.py:33
  162.9 15.5 %collective-permute-start.64 = (bf16[8,12288]{1,0:T(8,128)(2,1)S(1)}, bf16[8,12288]{1,0:T(8,128)(2,1)S(1)}, u32[]{:S(2)}, u32[]{:S(2)}) collective-permute-start(bf16[8,12288]{1,0:T(8,128)(2,1)S(1)} %get-tuple-element.50), channel_id=1, source_target_pairs={{2,0},{3,1},{0,2},{1,3},{6,4},{7,5},{4,6},{5,7},{10,8},{11,9},{8,1... | collective-permute-start | bytes 589832 | tf_op jit(solution)/shard_map/ppermute | solution.py:111
  163.8 27.4 %collective-permute-start.63 = (bf16[8,12288]{1,0:T(8,128)(2,1)S(1)}, bf16[8,12288]{1,0:T(8,128)(2,1)S(1)}, u32[]{:S(2)}, u32[]{:S(2)}) collective-permute-start(bf16[8,12288]{1,0:T(8,128)(2,1)S(1)} %get-tuple-element.51), channel_id=1, source_target_pairs={{1,0},{2,1},{3,2},{0,3},{5,4},{6,5},{7,6},{4,7},{9,8},{10,9},{11,1... | collective-permute-start | bytes 589832 | tf_op jit(solution)/shard_map/ppermute | solution.py:111
  165.9 25.3 %collective-permute-start.62 = (bf16[8,12288]{1,0:T(8,128)(2,1)S(1)}, bf16[8,12288]{1,0:T(8,128)(2,1)S(1)}, u32[]{:S(2)}, u32[]{:S(2)}) collective-permute-start(bf16[8,12288]{1,0:T(8,128)(2,1)S(1)} %get-tuple-element.49), channel_id=1, source_target_pairs={{3,0},{0,1},{1,2},{2,3},{7,4},{4,5},{5,6},{6,7},{11,8},{8,9},{9,10... | collective-permute-start | bytes 589832 | tf_op jit(solution)/shard_map/ppermute | solution.py:111
  169.4 24.2 %collective-permute-start.30 = (bf16[8,12288]{1,0:T(8,128)(2,1)S(1)}, bf16[8,12288]{1,0:T(8,128)(2,1)S(1)}, u32[]{:S(2)}, u32[]{:S(2)}) collective-permute-start(bf16[8,12288]{1,0:T(8,128)(2,1)S(1)} %get-tuple-element.41), channel_id=1, source_target_pairs={{2,0},{3,1},{0,2},{1,3},{6,4},{7,5},{4,6},{5,7},{10,8},{11,9},{8,1... | collective-permute-start | bytes 589832 | tf_op jit(solution)/shard_map/ppermute | solution.py:111
  171.8 26.2 %collective-permute-start.29 = (bf16[8,12288]{1,0:T(8,128)(2,1)S(1)}, bf16[8,12288]{1,0:T(8,128)(2,1)S(1)}, u32[]{:S(2)}, u32[]{:S(2)}) collective-permute-start(bf16[8,12288]{1,0:T(8,128)(2,1)S(1)} %get-tuple-element.42), channel_id=1, source_target_pairs={{1,0},{2,1},{3,2},{0,3},{5,4},{6,5},{7,6},{4,7},{9,8},{10,9},{11,1... | collective-permute-start | bytes 589832 | tf_op jit(solution)/shard_map/ppermute | solution.py:111
  178.4 19.6 %collective-permute-start.28 = (bf16[8,12288]{1,0:T(8,128)(2,1)S(1)}, bf16[8,12288]{1,0:T(8,128)(2,1)S(1)}, u32[]{:S(2)}, u32[]{:S(2)}) collective-permute-start(bf16[8,12288]{1,0:T(8,128)(2,1)S(1)} %get-tuple-element.40), channel_id=1, source_target_pairs={{3,0},{0,1},{1,2},{2,3},{7,4},{4,5},{5,6},{6,7},{11,8},{8,9},{9,10... | collective-permute-start | bytes 589832 | tf_op jit(solution)/shard_map/ppermute | solution.py:111
  192.5 6.8 %collective-permute-start.65 = (f32[8]{0:T(128)S(1)}, f32[8]{0:T(128)S(1)}, u32[]{:S(2)}, u32[]{:S(2)}) collective-permute-start(f32[8]{0:T(128)S(1)} %get-tuple-element.30), channel_id=1, source_target_pairs={{0,4},{4,0},{8,12},{12,8},{16,20},{20,16},{24,28},{28,24},{1,5},{5... | collective-permute-start | bytes 104 | tf_op jit(solution)/shard_map/ppermute | solution.py:33
  (25 other events, 149.5 us)

commit v12 on v11

--- a/solution.py
+++ b/solution.py
@@ -68,7 +68,7 @@
     return vector[:, None, None, None]
 
 
-def chain(occupied, potential, shifts, source_term):
+def chain(occupied, potential, shifts, source_term, flip=False):
     local_bands, width_x, width_y, width_z = source_term.shape
     local_occupied = occupied.shape[0]
     band_count = lax.axis_size("band")
@@ -90,7 +90,7 @@
         padded = jnp.pad(padded, ((0, 0), (0, 0), (4, 4), (4, 4)))
         kinetic = -0.5 * second_sum(padded, width_x, width_y, width_z)
         rounded = direction.astype(jnp.bfloat16).reshape(local_bands, local_cells)
-        order = sorted(range(1, band_count), key=lambda d: (min(d, band_count - d), -d))
+        order = sorted(range(1, band_count), key=lambda d: (min(d, band_count - d), d if flip else -d))
         arrived = {
             d: lax.ppermute(rounded, "band", [(i, (i + d) % band_count) for i in range(band_count)])
             for d in order
@@ -113,6 +113,8 @@
         applied = kinetic + potential_shift * direction + projected.reshape(direction.shape)
         curvature = grid_sum(inner_product(direction, applied), "grid")
         step_size = norm_now / curvature
+        if iteration + 1 == ITERS:
+            return (solution, residual, direction, applied, step_size)
         solution = solution + expand(step_size) * direction
         residual = residual - expand(step_size) * applied
         if iteration + 1 < ITERS:
@@ -126,10 +128,19 @@
     pieces = 2 if source_term.shape[0] % 2 == 0 else 1
     width = source_term.shape[0] // pieces
     results = [
-        chain(occupied, potential, shifts[k * width : (k + 1) * width], source_term[k * width : (k + 1) * width])
+        chain(
+            occupied,
+            potential,
+            shifts[k * width : (k + 1) * width],
+            source_term[k * width : (k + 1) * width],
+            k % 2 == 1,
+        )
         for k in range(pieces)
     ]
-    return tuple(jnp.concatenate([r[i] for r in results], axis=0) for i in range(2))
+    solution, residual, direction, applied, step_size = (
+        jnp.concatenate([r[i] for r in results], axis=0) for i in range(5)
+    )
+    return (solution + expand(step_size) * direction, residual - expand(step_size) * applied)
 
 
 def solution(mesh):

time: 211 us -> 210 us (level)
    ppermute x12, starting transfers between devices: 20.2 us -> 17.5 us  [chain(): lax.ppermute(part, 'band', [((i + d) % band_count, i) for i in range(band...]
    ppermute x12, starting transfers between devices: 19.9 us -> 22.1 us  [chain(): lax.ppermute(rounded, 'band', [(i, (i + d) % band_count) for i in range(b...]
where the time goes in v12:
time: 210 us; the launch traced here: 209 us
  waiting for transfers between devices  90.4 us (43%)
  starting transfers between devices  89 us (42%)
  matrix products  19.1 us (9%)
  other arithmetic  9.13 us (4%)
    ppermute x12, waiting for transfers between devices, chain(): lax.ppermute(part, 'band', [((i + d) % band_count, i) for i in range(band...  44.6 us
    ppermute x36, starting transfers between devices, grid_sum(): value = value + lax.ppermute(value, axis, pairs)  32.2 us
    ppermute x36, waiting for transfers between devices, grid_sum(): value = value + lax.ppermute(value, axis, pairs)  24.1 us
    ppermute x12, starting transfers between devices, chain(): lax.ppermute(rounded, 'band', [(i, (i + d) % band_count) for i in range(b...  22.1 us
    ppermute x12, waiting for transfers between devices, chain(): lax.ppermute(rounded, 'band', [(i, (i + d) % band_count) for i in range(b...  21.7 us
    ppermute x12, starting transfers between devices, chain(): lax.ppermute(part, 'band', [((i + d) % band_count, i) for i in range(band...  17.5 us
    ppermute x4, starting transfers between devices, with_halo(): before = lax.ppermute(last, axis, up)  12.1 us
    dot_general x4, matrix products, chain(): lax.dot_general(occupied_rows, gathered, (((1,), (1,)), ((), ())), prefer...  11 us
  transfers between devices with their start and end apart: 68, of which 33 were waited for; matrix products, arithmetic and copies ran while one was open for 12% of the time, Pallas kernels for 0%

profile of v12, /device:TPU:8, one launch (start us, length us, event | category | flops | bytes accessed | tf_op | source)
XLA Modules:
  0.0 209.5 jit_solution(6030346187096137172)
XLA Ops:
  2.1 3.0 %collective-permute-start.23 = (bf16[8,12288]{1,0:T(8,128)(2,1)S(1)}, bf16[8,12288]{1,0:T(8,128)(2,1)S(1)}, u32[]{:S(2)}, u32[]{:S(2)}) collective-permute-start(bf16[8,12288]{1,0:T(8,128)(2,1)S(1)} %bitcast.82), channel_id=1, source_target_pairs={{0,2},{1,3},{2,0},{3,1},{4,6},{5,7},{6,4},{7,5},{8,10},{9,11},{10,... | collective-permute-start | bytes 589832 | tf_op jit(solution)/shard_map/ppermute | solution.py:95
  5.2 2.5 %collective-permute-start.22 = (bf16[8,12288]{1,0:T(8,128)(2,1)S(1)}, bf16[8,12288]{1,0:T(8,128)(2,1)S(1)}, u32[]{:S(2)}, u32[]{:S(2)}) collective-permute-start(bf16[8,12288]{1,0:T(8,128)(2,1)S(1)} %bitcast.83), channel_id=1, source_target_pairs={{0,1},{1,2},{2,3},{3,0},{4,5},{5,6},{6,7},{7,4},{8,9},{9,10},{10,1... | collective-permute-start | bytes 589832 | tf_op jit(solution)/shard_map/ppermute | solution.py:95
  10.1 1.5 collective-permute-start.18
  11.6 2.0 collective-permute-done.18
  13.7 1.5 collective-permute-start.1
  15.2 2.0 collective-permute-done.1
  18.6 2.4 %collective-permute-start.5 = (bf16[8,12288]{1,0:T(8,128)(2,1)S(1)}, bf16[8,12288]{1,0:T(8,128)(2,1)S(1)}, u32[]{:S(2)}, u32[]{:S(2)}) collective-permute-start(bf16[8,12288]{1,0:T(8,128)(2,1)S(1)} %bitcast.79), channel_id=1, source_target_pairs={{0,1},{1,2},{2,3},{3,0},{4,5},{5,6},{6,7},{7,4},{8,9},{9,10},{10,1... | collective-permute-start | bytes 589832 | tf_op jit(solution)/shard_map/ppermute | solution.py:95
  22.3 8.8 %collective-permute-done.22 = bf16[8,12288]{1,0:T(8,128)(2,1)S(1)} collective-permute-done((bf16[8,12288]{1,0:T(8,128)(2,1)S(1)}, bf16[8,12288]{1,0:T(8,128)(2,1)S(1)}, u32[]{:S(2)}, u32[]{:S(2)}) %collective-permute-start.22) | collective-permute-done | bytes 196640 | tf_op jit(solution)/shard_map/ppermute | solution.py:95
  32.3 5.0 %fusion.15 = f32[256,32]{0,1:T(8,128)S(1)} fusion(bf16[32,8,96,128]{3,2,1,0:T(8,128)(2,1)} %bitcast.59, bf16[8,12288]{1,0:T(8,128)(2,1)S(1)} %collective-permute-done.24, bf16[8,12288]{1,0:T(8,128)(2,1)S(1)} %collective-permute-done.23, bf16[8,12288]{1,0:T(8,128)(2,1)S(1)} %collective-permute-done.22, bf16[8,12288]{1,0:T(8,128)(2,1)S(1)} %bitcast.84), kind=kOutput, calls=%fused_computation.81 | convolution fusion | flops 204472320 | bytes 7110656 | tf_op jit(solution)/shard_map/dot_general | solution.py:100
  38.7 4.8 %collective-permute-start.20 = (bf16[8,4,24,128]{3,2,1,0:T(8,128)(2,1)S(1)}, bf16[8,4,24,128]{3,2,1,0:T(8,128)(2,1)S(1)}, u32[]{:S(2)}, u32[]{:S(2)}) collective-permute-start(bf16[8,4,24,128]{3,2,1,0:T(8,128)(2,1)S(1)} %convert_element_type.113), channel_id=1, source_target_pairs={{0,4},{4,8},{8,12},{12,16},{16,20},{20,24},{24,28},{1,5},{5,9},{9,... | collective-permute-start | bytes 589832 | tf_op jit(solution)/shard_map/ppermute | solution.py:21
  43.4 1.8 collective-permute-start.25
  45.2 2.0 fusion.12
  47.3 1.6 collective-permute-start.19
  50.1 1.9 collective-permute-start.2
  53.8 2.1 collective-permute-start.27
  58.1 2.0 convolution_convert_fusion.2
  60.3 2.5 %collective-permute-start.29 = (bf16[8,12288]{1,0:T(8,128)(2,1)S(1)}, bf16[8,12288]{1,0:T(8,128)(2,1)S(1)}, u32[]{:S(2)}, u32[]{:S(2)}) collective-permute-start(bf16[8,12288]{1,0:T(8,128)(2,1)S(1)} %get-tuple-element.55), channel_id=1, source_target_pairs={{3,0},{0,1},{1,2},{2,3},{7,4},{4,5},{5,6},{6,7},{11,8},{8,9},{9,10... | collective-permute-start | bytes 589832 | tf_op jit(solution)/shard_map/ppermute | solution.py:111
  64.1 2.0 convolution_convert_fusion.3
  66.2 5.2 %collective-permute-done.30 = bf16[8,12288]{1,0:T(8,128)(2,1)S(1)} collective-permute-done((bf16[8,12288]{1,0:T(8,128)(2,1)S(1)}, bf16[8,12288]{1,0:T(8,128)(2,1)S(1)}, u32[]{:S(2)}, u32[]{:S(2)}) %collective-permute-start.30) | collective-permute-done | bytes 196640 | tf_op jit(solution)/shard_map/ppermute | solution.py:111
  71.5 3.8 %collective-permute-start.13 = (bf16[8,12288]{1,0:T(8,128)(2,1)S(1)}, bf16[8,12288]{1,0:T(8,128)(2,1)S(1)}, u32[]{:S(2)}, u32[]{:S(2)}) collective-permute-start(bf16[8,12288]{1,0:T(8,128)(2,1)S(1)} %get-tuple-element.49), channel_id=1, source_target_pairs={{2,0},{3,1},{0,2},{1,3},{6,4},{7,5},{4,6},{5,7},{10,8},{11,9},{8,1... | collective-permute-start | bytes 589832 | tf_op jit(solution)/shard_map/ppermute | solution.py:111
  75.2 11.4 %collective-permute-done.29 = bf16[8,12288]{1,0:T(8,128)(2,1)S(1)} collective-permute-done((bf16[8,12288]{1,0:T(8,128)(2,1)S(1)}, bf16[8,12288]{1,0:T(8,128)(2,1)S(1)}, u32[]{:S(2)}, u32[]{:S(2)}) %collective-permute-start.29) | collective-permute-done | bytes 196640 | tf_op jit(solution)/shard_map/ppermute | solution.py:111
  86.6 2.5 %collective-permute-start.11 = (bf16[8,12288]{1,0:T(8,128)(2,1)S(1)}, bf16[8,12288]{1,0:T(8,128)(2,1)S(1)}, u32[]{:S(2)}, u32[]{:S(2)}) collective-permute-start(bf16[8,12288]{1,0:T(8,128)(2,1)S(1)} %get-tuple-element.48), channel_id=1, source_target_pairs={{3,0},{0,1},{1,2},{2,3},{7,4},{4,5},{5,6},{6,7},{11,8},{8,9},{9,10... | collective-permute-start | bytes 589832 | tf_op jit(solution)/shard_map/ppermute | solution.py:111
  90.5 2.8 %collective-permute-done.12 = bf16[8,12288]{1,0:T(8,128)(2,1)S(1)} collective-permute-done((bf16[8,12288]{1,0:T(8,128)(2,1)S(1)}, bf16[8,12288]{1,0:T(8,128)(2,1)S(1)}, u32[]{:S(2)}, u32[]{:S(2)}) %collective-permute-start.12) | collective-permute-done | bytes 196640 | tf_op jit(solution)/shard_map/ppermute | solution.py:111
  98.3 1.7 collective-permute-start.33
  101.8 1.7 collective-permute-done.16
  107.1 1.5 collective-permute-done.52
  110.6 1.5 collective-permute-done.53
  112.4 4.5 %collective-permute-start.58 = (bf16[8,12288]{1,0:T(8,128)(2,1)S(1)}, bf16[8,12288]{1,0:T(8,128)(2,1)S(1)}, u32[]{:S(2)}, u32[]{:S(2)}) collective-permute-start(bf16[8,12288]{1,0:T(8,128)(2,1)S(1)} %bitcast.85), channel_id=1, source_target_pairs={{0,3},{1,0},{2,1},{3,2},{4,7},{5,4},{6,5},{7,6},{8,11},{9,8},{10,9... | collective-permute-start | bytes 589832 | tf_op jit(solution)/shard_map/ppermute | solution.py:95
  116.9 1.5 collective-permute-start.56
  119.7 3.0 %collective-permute-start.54 = (bf16[8,4,24,128]{3,2,1,0:T(8,128)(2,1)S(1)}, bf16[8,4,24,128]{3,2,1,0:T(8,128)(2,1)S(1)}, u32[]{:S(2)}, u32[]{:S(2)}) collective-permute-start(bf16[8,4,24,128]{3,2,1,0:T(8,128)(2,1)S(1)} %convert_element_type.129), channel_id=1, source_target_pairs={{0,4},{4,8},{8,12},{12,16},{16,20},{20,24},{24,28},{1,5},{5,9},{9,... | collective-permute-start | bytes 589832 | tf_op jit(solution)/shard_map/ppermute | solution.py:21
  123.6 4.7 %collective-permute-done.57 = bf16[8,12288]{1,0:T(8,128)(2,1)S(1)} collective-permute-done((bf16[8,12288]{1,0:T(8,128)(2,1)S(1)}, bf16[8,12288]{1,0:T(8,128)(2,1)S(1)}, u32[]{:S(2)}, u32[]{:S(2)}) %collective-permute-start.57) | collective-permute-done | bytes 196640 | tf_op jit(solution)/shard_map/ppermute | solution.py:95
  128.3 3.6 %collective-permute-start.40 = (bf16[8,12288]{1,0:T(8,128)(2,1)S(1)}, bf16[8,12288]{1,0:T(8,128)(2,1)S(1)}, u32[]{:S(2)}, u32[]{:S(2)}) collective-permute-start(bf16[8,12288]{1,0:T(8,128)(2,1)S(1)} %bitcast.90), channel_id=1, source_target_pairs={{0,2},{1,3},{2,0},{3,1},{4,6},{5,7},{6,4},{7,5},{8,10},{9,11},{10,... | collective-permute-start | bytes 589832 | tf_op jit(solution)/shard_map/ppermute | solution.py:95
  131.9 8.1 %collective-permute-done.56 = bf16[8,12288]{1,0:T(8,128)(2,1)S(1)} collective-permute-done((bf16[8,12288]{1,0:T(8,128)(2,1)S(1)}, bf16[8,12288]{1,0:T(8,128)(2,1)S(1)}, u32[]{:S(2)}, u32[]{:S(2)}) %collective-permute-start.56) | collective-permute-done | bytes 196640 | tf_op jit(solution)/shard_map/ppermute | solution.py:95
  140.1 2.5 %collective-permute-start.39 = (bf16[8,12288]{1,0:T(8,128)(2,1)S(1)}, bf16[8,12288]{1,0:T(8,128)(2,1)S(1)}, u32[]{:S(2)}, u32[]{:S(2)}) collective-permute-start(bf16[8,12288]{1,0:T(8,128)(2,1)S(1)} %bitcast.91), channel_id=1, source_target_pairs={{0,1},{1,2},{2,3},{3,0},{4,5},{5,6},{6,7},{7,4},{8,9},{9,10},{10,1... | collective-permute-start | bytes 589832 | tf_op jit(solution)/shard_map/ppermute | solution.py:95
  142.5 2.0 fusion.21
  145.9 3.0 %collective-permute-start.37 = (bf16[8,4,24,128]{3,2,1,0:T(8,128)(2,1)S(1)}, bf16[8,4,24,128]{3,2,1,0:T(8,128)(2,1)S(1)}, u32[]{:S(2)}, u32[]{:S(2)}) collective-permute-start(bf16[8,4,24,128]{3,2,1,0:T(8,128)(2,1)S(1)} %convert_element_type.121), channel_id=1, source_target_pairs={{0,4},{4,8},{8,12},{12,16},{16,20},{20,24},{24,28},{1,5},{5,9},{9,... | collective-permute-start | bytes 589832 | tf_op jit(solution)/shard_map/ppermute | solution.py:21
  149.9 2.0 fusion.18
  152.0 2.0 collective-permute-start.60
  158.3 1.9 collective-permute-done.61
  160.2 2.0 convolution_convert_fusion
  162.2 2.4 %collective-permute-start.64 = (bf16[8,12288]{1,0:T(8,128)(2,1)S(1)}, bf16[8,12288]{1,0:T(8,128)(2,1)S(1)}, u32[]{:S(2)}, u32[]{:S(2)}) collective-permute-start(bf16[8,12288]{1,0:T(8,128)(2,1)S(1)} %get-tuple-element.44), channel_id=1, source_target_pairs={{2,0},{3,1},{0,2},{1,3},{6,4},{7,5},{4,6},{5,7},{10,8},{11,9},{8,1... | collective-permute-start | bytes 589832 | tf_op jit(solution)/shard_map/ppermute | solution.py:111
  166.6 2.0 convolution_convert_fusion.1
  169.7 1.8 collective-permute-start.46
  171.5 10.9 %collective-permute-done.64 = bf16[8,12288]{1,0:T(8,128)(2,1)S(1)} collective-permute-done((bf16[8,12288]{1,0:T(8,128)(2,1)S(1)}, bf16[8,12288]{1,0:T(8,128)(2,1)S(1)}, u32[]{:S(2)}, u32[]{:S(2)}) %collective-permute-start.64) | collective-permute-done | bytes 196640 | tf_op jit(solution)/shard_map/ppermute | solution.py:111
  182.4 6.6 %collective-permute-done.63 = bf16[8,12288]{1,0:T(8,128)(2,1)S(1)} collective-permute-done((bf16[8,12288]{1,0:T(8,128)(2,1)S(1)}, bf16[8,12288]{1,0:T(8,128)(2,1)S(1)}, u32[]{:S(2)}, u32[]{:S(2)}) %collective-permute-start.63) | collective-permute-done | bytes 196640 | tf_op jit(solution)/shard_map/ppermute | solution.py:111
  190.3 2.9 %collective-permute-done.47 = bf16[8,12288]{1,0:T(8,128)(2,1)S(1)} collective-permute-done((bf16[8,12288]{1,0:T(8,128)(2,1)S(1)}, bf16[8,12288]{1,0:T(8,128)(2,1)S(1)}, u32[]{:S(2)}, u32[]{:S(2)}) %collective-permute-start.47) | collective-permute-done | bytes 196640 | tf_op jit(solution)/shard_map/ppermute | solution.py:111
  193.2 4.8 %collective-permute-done.46 = bf16[8,12288]{1,0:T(8,128)(2,1)S(1)} collective-permute-done((bf16[8,12288]{1,0:T(8,128)(2,1)S(1)}, bf16[8,12288]{1,0:T(8,128)(2,1)S(1)}, u32[]{:S(2)}, u32[]{:S(2)}) %collective-permute-start.46) | collective-permute-done | bytes 196640 | tf_op jit(solution)/shard_map/ppermute | solution.py:111
  205.0 1.5 collective-permute-done.67
  (167 shorter events, 53.1 us)
Async XLA Ops:
  2.1 16.5 %collective-permute-start.24 = (bf16[8,12288]{1,0:T(8,128)(2,1)S(1)}, bf16[8,12288]{1,0:T(8,128)(2,1)S(1)}, u32[]{:S(2)}, u32[]{:S(2)}) collective-permute-start(bf16[8,12288]{1,0:T(8,128)(2,1)S(1)} %bitcast.81), channel_id=1, source_target_pairs={{0,3},{1,0},{2,1},{3,2},{4,7},{5,4},{6,5},{7,6},{8,11},{9,8},{10,9... | collective-permute-start | bytes 589832 | tf_op jit(solution)/shard_map/ppermute | solution.py:95
  2.1 18.8 %collective-permute-start.23 = (bf16[8,12288]{1,0:T(8,128)(2,1)S(1)}, bf16[8,12288]{1,0:T(8,128)(2,1)S(1)}, u32[]{:S(2)}, u32[]{:S(2)}) collective-permute-start(bf16[8,12288]{1,0:T(8,128)(2,1)S(1)} %bitcast.82), channel_id=1, source_target_pairs={{0,2},{1,3},{2,0},{3,1},{4,6},{5,7},{6,4},{7,5},{8,10},{9,11},{10,... | collective-permute-start | bytes 589832 | tf_op jit(solution)/shard_map/ppermute | solution.py:95
  5.2 25.9 %collective-permute-start.22 = (bf16[8,12288]{1,0:T(8,128)(2,1)S(1)}, bf16[8,12288]{1,0:T(8,128)(2,1)S(1)}, u32[]{:S(2)}, u32[]{:S(2)}) collective-permute-start(bf16[8,12288]{1,0:T(8,128)(2,1)S(1)} %bitcast.83), channel_id=1, source_target_pairs={{0,1},{1,2},{2,3},{3,0},{4,5},{5,6},{6,7},{7,4},{8,9},{9,10},{10,1... | collective-permute-start | bytes 589832 | tf_op jit(solution)/shard_map/ppermute | solution.py:95
  7.8 29.6 %collective-permute-start.7 = (bf16[8,12288]{1,0:T(8,128)(2,1)S(1)}, bf16[8,12288]{1,0:T(8,128)(2,1)S(1)}, u32[]{:S(2)}, u32[]{:S(2)}) collective-permute-start(bf16[8,12288]{1,0:T(8,128)(2,1)S(1)} %bitcast.77), channel_id=1, source_target_pairs={{0,3},{1,0},{2,1},{3,2},{4,7},{5,4},{6,5},{7,6},{8,11},{9,8},{10,9... | collective-permute-start | bytes 589832 | tf_op jit(solution)/shard_map/ppermute | solution.py:95
  17.2 21.4 %collective-permute-start.6 = (bf16[8,12288]{1,0:T(8,128)(2,1)S(1)}, bf16[8,12288]{1,0:T(8,128)(2,1)S(1)}, u32[]{:S(2)}, u32[]{:S(2)}) collective-permute-start(bf16[8,12288]{1,0:T(8,128)(2,1)S(1)} %bitcast.78), channel_id=1, source_target_pairs={{0,2},{1,3},{2,0},{3,1},{4,6},{5,7},{6,4},{7,5},{8,10},{9,11},{10,... | collective-permute-start | bytes 589832 | tf_op jit(solution)/shard_map/ppermute | solution.py:95
  18.6 24.8 %collective-permute-start.5 = (bf16[8,12288]{1,0:T(8,128)(2,1)S(1)}, bf16[8,12288]{1,0:T(8,128)(2,1)S(1)}, u32[]{:S(2)}, u32[]{:S(2)}) collective-permute-start(bf16[8,12288]{1,0:T(8,128)(2,1)S(1)} %bitcast.79), channel_id=1, source_target_pairs={{0,1},{1,2},{2,3},{3,0},{4,5},{5,6},{6,7},{7,4},{8,9},{9,10},{10,1... | collective-permute-start | bytes 589832 | tf_op jit(solution)/shard_map/ppermute | solution.py:95
  21.0 27.9 %collective-permute-start.4 = (bf16[8,4,24,128]{3,2,1,0:T(8,128)(2,1)S(1)}, bf16[8,4,24,128]{3,2,1,0:T(8,128)(2,1)S(1)}, u32[]{:S(2)}, u32[]{:S(2)}) collective-permute-start(bf16[8,4,24,128]{3,2,1,0:T(8,128)(2,1)S(1)} %convert_element_type.105), channel_id=1, source_target_pairs={{4,0},{8,4},{12,8},{16,12},{20,16},{24,20},{28,24},{5,1},{9,5},{13... | collective-permute-start | bytes 589832 | tf_op jit(solution)/shard_map/ppermute | solution.py:22
  31.0 17.9 %collective-permute-start.3 = (bf16[8,4,24,128]{3,2,1,0:T(8,128)(2,1)S(1)}, bf16[8,4,24,128]{3,2,1,0:T(8,128)(2,1)S(1)}, u32[]{:S(2)}, u32[]{:S(2)}) collective-permute-start(bf16[8,4,24,128]{3,2,1,0:T(8,128)(2,1)S(1)} %convert_element_type.105), channel_id=1, source_target_pairs={{0,4},{4,8},{8,12},{12,16},{16,20},{20,24},{24,28},{1,5},{5,9},{9,... | collective-permute-start | bytes 589832 | tf_op jit(solution)/shard_map/ppermute | solution.py:21
  37.4 16.5 %collective-permute-start.21 = (bf16[8,4,24,128]{3,2,1,0:T(8,128)(2,1)S(1)}, bf16[8,4,24,128]{3,2,1,0:T(8,128)(2,1)S(1)}, u32[]{:S(2)}, u32[]{:S(2)}) collective-permute-start(bf16[8,4,24,128]{3,2,1,0:T(8,128)(2,1)S(1)} %convert_element_type.113), channel_id=1, source_target_pairs={{4,0},{8,4},{12,8},{16,12},{20,16},{24,20},{28,24},{5,1},{9,5},{13... | collective-permute-start | bytes 589832 | tf_op jit(solution)/shard_map/ppermute | solution.py:22
  38.7 17.2 %collective-permute-start.20 = (bf16[8,4,24,128]{3,2,1,0:T(8,128)(2,1)S(1)}, bf16[8,4,24,128]{3,2,1,0:T(8,128)(2,1)S(1)}, u32[]{:S(2)}, u32[]{:S(2)}) collective-permute-start(bf16[8,4,24,128]{3,2,1,0:T(8,128)(2,1)S(1)} %convert_element_type.113), channel_id=1, source_target_pairs={{0,4},{4,8},{8,12},{12,16},{16,20},{20,24},{24,28},{1,5},{5,9},{9,... | collective-permute-start | bytes 589832 | tf_op jit(solution)/shard_map/ppermute | solution.py:21
  43.4 3.8 %collective-permute-start.25 = (f32[256,32]{0,1:T(8,128)S(1)}, f32[256,32]{0,1:T(8,128)S(1)}, u32[]{:S(2)}, u32[]{:S(2)}) collective-permute-start(f32[256,32]{0,1:T(8,128)S(1)} %fusion.15), channel_id=1, source_target_pairs={{0,4},{4,0},{8,12},{12,8},{16,20},{20,16},{24,28},{28,24},{1,5},{5... | collective-permute-start | bytes 98312 | tf_op jit(solution)/shard_map/ppermute | solution.py:33
  47.3 53.7 %collective-permute-start.19 = (f32[8]{0:T(128)S(1)}, f32[8]{0:T(128)S(1)}, u32[]{:S(2)}, u32[]{:S(2)}) collective-permute-start(f32[8]{0:T(128)S(1)} %add.563), channel_id=1, source_target_pairs={{0,16},{4,20},{8,24},{12,28},{16,0},{20,4},{24,8},{28,12},{1,17},{... | collective-permute-start | bytes 104 | tf_op jit(solution)/shard_map/ppermute | solution.py:33
  49.0 4.0 %collective-permute-start.26 = (f32[256,32]{0,1:T(8,128)S(1)}, f32[256,32]{0,1:T(8,128)S(1)}, u32[]{:S(2)}, u32[]{:S(2)}) collective-permute-start(f32[256,32]{0,1:T(8,128)S(1)} %add.593), channel_id=1, source_target_pairs={{0,8},{4,12},{8,0},{12,4},{16,24},{20,28},{24,16},{28,20},{1,9},{5... | collective-permute-start | bytes 98312 | tf_op jit(solution)/shard_map/ppermute | solution.py:33
  50.1 50.9 %collective-permute-start.2 = (f32[8]{0:T(128)S(1)}, f32[8]{0:T(128)S(1)}, u32[]{:S(2)}, u32[]{:S(2)}) collective-permute-start(f32[8]{0:T(128)S(1)} %add.522), channel_id=1, source_target_pairs={{0,16},{4,20},{8,24},{12,28},{16,0},{20,4},{24,8},{28,12},{1,17},{... | collective-permute-start | bytes 104 | tf_op jit(solution)/shard_map/ppermute | solution.py:33
  52.9 3.9 %collective-permute-start.9 = (f32[256,32]{0,1:T(8,128)S(1)}, f32[256,32]{0,1:T(8,128)S(1)}, u32[]{:S(2)}, u32[]{:S(2)}) collective-permute-start(f32[256,32]{0,1:T(8,128)S(1)} %add.552), channel_id=1, source_target_pairs={{0,8},{4,12},{8,0},{12,4},{16,24},{20,28},{24,16},{28,20},{1,9},{5... | collective-permute-start | bytes 98312 | tf_op jit(solution)/shard_map/ppermute | solution.py:33
  53.8 4.2 %collective-permute-start.27 = (f32[256,32]{0,1:T(8,128)S(1)}, f32[256,32]{0,1:T(8,128)S(1)}, u32[]{:S(2)}, u32[]{:S(2)}) collective-permute-start(f32[256,32]{0,1:T(8,128)S(1)} %add.594), channel_id=1, source_target_pairs={{0,16},{4,20},{8,24},{12,28},{16,0},{20,4},{24,8},{28,12},{1,17},{... | collective-permute-start | bytes 98312 | tf_op jit(solution)/shard_map/ppermute | solution.py:33
  56.9 5.9 %collective-permute-start.10 = (f32[256,32]{0,1:T(8,128)S(1)}, f32[256,32]{0,1:T(8,128)S(1)}, u32[]{:S(2)}, u32[]{:S(2)}) collective-permute-start(f32[256,32]{0,1:T(8,128)S(1)} %add.553), channel_id=1, source_target_pairs={{0,16},{4,20},{8,24},{12,28},{16,0},{20,4},{24,8},{28,12},{1,17},{... | collective-permute-start | bytes 98312 | tf_op jit(solution)/shard_map/ppermute | solution.py:33
  60.1 11.3 %collective-permute-start.30 = (bf16[8,12288]{1,0:T(8,128)(2,1)S(1)}, bf16[8,12288]{1,0:T(8,128)(2,1)S(1)}, u32[]{:S(2)}, u32[]{:S(2)}) collective-permute-start(bf16[8,12288]{1,0:T(8,128)(2,1)S(1)} %get-tuple-element.54), channel_id=1, source_target_pairs={{2,0},{3,1},{0,2},{1,3},{6,4},{7,5},{4,6},{5,7},{10,8},{11,9},{8,1... | collective-permute-start | bytes 589832 | tf_op jit(solution)/shard_map/ppermute | solution.py:111
  60.3 26.4 %collective-permute-start.29 = (bf16[8,12288]{1,0:T(8,128)(2,1)S(1)}, bf16[8,12288]{1,0:T(8,128)(2,1)S(1)}, u32[]{:S(2)}, u32[]{:S(2)}) collective-permute-start(bf16[8,12288]{1,0:T(8,128)(2,1)S(1)} %get-tuple-element.55), channel_id=1, source_target_pairs={{3,0},{0,1},{1,2},{2,3},{7,4},{4,5},{5,6},{6,7},{11,8},{8,9},{9,10... | collective-permute-start | bytes 589832 | tf_op jit(solution)/shard_map/ppermute | solution.py:111
  62.7 23.9 %collective-permute-start.28 = (bf16[8,12288]{1,0:T(8,128)(2,1)S(1)}, bf16[8,12288]{1,0:T(8,128)(2,1)S(1)}, u32[]{:S(2)}, u32[]{:S(2)}) collective-permute-start(bf16[8,12288]{1,0:T(8,128)(2,1)S(1)} %get-tuple-element.53), channel_id=1, source_target_pairs={{1,0},{2,1},{3,2},{0,3},{5,4},{6,5},{7,6},{4,7},{9,8},{10,9},{11,1... | collective-permute-start | bytes 589832 | tf_op jit(solution)/shard_map/ppermute | solution.py:111
  71.5 19.1 %collective-permute-start.13 = (bf16[8,12288]{1,0:T(8,128)(2,1)S(1)}, bf16[8,12288]{1,0:T(8,128)(2,1)S(1)}, u32[]{:S(2)}, u32[]{:S(2)}) collective-permute-start(bf16[8,12288]{1,0:T(8,128)(2,1)S(1)} %get-tuple-element.49), channel_id=1, source_target_pairs={{2,0},{3,1},{0,2},{1,3},{6,4},{7,5},{4,6},{5,7},{10,8},{11,9},{8,1... | collective-permute-start | bytes 589832 | tf_op jit(solution)/shard_map/ppermute | solution.py:111
  86.6 6.7 %collective-permute-start.12 = (bf16[8,12288]{1,0:T(8,128)(2,1)S(1)}, bf16[8,12288]{1,0:T(8,128)(2,1)S(1)}, u32[]{:S(2)}, u32[]{:S(2)}) collective-permute-start(bf16[8,12288]{1,0:T(8,128)(2,1)S(1)} %get-tuple-element.50), channel_id=1, source_target_pairs={{1,0},{2,1},{3,2},{0,3},{5,4},{6,5},{7,6},{4,7},{9,8},{10,9},{11,1... | collective-permute-start | bytes 589832 | tf_op jit(solution)/shard_map/ppermute | solution.py:111
  86.6 6.7 %collective-permute-start.11 = (bf16[8,12288]{1,0:T(8,128)(2,1)S(1)}, bf16[8,12288]{1,0:T(8,128)(2,1)S(1)}, u32[]{:S(2)}, u32[]{:S(2)}) collective-permute-start(bf16[8,12288]{1,0:T(8,128)(2,1)S(1)} %get-tuple-element.48), channel_id=1, source_target_pairs={{3,0},{0,1},{1,2},{2,3},{7,4},{4,5},{5,6},{6,7},{11,8},{8,9},{9,10... | collective-permute-start | bytes 589832 | tf_op jit(solution)/shard_map/ppermute | solution.py:111
  90.5 4.1 %collective-permute-start.31 = (f32[8]{0:T(128)S(1)}, f32[8]{0:T(128)S(1)}, u32[]{:S(2)}, u32[]{:S(2)}) collective-permute-start(f32[8]{0:T(128)S(1)} %get-tuple-element.38), channel_id=1, source_target_pairs={{0,4},{4,0},{8,12},{12,8},{16,20},{20,16},{24,28},{28,24},{1,5},{5... | collective-permute-start | bytes 104 | tf_op jit(solution)/shard_map/ppermute | solution.py:33
  96.2 3.8 %collective-permute-start.15 = (f32[8]{0:T(128)S(1)}, f32[8]{0:T(128)S(1)}, u32[]{:S(2)}, u32[]{:S(2)}) collective-permute-start(f32[8]{0:T(128)S(1)} %add.559), channel_id=1, source_target_pairs={{0,8},{4,12},{8,0},{12,4},{16,24},{20,28},{24,16},{28,20},{1,9},{5... | collective-permute-start | bytes 104 | tf_op jit(solution)/shard_map/ppermute | solution.py:33
  105.8 3.8 %collective-permute-start.35 = (f32[8]{0:T(128)S(1)}, f32[8]{0:T(128)S(1)}, u32[]{:S(2)}, u32[]{:S(2)}) collective-permute-start(f32[8]{0:T(128)S(1)} %add.603), channel_id=1, source_target_pairs={{0,8},{4,12},{8,0},{12,4},{16,24},{20,28},{24,16},{28,20},{1,9},{5... | collective-permute-start | bytes 104 | tf_op jit(solution)/shard_map/ppermute | solution.py:33
  109.6 10.1 %collective-permute-start.36 = (f32[8]{0:T(128)S(1)}, f32[8]{0:T(128)S(1)}, u32[]{:S(2)}, u32[]{:S(2)}) collective-permute-start(f32[8]{0:T(128)S(1)} %add.604), channel_id=1, source_target_pairs={{0,16},{4,20},{8,24},{12,28},{16,0},{20,4},{24,8},{28,12},{1,17},{... | collective-permute-start | bytes 104 | tf_op jit(solution)/shard_map/ppermute | solution.py:33
  112.4 10.7 %collective-permute-start.58 = (bf16[8,12288]{1,0:T(8,128)(2,1)S(1)}, bf16[8,12288]{1,0:T(8,128)(2,1)S(1)}, u32[]{:S(2)}, u32[]{:S(2)}) collective-permute-start(bf16[8,12288]{1,0:T(8,128)(2,1)S(1)} %bitcast.85), channel_id=1, source_target_pairs={{0,3},{1,0},{2,1},{3,2},{4,7},{5,4},{6,5},{7,6},{8,11},{9,8},{10,9... | collective-permute-start | bytes 589832 | tf_op jit(solution)/shard_map/ppermute | solution.py:95
  116.9 11.4 %collective-permute-start.57 = (bf16[8,12288]{1,0:T(8,128)(2,1)S(1)}, bf16[8,12288]{1,0:T(8,128)(2,1)S(1)}, u32[]{:S(2)}, u32[]{:S(2)}) collective-permute-start(bf16[8,12288]{1,0:T(8,128)(2,1)S(1)} %bitcast.86), channel_id=1, source_target_pairs={{0,2},{1,3},{2,0},{3,1},{4,6},{5,7},{6,4},{7,5},{8,10},{9,11},{10,... | collective-permute-start | bytes 589832 | tf_op jit(solution)/shard_map/ppermute | solution.py:95
  116.9 23.2 %collective-permute-start.56 = (bf16[8,12288]{1,0:T(8,128)(2,1)S(1)}, bf16[8,12288]{1,0:T(8,128)(2,1)S(1)}, u32[]{:S(2)}, u32[]{:S(2)}) collective-permute-start(bf16[8,12288]{1,0:T(8,128)(2,1)S(1)} %bitcast.87), channel_id=1, source_target_pairs={{0,1},{1,2},{2,3},{3,0},{4,5},{5,6},{6,7},{7,4},{8,9},{9,10},{10,1... | collective-permute-start | bytes 589832 | tf_op jit(solution)/shard_map/ppermute | solution.py:95
  118.4 33.6 %collective-permute-start.55 = (bf16[8,4,24,128]{3,2,1,0:T(8,128)(2,1)S(1)}, bf16[8,4,24,128]{3,2,1,0:T(8,128)(2,1)S(1)}, u32[]{:S(2)}, u32[]{:S(2)}) collective-permute-start(bf16[8,4,24,128]{3,2,1,0:T(8,128)(2,1)S(1)} %convert_element_type.129), channel_id=1, source_target_pairs={{4,0},{8,4},{12,8},{16,12},{20,16},{24,20},{28,24},{5,1},{9,5},{13... | collective-permute-start | bytes 589832 | tf_op jit(solution)/shard_map/ppermute | solution.py:22
  119.7 34.3 %collective-permute-start.54 = (bf16[8,4,24,128]{3,2,1,0:T(8,128)(2,1)S(1)}, bf16[8,4,24,128]{3,2,1,0:T(8,128)(2,1)S(1)}, u32[]{:S(2)}, u32[]{:S(2)}) collective-permute-start(bf16[8,4,24,128]{3,2,1,0:T(8,128)(2,1)S(1)} %convert_element_type.129), channel_id=1, source_target_pairs={{0,4},{4,8},{8,12},{12,16},{16,20},{20,24},{24,28},{1,5},{5,9},{9,... | collective-permute-start | bytes 589832 | tf_op jit(solution)/shard_map/ppermute | solution.py:21
  123.1 21.6 %collective-permute-start.41 = (bf16[8,12288]{1,0:T(8,128)(2,1)S(1)}, bf16[8,12288]{1,0:T(8,128)(2,1)S(1)}, u32[]{:S(2)}, u32[]{:S(2)}) collective-permute-start(bf16[8,12288]{1,0:T(8,128)(2,1)S(1)} %bitcast.89), channel_id=1, source_target_pairs={{0,3},{1,0},{2,1},{3,2},{4,7},{5,4},{6,5},{7,6},{8,11},{9,8},{10,9... | collective-permute-start | bytes 589832 | tf_op jit(solution)/shard_map/ppermute | solution.py:95
  128.3 17.6 %collective-permute-start.40 = (bf16[8,12288]{1,0:T(8,128)(2,1)S(1)}, bf16[8,12288]{1,0:T(8,128)(2,1)S(1)}, u32[]{:S(2)}, u32[]{:S(2)}) collective-permute-start(bf16[8,12288]{1,0:T(8,128)(2,1)S(1)} %bitcast.90), channel_id=1, source_target_pairs={{0,2},{1,3},{2,0},{3,1},{4,6},{5,7},{6,4},{7,5},{8,10},{9,11},{10,... | collective-permute-start | bytes 589832 | tf_op jit(solution)/shard_map/ppermute | solution.py:95
  140.1 8.9 %collective-permute-start.39 = (bf16[8,12288]{1,0:T(8,128)(2,1)S(1)}, bf16[8,12288]{1,0:T(8,128)(2,1)S(1)}, u32[]{:S(2)}, u32[]{:S(2)}) collective-permute-start(bf16[8,12288]{1,0:T(8,128)(2,1)S(1)} %bitcast.91), channel_id=1, source_target_pairs={{0,1},{1,2},{2,3},{3,0},{4,5},{5,6},{6,7},{7,4},{8,9},{9,10},{10,1... | collective-permute-start | bytes 589832 | tf_op jit(solution)/shard_map/ppermute | solution.py:95
  144.6 12.4 %collective-permute-start.38 = (bf16[8,4,24,128]{3,2,1,0:T(8,128)(2,1)S(1)}, bf16[8,4,24,128]{3,2,1,0:T(8,128)(2,1)S(1)}, u32[]{:S(2)}, u32[]{:S(2)}) collective-permute-start(bf16[8,4,24,128]{3,2,1,0:T(8,128)(2,1)S(1)} %convert_element_type.121), channel_id=1, source_target_pairs={{4,0},{8,4},{12,8},{16,12},{20,16},{24,20},{28,24},{5,1},{9,5},{13... | collective-permute-start | bytes 589832 | tf_op jit(solution)/shard_map/ppermute | solution.py:22
  145.9 11.1 %collective-permute-start.37 = (bf16[8,4,24,128]{3,2,1,0:T(8,128)(2,1)S(1)}, bf16[8,4,24,128]{3,2,1,0:T(8,128)(2,1)S(1)}, u32[]{:S(2)}, u32[]{:S(2)}) collective-permute-start(bf16[8,4,24,128]{3,2,1,0:T(8,128)(2,1)S(1)} %convert_element_type.121), channel_id=1, source_target_pairs={{0,4},{4,8},{8,12},{12,16},{16,20},{20,24},{24,28},{1,5},{5,9},{9,... | collective-permute-start | bytes 589832 | tf_op jit(solution)/shard_map/ppermute | solution.py:21
  152.0 4.0 %collective-permute-start.60 = (f32[256,32]{0,1:T(8,128)S(1)}, f32[256,32]{0,1:T(8,128)S(1)}, u32[]{:S(2)}, u32[]{:S(2)}) collective-permute-start(f32[256,32]{0,1:T(8,128)S(1)} %add.675), channel_id=1, source_target_pairs={{0,8},{4,12},{8,0},{12,4},{16,24},{20,28},{24,16},{28,20},{1,9},{5... | collective-permute-start | bytes 98312 | tf_op jit(solution)/shard_map/ppermute | solution.py:33
  154.1 4.0 %collective-permute-start.43 = (f32[256,32]{0,1:T(8,128)S(1)}, f32[256,32]{0,1:T(8,128)S(1)}, u32[]{:S(2)}, u32[]{:S(2)}) collective-permute-start(f32[256,32]{0,1:T(8,128)S(1)} %add.634), channel_id=1, source_target_pairs={{0,8},{4,12},{8,0},{12,4},{16,24},{20,28},{24,16},{28,20},{1,9},{5... | collective-permute-start | bytes 98312 | tf_op jit(solution)/shard_map/ppermute | solution.py:33
  156.0 4.1 %collective-permute-start.61 = (f32[256,32]{0,1:T(8,128)S(1)}, f32[256,32]{0,1:T(8,128)S(1)}, u32[]{:S(2)}, u32[]{:S(2)}) collective-permute-start(f32[256,32]{0,1:T(8,128)S(1)} %add.676), channel_id=1, source_target_pairs={{0,16},{4,20},{8,24},{12,28},{16,0},{20,4},{24,8},{28,12},{1,17},{... | collective-permute-start | bytes 98312 | tf_op jit(solution)/shard_map/ppermute | solution.py:33
  158.1 8.5 %collective-permute-start.44 = (f32[256,32]{0,1:T(8,128)S(1)}, f32[256,32]{0,1:T(8,128)S(1)}, u32[]{:S(2)}, u32[]{:S(2)}) collective-permute-start(f32[256,32]{0,1:T(8,128)S(1)} %add.635), channel_id=1, source_target_pairs={{0,16},{4,20},{8,24},{12,28},{16,0},{20,4},{24,8},{28,12},{1,17},{... | collective-permute-start | bytes 98312 | tf_op jit(solution)/shard_map/ppermute | solution.py:33
  162.2 20.1 %collective-permute-start.64 = (bf16[8,12288]{1,0:T(8,128)(2,1)S(1)}, bf16[8,12288]{1,0:T(8,128)(2,1)S(1)}, u32[]{:S(2)}, u32[]{:S(2)}) collective-permute-start(bf16[8,12288]{1,0:T(8,128)(2,1)S(1)} %get-tuple-element.44), channel_id=1, source_target_pairs={{2,0},{3,1},{0,2},{1,3},{6,4},{7,5},{4,6},{5,7},{10,8},{11,9},{8,1... | collective-permute-start | bytes 589832 | tf_op jit(solution)/shard_map/ppermute | solution.py:111
  164.6 24.3 %collective-permute-start.63 = (bf16[8,12288]{1,0:T(8,128)(2,1)S(1)}, bf16[8,12288]{1,0:T(8,128)(2,1)S(1)}, u32[]{:S(2)}, u32[]{:S(2)}) collective-permute-start(bf16[8,12288]{1,0:T(8,128)(2,1)S(1)} %get-tuple-element.45), channel_id=1, source_target_pairs={{3,0},{0,1},{1,2},{2,3},{7,4},{4,5},{5,6},{6,7},{11,8},{8,9},{9,10... | collective-permute-start | bytes 589832 | tf_op jit(solution)/shard_map/ppermute | solution.py:111
  165.9 23.1 %collective-permute-start.62 = (bf16[8,12288]{1,0:T(8,128)(2,1)S(1)}, bf16[8,12288]{1,0:T(8,128)(2,1)S(1)}, u32[]{:S(2)}, u32[]{:S(2)}) collective-permute-start(bf16[8,12288]{1,0:T(8,128)(2,1)S(1)} %get-tuple-element.43), channel_id=1, source_target_pairs={{1,0},{2,1},{3,2},{0,3},{5,4},{6,5},{7,6},{4,7},{9,8},{10,9},{11,1... | collective-permute-start | bytes 589832 | tf_op jit(solution)/shard_map/ppermute | solution.py:111
  168.7 24.5 %collective-permute-start.47 = (bf16[8,12288]{1,0:T(8,128)(2,1)S(1)}, bf16[8,12288]{1,0:T(8,128)(2,1)S(1)}, u32[]{:S(2)}, u32[]{:S(2)}) collective-permute-start(bf16[8,12288]{1,0:T(8,128)(2,1)S(1)} %get-tuple-element.41), channel_id=1, source_target_pairs={{2,0},{3,1},{0,2},{1,3},{6,4},{7,5},{4,6},{5,7},{10,8},{11,9},{8,1... | collective-permute-start | bytes 589832 | tf_op jit(solution)/shard_map/ppermute | solution.py:111
  169.7 28.2 %collective-permute-start.46 = (bf16[8,12288]{1,0:T(8,128)(2,1)S(1)}, bf16[8,12288]{1,0:T(8,128)(2,1)S(1)}, u32[]{:S(2)}, u32[]{:S(2)}) collective-permute-start(bf16[8,12288]{1,0:T(8,128)(2,1)S(1)} %get-tuple-element.42), channel_id=1, source_target_pairs={{1,0},{2,1},{3,2},{0,3},{5,4},{6,5},{7,6},{4,7},{9,8},{10,9},{11,1... | collective-permute-start | bytes 589832 | tf_op jit(solution)/shard_map/ppermute | solution.py:111
  182.4 15.6 %collective-permute-start.45 = (bf16[8,12288]{1,0:T(8,128)(2,1)S(1)}, bf16[8,12288]{1,0:T(8,128)(2,1)S(1)}, u32[]{:S(2)}, u32[]{:S(2)}) collective-permute-start(bf16[8,12288]{1,0:T(8,128)(2,1)S(1)} %get-tuple-element.40), channel_id=1, source_target_pairs={{3,0},{0,1},{1,2},{2,3},{7,4},{4,5},{5,6},{6,7},{11,8},{8,9},{9,10... | collective-permute-start | bytes 589832 | tf_op jit(solution)/shard_map/ppermute | solution.py:111
  190.2 9.1 %collective-permute-start.65 = (f32[8]{0:T(128)S(1)}, f32[8]{0:T(128)S(1)}, u32[]{:S(2)}, u32[]{:S(2)}) collective-permute-start(f32[8]{0:T(128)S(1)} %get-tuple-element.22), channel_id=1, source_target_pairs={{0,4},{4,0},{8,12},{12,8},{16,20},{20,16},{24,28},{28,24},{1,5},{5... | collective-permute-start | bytes 104 | tf_op jit(solution)/shard_map/ppermute | solution.py:33
  (25 other events, 150.6 us)

commit v13 on v12

--- a/solution.py
+++ b/solution.py
@@ -68,7 +68,7 @@
     return vector[:, None, None, None]
 
 
-def chain(occupied, potential, shifts, source_term, flip=False):
+def chain(occupied, potential, shifts, source_term, flip=False, first_blocks=None):
     local_bands, width_x, width_y, width_z = source_term.shape
     local_occupied = occupied.shape[0]
     band_count = lax.axis_size("band")
@@ -91,11 +91,14 @@
         kinetic = -0.5 * second_sum(padded, width_x, width_y, width_z)
         rounded = direction.astype(jnp.bfloat16).reshape(local_bands, local_cells)
         order = sorted(range(1, band_count), key=lambda d: (min(d, band_count - d), d if flip else -d))
-        arrived = {
-            d: lax.ppermute(rounded, "band", [(i, (i + d) % band_count) for i in range(band_count)])
-            for d in order
-        }
-        blocks = [rounded] + [arrived[d] for d in range(1, band_count)]
+        if iteration == 0 and first_blocks is not None:
+            blocks = first_blocks
+        else:
+            arrived = {
+                d: lax.ppermute(rounded, "band", [(i, (i + d) % band_count) for i in range(band_count)])
+                for d in order
+            }
+            blocks = [rounded] + [arrived[d] for d in range(1, band_count)]
         gathered = jnp.concatenate(blocks, axis=0)
         partial_margin = lax.dot_general(
             occupied_rows, gathered, (((1,), (1,)), ((), ())), preferred_element_type=jnp.float32
@@ -127,6 +130,14 @@
 def body(occupied, potential, shifts, source_term):
     pieces = 2 if source_term.shape[0] % 2 == 0 else 1
     width = source_term.shape[0] // pieces
+    band_count = lax.axis_size("band")
+    rounded = source_term.astype(jnp.bfloat16).reshape(source_term.shape[0], -1)
+    order = sorted(range(1, band_count), key=lambda d: (min(d, band_count - d), -d))
+    arrived = {
+        d: lax.ppermute(rounded, "band", [(i, (i + d) % band_count) for i in range(band_count)])
+        for d in order
+    }
+    source_blocks = [rounded] + [arrived[d] for d in range(1, band_count)]
     results = [
         chain(
             occupied,
@@ -134,6 +145,7 @@
             shifts[k * width : (k + 1) * width],
             source_term[k * width : (k + 1) * width],
             k % 2 == 1,
+            [block[k * width : (k + 1) * width] for block in source_blocks],
         )
         for k in range(pieces)
     ]

time: 210 us -> 206 us (0.981)
  matrix products: 19.1 us -> 16.1 us
    ppermute x0 -> x3, waiting for transfers between devices: none -> 13.2 us  [body(): lax.ppermute(rounded, 'band', [(i, (i + d) % band_count) for i in range(b...]
    ppermute x12 -> x6, starting transfers between devices: 22.1 us -> 10.8 us  [chain(): lax.ppermute(rounded, 'band', [(i, (i + d) % band_count) for i in range(b...]
    ppermute x12 -> x6, waiting for transfers between devices: 21.7 us -> 13.9 us  [chain(): lax.ppermute(rounded, 'band', [(i, (i + d) % band_count) for i in range(b...]
    ppermute x12, waiting for transfers between devices: 44.6 us -> 37.4 us  [chain(): lax.ppermute(part, 'band', [((i + d) % band_count, i) for i in range(band...]
    ppermute x12, starting transfers between devices: 17.5 us -> 24.3 us  [chain(): lax.ppermute(part, 'band', [((i + d) % band_count, i) for i in range(band...]
    ppermute x0 -> x3, starting transfers between devices: none -> 5.56 us  [body(): lax.ppermute(rounded, 'band', [(i, (i + d) % band_count) for i in range(b...]
    dot_general x4, matrix products: 11 us -> 8.07 us  [chain(): lax.dot_general(occupied_rows, gathered, (((1,), (1,)), ((), ())), prefer...]
  transfers between devices with their start and end apart: 68 -> 65, of which waited for: 33 -> 35; matrix products, arithmetic and copies ran while one was open for 12% -> 11% of each run, Pallas kernels for 0% -> 0%
where the time goes in v13:
time: 206 us
  waiting for transfers between devices  89.7 us (44%)
  starting transfers between devices  88.5 us (43%)
  matrix products  16.1 us (8%)
  other arithmetic  9.27 us (4%)
    ppermute x12, waiting for transfers between devices, chain(): lax.ppermute(part, 'band', [((i + d) % band_count, i) for i in range(band...  37.4 us
    ppermute x36, starting transfers between devices, grid_sum(): value = value + lax.ppermute(value, axis, pairs)  32.1 us
    ppermute x36, waiting for transfers between devices, grid_sum(): value = value + lax.ppermute(value, axis, pairs)  25.2 us
    ppermute x12, starting transfers between devices, chain(): lax.ppermute(part, 'band', [((i + d) % band_count, i) for i in range(band...  24.3 us
    ppermute x6, waiting for transfers between devices, chain(): lax.ppermute(rounded, 'band', [(i, (i + d) % band_count) for i in range(b...  13.9 us
    ppermute x3, waiting for transfers between devices, body(): lax.ppermute(rounded, 'band', [(i, (i + d) % band_count) for i in range(b...  13.2 us
    ppermute x6, starting transfers between devices, chain(): lax.ppermute(rounded, 'band', [(i, (i + d) % band_count) for i in range(b...  10.8 us
    ppermute x4, starting transfers between devices, with_halo(): before = lax.ppermute(last, axis, up)  10.4 us
  transfers between devices with their start and end apart: 65, of which 35 were waited for; matrix products, arithmetic and copies ran while one was open for 11% of the time, Pallas kernels for 0%

profile of v13, /device:TPU:8, one launch (start us, length us, event | category | flops | bytes accessed | tf_op | source)
XLA Modules:
  0.0 205.6 jit_solution(4579027478672707926)
XLA Ops:
  2.1 3.0 %collective-permute-start.6 = (bf16[16,12288]{1,0:T(8,128)(2,1)S(1)}, bf16[16,12288]{1,0:T(8,128)(2,1)S(1)}, u32[]{:S(2)}, u32[]{:S(2)}) collective-permute-start(bf16[16,12288]{1,0:T(8,128)(2,1)S(1)} %bitcast.82), channel_id=1, source_target_pairs={{0,2},{1,3},{2,0},{3,1},{4,6},{5,7},{6,4},{7,5},{8,10},{9,11},{10,... | collective-permute-start | bytes 1179656 | tf_op jit(solution)/shard_map/ppermute | solution.py:137
  5.2 2.5 %collective-permute-start.5 = (bf16[16,12288]{1,0:T(8,128)(2,1)S(1)}, bf16[16,12288]{1,0:T(8,128)(2,1)S(1)}, u32[]{:S(2)}, u32[]{:S(2)}) collective-permute-start(bf16[16,12288]{1,0:T(8,128)(2,1)S(1)} %bitcast.83), channel_id=1, source_target_pairs={{0,1},{1,2},{2,3},{3,0},{4,5},{5,6},{6,7},{7,4},{8,9},{9,10},{10,1... | collective-permute-start | bytes 1179656 | tf_op jit(solution)/shard_map/ppermute | solution.py:137
  7.9 1.6 collective-permute-start.4
  14.1 2.0 collective-permute-done.18
  17.6 2.0 collective-permute-done.1
  21.0 10.0 %collective-permute-done.7 = bf16[16,12288]{1,0:T(8,128)(2,1)S(1)} collective-permute-done((bf16[16,12288]{1,0:T(8,128)(2,1)S(1)}, bf16[16,12288]{1,0:T(8,128)(2,1)S(1)}, u32[]{:S(2)}, u32[]{:S(2)}) %collective-permute-start.7) | collective-permute-done | bytes 393248 | tf_op jit(solution)/shard_map/ppermute | solution.py:137
  32.3 3.0 %collective-permute-start.20 = (bf16[8,4,24,128]{3,2,1,0:T(8,128)(2,1)S(1)}, bf16[8,4,24,128]{3,2,1,0:T(8,128)(2,1)S(1)}, u32[]{:S(2)}, u32[]{:S(2)}) collective-permute-start(bf16[8,4,24,128]{3,2,1,0:T(8,128)(2,1)S(1)} %convert_element_type.115), channel_id=1, source_target_pairs={{0,4},{4,8},{8,12},{12,16},{16,20},{20,24},{24,28},{1,5},{5,9},{9,... | collective-permute-start | bytes 589832 | tf_op jit(solution)/shard_map/ppermute | solution.py:21
  35.4 3.2 %collective-permute-done.5 = bf16[16,12288]{1,0:T(8,128)(2,1)S(1)} collective-permute-done((bf16[16,12288]{1,0:T(8,128)(2,1)S(1)}, bf16[16,12288]{1,0:T(8,128)(2,1)S(1)}, u32[]{:S(2)}, u32[]{:S(2)}) %collective-permute-start.5) | collective-permute-done | bytes 393248 | tf_op jit(solution)/shard_map/ppermute | solution.py:137
  38.6 2.0 fusion.15
  40.7 2.0 fusion.12
  42.7 1.6 collective-permute-start.19
  44.6 1.5 collective-permute-start.23
  46.7 1.7 collective-permute-done.23
  50.7 1.8 collective-permute-done.9
  54.0 2.0 convolution_convert_fusion.2
  56.1 5.0 %collective-permute-start.26 = (bf16[8,12288]{1,0:T(8,128)(2,1)S(1)}, bf16[8,12288]{1,0:T(8,128)(2,1)S(1)}, u32[]{:S(2)}, u32[]{:S(2)}) collective-permute-start(bf16[8,12288]{1,0:T(8,128)(2,1)S(1)} %get-tuple-element.55), channel_id=1, source_target_pairs={{3,0},{0,1},{1,2},{2,3},{7,4},{4,5},{5,6},{6,7},{11,8},{8,9},{9,10... | collective-permute-start | bytes 589832 | tf_op jit(solution)/shard_map/ppermute | solution.py:114
  61.1 2.0 convolution_convert_fusion.3
  63.2 3.9 %collective-permute-done.27 = bf16[8,12288]{1,0:T(8,128)(2,1)S(1)} collective-permute-done((bf16[8,12288]{1,0:T(8,128)(2,1)S(1)}, bf16[8,12288]{1,0:T(8,128)(2,1)S(1)}, u32[]{:S(2)}, u32[]{:S(2)}) %collective-permute-start.27) | collective-permute-done | bytes 196640 | tf_op jit(solution)/shard_map/ppermute | solution.py:114
  67.1 3.6 %collective-permute-start.13 = (bf16[8,12288]{1,0:T(8,128)(2,1)S(1)}, bf16[8,12288]{1,0:T(8,128)(2,1)S(1)}, u32[]{:S(2)}, u32[]{:S(2)}) collective-permute-start(bf16[8,12288]{1,0:T(8,128)(2,1)S(1)} %get-tuple-element.49), channel_id=1, source_target_pairs={{2,0},{3,1},{0,2},{1,3},{6,4},{7,5},{4,6},{5,7},{10,8},{11,9},{8,1... | collective-permute-start | bytes 589832 | tf_op jit(solution)/shard_map/ppermute | solution.py:114
  70.7 11.2 %collective-permute-done.26 = bf16[8,12288]{1,0:T(8,128)(2,1)S(1)} collective-permute-done((bf16[8,12288]{1,0:T(8,128)(2,1)S(1)}, bf16[8,12288]{1,0:T(8,128)(2,1)S(1)}, u32[]{:S(2)}, u32[]{:S(2)}) %collective-permute-start.26) | collective-permute-done | bytes 196640 | tf_op jit(solution)/shard_map/ppermute | solution.py:114
  81.9 2.6 %collective-permute-start.11 = (bf16[8,12288]{1,0:T(8,128)(2,1)S(1)}, bf16[8,12288]{1,0:T(8,128)(2,1)S(1)}, u32[]{:S(2)}, u32[]{:S(2)}) collective-permute-start(bf16[8,12288]{1,0:T(8,128)(2,1)S(1)} %get-tuple-element.48), channel_id=1, source_target_pairs={{3,0},{0,1},{1,2},{2,3},{7,4},{4,5},{5,6},{6,7},{11,8},{8,9},{9,10... | collective-permute-start | bytes 589832 | tf_op jit(solution)/shard_map/ppermute | solution.py:114
  86.3 2.9 %collective-permute-done.12 = bf16[8,12288]{1,0:T(8,128)(2,1)S(1)} collective-permute-done((bf16[8,12288]{1,0:T(8,128)(2,1)S(1)}, bf16[8,12288]{1,0:T(8,128)(2,1)S(1)}, u32[]{:S(2)}, u32[]{:S(2)}) %collective-permute-start.12) | collective-permute-done | bytes 196640 | tf_op jit(solution)/shard_map/ppermute | solution.py:114
  90.5 3.7 %collective-permute-start.29 = (f32[8]{0:T(128)S(1)}, f32[8]{0:T(128)S(1)}, u32[]{:S(2)}, u32[]{:S(2)}) collective-permute-start(f32[8]{0:T(128)S(1)} %add.600), channel_id=1, source_target_pairs={{0,8},{4,12},{8,0},{12,4},{16,24},{20,28},{24,16},{28,20},{1,9},{5... | collective-permute-start | bytes 104 | tf_op jit(solution)/shard_map/ppermute | solution.py:33
  95.8 1.9 collective-permute-start.30
  99.3 2.0 collective-permute-done.16
  104.8 1.5 collective-permute-done.49
  108.4 1.5 collective-permute-done.50
  111.6 1.5 collective-permute-start.53
  114.5 3.0 %collective-permute-start.51 = (bf16[8,4,24,128]{3,2,1,0:T(8,128)(2,1)S(1)}, bf16[8,4,24,128]{3,2,1,0:T(8,128)(2,1)S(1)}, u32[]{:S(2)}, u32[]{:S(2)}) collective-permute-start(bf16[8,4,24,128]{3,2,1,0:T(8,128)(2,1)S(1)} %convert_element_type.131), channel_id=1, source_target_pairs={{0,4},{4,8},{8,12},{12,16},{16,20},{20,24},{24,28},{1,5},{5,9},{9,... | collective-permute-start | bytes 589832 | tf_op jit(solution)/shard_map/ppermute | solution.py:21
  117.8 8.2 %collective-permute-done.55 = bf16[8,12288]{1,0:T(8,128)(2,1)S(1)} collective-permute-done((bf16[8,12288]{1,0:T(8,128)(2,1)S(1)}, bf16[8,12288]{1,0:T(8,128)(2,1)S(1)}, u32[]{:S(2)}, u32[]{:S(2)}) %collective-permute-start.55) | collective-permute-done | bytes 196640 | tf_op jit(solution)/shard_map/ppermute | solution.py:98
  127.0 5.7 %collective-permute-done.53 = bf16[8,12288]{1,0:T(8,128)(2,1)S(1)} collective-permute-done((bf16[8,12288]{1,0:T(8,128)(2,1)S(1)}, bf16[8,12288]{1,0:T(8,128)(2,1)S(1)}, u32[]{:S(2)}, u32[]{:S(2)}) %collective-permute-start.53) | collective-permute-done | bytes 196640 | tf_op jit(solution)/shard_map/ppermute | solution.py:98
  132.7 6.8 %collective-permute-start.36 = (bf16[8,12288]{1,0:T(8,128)(2,1)S(1)}, bf16[8,12288]{1,0:T(8,128)(2,1)S(1)}, u32[]{:S(2)}, u32[]{:S(2)}) collective-permute-start(bf16[8,12288]{1,0:T(8,128)(2,1)S(1)} %bitcast.92), channel_id=1, source_target_pairs={{0,1},{1,2},{2,3},{3,0},{4,5},{5,6},{6,7},{7,4},{8,9},{9,10},{10,1... | collective-permute-start | bytes 589832 | tf_op jit(solution)/shard_map/ppermute | solution.py:98
  139.5 2.0 fusion.21
  142.8 3.0 %collective-permute-start.34 = (bf16[8,4,24,128]{3,2,1,0:T(8,128)(2,1)S(1)}, bf16[8,4,24,128]{3,2,1,0:T(8,128)(2,1)S(1)}, u32[]{:S(2)}, u32[]{:S(2)}) collective-permute-start(bf16[8,4,24,128]{3,2,1,0:T(8,128)(2,1)S(1)} %convert_element_type.123), channel_id=1, source_target_pairs={{0,4},{4,8},{8,12},{12,16},{16,20},{20,24},{24,28},{1,5},{5,9},{9,... | collective-permute-start | bytes 589832 | tf_op jit(solution)/shard_map/ppermute | solution.py:21
  146.6 2.0 fusion.18
  148.7 1.5 collective-permute-start.57
  154.9 1.8 collective-permute-done.58
  156.7 2.0 convolution_convert_fusion
  159.7 3.8 %collective-permute-start.60 = (bf16[8,12288]{1,0:T(8,128)(2,1)S(1)}, bf16[8,12288]{1,0:T(8,128)(2,1)S(1)}, u32[]{:S(2)}, u32[]{:S(2)}) collective-permute-start(bf16[8,12288]{1,0:T(8,128)(2,1)S(1)} %get-tuple-element.45), channel_id=1, source_target_pairs={{3,0},{0,1},{1,2},{2,3},{7,4},{4,5},{5,6},{6,7},{11,8},{8,9},{9,10... | collective-permute-start | bytes 589832 | tf_op jit(solution)/shard_map/ppermute | solution.py:114
  163.5 2.0 convolution_convert_fusion.1
  165.5 1.5 collective-permute-start.44
  167.1 2.0 collective-permute-start.43
  170.5 4.7 %collective-permute-start.42 = (bf16[8,12288]{1,0:T(8,128)(2,1)S(1)}, bf16[8,12288]{1,0:T(8,128)(2,1)S(1)}, u32[]{:S(2)}, u32[]{:S(2)}) collective-permute-start(bf16[8,12288]{1,0:T(8,128)(2,1)S(1)} %get-tuple-element.40), channel_id=1, source_target_pairs={{3,0},{0,1},{1,2},{2,3},{7,4},{4,5},{5,6},{6,7},{11,8},{8,9},{9,10... | collective-permute-start | bytes 589832 | tf_op jit(solution)/shard_map/ppermute | solution.py:114
  175.2 10.1 %collective-permute-done.60 = bf16[8,12288]{1,0:T(8,128)(2,1)S(1)} collective-permute-done((bf16[8,12288]{1,0:T(8,128)(2,1)S(1)}, bf16[8,12288]{1,0:T(8,128)(2,1)S(1)}, u32[]{:S(2)}, u32[]{:S(2)}) %collective-permute-start.60) | collective-permute-done | bytes 196640 | tf_op jit(solution)/shard_map/ppermute | solution.py:114
  187.8 1.7 collective-permute-done.44
  189.5 4.6 %collective-permute-done.43 = bf16[8,12288]{1,0:T(8,128)(2,1)S(1)} collective-permute-done((bf16[8,12288]{1,0:T(8,128)(2,1)S(1)}, bf16[8,12288]{1,0:T(8,128)(2,1)S(1)}, u32[]{:S(2)}, u32[]{:S(2)}) %collective-permute-start.43) | collective-permute-done | bytes 196640 | tf_op jit(solution)/shard_map/ppermute | solution.py:114
  195.5 1.5 collective-permute-start.63
  201.1 1.5 collective-permute-done.64
  (164 shorter events, 51.5 us)
Async XLA Ops:
  2.1 28.9 %collective-permute-start.7 = (bf16[16,12288]{1,0:T(8,128)(2,1)S(1)}, bf16[16,12288]{1,0:T(8,128)(2,1)S(1)}, u32[]{:S(2)}, u32[]{:S(2)}) collective-permute-start(bf16[16,12288]{1,0:T(8,128)(2,1)S(1)} %bitcast.81), channel_id=1, source_target_pairs={{0,3},{1,0},{2,1},{3,2},{4,7},{5,4},{6,5},{7,6},{8,11},{9,8},{10,9... | collective-permute-start | bytes 1179656 | tf_op jit(solution)/shard_map/ppermute | solution.py:137
  2.1 30.2 %collective-permute-start.6 = (bf16[16,12288]{1,0:T(8,128)(2,1)S(1)}, bf16[16,12288]{1,0:T(8,128)(2,1)S(1)}, u32[]{:S(2)}, u32[]{:S(2)}) collective-permute-start(bf16[16,12288]{1,0:T(8,128)(2,1)S(1)} %bitcast.82), channel_id=1, source_target_pairs={{0,2},{1,3},{2,0},{3,1},{4,6},{5,7},{6,4},{7,5},{8,10},{9,11},{10,... | collective-permute-start | bytes 1179656 | tf_op jit(solution)/shard_map/ppermute | solution.py:137
  5.2 33.4 %collective-permute-start.5 = (bf16[16,12288]{1,0:T(8,128)(2,1)S(1)}, bf16[16,12288]{1,0:T(8,128)(2,1)S(1)}, u32[]{:S(2)}, u32[]{:S(2)}) collective-permute-start(bf16[16,12288]{1,0:T(8,128)(2,1)S(1)} %bitcast.83), channel_id=1, source_target_pairs={{0,1},{1,2},{2,3},{3,0},{4,5},{5,6},{6,7},{7,4},{8,9},{9,10},{10,1... | collective-permute-start | bytes 1179656 | tf_op jit(solution)/shard_map/ppermute | solution.py:137
  7.9 36.4 %collective-permute-start.4 = (bf16[8,4,24,128]{3,2,1,0:T(8,128)(2,1)S(1)}, bf16[8,4,24,128]{3,2,1,0:T(8,128)(2,1)S(1)}, u32[]{:S(2)}, u32[]{:S(2)}) collective-permute-start(bf16[8,4,24,128]{3,2,1,0:T(8,128)(2,1)S(1)} %convert_element_type.106), channel_id=1, source_target_pairs={{4,0},{8,4},{12,8},{16,12},{20,16},{24,20},{28,24},{5,1},{9,5},{13... | collective-permute-start | bytes 589832 | tf_op jit(solution)/shard_map/ppermute | solution.py:22
  19.7 24.9 %collective-permute-start.3 = (bf16[8,4,24,128]{3,2,1,0:T(8,128)(2,1)S(1)}, bf16[8,4,24,128]{3,2,1,0:T(8,128)(2,1)S(1)}, u32[]{:S(2)}, u32[]{:S(2)}) collective-permute-start(bf16[8,4,24,128]{3,2,1,0:T(8,128)(2,1)S(1)} %convert_element_type.106), channel_id=1, source_target_pairs={{0,4},{4,8},{8,12},{12,16},{16,20},{20,24},{24,28},{1,5},{5,9},{9,... | collective-permute-start | bytes 589832 | tf_op jit(solution)/shard_map/ppermute | solution.py:21
  31.0 19.0 %collective-permute-start.21 = (bf16[8,4,24,128]{3,2,1,0:T(8,128)(2,1)S(1)}, bf16[8,4,24,128]{3,2,1,0:T(8,128)(2,1)S(1)}, u32[]{:S(2)}, u32[]{:S(2)}) collective-permute-start(bf16[8,4,24,128]{3,2,1,0:T(8,128)(2,1)S(1)} %convert_element_type.115), channel_id=1, source_target_pairs={{4,0},{8,4},{12,8},{16,12},{20,16},{24,20},{28,24},{5,1},{9,5},{13... | collective-permute-start | bytes 589832 | tf_op jit(solution)/shard_map/ppermute | solution.py:22
  32.3 18.3 %collective-permute-start.20 = (bf16[8,4,24,128]{3,2,1,0:T(8,128)(2,1)S(1)}, bf16[8,4,24,128]{3,2,1,0:T(8,128)(2,1)S(1)}, u32[]{:S(2)}, u32[]{:S(2)}) collective-permute-start(bf16[8,4,24,128]{3,2,1,0:T(8,128)(2,1)S(1)} %convert_element_type.115), channel_id=1, source_target_pairs={{0,4},{4,8},{8,12},{12,16},{16,20},{20,24},{24,28},{1,5},{5,9},{9,... | collective-permute-start | bytes 589832 | tf_op jit(solution)/shard_map/ppermute | solution.py:21
  42.7 56.0 %collective-permute-start.19 = (f32[8]{0:T(128)S(1)}, f32[8]{0:T(128)S(1)}, u32[]{:S(2)}, u32[]{:S(2)}) collective-permute-start(f32[8]{0:T(128)S(1)} %add.563), channel_id=1, source_target_pairs={{0,16},{4,20},{8,24},{12,28},{16,0},{20,4},{24,8},{28,12},{1,17},{... | collective-permute-start | bytes 104 | tf_op jit(solution)/shard_map/ppermute | solution.py:33
  44.6 3.9 %collective-permute-start.23 = (f32[256,32]{0,1:T(8,128)S(1)}, f32[256,32]{0,1:T(8,128)S(1)}, u32[]{:S(2)}, u32[]{:S(2)}) collective-permute-start(f32[256,32]{0,1:T(8,128)S(1)} %add.593), channel_id=1, source_target_pairs={{0,8},{4,12},{8,0},{12,4},{16,24},{20,28},{24,16},{28,20},{1,9},{5... | collective-permute-start | bytes 98312 | tf_op jit(solution)/shard_map/ppermute | solution.py:33
  46.2 52.6 %collective-permute-start.2 = (f32[8]{0:T(128)S(1)}, f32[8]{0:T(128)S(1)}, u32[]{:S(2)}, u32[]{:S(2)}) collective-permute-start(f32[8]{0:T(128)S(1)} %add.522), channel_id=1, source_target_pairs={{0,16},{4,20},{8,24},{12,28},{16,0},{20,4},{24,8},{28,12},{1,17},{... | collective-permute-start | bytes 104 | tf_op jit(solution)/shard_map/ppermute | solution.py:33
  48.5 3.9 %collective-permute-start.9 = (f32[256,32]{0,1:T(8,128)S(1)}, f32[256,32]{0,1:T(8,128)S(1)}, u32[]{:S(2)}, u32[]{:S(2)}) collective-permute-start(f32[256,32]{0,1:T(8,128)S(1)} %add.552), channel_id=1, source_target_pairs={{0,8},{4,12},{8,0},{12,4},{16,24},{20,28},{24,16},{28,20},{1,9},{5... | collective-permute-start | bytes 98312 | tf_op jit(solution)/shard_map/ppermute | solution.py:33
  50.0 4.0 %collective-permute-start.24 = (f32[256,32]{0,1:T(8,128)S(1)}, f32[256,32]{0,1:T(8,128)S(1)}, u32[]{:S(2)}, u32[]{:S(2)}) collective-permute-start(f32[256,32]{0,1:T(8,128)S(1)} %add.594), channel_id=1, source_target_pairs={{0,16},{4,20},{8,24},{12,28},{16,0},{20,4},{24,8},{28,12},{1,17},{... | collective-permute-start | bytes 98312 | tf_op jit(solution)/shard_map/ppermute | solution.py:33
  52.4 8.7 %collective-permute-start.10 = (f32[256,32]{0,1:T(8,128)S(1)}, f32[256,32]{0,1:T(8,128)S(1)}, u32[]{:S(2)}, u32[]{:S(2)}) collective-permute-start(f32[256,32]{0,1:T(8,128)S(1)} %add.553), channel_id=1, source_target_pairs={{0,16},{4,20},{8,24},{12,28},{16,0},{20,4},{24,8},{28,12},{1,17},{... | collective-permute-start | bytes 98312 | tf_op jit(solution)/shard_map/ppermute | solution.py:33
  56.0 11.0 %collective-permute-start.27 = (bf16[8,12288]{1,0:T(8,128)(2,1)S(1)}, bf16[8,12288]{1,0:T(8,128)(2,1)S(1)}, u32[]{:S(2)}, u32[]{:S(2)}) collective-permute-start(bf16[8,12288]{1,0:T(8,128)(2,1)S(1)} %get-tuple-element.54), channel_id=1, source_target_pairs={{2,0},{3,1},{0,2},{1,3},{6,4},{7,5},{4,6},{5,7},{10,8},{11,9},{8,1... | collective-permute-start | bytes 589832 | tf_op jit(solution)/shard_map/ppermute | solution.py:114
  56.1 25.8 %collective-permute-start.26 = (bf16[8,12288]{1,0:T(8,128)(2,1)S(1)}, bf16[8,12288]{1,0:T(8,128)(2,1)S(1)}, u32[]{:S(2)}, u32[]{:S(2)}) collective-permute-start(bf16[8,12288]{1,0:T(8,128)(2,1)S(1)} %get-tuple-element.55), channel_id=1, source_target_pairs={{3,0},{0,1},{1,2},{2,3},{7,4},{4,5},{5,6},{6,7},{11,8},{8,9},{9,10... | collective-permute-start | bytes 589832 | tf_op jit(solution)/shard_map/ppermute | solution.py:114
  61.1 20.8 %collective-permute-start.25 = (bf16[8,12288]{1,0:T(8,128)(2,1)S(1)}, bf16[8,12288]{1,0:T(8,128)(2,1)S(1)}, u32[]{:S(2)}, u32[]{:S(2)}) collective-permute-start(bf16[8,12288]{1,0:T(8,128)(2,1)S(1)} %get-tuple-element.53), channel_id=1, source_target_pairs={{1,0},{2,1},{3,2},{0,3},{5,4},{6,5},{7,6},{4,7},{9,8},{10,9},{11,1... | collective-permute-start | bytes 589832 | tf_op jit(solution)/shard_map/ppermute | solution.py:114
  67.1 19.2 %collective-permute-start.13 = (bf16[8,12288]{1,0:T(8,128)(2,1)S(1)}, bf16[8,12288]{1,0:T(8,128)(2,1)S(1)}, u32[]{:S(2)}, u32[]{:S(2)}) collective-permute-start(bf16[8,12288]{1,0:T(8,128)(2,1)S(1)} %get-tuple-element.49), channel_id=1, source_target_pairs={{2,0},{3,1},{0,2},{1,3},{6,4},{7,5},{4,6},{5,7},{10,8},{11,9},{8,1... | collective-permute-start | bytes 589832 | tf_op jit(solution)/shard_map/ppermute | solution.py:114
  81.9 7.3 %collective-permute-start.12 = (bf16[8,12288]{1,0:T(8,128)(2,1)S(1)}, bf16[8,12288]{1,0:T(8,128)(2,1)S(1)}, u32[]{:S(2)}, u32[]{:S(2)}) collective-permute-start(bf16[8,12288]{1,0:T(8,128)(2,1)S(1)} %get-tuple-element.50), channel_id=1, source_target_pairs={{1,0},{2,1},{3,2},{0,3},{5,4},{6,5},{7,6},{4,7},{9,8},{10,9},{11,1... | collective-permute-start | bytes 589832 | tf_op jit(solution)/shard_map/ppermute | solution.py:114
  81.9 7.3 %collective-permute-start.11 = (bf16[8,12288]{1,0:T(8,128)(2,1)S(1)}, bf16[8,12288]{1,0:T(8,128)(2,1)S(1)}, u32[]{:S(2)}, u32[]{:S(2)}) collective-permute-start(bf16[8,12288]{1,0:T(8,128)(2,1)S(1)} %get-tuple-element.48), channel_id=1, source_target_pairs={{3,0},{0,1},{1,2},{2,3},{7,4},{4,5},{5,6},{6,7},{11,8},{8,9},{9,10... | collective-permute-start | bytes 589832 | tf_op jit(solution)/shard_map/ppermute | solution.py:114
  86.2 4.3 %collective-permute-start.28 = (f32[8]{0:T(128)S(1)}, f32[8]{0:T(128)S(1)}, u32[]{:S(2)}, u32[]{:S(2)}) collective-permute-start(f32[8]{0:T(128)S(1)} %get-tuple-element.38), channel_id=1, source_target_pairs={{0,4},{4,0},{8,12},{12,8},{16,20},{20,16},{24,28},{28,24},{1,5},{5... | collective-permute-start | bytes 104 | tf_op jit(solution)/shard_map/ppermute | solution.py:33
  90.4 3.8 %collective-permute-start.14 = (f32[8]{0:T(128)S(1)}, f32[8]{0:T(128)S(1)}, u32[]{:S(2)}, u32[]{:S(2)}) collective-permute-start(f32[8]{0:T(128)S(1)} %get-tuple-element.34), channel_id=1, source_target_pairs={{0,4},{4,0},{8,12},{12,8},{16,20},{20,16},{24,28},{28,24},{1,5},{5... | collective-permute-start | bytes 104 | tf_op jit(solution)/shard_map/ppermute | solution.py:33
  90.5 5.2 %collective-permute-start.29 = (f32[8]{0:T(128)S(1)}, f32[8]{0:T(128)S(1)}, u32[]{:S(2)}, u32[]{:S(2)}) collective-permute-start(f32[8]{0:T(128)S(1)} %add.600), channel_id=1, source_target_pairs={{0,8},{4,12},{8,0},{12,4},{16,24},{20,28},{24,16},{28,20},{1,9},{5... | collective-permute-start | bytes 104 | tf_op jit(solution)/shard_map/ppermute | solution.py:33
  94.2 3.5 %collective-permute-start.15 = (f32[8]{0:T(128)S(1)}, f32[8]{0:T(128)S(1)}, u32[]{:S(2)}, u32[]{:S(2)}) collective-permute-start(f32[8]{0:T(128)S(1)} %add.559), channel_id=1, source_target_pairs={{0,8},{4,12},{8,0},{12,4},{16,24},{20,28},{24,16},{28,20},{1,9},{5... | collective-permute-start | bytes 104 | tf_op jit(solution)/shard_map/ppermute | solution.py:33
  103.8 3.5 %collective-permute-start.32 = (f32[8]{0:T(128)S(1)}, f32[8]{0:T(128)S(1)}, u32[]{:S(2)}, u32[]{:S(2)}) collective-permute-start(f32[8]{0:T(128)S(1)} %add.603), channel_id=1, source_target_pairs={{0,8},{4,12},{8,0},{12,4},{16,24},{20,28},{24,16},{28,20},{1,9},{5... | collective-permute-start | bytes 104 | tf_op jit(solution)/shard_map/ppermute | solution.py:33
  107.4 7.1 %collective-permute-start.33 = (f32[8]{0:T(128)S(1)}, f32[8]{0:T(128)S(1)}, u32[]{:S(2)}, u32[]{:S(2)}) collective-permute-start(f32[8]{0:T(128)S(1)} %add.604), channel_id=1, source_target_pairs={{0,16},{4,20},{8,24},{12,28},{16,0},{20,4},{24,8},{28,12},{1,17},{... | collective-permute-start | bytes 104 | tf_op jit(solution)/shard_map/ppermute | solution.py:33
  110.2 15.8 %collective-permute-start.55 = (bf16[8,12288]{1,0:T(8,128)(2,1)S(1)}, bf16[8,12288]{1,0:T(8,128)(2,1)S(1)}, u32[]{:S(2)}, u32[]{:S(2)}) collective-permute-start(bf16[8,12288]{1,0:T(8,128)(2,1)S(1)} %bitcast.86), channel_id=1, source_target_pairs={{0,3},{1,0},{2,1},{3,2},{4,7},{5,4},{6,5},{7,6},{8,11},{9,8},{10,9... | collective-permute-start | bytes 589832 | tf_op jit(solution)/shard_map/ppermute | solution.py:98
  111.6 14.4 %collective-permute-start.54 = (bf16[8,12288]{1,0:T(8,128)(2,1)S(1)}, bf16[8,12288]{1,0:T(8,128)(2,1)S(1)}, u32[]{:S(2)}, u32[]{:S(2)}) collective-permute-start(bf16[8,12288]{1,0:T(8,128)(2,1)S(1)} %bitcast.87), channel_id=1, source_target_pairs={{0,2},{1,3},{2,0},{3,1},{4,6},{5,7},{6,4},{7,5},{8,10},{9,11},{10,... | collective-permute-start | bytes 589832 | tf_op jit(solution)/shard_map/ppermute | solution.py:98
  111.6 21.0 %collective-permute-start.53 = (bf16[8,12288]{1,0:T(8,128)(2,1)S(1)}, bf16[8,12288]{1,0:T(8,128)(2,1)S(1)}, u32[]{:S(2)}, u32[]{:S(2)}) collective-permute-start(bf16[8,12288]{1,0:T(8,128)(2,1)S(1)} %bitcast.88), channel_id=1, source_target_pairs={{0,1},{1,2},{2,3},{3,0},{4,5},{5,6},{6,7},{7,4},{8,9},{9,10},{10,1... | collective-permute-start | bytes 589832 | tf_op jit(solution)/shard_map/ppermute | solution.py:98
  113.2 35.5 %collective-permute-start.52 = (bf16[8,4,24,128]{3,2,1,0:T(8,128)(2,1)S(1)}, bf16[8,4,24,128]{3,2,1,0:T(8,128)(2,1)S(1)}, u32[]{:S(2)}, u32[]{:S(2)}) collective-permute-start(bf16[8,4,24,128]{3,2,1,0:T(8,128)(2,1)S(1)} %convert_element_type.131), channel_id=1, source_target_pairs={{4,0},{8,4},{12,8},{16,12},{20,16},{24,20},{28,24},{5,1},{9,5},{13... | collective-permute-start | bytes 589832 | tf_op jit(solution)/shard_map/ppermute | solution.py:22
  114.5 35.7 %collective-permute-start.51 = (bf16[8,4,24,128]{3,2,1,0:T(8,128)(2,1)S(1)}, bf16[8,4,24,128]{3,2,1,0:T(8,128)(2,1)S(1)}, u32[]{:S(2)}, u32[]{:S(2)}) collective-permute-start(bf16[8,4,24,128]{3,2,1,0:T(8,128)(2,1)S(1)} %convert_element_type.131), channel_id=1, source_target_pairs={{0,4},{4,8},{8,12},{12,16},{16,20},{20,24},{24,28},{1,5},{5,9},{9,... | collective-permute-start | bytes 589832 | tf_op jit(solution)/shard_map/ppermute | solution.py:21
  126.0 15.5 %collective-permute-start.38 = (bf16[8,12288]{1,0:T(8,128)(2,1)S(1)}, bf16[8,12288]{1,0:T(8,128)(2,1)S(1)}, u32[]{:S(2)}, u32[]{:S(2)}) collective-permute-start(bf16[8,12288]{1,0:T(8,128)(2,1)S(1)} %bitcast.90), channel_id=1, source_target_pairs={{0,3},{1,0},{2,1},{3,2},{4,7},{5,4},{6,5},{7,6},{8,11},{9,8},{10,9... | collective-permute-start | bytes 589832 | tf_op jit(solution)/shard_map/ppermute | solution.py:98
  126.0 16.8 %collective-permute-start.37 = (bf16[8,12288]{1,0:T(8,128)(2,1)S(1)}, bf16[8,12288]{1,0:T(8,128)(2,1)S(1)}, u32[]{:S(2)}, u32[]{:S(2)}) collective-permute-start(bf16[8,12288]{1,0:T(8,128)(2,1)S(1)} %bitcast.91), channel_id=1, source_target_pairs={{0,2},{1,3},{2,0},{3,1},{4,6},{5,7},{6,4},{7,5},{8,10},{9,11},{10,... | collective-permute-start | bytes 589832 | tf_op jit(solution)/shard_map/ppermute | solution.py:98
  132.7 13.2 %collective-permute-start.36 = (bf16[8,12288]{1,0:T(8,128)(2,1)S(1)}, bf16[8,12288]{1,0:T(8,128)(2,1)S(1)}, u32[]{:S(2)}, u32[]{:S(2)}) collective-permute-start(bf16[8,12288]{1,0:T(8,128)(2,1)S(1)} %bitcast.92), channel_id=1, source_target_pairs={{0,1},{1,2},{2,3},{3,0},{4,5},{5,6},{6,7},{7,4},{8,9},{9,10},{10,1... | collective-permute-start | bytes 589832 | tf_op jit(solution)/shard_map/ppermute | solution.py:98
  141.5 12.1 %collective-permute-start.35 = (bf16[8,4,24,128]{3,2,1,0:T(8,128)(2,1)S(1)}, bf16[8,4,24,128]{3,2,1,0:T(8,128)(2,1)S(1)}, u32[]{:S(2)}, u32[]{:S(2)}) collective-permute-start(bf16[8,4,24,128]{3,2,1,0:T(8,128)(2,1)S(1)} %convert_element_type.123), channel_id=1, source_target_pairs={{4,0},{8,4},{12,8},{16,12},{20,16},{24,20},{28,24},{5,1},{9,5},{13... | collective-permute-start | bytes 589832 | tf_op jit(solution)/shard_map/ppermute | solution.py:22
  142.8 10.8 %collective-permute-start.34 = (bf16[8,4,24,128]{3,2,1,0:T(8,128)(2,1)S(1)}, bf16[8,4,24,128]{3,2,1,0:T(8,128)(2,1)S(1)}, u32[]{:S(2)}, u32[]{:S(2)}) collective-permute-start(bf16[8,4,24,128]{3,2,1,0:T(8,128)(2,1)S(1)} %convert_element_type.123), channel_id=1, source_target_pairs={{0,4},{4,8},{8,12},{12,16},{16,20},{20,24},{24,28},{1,5},{5,9},{9,... | collective-permute-start | bytes 589832 | tf_op jit(solution)/shard_map/ppermute | solution.py:21
  148.7 4.0 %collective-permute-start.57 = (f32[256,32]{0,1:T(8,128)S(1)}, f32[256,32]{0,1:T(8,128)S(1)}, u32[]{:S(2)}, u32[]{:S(2)}) collective-permute-start(f32[256,32]{0,1:T(8,128)S(1)} %add.675), channel_id=1, source_target_pairs={{0,8},{4,12},{8,0},{12,4},{16,24},{20,28},{24,16},{28,20},{1,9},{5... | collective-permute-start | bytes 98312 | tf_op jit(solution)/shard_map/ppermute | solution.py:33
  150.3 4.0 %collective-permute-start.40 = (f32[256,32]{0,1:T(8,128)S(1)}, f32[256,32]{0,1:T(8,128)S(1)}, u32[]{:S(2)}, u32[]{:S(2)}) collective-permute-start(f32[256,32]{0,1:T(8,128)S(1)} %add.634), channel_id=1, source_target_pairs={{0,8},{4,12},{8,0},{12,4},{16,24},{20,28},{24,16},{28,20},{1,9},{5... | collective-permute-start | bytes 98312 | tf_op jit(solution)/shard_map/ppermute | solution.py:33
  152.7 4.0 %collective-permute-start.58 = (f32[256,32]{0,1:T(8,128)S(1)}, f32[256,32]{0,1:T(8,128)S(1)}, u32[]{:S(2)}, u32[]{:S(2)}) collective-permute-start(f32[256,32]{0,1:T(8,128)S(1)} %add.676), channel_id=1, source_target_pairs={{0,16},{4,20},{8,24},{12,28},{16,0},{20,4},{24,8},{28,12},{1,17},{... | collective-permute-start | bytes 98312 | tf_op jit(solution)/shard_map/ppermute | solution.py:33
  154.3 9.2 %collective-permute-start.41 = (f32[256,32]{0,1:T(8,128)S(1)}, f32[256,32]{0,1:T(8,128)S(1)}, u32[]{:S(2)}, u32[]{:S(2)}) collective-permute-start(f32[256,32]{0,1:T(8,128)S(1)} %add.635), channel_id=1, source_target_pairs={{0,16},{4,20},{8,24},{12,28},{16,0},{20,4},{24,8},{28,12},{1,17},{... | collective-permute-start | bytes 98312 | tf_op jit(solution)/shard_map/ppermute | solution.py:33
  158.7 11.8 %collective-permute-start.61 = (bf16[8,12288]{1,0:T(8,128)(2,1)S(1)}, bf16[8,12288]{1,0:T(8,128)(2,1)S(1)}, u32[]{:S(2)}, u32[]{:S(2)}) collective-permute-start(bf16[8,12288]{1,0:T(8,128)(2,1)S(1)} %get-tuple-element.44), channel_id=1, source_target_pairs={{2,0},{3,1},{0,2},{1,3},{6,4},{7,5},{4,6},{5,7},{10,8},{11,9},{8,1... | collective-permute-start | bytes 589832 | tf_op jit(solution)/shard_map/ppermute | solution.py:114
  159.7 25.6 %collective-permute-start.60 = (bf16[8,12288]{1,0:T(8,128)(2,1)S(1)}, bf16[8,12288]{1,0:T(8,128)(2,1)S(1)}, u32[]{:S(2)}, u32[]{:S(2)}) collective-permute-start(bf16[8,12288]{1,0:T(8,128)(2,1)S(1)} %get-tuple-element.45), channel_id=1, source_target_pairs={{3,0},{0,1},{1,2},{2,3},{7,4},{4,5},{5,6},{6,7},{11,8},{8,9},{9,10... | collective-permute-start | bytes 589832 | tf_op jit(solution)/shard_map/ppermute | solution.py:114
  163.5 23.0 %collective-permute-start.59 = (bf16[8,12288]{1,0:T(8,128)(2,1)S(1)}, bf16[8,12288]{1,0:T(8,128)(2,1)S(1)}, u32[]{:S(2)}, u32[]{:S(2)}) collective-permute-start(bf16[8,12288]{1,0:T(8,128)(2,1)S(1)} %get-tuple-element.43), channel_id=1, source_target_pairs={{1,0},{2,1},{3,2},{0,3},{5,4},{6,5},{7,6},{4,7},{9,8},{10,9},{11,1... | collective-permute-start | bytes 589832 | tf_op jit(solution)/shard_map/ppermute | solution.py:114
  165.5 24.0 %collective-permute-start.44 = (bf16[8,12288]{1,0:T(8,128)(2,1)S(1)}, bf16[8,12288]{1,0:T(8,128)(2,1)S(1)}, u32[]{:S(2)}, u32[]{:S(2)}) collective-permute-start(bf16[8,12288]{1,0:T(8,128)(2,1)S(1)} %get-tuple-element.41), channel_id=1, source_target_pairs={{2,0},{3,1},{0,2},{1,3},{6,4},{7,5},{4,6},{5,7},{10,8},{11,9},{8,1... | collective-permute-start | bytes 589832 | tf_op jit(solution)/shard_map/ppermute | solution.py:114
  167.1 27.0 %collective-permute-start.43 = (bf16[8,12288]{1,0:T(8,128)(2,1)S(1)}, bf16[8,12288]{1,0:T(8,128)(2,1)S(1)}, u32[]{:S(2)}, u32[]{:S(2)}) collective-permute-start(bf16[8,12288]{1,0:T(8,128)(2,1)S(1)} %get-tuple-element.42), channel_id=1, source_target_pairs={{1,0},{2,1},{3,2},{0,3},{5,4},{6,5},{7,6},{4,7},{9,8},{10,9},{11,1... | collective-permute-start | bytes 589832 | tf_op jit(solution)/shard_map/ppermute | solution.py:114
  170.5 23.6 %collective-permute-start.42 = (bf16[8,12288]{1,0:T(8,128)(2,1)S(1)}, bf16[8,12288]{1,0:T(8,128)(2,1)S(1)}, u32[]{:S(2)}, u32[]{:S(2)}) collective-permute-start(bf16[8,12288]{1,0:T(8,128)(2,1)S(1)} %get-tuple-element.40), channel_id=1, source_target_pairs={{3,0},{0,1},{1,2},{2,3},{7,4},{4,5},{5,6},{6,7},{11,8},{8,9},{9,10... | collective-permute-start | bytes 589832 | tf_op jit(solution)/shard_map/ppermute | solution.py:114
  187.7 7.7 %collective-permute-start.62 = (f32[8]{0:T(128)S(1)}, f32[8]{0:T(128)S(1)}, u32[]{:S(2)}, u32[]{:S(2)}) collective-permute-start(f32[8]{0:T(128)S(1)} %get-tuple-element.22), channel_id=1, source_target_pairs={{0,4},{4,0},{8,12},{12,8},{16,20},{20,16},{24,28},{28,24},{1,5},{5... | collective-permute-start | bytes 104 | tf_op jit(solution)/shard_map/ppermute | solution.py:33
  195.5 3.6 %collective-permute-start.63 = (f32[8]{0:T(128)S(1)}, f32[8]{0:T(128)S(1)}, u32[]{:S(2)}, u32[]{:S(2)}) collective-permute-start(f32[8]{0:T(128)S(1)} %add.682), channel_id=1, source_target_pairs={{0,8},{4,12},{8,0},{12,4},{16,24},{20,28},{24,16},{28,20},{1,9},{5... | collective-permute-start | bytes 104 | tf_op jit(solution)/shard_map/ppermute | solution.py:33
  197.0 3.5 %collective-permute-start.46 = (f32[8]{0:T(128)S(1)}, f32[8]{0:T(128)S(1)}, u32[]{:S(2)}, u32[]{:S(2)}) collective-permute-start(f32[8]{0:T(128)S(1)} %add.641), channel_id=1, source_target_pairs={{0,8},{4,12},{8,0},{12,4},{16,24},{20,28},{24,16},{28,20},{1,9},{5... | collective-permute-start | bytes 104 | tf_op jit(solution)/shard_map/ppermute | solution.py:33
  (21 other events, 109.9 us)
